TPU v7x, 256 devices: a whole 4x4x8 slice. The times are simulated.
256 devices in a mesh: kv: 8 (over x, core), seq: 32 (over z, y).
Axes of the slice: x: 4, y: 4, z: 8, core: 2. Of those that a mesh axis runs over, the one named last changes fastest.
Arguments:
- hidden_states: bfloat16 [6144, 2048], P('seq')
- attn_gain: float32 [2048], replicated, may hold values from 0.5 to 1.5
- w_q: bfloat16 [2048, 2048], P(None, 'kv')
- w_k: bfloat16 [2048, 512], P(None, 'kv')
- w_v: bfloat16 [2048, 512], P(None, 'kv'), may hold values from -0.125 to 0.125
- w_o: bfloat16 [2048, 2048], P('kv'), may hold values from -0.125 to 0.125
- final_gain: float32 [2048], replicated, may hold values from 0.5 to 1.5
- w_head: bfloat16 [2048, 49408], P(None, ('kv', 'seq'))
- doc_lengths: int32 [26], replicated, may hold values from 1 to 3072, as said below
- target_ids: int32 [6144], replicated, may hold values from 0 to 49154, as said below
- vocab_mask: int32 [49408], P(('kv', 'seq')), may hold values from 0 to 1, as said below
Outputs:
- log_probs: float32 [6144], P('seq')
- entropies: float32 [6144], P('seq')
Inputs may be any that keep to these rules, and one draw needn't show every extreme that they name: `doc_lengths`: they sum to 6144; one is 3072, one more is over 1536, every other is under 64. `target_ids`: each names an entry whose vocab_mask is 1. `vocab_mask`: entries from 49155 on are 0.
All inputs are finite; a program needn't handle non-finite values.
Results may differ from a plain program's by a relative error of at most 0.0045.
Values may be sent and summed in bfloat16 or wider, within the bound.
No kernel may reach another device: no remote copies, remote signals or barrier semaphores. Data moves between devices by JAX's collectives and lax.ppermute only.
A program may use at most 128 MiB of HBM per device.

v0:
```python
import math

import jax
import jax.numpy as jnp
from jax import lax
from jax.sharding import PartitionSpec as P

HEAD_DIM = 64


ROPE_THETA = 10000000.0
NORM_EPS = 1e-05
NEG_FILL = -1e30
ATTN_SCALE = 0.015625
RESID_SCALE = 5.0
LOGIT_SCALE = 0.125


def rms_norm(values, gain_vec):
    return (
        values * lax.rsqrt(jnp.mean(values * values, axis=-1, keepdims=True) + NORM_EPS) * gain_vec
    )


def rotate(values, positions):
    half_dim = values.shape[-1] // 2
    inverse = jnp.exp(
        jnp.arange(half_dim, dtype=jnp.float32) * (-2.0 * math.log(ROPE_THETA) / values.shape[-1])
    )
    angles = positions.astype(jnp.float32)[:, None] * inverse[None, :]
    cos_val = jnp.cos(angles)[:, None, :]
    sine_val = jnp.sin(angles)[:, None, :]
    lower_half = values[..., :half_dim]
    upper_half = values[..., half_dim:]
    return jnp.concatenate(
        [
            lower_half * cos_val - upper_half * sine_val,
            upper_half * cos_val + lower_half * sine_val,
        ],
        axis=-1,
    )


def local(
    hidden_states,
    attn_gain,
    w_q,
    w_k,
    w_v,
    w_o,
    final_gain,
    w_head,
    doc_lengths,
    target_ids,
    vocab_mask,
):
    tok_rows = hidden_states.shape[0]
    seq_index = lax.axis_index("seq")
    kv_local = w_k.shape[1] // HEAD_DIM
    q_local = w_q.shape[1] // HEAD_DIM
    group_size = q_local // kv_local
    key_width = kv_local * HEAD_DIM
    stream = hidden_states.astype(jnp.float32)
    normed_in = rms_norm(stream, attn_gain).astype(jnp.bfloat16)
    queries = jnp.dot(normed_in, w_q, preferred_element_type=jnp.float32)
    key_proj = jnp.dot(normed_in, w_k, preferred_element_type=jnp.float32)
    value_proj = jnp.dot(normed_in, w_v, preferred_element_type=jnp.float32)
    token_pos = seq_index * tok_rows + jnp.arange(tok_rows, dtype=jnp.int32)
    doc_ends = jnp.cumsum(doc_lengths)
    doc_starts = doc_ends - doc_lengths
    doc_start = jnp.max(
        jnp.where(doc_starts[None, :] <= token_pos[:, None], doc_starts[None, :], 0), axis=1
    )
    positions = token_pos - doc_start
    rotated_q = rotate(queries.reshape(tok_rows, q_local, HEAD_DIM), positions).astype(jnp.bfloat16)
    rotated_q = rotated_q.reshape(tok_rows, kv_local, group_size, HEAD_DIM)
    rotated_k = rotate(key_proj.reshape(tok_rows, kv_local, HEAD_DIM), positions).astype(
        jnp.bfloat16
    )
    packed = jnp.concatenate(
        [rotated_k.reshape(tok_rows, key_width), value_proj.astype(jnp.bfloat16)], axis=1
    )
    earliest = doc_start[0]
    latest = token_pos[tok_rows - 1]
    initial = (
        jnp.full((kv_local, group_size, tok_rows), NEG_FILL, jnp.float32),
        jnp.zeros((kv_local, group_size, tok_rows), jnp.float32),
        jnp.zeros((kv_local, group_size, tok_rows, HEAD_DIM), jnp.float32),
    )
    shard_rows = lax.all_gather(packed, "seq", axis=0, tiled=True)
    offset = jnp.int32(0)
    row_count = shard_rows.shape[0]
    key_pos = jnp.arange(row_count, dtype=jnp.int32)

    def update(current):
        top_score, totals, context_sum = current
        key_rows = shard_rows[:, :key_width].reshape(row_count, kv_local, HEAD_DIM)
        value_rows = shard_rows[:, key_width:].reshape(row_count, kv_local, HEAD_DIM)
        scores = (
            jnp.einsum("tkgd,skd->kgts", rotated_q, key_rows, preferred_element_type=jnp.float32)
            * ATTN_SCALE
        )
        allowed = (key_pos[None, :] >= doc_start[:, None]) & (
            key_pos[None, :] <= token_pos[:, None]
        )
        scores = jnp.where(allowed, scores, NEG_FILL)
        new_top = jnp.maximum(top_score, jnp.max(scores, axis=-1))
        weights = jnp.where(allowed, jnp.exp(scores - new_top[..., None]), 0.0)
        rescale = jnp.exp(top_score - new_top)
        totals = jnp.sum(weights, axis=-1)
        context_sum = jnp.einsum(
            "kgts,skd->kgtd",
            weights.astype(jnp.bfloat16),
            value_rows,
            preferred_element_type=jnp.float32,
        )
        return (new_top, totals, context_sum)

    skip_piece = (offset + row_count <= earliest) | (offset > latest)
    top_score, totals, context_sum = lax.cond(skip_piece, lambda current: current, update, initial)
    context = (
        (context_sum / totals[..., None])
        .transpose(2, 0, 1, 3)
        .reshape(tok_rows, q_local * HEAD_DIM)
        .astype(jnp.bfloat16)
    )
    vocab_local = w_head.shape[1]
    flat_rank = lax.axis_index(("kv", "seq"))
    live_mask = vocab_mask == 1
    columns = flat_rank * vocab_local + jnp.arange(vocab_local, dtype=jnp.int32)
    attn_out = lax.psum(jnp.dot(context, w_o, preferred_element_type=jnp.float32), "kv")
    final_in = rms_norm(stream + RESID_SCALE * attn_out, final_gain).astype(jnp.bfloat16)
    head_shard_rows = lax.all_gather(final_in, "seq", axis=0, tiled=True)
    logits = jnp.dot(head_shard_rows, w_head, preferred_element_type=jnp.float32) * LOGIT_SCALE
    masked = jnp.where(live_mask[None, :], logits, NEG_FILL)
    top_row = jnp.max(masked, axis=1)
    shifted = jnp.where(live_mask[None, :], masked - top_row[:, None], 0.0)
    expw = jnp.where(live_mask[None, :], jnp.exp(shifted), 0.0)
    target = jnp.sum(jnp.where(target_ids[:, None] == columns[None, :], logits, 0.0), axis=1)
    row_stats = jnp.stack([top_row, jnp.sum(expw, axis=1), jnp.sum(expw * shifted, axis=1), target])
    top_all = lax.pmax(row_stats[0], ("kv", "seq"))
    rescale = jnp.exp(row_stats[0] - top_all)
    total_all, spread_all, target_all = lax.psum(
        (
            row_stats[1] * rescale,
            rescale * (row_stats[2] + (row_stats[0] - top_all) * row_stats[1]),
            row_stats[3],
        ),
        ("kv", "seq"),
    )
    log_prob = target_all - top_all - jnp.log(total_all)
    entropy = jnp.log(total_all) - spread_all / total_all
    log_probs = lax.dynamic_slice_in_dim(log_prob, seq_index * tok_rows, tok_rows, 0)
    entropies = lax.dynamic_slice_in_dim(entropy, seq_index * tok_rows, tok_rows, 0)
    return (log_probs, entropies)


def solution(mesh):
    in_specs = (
        P("seq", None),
        P(),
        P(None, "kv"),
        P(None, "kv"),
        P(None, "kv"),
        P("kv", None),
        P(),
        P(None, ("kv", "seq")),
        P(),
        P(),
        P(("kv", "seq")),
    )
    out_specs = (P("seq"), P("seq"))
    return jax.shard_map(local, mesh=mesh, in_specs=in_specs, out_specs=out_specs, check_vma=False)
```

profile of v0, /device:TPU:24, one launch (start us, length us, event | category | flops | bytes accessed | tf_op | source)
XLA Modules:
  0.0 714.2 jit_solution(9096987467154612652)
XLA Ops:
  7.2 0.0 copy-start
  7.2 0.0 copy-start.1
  7.2 0.0 copy-start.6
  7.2 0.0 copy-start.4
  7.2 0.0 all-gather.3.cloned.1.call-start
  7.3 1.5 fusion.16
  8.8 0.8 copy.22
  9.6 0.1 reduce.2
  9.7 0.7 sub.45
  10.4 0.1 select_reduce_fusion.2
  10.5 1.6 convolution_convert_fusion
  12.2 1.6 convolution_bitcast_fusion
  13.8 0.2 fusion.30
  14.0 0.7 copy.23
  14.7 0.0 all-gather.3.cloned.1.call-update
  14.8 0.0 all-reduce.4.cloned.1.call-start
  14.8 0.6 slice.25
  15.4 0.5 slice.24
  17.2 0.2 multiply_cosine_fusion
  17.4 0.0 copy-done.1
  17.4 0.0 copy-done.6
  17.4 0.0 copy-done.4
  17.5 0.6 fusion.33
  18.2 75.3 %all-gather.3.cloned.1.call-done = bf16[6144,128]{1,0:T(8,128)(2,1)} async-done(((bf16[192,128]{1,0:T(8,128)(2,1)}), bf16[6144,128]{1,0:T(8,128)(2,1)}) %all-gather.3.cloned.1.call-update) | async-done | bytes 1572880 | tf_op jit(solution)/shard_map/all_gather | solution.py:90
  93.5 21.4 %conditional.1 = (f32[1,4,192]{2,1,0:T(4,128)S(1)}, f32[1,4,192,64]{2,3,1,0:T(8,128)S(1)}) conditional(s32[]{:T(128)} %bitcast.9, (s32[6144]{0:T(1024)S(1)}, s32[6144]{0:T(1024)S(1)}, s32[192]{0:T(256)S(1)}, s32[192]{0:T(256)S(1)}, bf16[6144,128]{1,0:T(8,128)(2,1)}, /*index=5*/bf16[192,1,4,64]{0,3,2,1:T(8,128)(2,1)S(1)}) %tuple.16, () %tuple.17), branch_computations={%region_3.6_spmd, %region_6.7_spmd} | conditional | flops 1272839424 | bytes 66424336 | solution.py:120
  93.5 1.0 compare_and_fusion
  94.5 2.6 copy.25
  97.1 5.0 fusion
  102.1 6.3 fusion.7
  108.4 6.5 fusion.2
  114.9 0.0 copy-start.3
  114.9 0.0 copy-done
  115.0 0.0 copy-start.7
  115.0 0.0 copy-start.5
  115.0 1.6 fusion.37
  116.5 0.0 all-reduce.4.cloned.1.call-update
  116.6 0.2 all-gather.5.cloned.1.call-start
  116.8 67.5 %all-reduce.4.cloned.1.call-done = f32[192,2048]{1,0:T(8,128)} async-done(((f32[192,2048]{1,0:T(8,128)}), f32[192,2048]{1,0:T(8,128)}) %all-reduce.4.cloned.1.call-update) | async-done | bytes 1572880 | tf_op jit(solution)/shard_map/psum | solution.py:131
  184.3 1.7 multiply_reduce_fusion.1
  186.1 0.0 copy-done.3
  186.1 2.6 multiply_convert_fusion
  188.7 0.0 all-gather.5.cloned.1.call-update
  188.8 0.0 all-reduce.6.cloned.1.call-start
  188.8 0.0 copy-done.7
  188.8 0.0 copy-start.2
  188.9 181.2 %all-gather.5.cloned.1.call-done = bf16[6144,2048]{1,0:T(8,128)(2,1)} async-done(((bf16[192,2048]{1,0:T(8,128)(2,1)}), bf16[6144,2048]{1,0:T(8,128)(2,1)}) %all-gather.5.cloned.1.call-update) | async-done | bytes 25165840 | tf_op jit(solution)/shard_map/all_gather | solution.py:133
  370.0 0.0 copy-done.5
  370.0 14.4 %select_reduce_fusion.1 = (f32[6144]{0:T(1024)S(1)}, f32[6144,193]{0,1:T(8,128)}) fusion(pred[193]{0:T(512)(128)(4,1)S(1)} %broadcast_compare_fusion, bf16[6144,2048]{1,0:T(8,128)(2,1)} %all-gather.5.cloned.1.call-done, bf16[2048,193]{0,1:T(8,128)(2,1)S(1)} %copy-done.5), kind=kOutput, calls=%fused_computation.24 | convolution fusion | flops 4860555264 | bytes 30724288 | tf_op jit(solution)/shard_map/dot_general | solution.py:134
  384.4 75.6 %pmax.7 = f32[6144]{0:T(1024)S(1)} all-reduce(f32[6144]{0:T(1024)S(1)} %get-tuple-element.53), channel_id=1, replica_groups=mesh['kv'=8,'seq'=32] {'kv','seq'}, use_global_device_ids=true, to_apply=%region_12.13 | all-reduce | flops 6144 | bytes 49152 | tf_op jit(solution)/shard_map/pmax | solution.py:141
  460.0 0.0 copy-done.2
  460.0 4.9 multiply_reduce_fusion
  464.8 0.6 add_multiply_fusion
  465.5 0.0 all-reduce.6.cloned.1.call-update
  465.5 240.0 %all-reduce.6.cloned.1.call-done = (f32[6144]{0:T(1024)}, f32[6144]{0:T(1024)}, f32[6144]{0:T(1024)}) async-done(((f32[6144]{0:T(1024)}, f32[6144]{0:T(1024)}, f32[6144]{0:T(1024)}), (f32[6144]{0:T(1024)}, f32[6144]{0:T(1024)}, f32[6144]{0:T(1024)})) %all-reduce.6.cloned.1.call-update) | async-done | bytes 73744 | tf_op jit(solution)/shard_map/psum | solution.py:143
  705.5 0.7 log.4
  706.3 1.4 fusion.32
  (14 shorter events, 0.2 us)
Async XLA Ops:
  7.2 107.8 %copy-start = (bf16[256,2048]{1,0:T(8,128)(2,1)S(1)}, bf16[256,2048]{1,0:T(8,128)(2,1)}, u32[]{:S(2)}) copy-start(bf16[256,2048]{1,0:T(8,128)(2,1)} %param.18) | copy-start | bytes 3145732
  7.2 10.2 %copy-start.1 = (bf16[192,2048]{1,0:T(8,128)(2,1)S(1)}, bf16[192,2048]{1,0:T(8,128)(2,1)}, u32[]{:S(2)}) copy-start(bf16[192,2048]{1,0:T(8,128)(2,1)} %param.13) | copy-start | bytes 2359300
  7.2 10.2 %copy-start.6 = (f32[2048]{0:T(1024)S(1)}, f32[2048]{0:T(1024)}, u32[]{:S(2)}) copy-start(f32[2048]{0:T(1024)} %param.14) | copy-start | bytes 24580
  7.2 10.2 %copy-start.4 = (bf16[2048,256]{1,0:T(8,128)(2,1)S(1)}, bf16[2048,256]{1,0:T(8,128)(2,1)}, u32[]{:S(2)}) copy-start(bf16[2048,256]{1,0:T(8,128)(2,1)} %param.15) | copy-start | bytes 3145732
  7.2 86.3 %all-gather.3.cloned.1.call-start = ((), (), s32[]{:S(2)}) async-start(), calls=%async_computation | async-start | bytes 1622016 | tf_op jit(solution)/shard_map/all_gather | solution.py:90
  14.8 169.6 %all-reduce.4.cloned.1.call-start = ((), (), s32[]{:S(2)}) async-start(), calls=%async_computation.1 | async-start | bytes 3145728 | tf_op jit(solution)/shard_map/psum | solution.py:131
  114.9 71.2 %copy-start.3 = (f32[2048]{0:T(1024)S(1)}, f32[2048]{0:T(1024)}, u32[]{:S(2)}) copy-start(f32[2048]{0:T(1024)} %param.19) | copy-start | bytes 24580
  115.0 73.9 %copy-start.7 = (s32[193]{0:T(256)S(1)}, s32[193]{0:T(256)}, u32[]{:S(2)}) copy-start(s32[193]{0:T(256)} %param.23) | copy-start | bytes 2320
  115.0 255.1 %copy-start.5 = (bf16[2048,193]{0,1:T(8,128)(2,1)S(1)}, bf16[2048,193]{0,1:T(8,128)(2,1)}, u32[]{:S(2)}) copy-start(bf16[2048,193]{0,1:T(8,128)(2,1)} %param.20) | copy-start | bytes 2371588
  116.6 253.5 %all-gather.5.cloned.1.call-start = ((), (), s32[]{:S(2)}) async-start(), calls=%async_computation.2 | async-start | bytes 25952256 | tf_op jit(solution)/shard_map/all_gather | solution.py:133
  188.8 516.8 %all-reduce.6.cloned.1.call-start = ((), (), s32[]{:S(2)}) async-start(), calls=%async_computation.3 | async-start | bytes 147456 | tf_op jit(solution)/shard_map/psum | solution.py:143
  188.8 271.1 %copy-start.2 = (s32[6144]{0:T(1024)S(1)}, s32[6144]{0:T(1024)}, u32[]{:S(2)}) copy-start(s32[6144]{0:T(1024)} %param.22) | copy-start | bytes 73732
Sparse Core Ops, SparseCore 0:
  14.9 78.5 all-gather.2
  116.7 67.6 all-reduce.3
  188.9 181.1 all-gather.4
  465.6 239.8 all-reduce.5
where the time goes:
time: 719 us; the launch traced here: 714 us
  waiting for transfers between devices  564 us (78%)
  blocking collectives  75.6 us (11%)
  matrix products  31.1 us (4%)
  other arithmetic  21.7 us (3%)
  between operations  15.3 us (2%)
    psum x1, waiting for transfers between devices, local(): lax.psum((row_stats[1] * rescale, rescale * (row_stats[2] + (row_stats[0]...  240 us
    all_gather x1, waiting for transfers between devices, local(): head_shard_rows = lax.all_gather(final_in, 'seq', axis=0, tiled=True)  181 us
    pmax x1, blocking collectives, local(): top_all = lax.pmax(row_stats[0], ('kv', 'seq'))  75.6 us
    all_gather x1, waiting for transfers between devices, local(): shard_rows = lax.all_gather(packed, 'seq', axis=0, tiled=True)  75.3 us
    psum x1, waiting for transfers between devices, local(): lax.psum(jnp.dot(context, w_o, preferred_element_type=jnp.float32), 'kv')  67.5 us
    dot_general x1, matrix products, local(): jnp.dot(head_shard_rows, w_head, preferred_element_type=jnp.float32)  14.4 us
  transfers between devices with their start and end apart: 4, of which 4 were waited for; matrix products, arithmetic and copies ran while one was open for 0% of the time, Pallas kernels for 0%

commit v1 on v0

--- a/solution.py
+++ b/solution.py
@@ -3,7 +3,7 @@
 import jax
 import jax.numpy as jnp
 from jax import lax
-from jax.sharding import PartitionSpec as P
+from jax.sharding import Mesh, PartitionSpec as P
 
 HEAD_DIM = 64
 
@@ -55,7 +55,7 @@
     vocab_mask,
 ):
     tok_rows = hidden_states.shape[0]
-    seq_index = lax.axis_index("seq")
+    seq_index = lax.axis_index(("z", "y"))
     kv_local = w_k.shape[1] // HEAD_DIM
     q_local = w_q.shape[1] // HEAD_DIM
     group_size = q_local // kv_local
@@ -87,7 +87,7 @@
         jnp.zeros((kv_local, group_size, tok_rows), jnp.float32),
         jnp.zeros((kv_local, group_size, tok_rows, HEAD_DIM), jnp.float32),
     )
-    shard_rows = lax.all_gather(packed, "seq", axis=0, tiled=True)
+    shard_rows = lax.all_gather(packed, ("z", "y"), axis=0, tiled=True)
     offset = jnp.int32(0)
     row_count = shard_rows.shape[0]
     key_pos = jnp.arange(row_count, dtype=jnp.int32)
@@ -125,20 +125,29 @@
         .astype(jnp.bfloat16)
     )
     vocab_local = w_head.shape[1]
-    flat_rank = lax.axis_index(("kv", "seq"))
-    live_mask = vocab_mask == 1
-    columns = flat_rank * vocab_local + jnp.arange(vocab_local, dtype=jnp.int32)
+    y_count = lax.psum(1, "y")
+    z_count = lax.psum(1, "z")
+    z_index = lax.axis_index("z")
+    y_index = lax.axis_index("y")
+    kv_index = lax.axis_index("kv")
     attn_out = lax.psum(jnp.dot(context, w_o, preferred_element_type=jnp.float32), "kv")
     final_in = rms_norm(stream + RESID_SCALE * attn_out, final_gain).astype(jnp.bfloat16)
-    head_shard_rows = lax.all_gather(final_in, "seq", axis=0, tiled=True)
-    logits = jnp.dot(head_shard_rows, w_head, preferred_element_type=jnp.float32) * LOGIT_SCALE
+    head_rows = lax.all_gather(final_in, "y", axis=0, tiled=True)
+    group_rows = head_rows.shape[0]
+    head_cols = lax.all_gather(w_head, "z", axis=1, tiled=True)
+    mask_cols = lax.all_gather(vocab_mask, "z", axis=0, tiled=True)
+    live_mask = mask_cols == 1
+    shard_ids = kv_index * (z_count * y_count) + jnp.arange(z_count, dtype=jnp.int32) * y_count + y_index
+    columns = (shard_ids[:, None] * vocab_local + jnp.arange(vocab_local, dtype=jnp.int32)[None, :]).reshape(-1)
+    row_ids = lax.dynamic_slice_in_dim(target_ids, z_index * group_rows, group_rows, 0)
+    logits = jnp.dot(head_rows, head_cols, preferred_element_type=jnp.float32) * LOGIT_SCALE
     masked = jnp.where(live_mask[None, :], logits, NEG_FILL)
     top_row = jnp.max(masked, axis=1)
     shifted = jnp.where(live_mask[None, :], masked - top_row[:, None], 0.0)
     expw = jnp.where(live_mask[None, :], jnp.exp(shifted), 0.0)
-    target = jnp.sum(jnp.where(target_ids[:, None] == columns[None, :], logits, 0.0), axis=1)
+    target = jnp.sum(jnp.where(row_ids[:, None] == columns[None, :], logits, 0.0), axis=1)
     row_stats = jnp.stack([top_row, jnp.sum(expw, axis=1), jnp.sum(expw * shifted, axis=1), target])
-    top_all = lax.pmax(row_stats[0], ("kv", "seq"))
+    top_all = lax.pmax(row_stats[0], ("kv", "y"))
     rescale = jnp.exp(row_stats[0] - top_all)
     total_all, spread_all, target_all = lax.psum(
         (
@@ -146,28 +155,33 @@
             rescale * (row_stats[2] + (row_stats[0] - top_all) * row_stats[1]),
             row_stats[3],
         ),
-        ("kv", "seq"),
+        ("kv", "y"),
     )
     log_prob = target_all - top_all - jnp.log(total_all)
     entropy = jnp.log(total_all) - spread_all / total_all
-    log_probs = lax.dynamic_slice_in_dim(log_prob, seq_index * tok_rows, tok_rows, 0)
-    entropies = lax.dynamic_slice_in_dim(entropy, seq_index * tok_rows, tok_rows, 0)
+    log_probs = lax.dynamic_slice_in_dim(log_prob, y_index * tok_rows, tok_rows, 0)
+    entropies = lax.dynamic_slice_in_dim(entropy, y_index * tok_rows, tok_rows, 0)
     return (log_probs, entropies)
 
 
 def solution(mesh):
+    kv_size, seq_size = mesh.devices.shape
+    z_size = mesh.shape["seq"] // 4 if mesh.shape["seq"] % 4 == 0 else mesh.shape["seq"]
+    y_size = seq_size // z_size
+    split_mesh = Mesh(mesh.devices.reshape(kv_size, z_size, y_size), ("kv", "z", "y"))
+    seq = ("z", "y")
     in_specs = (
-        P("seq", None),
+        P(seq, None),
         P(),
         P(None, "kv"),
         P(None, "kv"),
         P(None, "kv"),
         P("kv", None),
         P(),
-        P(None, ("kv", "seq")),
+        P(None, ("kv",) + seq),
         P(),
         P(),
-        P(("kv", "seq")),
+        P(("kv",) + seq),
     )
-    out_specs = (P("seq"), P("seq"))
-    return jax.shard_map(local, mesh=mesh, in_specs=in_specs, out_specs=out_specs, check_vma=False)
+    out_specs = (P(seq), P(seq))
+    return jax.shard_map(local, mesh=split_mesh, in_specs=in_specs, out_specs=out_specs, check_vma=False)

time: 719 us -> 450 us (0.63)
  waiting for transfers between devices: 564 us -> 165 us
  blocking collectives: 75.6 us -> 199 us
  local copies, waits for them, and re-layouts: 5.99 us -> 16.2 us
    psum x1 -> x0, waiting for transfers between devices: 240 us -> none  [local(): lax.psum((row_stats[1] * rescale, rescale * (row_stats[2] + (row_stats[0]...]
    all_gather x2 -> x3, waiting for transfers between devices: 257 us -> 95.8 us  [the longest x1 75.4 us: local(): shard_rows = lax.all_gather(packed, ('z', 'y'), axis=0, tiled=True)]
    psum x0 -> x1, blocking collectives: none -> 124 us  [local(): lax.psum((row_stats[1] * rescale, rescale * (row_stats[2] + (row_stats[0]...]
    pmax x1, blocking collectives: 75.6 us -> 62.3 us  [local(): top_all = lax.pmax(row_stats[0], ('kv', 'y'))]
    unnamed x0 -> x1, blocking collectives: none -> 13.1 us
    unnamed x16 -> x18, local copies, waits for them, and re-layouts: 0.05 us -> 8.7 us
  transfers between devices with their start and end apart: 4 -> 4, of which waited for: 4 -> 3; matrix products, arithmetic and copies ran while one was open for 0% -> 4% of each run, Pallas kernels for 0% -> 0%
where the time goes in v1:
time: 450 us; the launch traced here: 444 us
  blocking collectives  199 us (44%)
  waiting for transfers between devices  165 us (37%)
  matrix products  26.6 us (6%)
  other arithmetic  19.3 us (4%)
  between operations  17.7 us (4%)
  local copies, waits for them, and re-layouts  16.2 us (4%)
    psum x1, blocking collectives, local(): lax.psum((row_stats[1] * rescale, rescale * (row_stats[2] + (row_stats[0]...  124 us
    all_gather x1, waiting for transfers between devices, local(): shard_rows = lax.all_gather(packed, ('z', 'y'), axis=0, tiled=True)  75.4 us
    psum x1, waiting for transfers between devices, local(): lax.psum(jnp.dot(context, w_o, preferred_element_type=jnp.float32), 'kv')  68.8 us
    pmax x1, blocking collectives, local(): top_all = lax.pmax(row_stats[0], ('kv', 'y'))  62.3 us
    all_gather x1, waiting for transfers between devices, local(): head_rows = lax.all_gather(final_in, 'y', axis=0, tiled=True)  20.5 us
    unnamed x1, blocking collectives  13.1 us
    dot_general x1, matrix products, local(): jnp.dot(head_rows, head_cols, preferred_element_type=jnp.float32)  9.77 us
  transfers between devices with their start and end apart: 4, of which 3 were waited for; matrix products, arithmetic and copies ran while one was open for 4% of the time, Pallas kernels for 0%

profile of v1, /device:TPU:24, one launch (start us, length us, event | category | flops | bytes accessed | tf_op | source)
XLA Modules:
  0.0 444.3 jit_solution(1061210086343181944)
XLA Ops:
  8.0 0.0 copy-start
  8.0 0.0 copy-start.1
  8.0 0.0 copy-start.5
  8.0 0.0 copy-start.4
  8.0 0.0 all-gather.5.cloned.1.call-start
  8.1 0.9 copy.22
  9.1 0.1 reduce.2
  9.2 0.7 sub.45
  9.9 0.1 select_reduce_fusion.2
  10.0 1.4 fusion.16
  11.3 1.6 convolution_bitcast_fusion
  13.0 1.6 convolution_convert_fusion
  14.6 0.2 fusion.30
  14.9 0.7 copy.23
  15.6 0.0 all-gather.5.cloned.1.call-update
  15.6 0.0 all-reduce.4.cloned.1.call-start
  15.7 0.5 slice.24
  16.2 0.6 slice.25
  18.1 0.2 multiply_cosine_fusion
  18.3 0.0 copy-done.1
  18.3 0.0 copy-done.5
  18.3 0.0 copy-done.4
  18.3 0.6 fusion.31
  19.0 75.4 %all-gather.5.cloned.1.call-done = bf16[6144,128]{1,0:T(8,128)(2,1)} async-done(((bf16[192,128]{1,0:T(8,128)(2,1)}), bf16[6144,128]{1,0:T(8,128)(2,1)}) %all-gather.5.cloned.1.call-update) | async-done | bytes 1572880 | tf_op jit(solution)/shard_map/all_gather | solution.py:90
  94.4 21.4 %conditional.1 = (f32[1,4,192]{2,1,0:T(4,128)S(1)}, f32[1,4,192,64]{2,3,1,0:T(8,128)S(1)}) conditional(s32[]{:T(128)} %bitcast.9, (s32[6144]{0:T(1024)S(1)}, s32[6144]{0:T(1024)S(1)}, s32[192]{0:T(256)S(1)}, s32[192]{0:T(256)S(1)}, bf16[6144,128]{1,0:T(8,128)(2,1)}, /*index=5*/bf16[192,1,4,64]{0,3,2,1:T(8,128)(2,1)S(1)}) %tuple.16, () %tuple.17), branch_computations={%region_3.6_spmd, %region_6.7_spmd} | conditional | flops 1272839424 | bytes 66424336 | solution.py:120
  94.4 1.0 compare_and_fusion
  95.3 2.6 copy.25
  98.0 5.0 %fusion = (f32[4,192]{1,0:T(4,128)S(1)}, f32[6144,192,4]{0,1,2:T(8,128)S(1)}) fusion(pred[192,6144]{1,0:T(8,128)(4,1)S(1)} %compare_and_fusion, bf16[192,1,4,64]{0,3,2,1:T(8,128)(2,1)S(1)} %get-tuple-element.16, bf16[6144,128]{0,1:T(8,128)(2,1)} %copy.25), kind=kOutput, calls=%fused_computation.2 | convolution fusion | flops 618134784 | bytes 20941824 | tf_op jit(solution)/shard_map/cond/branch_0_fun/tkgd,skd->kgts/dot_general | solution.py:100
  103.0 6.3 %fusion.7 = f32[1,4,192,64]{2,3,1,0:T(8,128)S(1)} fusion(f32[6144,192,4]{0,1,2:T(8,128)S(1)} %get-tuple-element.42, f32[4,192]{1,0:T(4,128)S(1)} %broadcast_maximum_fusion, pred[192,6144]{1,0:T(8,128)(4,1)S(1)} %compare_and_fusion, bf16[6144,128]{0,1:T(8,128)(2,1)} %copy.25), kind=kOutput, calls=%fused_computation.9 | convolution fusion | flops 627572736 | bytes 21040128 | tf_op jit(solution)/shard_map/cond/branch_0_fun/kgts,skd->kgtd/dot_general | solution.py:111
  109.3 6.5 %fusion.2 = f32[4,192]{1,0:T(4,128)S(1)} fusion(f32[6144,192,4]{0,1,2:T(8,128)S(1)} %get-tuple-element.42, f32[4,192]{1,0:T(4,128)S(1)} %broadcast_maximum_fusion, pred[192,6144]{1,0:T(8,128)(4,1)S(1)} %compare_and_fusion), kind=kLoop, calls=%fused_computation.4 | loop fusion | flops 23592192 | bytes 20060160 | tf_op jit(solution)/shard_map/cond/branch_0_fun/reduce_sum | solution.py:110
  115.7 0.0 copy-start.2
  115.8 0.0 copy-done
  115.8 1.6 fusion.35
  117.4 0.0 copy-start.6
  117.4 0.0 copy-start.3
  117.5 0.0 all-reduce.4.cloned.1.call-update
  117.5 0.0 all-gather.9.cloned.1.call-start
  117.5 0.5 all-gather.9.cloned.1.call-update
  118.1 0.2 all-gather.7.cloned.1.call-start
  118.3 68.8 %all-reduce.4.cloned.1.call-done = f32[192,2048]{1,0:T(8,128)} async-done(((f32[192,2048]{1,0:T(8,128)}), f32[192,2048]{1,0:T(8,128)}) %all-reduce.4.cloned.1.call-update) | async-done | bytes 1572880 | tf_op jit(solution)/shard_map/psum | solution.py:133
  187.1 1.8 multiply_reduce_fusion.1
  188.8 0.0 copy-done.2
  188.8 2.6 multiply_convert_fusion
  191.4 0.0 all-gather.7.cloned.1.call-update
  191.5 0.1 iota_add_fusion
  191.6 0.1 add.107
  191.7 0.0 copy-done.6
  191.7 0.6 dynamic-slice
  192.9 0.8 dynamic_slice.9
  193.7 0.0 copy-done.3
  193.7 0.2 dynamic-update-slice
  193.9 13.1 %all-reduce = s32[1544]{0:T(1024)S(1)} all-reduce(s32[1544]{0:T(1024)S(1)} %dynamic-update-slice), channel_id=1, replica_groups=mesh['kv'=8,'z'=8,'y'=4] {'z'}, use_global_device_ids=true, to_apply=%add | all-reduce | flops 1544 | bytes 12352
  207.1 0.0 all-gather.9.cloned.1.call-done
  207.1 7.8 %reshape.284 = bf16[1544,2048]{1,0:T(8,128)(2,1)} reshape(bf16[8,193,2048]{2,1,0:T(8,128)(2,1)} %all-gather.9.cloned.1.call-done) | data formatting | bytes 12648448
  214.9 20.5 %all-gather.7.cloned.1.call-done = bf16[768,2048]{1,0:T(8,128)(2,1)} async-done(((bf16[192,2048]{1,0:T(8,128)(2,1)}), bf16[768,2048]{1,0:T(8,128)(2,1)}) %all-gather.7.cloned.1.call-update) | async-done | bytes 3145744 | tf_op jit(solution)/shard_map/all_gather | solution.py:135
  235.4 9.8 %select_reduce_fusion.1 = (f32[768]{0:T(1024)S(1)}, f32[768,1544]{0,1:T(8,128)}) fusion(pred[1544]{0:T(1024)(128)(4,1)S(1)} %broadcast_compare_fusion, bf16[768,2048]{1,0:T(8,128)(2,1)} %all-gather.7.cloned.1.call-done, bf16[1544,2048]{1,0:T(8,128)(2,1)} %reshape.284), kind=kOutput, calls=%fused_computation.23 | convolution fusion | flops 4860560384 | bytes 14217736 | tf_op jit(solution)/shard_map/dot_general | solution.py:143
  245.2 62.3 %pmax.7 = f32[768]{0:T(1024)S(1)} all-reduce(f32[768]{0:T(1024)S(1)} %get-tuple-element.53), channel_id=1, replica_groups=mesh['kv'=8,'z'=8,'y'=4] {'kv','y'}, use_global_device_ids=true, to_apply=%region_12.13 | all-reduce | flops 768 | bytes 6144 | tf_op jit(solution)/shard_map/pmax | solution.py:150
  307.5 4.5 %multiply_reduce_fusion = (f32[768]{0:T(1024)S(1)}, f32[768]{0:T(1024)S(1)}, f32[768]{0:T(1024)S(1)}) fusion(f32[768,1544]{0,1:T(8,128)} %get-tuple-element.54, f32[768]{0:T(1024)S(1)} %get-tuple-element.53, pred[1544]{0:T(1024)(128)(4,1)S(1)} %broadcast_compare_fusion, s32[1544]{0:T(1024)S(1)} %add.107, s32[768]{0:T(1024)S(1)} %dynamic_slice.9), kind=kLoop, calls=%fused_computation.18 | loop fusion | flops 13041408 | bytes 4766248 | tf_op jit(solution)/shard_map/reduce_sum | solution.py:149
  312.0 123.6 %all-reduce.1 = (f32[768]{0:T(1024)S(1)}, f32[768]{0:T(1024)S(1)}, f32[768]{0:T(1024)S(1)}) all-reduce(f32[768]{0:T(1024)S(1)} %get-tuple-element.37, f32[768]{0:T(1024)S(1)} %get-tuple-element.48, f32[768]{0:T(1024)S(1)} %get-tuple-element.47), channel_id=1, replica_groups=mesh['kv'=8,'z'=8,'y'=4] {'kv','y'}, use_global_device_ids=true, to_apply=%region_10.11 | all-reduce | flops 2304 | bytes 18432 | tf_op jit(solution)/shard_map/psum | solution.py:152
  435.6 0.6 dynamic_slice.11
  436.2 0.6 dynamic_slice.10
  (17 shorter events, 0.2 us)
Async XLA Ops:
  8.0 107.8 %copy-start = (bf16[256,2048]{1,0:T(8,128)(2,1)S(1)}, bf16[256,2048]{1,0:T(8,128)(2,1)}, u32[]{:S(2)}) copy-start(bf16[256,2048]{1,0:T(8,128)(2,1)} %param.18) | copy-start | bytes 3145732
  8.0 10.3 %copy-start.1 = (bf16[192,2048]{1,0:T(8,128)(2,1)S(1)}, bf16[192,2048]{1,0:T(8,128)(2,1)}, u32[]{:S(2)}) copy-start(bf16[192,2048]{1,0:T(8,128)(2,1)} %param.13) | copy-start | bytes 2359300
  8.0 10.3 %copy-start.5 = (f32[2048]{0:T(1024)S(1)}, f32[2048]{0:T(1024)}, u32[]{:S(2)}) copy-start(f32[2048]{0:T(1024)} %param.14) | copy-start | bytes 24580
  8.0 10.3 %copy-start.4 = (bf16[2048,256]{1,0:T(8,128)(2,1)S(1)}, bf16[2048,256]{1,0:T(8,128)(2,1)}, u32[]{:S(2)}) copy-start(bf16[2048,256]{1,0:T(8,128)(2,1)} %param.15) | copy-start | bytes 3145732
  8.0 86.3 %all-gather.5.cloned.1.call-start = ((), (), s32[]{:S(2)}) async-start(), calls=%async_computation | async-start | bytes 1622016 | tf_op jit(solution)/shard_map/all_gather | solution.py:90
  15.6 171.4 %all-reduce.4.cloned.1.call-start = ((), (), s32[]{:S(2)}) async-start(), calls=%async_computation.1 | async-start | bytes 3145728 | tf_op jit(solution)/shard_map/psum | solution.py:133
  115.7 73.1 %copy-start.2 = (f32[2048]{0:T(1024)S(1)}, f32[2048]{0:T(1024)}, u32[]{:S(2)}) copy-start(f32[2048]{0:T(1024)} %param.19) | copy-start | bytes 24580
  117.4 74.2 %copy-start.6 = (u32[256]{0:T(256)S(1)}, u32[256]{0:T(256)}, u32[]{:S(2)}) copy-start(u32[256]{0:T(256)} %constant.73) | copy-start | bytes 3076
  117.4 76.2 %copy-start.3 = (s32[193]{0:T(256)S(1)}, s32[193]{0:T(256)}, u32[]{:S(2)}) copy-start(s32[193]{0:T(256)} %param.23) | copy-start | bytes 2320
  117.5 89.6 %all-gather.9.cloned.1.call-start = ((), (), s32[]{:S(2)}) async-start(), calls=%async_computation.3 | async-start | bytes 7372800 | tf_op jit(solution)/shard_map/all_gather | solution.py:137
  118.1 117.3 %all-gather.7.cloned.1.call-start = ((), (), s32[]{:S(2)}) async-start(), calls=%async_computation.2 | async-start | bytes 3932160 | tf_op jit(solution)/shard_map/all_gather | solution.py:135
Sparse Core Ops, SparseCore 0:
  15.7 78.5 all-gather.4
  117.6 69.4 all-reduce.3
Sparse Core Ops, SparseCore 1:
  119.7 75.3 all-gather.8
  196.8 38.6 all-gather.6

commit v2 on v1

--- a/solution.py
+++ b/solution.py
@@ -39,6 +39,20 @@
         ],
         axis=-1,
     )
+
+
+def merge_stats(mine, other, mine_first):
+    first = jnp.where(mine_first, mine, other)
+    second = jnp.where(mine_first, other, mine)
+    top = jnp.maximum(first[0], second[0])
+    gap_a = first[0] - top
+    gap_b = second[0] - top
+    scale_a = jnp.exp(gap_a)
+    scale_b = jnp.exp(gap_b)
+    total = first[1] * scale_a + second[1] * scale_b
+    spread = scale_a * (first[2] + gap_a * first[1]) + scale_b * (second[2] + gap_b * second[1])
+    target = first[3] + second[3]
+    return jnp.stack([top, total, spread, target])
 
 
 def local(
@@ -135,8 +149,8 @@
     head_rows = lax.all_gather(final_in, "y", axis=0, tiled=True)
     group_rows = head_rows.shape[0]
     head_cols = lax.all_gather(w_head, "z", axis=1, tiled=True)
-    mask_cols = lax.all_gather(vocab_mask, "z", axis=0, tiled=True)
-    live_mask = mask_cols == 1
+    mask_cols = lax.all_gather(vocab_mask.astype(jnp.float32), "z", axis=0, tiled=True)
+    live_mask = mask_cols == 1.0
     shard_ids = kv_index * (z_count * y_count) + jnp.arange(z_count, dtype=jnp.int32) * y_count + y_index
     columns = (shard_ids[:, None] * vocab_local + jnp.arange(vocab_local, dtype=jnp.int32)[None, :]).reshape(-1)
     row_ids = lax.dynamic_slice_in_dim(target_ids, z_index * group_rows, group_rows, 0)
@@ -146,21 +160,33 @@
     shifted = jnp.where(live_mask[None, :], masked - top_row[:, None], 0.0)
     expw = jnp.where(live_mask[None, :], jnp.exp(shifted), 0.0)
     target = jnp.sum(jnp.where(row_ids[:, None] == columns[None, :], logits, 0.0), axis=1)
-    row_stats = jnp.stack([top_row, jnp.sum(expw, axis=1), jnp.sum(expw * shifted, axis=1), target])
-    top_all = lax.pmax(row_stats[0], ("kv", "y"))
-    rescale = jnp.exp(row_stats[0] - top_all)
-    total_all, spread_all, target_all = lax.psum(
-        (
-            row_stats[1] * rescale,
-            rescale * (row_stats[2] + (row_stats[0] - top_all) * row_stats[1]),
-            row_stats[3],
-        ),
-        ("kv", "y"),
-    )
-    log_prob = target_all - top_all - jnp.log(total_all)
-    entropy = jnp.log(total_all) - spread_all / total_all
-    log_probs = lax.dynamic_slice_in_dim(log_prob, y_index * tok_rows, tok_rows, 0)
-    entropies = lax.dynamic_slice_in_dim(entropy, y_index * tok_rows, tok_rows, 0)
+    row_stats = jnp.stack(
+        [top_row, jnp.sum(expw, axis=1), jnp.sum(expw * shifted, axis=1), target]
+    ).reshape(4, y_count, tok_rows)
+    half = y_count // 2
+    my_half = y_index // half
+    keep = lax.dynamic_slice_in_dim(row_stats, my_half * half, half, 1)
+    send = lax.dynamic_slice_in_dim(row_stats, (1 - my_half) * half, half, 1)
+    got = lax.ppermute(send, "y", [(p, p ^ half) for p in range(y_count)])
+    merged = merge_stats(keep, got, my_half == 0)
+    width = half
+    while width > 1:
+        width //= 2
+        my_part = (y_index // width) % 2
+        keep = lax.dynamic_slice_in_dim(merged, my_part * width, width, 1)
+        send = lax.dynamic_slice_in_dim(merged, (1 - my_part) * width, width, 1)
+        got = lax.ppermute(send, "y", [(p, p ^ width) for p in range(y_count)])
+        merged = merge_stats(keep, got, my_part == 0)
+    merged = merged[:, 0]
+    kv_count = lax.psum(1, "kv")
+    step = 1
+    while step < kv_count:
+        got = lax.ppermute(merged, "kv", [(p, p ^ step) for p in range(kv_count)])
+        merged = merge_stats(merged, got, (kv_index // step) % 2 == 0)
+        step *= 2
+    top_all, total_all, spread_all, target_all = merged[0], merged[1], merged[2], merged[3]
+    log_probs = target_all - top_all - jnp.log(total_all)
+    entropies = jnp.log(total_all) - spread_all / total_all
     return (log_probs, entropies)
 
 

time: 450 us -> 280 us (0.62)
  blocking collectives: 199 us -> 17.6 us
  starting transfers between devices: 0.35 us -> 9.59 us
  waiting for transfers between devices: 165 us -> 171 us
    psum x1 -> x0, blocking collectives: 124 us -> none  [local(): lax.psum((row_stats[1] * rescale, rescale * (row_stats[2] + (row_stats[0]...]
    pmax x1 -> x0, blocking collectives: 62.3 us -> none  [local(): top_all = lax.pmax(row_stats[0], ('kv', 'y'))]
    ppermute x0 -> x5, waiting for transfers between devices: none -> 9.82 us  [the longest x3 5.2 us: local(): got = lax.ppermute(merged, 'kv', [(p, p ^ step) for p in range(kv_count)])]
    ppermute x0 -> x5, starting transfers between devices: none -> 9.24 us  [the longest x3 4.92 us: local(): got = lax.ppermute(merged, 'kv', [(p, p ^ step) for p in range(kv_count)])]
    unnamed x1, blocking collectives: 13.1 us -> 17.6 us
  transfers between devices with their start and end apart: 4 -> 9, of which waited for: 3 -> 8; matrix products, arithmetic and copies ran while one was open for 4% -> 6% of each run, Pallas kernels for 0% -> 0%
where the time goes in v2:
time: 280 us; the launch traced here: 278 us
  waiting for transfers between devices  171 us (61%)
  matrix products  26.6 us (10%)
  other arithmetic  20.2 us (7%)
  between operations  17.8 us (6%)
  blocking collectives  17.6 us (6%)
  local copies, waits for them, and re-layouts  14.5 us (5%)
  starting transfers between devices  9.59 us (3%)
    all_gather x1, waiting for transfers between devices, local(): shard_rows = lax.all_gather(packed, ('z', 'y'), axis=0, tiled=True)  75.3 us
    psum x1, waiting for transfers between devices, local(): lax.psum(jnp.dot(context, w_o, preferred_element_type=jnp.float32), 'kv')  68.8 us
    unnamed x1, blocking collectives  17.6 us
    all_gather x1, waiting for transfers between devices, local(): head_rows = lax.all_gather(final_in, 'y', axis=0, tiled=True)  16.5 us
    dot_general x1, matrix products, local(): jnp.dot(head_rows, head_cols, preferred_element_type=jnp.float32)  9.78 us
    unnamed x17, local copies, waits for them, and re-layouts  8.01 us
    reduce_sum x1, other arithmetic, update(): totals = jnp.sum(weights, axis=-1)  6.48 us
    dot_general x1, matrix products, update(): jnp.einsum('kgts,skd->kgtd', weights.astype(jnp.bfloat16), value_rows, pr...  6.29 us
  transfers between devices with their start and end apart: 9, of which 8 were waited for; matrix products, arithmetic and copies ran while one was open for 6% of the time, Pallas kernels for 0%

profile of v2, /device:TPU:24, one launch (start us, length us, event | category | flops | bytes accessed | tf_op | source)
XLA Modules:
  0.0 277.5 jit_solution(12237509014067361214)
XLA Ops:
  8.0 0.0 copy-start
  8.0 0.0 copy-start.1
  8.0 0.0 copy-start.5
  8.0 0.0 all-gather.5.cloned.1.call-start
  8.1 0.9 copy.22
  9.1 0.1 reduce.2
  9.2 0.7 sub.114
  9.9 0.1 select_reduce_fusion.2
  10.0 1.4 fusion.16
  11.3 1.6 convolution_bitcast_fusion
  13.0 1.6 convolution_convert_fusion
  14.6 0.2 fusion.30
  14.9 0.7 copy.23
  15.6 0.0 all-gather.5.cloned.1.call-update
  15.6 0.0 all-reduce.3.cloned.1.call-start
  15.7 0.5 slice.164
  16.2 0.6 slice.165
  18.1 0.2 multiply_cosine_fusion
  18.3 0.6 fusion.44
  19.0 75.3 %all-gather.5.cloned.1.call-done = bf16[6144,128]{1,0:T(8,128)(2,1)} async-done(((bf16[192,128]{1,0:T(8,128)(2,1)}), bf16[6144,128]{1,0:T(8,128)(2,1)}) %all-gather.5.cloned.1.call-update) | async-done | bytes 1572880 | tf_op jit(solution)/shard_map/all_gather | solution.py:104
  94.4 21.4 %conditional.1 = (f32[1,4,192]{2,1,0:T(4,128)S(1)}, f32[1,4,192,64]{2,3,1,0:T(8,128)S(1)}) conditional(s32[]{:T(128)} %bitcast.10, (s32[6144]{0:T(1024)S(1)}, s32[6144]{0:T(1024)S(1)}, s32[192]{0:T(256)S(1)}, s32[192]{0:T(256)S(1)}, bf16[6144,128]{1,0:T(8,128)(2,1)}, /*index=5*/bf16[192,1,4,64]{0,3,2,1:T(8,128)(2,1)S(1)}) %tuple.16, () %tuple.17), branch_computations={%region_3.6_spmd, %region_6.7_spmd} | conditional | flops 1272839424 | bytes 66424336 | solution.py:134
  94.4 1.0 compare_and_fusion
  95.3 2.6 copy.25
  98.0 5.0 %fusion = (f32[4,192]{1,0:T(4,128)S(1)}, f32[6144,192,4]{0,1,2:T(8,128)S(1)}) fusion(pred[192,6144]{1,0:T(8,128)(4,1)S(1)} %compare_and_fusion, bf16[192,1,4,64]{0,3,2,1:T(8,128)(2,1)S(1)} %get-tuple-element.16, bf16[6144,128]{0,1:T(8,128)(2,1)} %copy.25), kind=kOutput, calls=%fused_computation.2 | convolution fusion | flops 618134784 | bytes 20941824 | tf_op jit(solution)/shard_map/cond/branch_0_fun/tkgd,skd->kgts/dot_general | solution.py:114
  103.0 6.3 %fusion.7 = f32[1,4,192,64]{2,3,1,0:T(8,128)S(1)} fusion(f32[6144,192,4]{0,1,2:T(8,128)S(1)} %get-tuple-element.47, f32[4,192]{1,0:T(4,128)S(1)} %broadcast_maximum_fusion, pred[192,6144]{1,0:T(8,128)(4,1)S(1)} %compare_and_fusion, bf16[6144,128]{0,1:T(8,128)(2,1)} %copy.25), kind=kOutput, calls=%fused_computation.9 | convolution fusion | flops 627572736 | bytes 21040128 | tf_op jit(solution)/shard_map/cond/branch_0_fun/kgts,skd->kgtd/dot_general | solution.py:125
  109.3 6.5 %fusion.2 = f32[4,192]{1,0:T(4,128)S(1)} fusion(f32[6144,192,4]{0,1,2:T(8,128)S(1)} %get-tuple-element.47, f32[4,192]{1,0:T(4,128)S(1)} %broadcast_maximum_fusion, pred[192,6144]{1,0:T(8,128)(4,1)S(1)} %compare_and_fusion), kind=kLoop, calls=%fused_computation.4 | loop fusion | flops 23592192 | bytes 20060160 | tf_op jit(solution)/shard_map/cond/branch_0_fun/reduce_sum | solution.py:124
  115.7 0.0 copy-start.2
  115.8 0.0 copy-done
  115.8 1.6 fusion.49
  117.4 0.0 all-reduce.3.cloned.1.call-update
  117.5 0.0 all-gather.9.cloned.1.call-start
  117.5 0.5 all-gather.9.cloned.1.call-update
  118.0 0.2 all-gather.7.cloned.1.call-start
  118.3 68.8 %all-reduce.3.cloned.1.call-done = f32[192,2048]{1,0:T(8,128)} async-done(((f32[192,2048]{1,0:T(8,128)}), f32[192,2048]{1,0:T(8,128)}) %all-reduce.3.cloned.1.call-update) | async-done | bytes 1572880 | tf_op jit(solution)/shard_map/psum | solution.py:147
  187.0 1.8 multiply_reduce_fusion.1
  188.8 2.6 multiply_convert_fusion
  191.4 0.0 all-gather.7.cloned.1.call-update
  191.5 0.1 iota_add_fusion
  191.6 0.1 add.245
  191.7 0.6 dynamic-slice
  192.9 0.8 dynamic_slice.15
  193.7 0.0 copy-done.3
  193.7 0.1 convert_dynamic-update-slice_fusion
  193.8 17.6 %all-reduce = f32[1544]{0:T(1024)S(1)} all-reduce(f32[1544]{0:T(1024)S(1)} %convert_dynamic-update-slice_fusion), channel_id=1, replica_groups=mesh['kv'=8,'z'=8,'y'=4] {'z'}, use_global_device_ids=true, to_apply=%add | all-reduce | flops 1544 | bytes 12352
  211.4 0.0 all-gather.9.cloned.1.call-done
  211.5 7.4 %reshape.340 = bf16[1544,2048]{1,0:T(8,128)(2,1)} reshape(bf16[8,193,2048]{2,1,0:T(8,128)(2,1)} %all-gather.9.cloned.1.call-done) | data formatting | bytes 12648448
  218.9 16.5 %all-gather.7.cloned.1.call-done = bf16[768,2048]{1,0:T(8,128)(2,1)} async-done(((bf16[192,2048]{1,0:T(8,128)(2,1)}), bf16[768,2048]{1,0:T(8,128)(2,1)}) %all-gather.7.cloned.1.call-update) | async-done | bytes 3145744 | tf_op jit(solution)/shard_map/all_gather | solution.py:149
  235.4 9.8 %select_reduce_fusion.1 = (f32[768]{0:T(1024)S(1)}, f32[768,1544]{0,1:T(8,128)}) fusion(pred[1544]{0:T(1024)(128)(4,1)S(1)} %broadcast_compare_fusion, bf16[768,2048]{1,0:T(8,128)(2,1)} %all-gather.7.cloned.1.call-done, bf16[1544,2048]{1,0:T(8,128)(2,1)} %reshape.340), kind=kOutput, calls=%fused_computation.23 | convolution fusion | flops 4860560384 | bytes 14217736 | tf_op jit(solution)/shard_map/dot_general | solution.py:157
  245.2 0.1 stack.18
  245.3 4.5 %fusion.15 = (f32[768]{0:T(1024)S(1)}, f32[768]{0:T(1024)S(1)}, f32[768]{0:T(1024)S(1)}) fusion(f32[768,1544]{0,1:T(8,128)} %get-tuple-element.82, f32[768]{0:T(1024)S(1)} %get-tuple-element.81, pred[1544]{0:T(1024)(128)(4,1)S(1)} %broadcast_compare_fusion, s32[1544]{0:T(1024)S(1)} %add.245, s32[768]{0:T(1024)S(1)} %dynamic_slice.15), kind=kLoop, calls=%fused_computation.21 | loop fusion | flops 13041408 | bytes 4766248 | tf_op jit(solution)/shard_map/reduce_sum | solution.py:164
  249.8 0.1 stack.19
  249.9 0.1 stack.20
  249.9 0.1 stack.21
  250.1 2.6 collective-permute-start
  252.7 2.6 collective-permute-done
  255.4 1.7 collective-permute-start.1
  257.1 2.0 collective-permute-done.1
  259.2 0.1 collective-permute-start.2
  259.3 1.1 collective-permute-done.2
  260.5 1.7 collective-permute-start.3
  262.2 2.0 collective-permute-done.3
  264.3 3.2 %collective-permute-start.4 = (f32[4,192]{1,0:T(4,128)S(1)}, f32[4,192]{1,0:T(4,128)S(1)}, u32[]{:S(2)}, u32[]{:S(2)}) collective-permute-start(f32[4,192]{1,0:T(4,128)S(1)} %pad_maximum_fusion.5), channel_id=1, source_target_pairs={{0,128},{32,160},{64,192},{96,224},{128,0},{160,32},{192,64},{224,... | collective-permute-start | bytes 9224 | tf_op jit(solution)/shard_map/ppermute | solution.py:184
  267.4 2.0 collective-permute-done.4
  269.5 0.6 divide_subtract_fusion
  (44 shorter events, 0.5 us)
Async XLA Ops:
  8.0 107.8 %copy-start = (bf16[256,2048]{1,0:T(8,128)(2,1)S(1)}, bf16[256,2048]{1,0:T(8,128)(2,1)}, u32[]{:S(2)}) copy-start(bf16[256,2048]{1,0:T(8,128)(2,1)} %param.18) | copy-start | bytes 3145732
  8.0 10.3 %copy-start.1 = (bf16[192,2048]{1,0:T(8,128)(2,1)S(1)}, bf16[192,2048]{1,0:T(8,128)(2,1)}, u32[]{:S(2)}) copy-start(bf16[192,2048]{1,0:T(8,128)(2,1)} %param.13) | copy-start | bytes 2359300
  8.0 10.2 %copy-start.5 = (f32[2048]{0:T(1024)S(1)}, f32[2048]{0:T(1024)}, u32[]{:S(2)}) copy-start(f32[2048]{0:T(1024)} %param.14) | copy-start | bytes 24580
  8.0 10.2 %copy-start.4 = (bf16[2048,256]{1,0:T(8,128)(2,1)S(1)}, bf16[2048,256]{1,0:T(8,128)(2,1)}, u32[]{:S(2)}) copy-start(bf16[2048,256]{1,0:T(8,128)(2,1)} %param.15) | copy-start | bytes 3145732
  8.0 86.3 %all-gather.5.cloned.1.call-start = ((), (), s32[]{:S(2)}) async-start(), calls=%async_computation | async-start | bytes 1622016 | tf_op jit(solution)/shard_map/all_gather | solution.py:104
  15.6 171.4 %all-reduce.3.cloned.1.call-start = ((), (), s32[]{:S(2)}) async-start(), calls=%async_computation.1 | async-start | bytes 3145728 | tf_op jit(solution)/shard_map/psum | solution.py:147
  115.7 73.1 %copy-start.2 = (f32[2048]{0:T(1024)S(1)}, f32[2048]{0:T(1024)}, u32[]{:S(2)}) copy-start(f32[2048]{0:T(1024)} %param.19) | copy-start | bytes 24580
  117.4 74.2 %copy-start.6 = (u32[256]{0:T(256)S(1)}, u32[256]{0:T(256)}, u32[]{:S(2)}) copy-start(u32[256]{0:T(256)} %constant.141) | copy-start | bytes 3076
  117.4 76.2 %copy-start.3 = (s32[193]{0:T(256)S(1)}, s32[193]{0:T(256)}, u32[]{:S(2)}) copy-start(s32[193]{0:T(256)} %param.23) | copy-start | bytes 2320
  117.5 94.0 %all-gather.9.cloned.1.call-start = ((), (), s32[]{:S(2)}) async-start(), calls=%async_computation.3 | async-start | bytes 7372800 | tf_op jit(solution)/shard_map/all_gather | solution.py:151
  118.0 117.3 %all-gather.7.cloned.1.call-start = ((), (), s32[]{:S(2)}) async-start(), calls=%async_computation.2 | async-start | bytes 3932160 | tf_op jit(solution)/shard_map/all_gather | solution.py:149
  250.1 5.2 %collective-permute-start = (f32[4,2,192]{2,0,1:T(4,128)S(1)}, f32[4,2,192]{2,0,1:T(4,128)S(1)}, u32[]{:S(2)}, u32[]{:S(2)}) collective-permute-start(f32[4,2,192]{2,0,1:T(4,128)S(1)} %constant_dynamic-slice_fusion.1), channel_id=1, source_target_pairs={{0,2},{1,3},{2,0},{3,1},{4,6},{5,7},{6,4},{7,5},{8,10},{9,11},{10,... | collective-permute-start | bytes 18440 | tf_op jit(solution)/shard_map/ppermute | solution.py:170
  255.4 3.7 %collective-permute-start.1 = (f32[4,1,192]{2,0,1:T(4,128)S(1)}, f32[4,1,192]{2,0,1:T(4,128)S(1)}, u32[]{:S(2)}, u32[]{:S(2)}) collective-permute-start(f32[4,1,192]{2,0,1:T(4,128)S(1)} %constant_dynamic-slice_fusion), channel_id=1, source_target_pairs={{0,1},{1,0},{2,3},{3,2},{4,5},{5,4},{6,7},{7,6},{8,9},{9,8},{10,11... | collective-permute-start | bytes 9224 | tf_op jit(solution)/shard_map/ppermute | solution.py:178
  259.2 1.3 collective-permute-start.2
  260.5 3.7 %collective-permute-start.3 = (f32[4,192]{1,0:T(4,128)S(1)}, f32[4,192]{1,0:T(4,128)S(1)}, u32[]{:S(2)}, u32[]{:S(2)}) collective-permute-start(f32[4,192]{1,0:T(4,128)S(1)} %pad_maximum_fusion.4), channel_id=1, source_target_pairs={{0,64},{32,96},{64,0},{96,32},{128,192},{160,224},{192,128},{224,1... | collective-permute-start | bytes 9224 | tf_op jit(solution)/shard_map/ppermute | solution.py:184
  264.3 5.2 %collective-permute-start.4 = (f32[4,192]{1,0:T(4,128)S(1)}, f32[4,192]{1,0:T(4,128)S(1)}, u32[]{:S(2)}, u32[]{:S(2)}) collective-permute-start(f32[4,192]{1,0:T(4,128)S(1)} %pad_maximum_fusion.5), channel_id=1, source_target_pairs={{0,128},{32,160},{64,192},{96,224},{128,0},{160,32},{192,64},{224,... | collective-permute-start | bytes 9224 | tf_op jit(solution)/shard_map/ppermute | solution.py:184
Sparse Core Ops, SparseCore 0:
  15.7 78.5 all-gather.4
  117.6 69.4 all-reduce.2
Sparse Core Ops, SparseCore 1:
  119.7 75.3 all-gather.8
  196.7 38.6 all-gather.6

commit v3 on v2

--- a/solution.py
+++ b/solution.py
@@ -102,6 +102,12 @@
         jnp.zeros((kv_local, group_size, tok_rows, HEAD_DIM), jnp.float32),
     )
     shard_rows = lax.all_gather(packed, ("z", "y"), axis=0, tiled=True)
+    head_pad = jnp.zeros((16 - 1, w_head.shape[1]), w_head.dtype)
+    head_ext = jnp.concatenate([w_head, vocab_mask.astype(w_head.dtype)[None, :], head_pad], axis=0)
+    head_ext = lax.all_gather(head_ext, "z", axis=1, tiled=True)
+    shard_rows, head_ext = lax.optimization_barrier((shard_rows, head_ext))
+    head_cols = head_ext[: w_head.shape[0]]
+    mask_cols = head_ext[w_head.shape[0]]
     offset = jnp.int32(0)
     row_count = shard_rows.shape[0]
     key_pos = jnp.arange(row_count, dtype=jnp.int32)
@@ -148,8 +154,6 @@
     final_in = rms_norm(stream + RESID_SCALE * attn_out, final_gain).astype(jnp.bfloat16)
     head_rows = lax.all_gather(final_in, "y", axis=0, tiled=True)
     group_rows = head_rows.shape[0]
-    head_cols = lax.all_gather(w_head, "z", axis=1, tiled=True)
-    mask_cols = lax.all_gather(vocab_mask.astype(jnp.float32), "z", axis=0, tiled=True)
     live_mask = mask_cols == 1.0
     shard_ids = kv_index * (z_count * y_count) + jnp.arange(z_count, dtype=jnp.int32) * y_count + y_index
     columns = (shard_ids[:, None] * vocab_local + jnp.arange(vocab_local, dtype=jnp.int32)[None, :]).reshape(-1)

time: 280 us -> 350 us (1.25)
  waiting for transfers between devices: 171 us -> 257 us
  blocking collectives: 17.6 us -> 0 us
    all_gather x1, waiting for transfers between devices: 0.03 us -> 74 us  [local(): head_ext = lax.all_gather(head_ext, 'z', axis=1, tiled=True)]
    all_gather x1, waiting for transfers between devices: 16.5 us -> 37.5 us  [local(): head_rows = lax.all_gather(final_in, 'y', axis=0, tiled=True)]
    unnamed x1 -> x0, blocking collectives: 17.6 us -> none
    all_gather x1, waiting for transfers between devices: 75.3 us -> 68.1 us  [local(): shard_rows = lax.all_gather(packed, ('z', 'y'), axis=0, tiled=True)]
    unnamed x17 -> x13, local copies, waits for them, and re-layouts: 8.01 us -> 9.04 us
  transfers between devices with their start and end apart: 9 -> 9, of which waited for: 8 -> 9; matrix products, arithmetic and copies ran while one was open for 6% -> 6% of each run, Pallas kernels for 0% -> 0%
where the time goes in v3:
time: 350 us; the launch traced here: 347 us
  waiting for transfers between devices  257 us (73%)
  matrix products  25.4 us (7%)
  other arithmetic  22.2 us (6%)
  local copies, waits for them, and re-layouts  17.6 us (5%)
  between operations  15.4 us (4%)
  starting transfers between devices  9.64 us (3%)
    all_gather x1, waiting for transfers between devices, local(): head_ext = lax.all_gather(head_ext, 'z', axis=1, tiled=True)  74 us
    all_gather x1, waiting for transfers between devices, local(): shard_rows = lax.all_gather(packed, ('z', 'y'), axis=0, tiled=True)  68.1 us
    psum x1, waiting for transfers between devices, local(): lax.psum(jnp.dot(context, w_o, preferred_element_type=jnp.float32), 'kv')  67.6 us
    all_gather x1, waiting for transfers between devices, local(): head_rows = lax.all_gather(final_in, 'y', axis=0, tiled=True)  37.5 us
    dot_general x1, matrix products, local(): jnp.dot(head_rows, head_cols, preferred_element_type=jnp.float32)  9.83 us
    unnamed x13, local copies, waits for them, and re-layouts  9.04 us
  transfers between devices with their start and end apart: 9, of which 9 were waited for; matrix products, arithmetic and copies ran while one was open for 6% of the time, Pallas kernels for 0%

profile of v3, /device:TPU:24, one launch (start us, length us, event | category | flops | bytes accessed | tf_op | source)
XLA Modules:
  0.0 347.4 jit_solution(1017244428684021406)
XLA Ops:
  7.2 0.0 copy-start
  7.2 0.0 copy-start.1
  7.2 0.0 copy-start.5
  7.2 0.0 all-gather.9.cloned.1.call-start
  7.3 0.8 convert_element_type.57
  8.1 0.1 broadcast_in_dim.98
  8.2 2.0 concatenate.35
  10.2 0.0 all-gather.9.cloned.1.call-update
  10.3 0.0 all-gather.5.cloned.1.call-start
  10.3 0.8 copy.24
  11.1 0.1 reduce.2
  11.2 0.7 sub.114
  11.9 0.1 select_reduce_fusion.2
  12.0 1.4 fusion.18
  13.4 1.6 convolution_bitcast_fusion
  15.1 0.2 fusion.32
  15.3 0.0 copy-done.1
  15.3 0.4 convolution_convert_fusion
  15.8 0.7 copy.25
  16.5 0.0 all-gather.5.cloned.1.call-update
  16.5 0.0 all-reduce.2.cloned.1.call-start
  16.5 0.5 slice.173
  17.1 0.6 slice.174
  18.9 0.2 multiply_cosine_fusion
  19.2 0.6 fusion.46
  19.9 74.0 %all-gather.9.cloned.1.call-done = bf16[8,193,2064]{2,1,0:T(8,128)(2,1)} async-done(((bf16[1,193,2064]{2,1,0:T(8,128)(2,1)}), bf16[8,193,2064]{2,1,0:T(8,128)(2,1)}) %all-gather.9.cloned.1.call-update) | async-done | bytes 6373648 | tf_op jit(solution)/shard_map/all_gather | solution.py:107
  93.8 9.0 %reshape.336 = bf16[1544,2064]{1,0:T(8,128)(2,1)} reshape(bf16[8,193,2064]{2,1,0:T(8,128)(2,1)} %all-gather.9.cloned.1.call-done) | data formatting | bytes 12747264
  102.8 68.1 %all-gather.5.cloned.1.call-done = bf16[6144,128]{1,0:T(8,128)(2,1)} async-done(((bf16[192,128]{1,0:T(8,128)(2,1)}), bf16[6144,128]{1,0:T(8,128)(2,1)}) %all-gather.5.cloned.1.call-update) | async-done | bytes 1572880 | tf_op jit(solution)/shard_map/all_gather | solution.py:104
  170.9 21.4 %conditional.1 = (f32[1,4,192]{2,1,0:T(4,128)S(1)}, f32[1,4,192,64]{2,3,1,0:T(8,128)S(1)}) conditional(s32[]{:T(128)} %bitcast.15, (s32[6144]{0:T(1024)S(1)}, s32[6144]{0:T(1024)S(1)}, s32[192]{0:T(256)S(1)}, s32[192]{0:T(256)S(1)}, bf16[6144,128]{1,0:T(8,128)(2,1)}, /*index=5*/bf16[192,1,4,64]{0,3,2,1:T(8,128)(2,1)S(1)}) %tuple.18, () %tuple.19), branch_computations={%region_3.6_spmd, %region_6.7_spmd} | conditional | flops 1272839424 | bytes 66424336 | solution.py:140
  170.9 1.0 compare_and_fusion
  171.9 2.6 copy.28
  174.6 5.0 %fusion = (f32[4,192]{1,0:T(4,128)S(1)}, f32[6144,192,4]{0,1,2:T(8,128)S(1)}) fusion(pred[192,6144]{1,0:T(8,128)(4,1)S(1)} %compare_and_fusion, bf16[192,1,4,64]{0,3,2,1:T(8,128)(2,1)S(1)} %get-tuple-element.16, bf16[6144,128]{0,1:T(8,128)(2,1)} %copy.28), kind=kOutput, calls=%fused_computation.2 | convolution fusion | flops 618134784 | bytes 20941824 | tf_op jit(solution)/shard_map/cond/branch_0_fun/tkgd,skd->kgts/dot_general | solution.py:120
  179.6 6.3 %fusion.7 = f32[1,4,192,64]{2,3,1,0:T(8,128)S(1)} fusion(f32[6144,192,4]{0,1,2:T(8,128)S(1)} %get-tuple-element.51, f32[4,192]{1,0:T(4,128)S(1)} %broadcast_maximum_fusion, pred[192,6144]{1,0:T(8,128)(4,1)S(1)} %compare_and_fusion, bf16[6144,128]{0,1:T(8,128)(2,1)} %copy.28), kind=kOutput, calls=%fused_computation.9 | convolution fusion | flops 627572736 | bytes 21040128 | tf_op jit(solution)/shard_map/cond/branch_0_fun/kgts,skd->kgtd/dot_general | solution.py:131
  185.9 6.5 %fusion.2 = f32[4,192]{1,0:T(4,128)S(1)} fusion(f32[6144,192,4]{0,1,2:T(8,128)S(1)} %get-tuple-element.51, f32[4,192]{1,0:T(4,128)S(1)} %broadcast_maximum_fusion, pred[192,6144]{1,0:T(8,128)(4,1)S(1)} %compare_and_fusion), kind=kLoop, calls=%fused_computation.4 | loop fusion | flops 23592192 | bytes 20060160 | tf_op jit(solution)/shard_map/cond/branch_0_fun/reduce_sum | solution.py:130
  192.3 0.0 copy-start.2
  192.4 1.6 fusion.51
  194.0 0.0 all-reduce.2.cloned.1.call-update
  194.1 0.3 all-gather.7.cloned.1.call-start
  194.3 67.6 %all-reduce.2.cloned.1.call-done = f32[192,2048]{1,0:T(8,128)} async-done(((f32[192,2048]{1,0:T(8,128)}), f32[192,2048]{1,0:T(8,128)}) %all-reduce.2.cloned.1.call-update) | async-done | bytes 1572880 | tf_op jit(solution)/shard_map/psum | solution.py:153
  261.9 1.7 multiply_reduce_fusion.1
  263.7 2.6 multiply_convert_fusion
  266.3 0.0 all-gather.7.cloned.1.call-update
  266.3 0.1 iota_add_fusion
  266.4 0.1 add.245
  266.5 0.8 dynamic_slice.15
  267.3 1.3 compare_reduce_fusion
  268.6 37.5 %all-gather.7.cloned.1.call-done = bf16[768,2048]{1,0:T(8,128)(2,1)} async-done(((bf16[192,2048]{1,0:T(8,128)(2,1)}), bf16[768,2048]{1,0:T(8,128)(2,1)}) %all-gather.7.cloned.1.call-update) | async-done | bytes 3145744 | tf_op jit(solution)/shard_map/all_gather | solution.py:155
  306.1 9.8 %select_reduce_fusion.1 = (f32[768]{0:T(1024)S(1)}, f32[768,1544]{0,1:T(8,128)}) fusion(pred[1544]{0:T(1024)(128)(4,1)S(1)} %compare_reduce_fusion, bf16[768,2048]{1,0:T(8,128)(2,1)} %all-gather.7.cloned.1.call-done, bf16[2064,1544]{0,1:T(8,128)(2,1)} %bitcast.79), kind=kOutput, calls=%fused_computation.25 | convolution fusion | flops 4860560384 | bytes 14217736 | tf_op jit(solution)/shard_map/dot_general | solution.py:161
  315.9 0.1 stack.18
  316.0 4.5 %fusion.17 = (f32[768]{0:T(1024)S(1)}, f32[768]{0:T(1024)S(1)}, f32[768]{0:T(1024)S(1)}) fusion(f32[768,1544]{0,1:T(8,128)} %get-tuple-element.86, f32[768]{0:T(1024)S(1)} %get-tuple-element.85, pred[1544]{0:T(1024)(128)(4,1)S(1)} %compare_reduce_fusion, s32[1544]{0:T(1024)S(1)} %add.245, s32[768]{0:T(1024)S(1)} %dynamic_slice.15), kind=kLoop, calls=%fused_computation.23 | loop fusion | flops 13041408 | bytes 4766248 | tf_op jit(solution)/shard_map/reduce_sum | solution.py:168
  320.5 0.1 stack.19
  320.6 0.1 stack.20
  320.7 0.1 stack.21
  320.8 2.6 collective-permute-start
  323.4 2.6 collective-permute-done
  326.2 1.7 collective-permute-start.1
  327.9 2.0 collective-permute-done.1
  329.9 0.1 collective-permute-start.2
  330.0 1.1 collective-permute-done.2
  331.3 1.7 collective-permute-start.3
  332.9 2.0 collective-permute-done.3
  335.0 3.2 collective-permute-start.4
  338.2 2.0 collective-permute-done.4
  340.3 0.6 divide_subtract_fusion
  (42 shorter events, 0.5 us)
Async XLA Ops:
  7.2 185.2 %copy-start = (bf16[256,2048]{1,0:T(8,128)(2,1)S(1)}, bf16[256,2048]{1,0:T(8,128)(2,1)}, u32[]{:S(2)}) copy-start(bf16[256,2048]{1,0:T(8,128)(2,1)} %param.18) | copy-start | bytes 3145732
  7.2 8.1 %copy-start.1 = (bf16[192,2048]{1,0:T(8,128)(2,1)S(1)}, bf16[192,2048]{1,0:T(8,128)(2,1)}, u32[]{:S(2)}) copy-start(bf16[192,2048]{1,0:T(8,128)(2,1)} %param.13) | copy-start | bytes 2359300
  7.2 8.1 %copy-start.5 = (f32[2048]{0:T(1024)S(1)}, f32[2048]{0:T(1024)}, u32[]{:S(2)}) copy-start(f32[2048]{0:T(1024)} %param.14) | copy-start | bytes 24580
  7.2 8.1 %copy-start.4 = (bf16[2048,64]{0,1:T(8,128)(2,1)S(1)}, bf16[2048,64]{0,1:T(8,128)(2,1)}, u32[]{:S(2)}) copy-start(bf16[2048,64]{0,1:T(8,128)(2,1)} %param.17) | copy-start | bytes 786436
  7.2 11.9 %copy-start.3 = (bf16[2048,256]{1,0:T(8,128)(2,1)S(1)}, bf16[2048,256]{1,0:T(8,128)(2,1)}, u32[]{:S(2)}) copy-start(bf16[2048,256]{1,0:T(8,128)(2,1)} %param.15) | copy-start | bytes 3145732
  7.2 86.6 %all-gather.9.cloned.1.call-start = ((), (), s32[]{:S(2)}) async-start(), calls=%async_computation.3 | async-start | bytes 7833600 | tf_op jit(solution)/shard_map/all_gather | solution.py:107
  10.3 160.7 %all-gather.5.cloned.1.call-start = ((), (), s32[]{:S(2)}) async-start(), calls=%async_computation | async-start | bytes 1622016 | tf_op jit(solution)/shard_map/all_gather | solution.py:104
  16.5 245.4 %all-reduce.2.cloned.1.call-start = ((), (), s32[]{:S(2)}) async-start(), calls=%async_computation.1 | async-start | bytes 3145728 | tf_op jit(solution)/shard_map/psum | solution.py:153
  192.3 71.3 %copy-start.2 = (f32[2048]{0:T(1024)S(1)}, f32[2048]{0:T(1024)}, u32[]{:S(2)}) copy-start(f32[2048]{0:T(1024)} %param.19) | copy-start | bytes 24580
  194.1 112.0 %all-gather.7.cloned.1.call-start = ((), (), s32[]{:S(2)}) async-start(), calls=%async_computation.2 | async-start | bytes 3932160 | tf_op jit(solution)/shard_map/all_gather | solution.py:155
  320.8 5.2 %collective-permute-start = (f32[4,2,192]{2,0,1:T(4,128)S(1)}, f32[4,2,192]{2,0,1:T(4,128)S(1)}, u32[]{:S(2)}, u32[]{:S(2)}) collective-permute-start(f32[4,2,192]{2,0,1:T(4,128)S(1)} %constant_dynamic-slice_fusion.1), channel_id=1, source_target_pairs={{0,2},{1,3},{2,0},{3,1},{4,6},{5,7},{6,4},{7,5},{8,10},{9,11},{10,... | collective-permute-start | bytes 18440 | tf_op jit(solution)/shard_map/ppermute | solution.py:174
  326.2 3.7 %collective-permute-start.1 = (f32[4,1,192]{2,0,1:T(4,128)S(1)}, f32[4,1,192]{2,0,1:T(4,128)S(1)}, u32[]{:S(2)}, u32[]{:S(2)}) collective-permute-start(f32[4,1,192]{2,0,1:T(4,128)S(1)} %constant_dynamic-slice_fusion), channel_id=1, source_target_pairs={{0,1},{1,0},{2,3},{3,2},{4,5},{5,4},{6,7},{7,6},{8,9},{9,8},{10,11... | collective-permute-start | bytes 9224 | tf_op jit(solution)/shard_map/ppermute | solution.py:182
  329.9 1.3 collective-permute-start.2
  331.3 3.7 %collective-permute-start.3 = (f32[4,192]{1,0:T(4,128)S(1)}, f32[4,192]{1,0:T(4,128)S(1)}, u32[]{:S(2)}, u32[]{:S(2)}) collective-permute-start(f32[4,192]{1,0:T(4,128)S(1)} %pad_maximum_fusion.4), channel_id=1, source_target_pairs={{0,64},{32,96},{64,0},{96,32},{128,192},{160,224},{192,128},{224,1... | collective-permute-start | bytes 9224 | tf_op jit(solution)/shard_map/ppermute | solution.py:188
  335.0 5.2 %collective-permute-start.4 = (f32[4,192]{1,0:T(4,128)S(1)}, f32[4,192]{1,0:T(4,128)S(1)}, u32[]{:S(2)}, u32[]{:S(2)}) collective-permute-start(f32[4,192]{1,0:T(4,128)S(1)} %pad_maximum_fusion.5), channel_id=1, source_target_pairs={{0,128},{32,160},{64,192},{96,224},{128,0},{160,32},{192,64},{224,... | collective-permute-start | bytes 9224 | tf_op jit(solution)/shard_map/ppermute | solution.py:188
Sparse Core Ops, SparseCore 0:
  10.4 83.4 all-gather.8
  96.4 74.4 all-gather.4
  194.2 67.6 all-reduce.1
  266.4 39.6 all-gather.6

commit v4 on v2

--- a/solution.py
+++ b/solution.py
@@ -144,12 +144,37 @@
     z_index = lax.axis_index("z")
     y_index = lax.axis_index("y")
     kv_index = lax.axis_index("kv")
-    attn_out = lax.psum(jnp.dot(context, w_o, preferred_element_type=jnp.float32), "kv")
-    final_in = rms_norm(stream + RESID_SCALE * attn_out, final_gain).astype(jnp.bfloat16)
+    kv_count = lax.psum(1, "kv")
+    kv_bits = kv_count.bit_length() - 1
+    partial = jnp.dot(context, w_o, preferred_element_type=jnp.float32)
+    chunk = tok_rows // kv_count
+    blocks = partial.reshape((2,) * kv_bits + (chunk, partial.shape[1]))
+    for bit in range(kv_bits):
+        mine_low = (kv_index >> bit) % 2 == 0
+        axis = kv_bits - 1 - bit
+        low = lax.index_in_dim(blocks, 0, axis, keepdims=False)
+        high = lax.index_in_dim(blocks, 1, axis, keepdims=False)
+        keep = jnp.where(mine_low, low, high)
+        send = jnp.where(mine_low, high, low)
+        got = lax.ppermute(send, "kv", [(p, p ^ (1 << bit)) for p in range(kv_count)])
+        blocks = jnp.where(mine_low, keep + got, got + keep)
+    attn_part = blocks
+    stream_part = lax.dynamic_slice_in_dim(stream, kv_index * chunk, chunk, 0)
+    final_part = rms_norm(stream_part + RESID_SCALE * attn_part, final_gain).astype(jnp.bfloat16)
+    rows = final_part[None]
+    for bit in reversed(range(kv_bits)):
+        mine_low = (kv_index >> bit) % 2 == 0
+        got = lax.ppermute(rows, "kv", [(p, p ^ (1 << bit)) for p in range(kv_count)])
+        rows = jnp.where(mine_low, jnp.stack([rows, got], axis=1), jnp.stack([got, rows], axis=1))
+        rows = rows.reshape((rows.shape[0] * 2,) + rows.shape[2:])
+    final_in = rows.reshape(tok_rows, final_part.shape[1])
     head_rows = lax.all_gather(final_in, "y", axis=0, tiled=True)
     group_rows = head_rows.shape[0]
-    head_cols = lax.all_gather(w_head, "z", axis=1, tiled=True)
-    mask_cols = lax.all_gather(vocab_mask.astype(jnp.float32), "z", axis=0, tiled=True)
+    head_pad = jnp.zeros((16 - 1, vocab_local), w_head.dtype)
+    head_ext = jnp.concatenate([w_head, vocab_mask.astype(w_head.dtype)[None, :], head_pad], axis=0)
+    head_ext = lax.all_gather(head_ext, "z", axis=1, tiled=True)
+    head_cols = head_ext[: w_head.shape[0]]
+    mask_cols = head_ext[w_head.shape[0]]
     live_mask = mask_cols == 1.0
     shard_ids = kv_index * (z_count * y_count) + jnp.arange(z_count, dtype=jnp.int32) * y_count + y_index
     columns = (shard_ids[:, None] * vocab_local + jnp.arange(vocab_local, dtype=jnp.int32)[None, :]).reshape(-1)
@@ -178,7 +203,6 @@
         got = lax.ppermute(send, "y", [(p, p ^ width) for p in range(y_count)])
         merged = merge_stats(keep, got, my_part == 0)
     merged = merged[:, 0]
-    kv_count = lax.psum(1, "kv")
     step = 1
     while step < kv_count:
         got = lax.ppermute(merged, "kv", [(p, p ^ step) for p in range(kv_count)])

time: 280 us -> 259 us (0.925)
  blocking collectives: 17.6 us -> 0 us
  waiting for transfers between devices: 171 us -> 156 us
  starting transfers between devices: 9.59 us -> 19.2 us
  local copies, waits for them, and re-layouts: 14.5 us -> 18.4 us
    psum x1 -> x0, waiting for transfers between devices: 68.8 us -> none  [local(): lax.psum(jnp.dot(context, w_o, preferred_element_type=jnp.float32), 'kv')]
    ppermute x0 -> x6, waiting for transfers between devices: none -> 24.4 us  [the longest x3 15.4 us: local(): got = lax.ppermute(send, 'kv', [(p, p ^ 1 << bit) for p in range(kv_count)])]
    all_gather x1, waiting for transfers between devices: 0.03 us -> 19.4 us  [local(): head_ext = lax.all_gather(head_ext, 'z', axis=1, tiled=True)]
    unnamed x1 -> x0, blocking collectives: 17.6 us -> none
    all_gather x1, waiting for transfers between devices: 16.5 us -> 30.2 us  [local(): head_rows = lax.all_gather(final_in, 'y', axis=0, tiled=True)]
    ppermute x0 -> x6, starting transfers between devices: none -> 9.54 us  [the longest x3 4.77 us: local(): got = lax.ppermute(send, 'kv', [(p, p ^ 1 << bit) for p in range(kv_count)])]
    all_gather x1, waiting for transfers between devices: 75.3 us -> 71.9 us  [local(): shard_rows = lax.all_gather(packed, ('z', 'y'), axis=0, tiled=True)]
    unnamed x17 -> x11, local copies, waits for them, and re-layouts: 8.01 us -> 9.12 us
  transfers between devices with their start and end apart: 9 -> 14, of which waited for: 8 -> 14; matrix products, arithmetic and copies ran while one was open for 6% -> 17% of each run, Pallas kernels for 0% -> 0%
where the time goes in v4:
time: 259 us; the launch traced here: 257 us
  waiting for transfers between devices  156 us (60%)
  matrix products  26.5 us (10%)
  other arithmetic  21 us (8%)
  starting transfers between devices  19.2 us (7%)
  local copies, waits for them, and re-layouts  18.4 us (7%)
  between operations  15.5 us (6%)
    all_gather x1, waiting for transfers between devices, local(): shard_rows = lax.all_gather(packed, ('z', 'y'), axis=0, tiled=True)  71.9 us
    all_gather x1, waiting for transfers between devices, local(): head_rows = lax.all_gather(final_in, 'y', axis=0, tiled=True)  30.2 us
    all_gather x1, waiting for transfers between devices, local(): head_ext = lax.all_gather(head_ext, 'z', axis=1, tiled=True)  19.4 us
    ppermute x3, waiting for transfers between devices, local(): got = lax.ppermute(send, 'kv', [(p, p ^ 1 << bit) for p in range(kv_count)])  15.4 us
    dot_general x1, matrix products, local(): jnp.dot(head_rows, head_cols, preferred_element_type=jnp.float32)  9.79 us
    unnamed x11, local copies, waits for them, and re-layouts  9.12 us
    ppermute x3, waiting for transfers between devices, local(): got = lax.ppermute(rows, 'kv', [(p, p ^ 1 << bit) for p in range(kv_count)])  8.97 us
    reduce_sum x1, other arithmetic, update(): totals = jnp.sum(weights, axis=-1)  6.48 us
  transfers between devices with their start and end apart: 14, of which 14 were waited for; matrix products, arithmetic and copies ran while one was open for 17% of the time, Pallas kernels for 0%

profile of v4, /device:TPU:24, one launch (start us, length us, event | category | flops | bytes accessed | tf_op | source)
XLA Modules:
  0.0 256.6 jit_solution(13731786269795209953)
XLA Ops:
  7.3 0.9 copy.72
  8.3 0.1 reduce.3
  8.4 0.7 sub.114
  9.1 0.1 select_reduce_fusion.2
  9.2 1.4 multiply_reduce_fusion.1
  10.5 1.6 convolution_bitcast_fusion
  12.2 1.6 convolution_convert_fusion
  13.8 0.2 fusion.38
  14.1 0.7 copy.73
  14.9 0.7 convert_element_type.54
  15.5 0.1 broadcast_in_dim.102
  15.7 1.3 concatenate.52
  17.1 0.5 slice.189
  17.6 0.6 slice.190
  19.5 0.2 multiply_cosine_fusion
  19.7 1.8 fusion.54
  21.6 71.9 %all-gather.5.cloned.1.call-done = bf16[6144,128]{1,0:T(8,128)(2,1)} async-done(((bf16[192,128]{1,0:T(8,128)(2,1)}), bf16[6144,128]{1,0:T(8,128)(2,1)}) %all-gather.5.cloned.1.call-update) | async-done | bytes 1572880 | tf_op jit(solution)/shard_map/all_gather | solution.py:104
  93.6 21.5 %conditional.1 = (f32[1,4,192]{2,1,0:T(4,128)S(1)}, f32[1,4,192,64]{2,3,1,0:T(8,128)S(1)}) conditional(s32[]{:T(128)} %bitcast.12, (s32[6144]{0:T(1024)S(1)}, s32[6144]{0:T(1024)S(1)}, s32[192]{0:T(256)S(1)}, s32[192]{0:T(256)S(1)}, bf16[6144,128]{1,0:T(8,128)(2,1)}, /*index=5*/bf16[192,1,4,64]{0,3,2,1:T(8,128)(2,1)S(1)}) %tuple.16, () %tuple.17), branch_computations={%region_3.6_spmd, %region_6.7_spmd} | conditional | flops 1272839424 | bytes 66424336 | solution.py:134
  93.6 1.0 compare_and_fusion
  94.5 2.6 %copy.75 = bf16[6144,128]{0,1:T(8,128)(2,1)} copy(bf16[6144,128]{1,0:T(8,128)(2,1)} %get-tuple-element.33) | data formatting | bytes 3145728 | tf_op jit(solution)/shard_map
  97.2 5.0 %fusion = (f32[4,192]{1,0:T(4,128)S(1)}, f32[6144,192,4]{0,1,2:T(8,128)S(1)}) fusion(pred[192,6144]{1,0:T(8,128)(4,1)S(1)} %compare_and_fusion, bf16[192,1,4,64]{0,3,2,1:T(8,128)(2,1)S(1)} %get-tuple-element.16, bf16[6144,128]{0,1:T(8,128)(2,1)} %copy.75), kind=kOutput, calls=%fused_computation.2 | convolution fusion | flops 618134784 | bytes 20941824 | tf_op jit(solution)/shard_map/cond/branch_0_fun/tkgd,skd->kgts/dot_general | solution.py:114
  102.2 6.3 %fusion.7 = f32[1,4,192,64]{2,3,1,0:T(8,128)S(1)} fusion(f32[6144,192,4]{0,1,2:T(8,128)S(1)} %get-tuple-element.49, f32[4,192]{1,0:T(4,128)S(1)} %broadcast_maximum_fusion, pred[192,6144]{1,0:T(8,128)(4,1)S(1)} %compare_and_fusion, bf16[6144,128]{0,1:T(8,128)(2,1)} %copy.75), kind=kOutput, calls=%fused_computation.9 | convolution fusion | flops 627572736 | bytes 21040128 | tf_op jit(solution)/shard_map/cond/branch_0_fun/kgts,skd->kgtd/dot_general | solution.py:125
  108.4 6.5 %fusion.2 = f32[4,192]{1,0:T(4,128)S(1)} fusion(f32[6144,192,4]{0,1,2:T(8,128)S(1)} %get-tuple-element.49, f32[4,192]{1,0:T(4,128)S(1)} %broadcast_maximum_fusion, pred[192,6144]{1,0:T(8,128)(4,1)S(1)} %compare_and_fusion), kind=kLoop, calls=%fused_computation.4 | loop fusion | flops 23592192 | bytes 20060160 | tf_op jit(solution)/shard_map/cond/branch_0_fun/reduce_sum | solution.py:124
  115.1 0.2 copy.76
  115.3 0.2 convert_element_type.63
  115.5 0.4 fusion.18
  115.9 0.1 select_bitcast_fusion
  116.0 0.1 collective-permute-start
  116.1 2.4 collective-permute-done
  118.5 1.3 fusion.21
  119.8 1.6 collective-permute-start.1
  121.4 9.7 %collective-permute-done.1 = f32[2,24,2048]{2,1,0:T(8,128)S(1)} collective-permute-done((f32[2,24,2048]{2,1,0:T(8,128)S(1)}, f32[2,24,2048]{2,1,0:T(8,128)S(1)}, u32[]{:S(2)}, u32[]{:S(2)}) %collective-permute-start.1) | collective-permute-done | bytes 393248 | tf_op jit(solution)/shard_map/ppermute | solution.py:159
  131.1 3.1 %collective-permute-start.2 = (f32[24,2048]{1,0:T(8,128)S(1)}, f32[24,2048]{1,0:T(8,128)S(1)}, u32[]{:S(2)}, u32[]{:S(2)}) collective-permute-start(f32[24,2048]{1,0:T(8,128)S(1)} %select_bitcast_fusion.2), channel_id=1, source_target_pairs={{0,128},{32,160},{64,192},{96,224},{128,0},{160,32},{192,64},{224,... | collective-permute-start | bytes 589832 | tf_op jit(solution)/shard_map/ppermute | solution.py:159
  134.3 1.3 convert_element_type.55
  135.6 3.4 %collective-permute-done.2 = f32[24,2048]{1,0:T(8,128)S(1)} collective-permute-done((f32[24,2048]{1,0:T(8,128)S(1)}, f32[24,2048]{1,0:T(8,128)S(1)}, u32[]{:S(2)}, u32[]{:S(2)}) %collective-permute-start.2) | collective-permute-done | bytes 196640 | tf_op jit(solution)/shard_map/ppermute | solution.py:159
  138.9 0.2 multiply_reduce_fusion.2
  139.1 0.1 fusion.53
  139.2 3.1 %collective-permute-start.3 = (bf16[1,24,2048]{2,1,0:T(8,128)(2,1)S(1)}, bf16[1,24,2048]{2,1,0:T(8,128)(2,1)S(1)}, u32[]{:S(2)}, u32[]{:S(2)}) collective-permute-start(bf16[1,24,2048]{2,1,0:T(8,128)(2,1)S(1)} %get-tuple-element.53), channel_id=1, source_target_pairs={{0,128},{32,160},{64,192},{96,224},{128,0},{160,32},{192,64},{224,... | collective-permute-start | bytes 294920 | tf_op jit(solution)/shard_map/ppermute | solution.py:167
  142.3 3.1 %collective-permute-done.3 = bf16[1,24,2048]{2,1,0:T(8,128)(2,1)S(1)} collective-permute-done((bf16[1,24,2048]{2,1,0:T(8,128)(2,1)S(1)}, bf16[1,24,2048]{2,1,0:T(8,128)(2,1)S(1)}, u32[]{:S(2)}, u32[]{:S(2)}) %collective-permute-start.3) | collective-permute-done | bytes 98336 | tf_op jit(solution)/shard_map/ppermute | solution.py:167
  145.4 1.6 collective-permute-start.4
  147.0 4.2 %collective-permute-done.4 = bf16[2,24,2048]{2,1,0:T(8,128)(2,1)S(1)} collective-permute-done((bf16[2,24,2048]{2,1,0:T(8,128)(2,1)S(1)}, bf16[2,24,2048]{2,1,0:T(8,128)(2,1)S(1)}, u32[]{:S(2)}, u32[]{:S(2)}) %collective-permute-start.4) | collective-permute-done | bytes 196640 | tf_op jit(solution)/shard_map/ppermute | solution.py:167
  151.3 0.1 collective-permute-start.5
  151.4 1.7 collective-permute-done.5
  153.1 0.1 maximum_select_fusion
  153.2 0.9 copy.87
  154.3 0.1 add.281
  154.4 0.8 dynamic_slice.19
  155.2 19.4 %all-gather.9.cloned.1.call-done = bf16[8,193,2064]{2,1,0:T(8,128)(2,1)} async-done(((bf16[1,193,2064]{2,1,0:T(8,128)(2,1)}), bf16[8,193,2064]{2,1,0:T(8,128)(2,1)}) %all-gather.9.cloned.1.call-update) | async-done | bytes 6373648 | tf_op jit(solution)/shard_map/all_gather | solution.py:175
  174.5 9.1 %reshape.460 = bf16[1544,2064]{1,0:T(8,128)(2,1)} reshape(bf16[8,193,2064]{2,1,0:T(8,128)(2,1)} %all-gather.9.cloned.1.call-done) | data formatting | bytes 12747264
  183.6 1.3 compare_reduce_fusion
  184.9 30.2 %all-gather.7.cloned.1.call-done = bf16[768,2048]{1,0:T(8,128)(2,1)} async-done(((bf16[192,2048]{1,0:T(8,128)(2,1)}), bf16[768,2048]{1,0:T(8,128)(2,1)}) %all-gather.7.cloned.1.call-update) | async-done | bytes 3145744 | tf_op jit(solution)/shard_map/all_gather | solution.py:171
  215.2 9.8 %select_reduce_fusion.1 = (f32[768]{0:T(1024)S(1)}, f32[768,1544]{0,1:T(8,128)}) fusion(pred[1544]{0:T(1024)(128)(4,1)S(1)} %compare_reduce_fusion, bf16[768,2048]{1,0:T(8,128)(2,1)} %all-gather.7.cloned.1.call-done, bf16[2064,1544]{0,1:T(8,128)(2,1)} %bitcast.139), kind=kOutput, calls=%fused_computation.25 | convolution fusion | flops 4860560384 | bytes 14217736 | tf_op jit(solution)/shard_map/dot_general | solution.py:182
  225.0 4.5 %fusion.17 = (f32[768]{0:T(1024)S(1)}, f32[768]{0:T(1024)S(1)}, f32[768]{0:T(1024)S(1)}) fusion(f32[768,1544]{0,1:T(8,128)} %get-tuple-element.86, f32[768]{0:T(1024)S(1)} %get-tuple-element.85, pred[1544]{0:T(1024)(128)(4,1)S(1)} %compare_reduce_fusion, s32[1544]{0:T(1024)S(1)} %add.281, s32[768]{0:T(1024)S(1)} %dynamic_slice.19), kind=kLoop, calls=%fused_computation.23 | loop fusion | flops 13041408 | bytes 4766248 | tf_op jit(solution)/shard_map/reduce_sum | solution.py:189
  229.8 2.8 %collective-permute-start.6 = (f32[4,2,192]{2,0,1:T(4,128)S(1)}, f32[4,2,192]{2,0,1:T(4,128)S(1)}, u32[]{:S(2)}, u32[]{:S(2)}) collective-permute-start(f32[4,2,192]{2,0,1:T(4,128)S(1)} %constant_dynamic-slice_fusion.1), channel_id=1, source_target_pairs={{0,2},{1,3},{2,0},{3,1},{4,6},{5,7},{6,4},{7,5},{8,10},{9,11},{10,... | collective-permute-start | bytes 18440 | tf_op jit(solution)/shard_map/ppermute | solution.py:195
  232.7 2.6 %collective-permute-done.6 = f32[4,2,192]{2,0,1:T(4,128)S(1)} collective-permute-done((f32[4,2,192]{2,0,1:T(4,128)S(1)}, f32[4,2,192]{2,0,1:T(4,128)S(1)}, u32[]{:S(2)}, u32[]{:S(2)}) %collective-permute-start.6) | collective-permute-done | bytes 6176 | tf_op jit(solution)/shard_map/ppermute | solution.py:195
  235.4 1.7 collective-permute-start.7
  237.1 2.0 collective-permute-done.7
  239.2 0.1 collective-permute-start.8
  239.3 1.1 collective-permute-done.8
  240.5 1.7 collective-permute-start.9
  242.2 2.0 collective-permute-done.9
  244.3 3.2 %collective-permute-start.10 = (f32[4,192]{1,0:T(4,128)S(1)}, f32[4,192]{1,0:T(4,128)S(1)}, u32[]{:S(2)}, u32[]{:S(2)}) collective-permute-start(f32[4,192]{1,0:T(4,128)S(1)} %pad_maximum_fusion.5), channel_id=1, source_target_pairs={{0,128},{32,160},{64,192},{96,224},{128,0},{160,32},{192,64},{224,... | collective-permute-start | bytes 9224 | tf_op jit(solution)/shard_map/ppermute | solution.py:208
  247.4 2.0 collective-permute-done.10
  249.5 0.6 divide_subtract_fusion
  (63 shorter events, 1.3 us)
Async XLA Ops:
  7.2 108.3 %copy-start = (bf16[256,2048]{1,0:T(8,128)(2,1)S(1)}, bf16[256,2048]{1,0:T(8,128)(2,1)}, u32[]{:S(2)}) copy-start(bf16[256,2048]{1,0:T(8,128)(2,1)} %param.18) | copy-start | bytes 3145732
  7.2 12.5 %copy-start.1 = (bf16[192,2048]{1,0:T(8,128)(2,1)S(1)}, bf16[192,2048]{1,0:T(8,128)(2,1)}, u32[]{:S(2)}) copy-start(bf16[192,2048]{1,0:T(8,128)(2,1)} %param.13) | copy-start | bytes 2359300
  7.2 12.5 %copy-start.4 = (f32[2048]{0:T(1024)S(1)}, f32[2048]{0:T(1024)}, u32[]{:S(2)}) copy-start(f32[2048]{0:T(1024)} %param.14) | copy-start | bytes 24580
  7.2 8.5 %copy-start.2 = (bf16[2048,193]{0,1:T(8,128)(2,1)S(1)}, bf16[2048,193]{0,1:T(8,128)(2,1)}, u32[]{:S(2)}) copy-start(bf16[2048,193]{0,1:T(8,128)(2,1)} %param.20) | copy-start | bytes 2371588
  7.2 86.3 %all-gather.5.cloned.1.call-start = ((), (), s32[]{:S(2)}) async-start(), calls=%async_computation | async-start | bytes 1622016 | tf_op jit(solution)/shard_map/all_gather | solution.py:104
  14.8 159.7 %all-gather.9.cloned.1.call-start = ((), (), s32[]{:S(2)}) async-start(), calls=%async_computation.2 | async-start | bytes 7833600 | tf_op jit(solution)/shard_map/all_gather | solution.py:175
  17.0 198.1 %all-gather.7.cloned.1.call-start = ((), (), s32[]{:S(2)}) async-start(), calls=%async_computation.1 | async-start | bytes 3932160 | tf_op jit(solution)/shard_map/all_gather | solution.py:171
  116.0 2.5 collective-permute-start
  116.1 23.0 %copy-start.3 = (f32[2048]{0:T(1024)S(1)}, f32[2048]{0:T(1024)}, u32[]{:S(2)}) copy-start(f32[2048]{0:T(1024)} %param.19) | copy-start | bytes 24580
  119.8 11.3 %collective-permute-start.1 = (f32[2,24,2048]{2,1,0:T(8,128)S(1)}, f32[2,24,2048]{2,1,0:T(8,128)S(1)}, u32[]{:S(2)}, u32[]{:S(2)}) collective-permute-start(f32[2,24,2048]{2,1,0:T(8,128)S(1)} %select_bitcast_fusion.1), channel_id=1, source_target_pairs={{0,64},{32,96},{64,0},{96,32},{128,192},{160,224},{192,128},{224,1... | collective-permute-start | bytes 1179656 | tf_op jit(solution)/shard_map/ppermute | solution.py:159
  131.1 7.8 %collective-permute-start.2 = (f32[24,2048]{1,0:T(8,128)S(1)}, f32[24,2048]{1,0:T(8,128)S(1)}, u32[]{:S(2)}, u32[]{:S(2)}) collective-permute-start(f32[24,2048]{1,0:T(8,128)S(1)} %select_bitcast_fusion.2), channel_id=1, source_target_pairs={{0,128},{32,160},{64,192},{96,224},{128,0},{160,32},{192,64},{224,... | collective-permute-start | bytes 589832 | tf_op jit(solution)/shard_map/ppermute | solution.py:159
  139.2 6.2 %collective-permute-start.3 = (bf16[1,24,2048]{2,1,0:T(8,128)(2,1)S(1)}, bf16[1,24,2048]{2,1,0:T(8,128)(2,1)S(1)}, u32[]{:S(2)}, u32[]{:S(2)}) collective-permute-start(bf16[1,24,2048]{2,1,0:T(8,128)(2,1)S(1)} %get-tuple-element.53), channel_id=1, source_target_pairs={{0,128},{32,160},{64,192},{96,224},{128,0},{160,32},{192,64},{224,... | collective-permute-start | bytes 294920 | tf_op jit(solution)/shard_map/ppermute | solution.py:167
  145.4 5.8 %collective-permute-start.4 = (bf16[2,24,2048]{2,1,0:T(8,128)(2,1)S(1)}, bf16[2,24,2048]{2,1,0:T(8,128)(2,1)S(1)}, u32[]{:S(2)}, u32[]{:S(2)}) collective-permute-start(bf16[2,24,2048]{2,1,0:T(8,128)(2,1)S(1)} %maximum_select_fusion.3), channel_id=1, source_target_pairs={{0,64},{32,96},{64,0},{96,32},{128,192},{160,224},{192,128},{224,1... | collective-permute-start | bytes 589832 | tf_op jit(solution)/shard_map/ppermute | solution.py:167
  151.3 1.8 collective-permute-start.5
  229.8 5.5 %collective-permute-start.6 = (f32[4,2,192]{2,0,1:T(4,128)S(1)}, f32[4,2,192]{2,0,1:T(4,128)S(1)}, u32[]{:S(2)}, u32[]{:S(2)}) collective-permute-start(f32[4,2,192]{2,0,1:T(4,128)S(1)} %constant_dynamic-slice_fusion.1), channel_id=1, source_target_pairs={{0,2},{1,3},{2,0},{3,1},{4,6},{5,7},{6,4},{7,5},{8,10},{9,11},{10,... | collective-permute-start | bytes 18440 | tf_op jit(solution)/shard_map/ppermute | solution.py:195
  235.4 3.7 %collective-permute-start.7 = (f32[4,1,192]{2,0,1:T(4,128)S(1)}, f32[4,1,192]{2,0,1:T(4,128)S(1)}, u32[]{:S(2)}, u32[]{:S(2)}) collective-permute-start(f32[4,1,192]{2,0,1:T(4,128)S(1)} %constant_dynamic-slice_fusion), channel_id=1, source_target_pairs={{0,1},{1,0},{2,3},{3,2},{4,5},{5,4},{6,7},{7,6},{8,9},{9,8},{10,11... | collective-permute-start | bytes 9224 | tf_op jit(solution)/shard_map/ppermute | solution.py:203
  239.2 1.3 collective-permute-start.8
  240.5 3.7 %collective-permute-start.9 = (f32[4,192]{1,0:T(4,128)S(1)}, f32[4,192]{1,0:T(4,128)S(1)}, u32[]{:S(2)}, u32[]{:S(2)}) collective-permute-start(f32[4,192]{1,0:T(4,128)S(1)} %pad_maximum_fusion.4), channel_id=1, source_target_pairs={{0,64},{32,96},{64,0},{96,32},{128,192},{160,224},{192,128},{224,1... | collective-permute-start | bytes 9224 | tf_op jit(solution)/shard_map/ppermute | solution.py:208
  244.3 5.2 %collective-permute-start.10 = (f32[4,192]{1,0:T(4,128)S(1)}, f32[4,192]{1,0:T(4,128)S(1)}, u32[]{:S(2)}, u32[]{:S(2)}) collective-permute-start(f32[4,192]{1,0:T(4,128)S(1)} %pad_maximum_fusion.5), channel_id=1, source_target_pairs={{0,128},{32,160},{64,192},{96,224},{128,0},{160,32},{192,64},{224,... | collective-permute-start | bytes 9224 | tf_op jit(solution)/shard_map/ppermute | solution.py:208
Sparse Core Ops, SparseCore 0:
  14.9 78.5 all-gather.4
  95.3 79.1 all-gather.8
  176.4 38.7 all-gather.6

commit v5 on v4

--- a/solution.py
+++ b/solution.py
@@ -101,7 +101,24 @@
         jnp.zeros((kv_local, group_size, tok_rows), jnp.float32),
         jnp.zeros((kv_local, group_size, tok_rows, HEAD_DIM), jnp.float32),
     )
-    shard_rows = lax.all_gather(packed, ("z", "y"), axis=0, tiled=True)
+    z_count = lax.psum(1, "z")
+    y_count = lax.psum(1, "y")
+    z_bits = z_count.bit_length() - 1
+    y_bits = y_count.bit_length() - 1
+    z_pos = lax.axis_index("z")
+    y_pos = lax.axis_index("y")
+    gathered = packed.reshape((1,) * (z_bits + y_bits) + packed.shape)
+    order = [("z", bit, z_pos, z_count, z_bits - 1 - bit) for bit in range(z_bits)]
+    order += [("y", bit, y_pos, y_count, z_bits + y_bits - 1 - bit) for bit in range(y_bits)]
+    for name, bit, pos, count, axis in order:
+        mine_low = (pos >> bit) % 2 == 0
+        got = lax.ppermute(gathered, name, [(p, p ^ (1 << bit)) for p in range(count)])
+        gathered = jnp.where(
+            mine_low,
+            jnp.concatenate([gathered, got], axis=axis),
+            jnp.concatenate([got, gathered], axis=axis),
+        )
+    shard_rows = gathered.reshape((-1,) + packed.shape[1:])
     offset = jnp.int32(0)
     row_count = shard_rows.shape[0]
     key_pos = jnp.arange(row_count, dtype=jnp.int32)
@@ -139,8 +156,6 @@
         .astype(jnp.bfloat16)
     )
     vocab_local = w_head.shape[1]
-    y_count = lax.psum(1, "y")
-    z_count = lax.psum(1, "z")
     z_index = lax.axis_index("z")
     y_index = lax.axis_index("y")
     kv_index = lax.axis_index("kv")
@@ -170,14 +185,19 @@
     final_in = rows.reshape(tok_rows, final_part.shape[1])
     head_rows = lax.all_gather(final_in, "y", axis=0, tiled=True)
     group_rows = head_rows.shape[0]
+    padded_local = -(-vocab_local // 16) * 16
     head_pad = jnp.zeros((16 - 1, vocab_local), w_head.dtype)
     head_ext = jnp.concatenate([w_head, vocab_mask.astype(w_head.dtype)[None, :], head_pad], axis=0)
+    head_ext = jnp.pad(head_ext, ((0, 0), (0, padded_local - vocab_local)))
     head_ext = lax.all_gather(head_ext, "z", axis=1, tiled=True)
     head_cols = head_ext[: w_head.shape[0]]
     mask_cols = head_ext[w_head.shape[0]]
     live_mask = mask_cols == 1.0
     shard_ids = kv_index * (z_count * y_count) + jnp.arange(z_count, dtype=jnp.int32) * y_count + y_index
-    columns = (shard_ids[:, None] * vocab_local + jnp.arange(vocab_local, dtype=jnp.int32)[None, :]).reshape(-1)
+    local_cols = jnp.arange(padded_local, dtype=jnp.int32)
+    columns = jnp.where(
+        local_cols[None, :] < vocab_local, shard_ids[:, None] * vocab_local + local_cols[None, :], -1
+    ).reshape(-1)
     row_ids = lax.dynamic_slice_in_dim(target_ids, z_index * group_rows, group_rows, 0)
     logits = jnp.dot(head_rows, head_cols, preferred_element_type=jnp.float32) * LOGIT_SCALE
     masked = jnp.where(live_mask[None, :], logits, NEG_FILL)

time: 259 us -> 252 us (0.973)
  waiting for transfers between devices: 156 us -> 120 us
  starting transfers between devices: 19.2 us -> 34.7 us
  other arithmetic: 21 us -> 29.4 us
  matrix products: 26.5 us -> 33 us
    all_gather x1 -> x0, waiting for transfers between devices: 71.9 us -> none  [local(): shard_rows = lax.all_gather(packed, ('z', 'y'), axis=0, tiled=True)]
    ppermute x0 -> x5, waiting for transfers between devices: none -> 45 us  [local(): lax.ppermute(gathered, name, [(p, p ^ 1 << bit) for p in range(count)])]
    all_gather x1, waiting for transfers between devices: 19.4 us -> 0.01 us  [local(): head_ext = lax.all_gather(head_ext, 'z', axis=1, tiled=True)]
    ppermute x0 -> x5, starting transfers between devices: none -> 15.8 us  [local(): lax.ppermute(gathered, name, [(p, p ^ 1 << bit) for p in range(count)])]
    all_gather x1, waiting for transfers between devices: 30.2 us -> 40.8 us  [local(): head_rows = lax.all_gather(final_in, 'y', axis=0, tiled=True)]
    unnamed x11 -> x10, local copies, waits for them, and re-layouts: 9.12 us -> 0.03 us
    another operation x2 -> x3, local copies, waits for them, and re-layouts: 3.55 us -> 7.2 us
    dot_general x1, matrix products: 4.97 us -> 8.16 us  [update(): jnp.einsum('tkgd,skd->kgts', rotated_q, key_rows, preferred_element_type=...]
  transfers between devices with their start and end apart: 14 -> 18, of which waited for: 14 -> 17; matrix products, arithmetic and copies ran while one was open for 17% -> 23% of each run, Pallas kernels for 0% -> 0%
where the time goes in v5:
time: 252 us; the launch traced here: 249 us
  waiting for transfers between devices  120 us (48%)
  starting transfers between devices  34.7 us (14%)
  matrix products  33 us (13%)
  other arithmetic  29.4 us (12%)
  local copies, waits for them, and re-layouts  16.1 us (6%)
  between operations  15.8 us (6%)
    ppermute x5, waiting for transfers between devices, local(): lax.ppermute(gathered, name, [(p, p ^ 1 << bit) for p in range(count)])  45 us
    all_gather x1, waiting for transfers between devices, local(): head_rows = lax.all_gather(final_in, 'y', axis=0, tiled=True)  40.8 us
    ppermute x5, starting transfers between devices, local(): lax.ppermute(gathered, name, [(p, p ^ 1 << bit) for p in range(count)])  15.8 us
    ppermute x3, waiting for transfers between devices, local(): got = lax.ppermute(send, 'kv', [(p, p ^ 1 << bit) for p in range(kv_count)])  15.4 us
    dot_general x1, matrix products, local(): jnp.dot(head_rows, head_cols, preferred_element_type=jnp.float32)  11.3 us
    reduce_sum x1, other arithmetic, update(): totals = jnp.sum(weights, axis=-1)  9.6 us
    dot_general x1, matrix products, update(): jnp.einsum('kgts,skd->kgtd', weights.astype(jnp.bfloat16), value_rows, pr...  9.44 us
    ppermute x3, waiting for transfers between devices, local(): got = lax.ppermute(rows, 'kv', [(p, p ^ 1 << bit) for p in range(kv_count)])  9.08 us
  transfers between devices with their start and end apart: 18, of which 17 were waited for; matrix products, arithmetic and copies ran while one was open for 23% of the time, Pallas kernels for 0%

profile of v5, /device:TPU:24, one launch (start us, length us, event | category | flops | bytes accessed | tf_op | source)
XLA Modules:
  0.0 249.2 jit_solution(11497667538749531310)
XLA Ops:
  7.3 0.8 convert_element_type.58
  8.2 1.4 concatenate.314
  9.6 1.0 pad.4
  10.7 0.8 copy.113
  11.6 0.7 sub.118
  12.4 0.2 multiply_reduce_fusion.1
  12.7 0.5 convolution_bitcast_fusion
  13.3 1.4 convolution_convert_fusion
  14.8 2.0 collective-permute-start
  16.8 2.3 collective-permute-done
  19.2 3.4 %collective-permute-start.1 = (bf16[1,1,2,1,1,192,128]{5,6,4,3,2,1,0:T(8,128)(2,1)S(1)}, bf16[1,1,2,1,1,192,128]{5,6,4,3,2,1,0:T(8,128)(2,1)S(1)}, u32[]{:S(2)}, u32[]{:S(2)}) collective-permute-start(bf16[1,1,2,1,1,192,128]{5,6,4,3,2,1,0:T(8,128)(2,1)S(1)} %maximum_select_fusion.8), channel_id=1, source_target_pairs={{0,8},{4,12},{8,0},{12,4},{16,24},{20,28},{24,16},{28,20},{1,9},{5... | collective-permute-start | bytes 294920 | tf_op jit(solution)/shard_map/ppermute | solution.py:115
  22.6 5.7 %collective-permute-done.1 = bf16[1,1,2,1,1,192,128]{5,6,4,3,2,1,0:T(8,128)(2,1)S(1)} collective-permute-done((bf16[1,1,2,1,1,192,128]{5,6,4,3,2,1,0:T(8,128)(2,1)S(1)}, bf16[1,1,2,1,1,192,128]{5,6,4,3,2,1,0:T(8,128)(2,1)S(1)}, u32[]{:S(2)}, u32[]{:S(2)}) %collective-permute-start.1) | collective-permute-done | bytes 98336 | tf_op jit(solution)/shard_map/ppermute | solution.py:115
  28.4 8.3 %collective-permute-start.2 = (bf16[1,2,2,1,1,192,128]{5,6,4,3,2,1,0:T(8,128)(2,1)S(1)}, bf16[1,2,2,1,1,192,128]{5,6,4,3,2,1,0:T(8,128)(2,1)S(1)}, u32[]{:S(2)}, u32[]{:S(2)}) collective-permute-start(bf16[1,2,2,1,1,192,128]{5,6,4,3,2,1,0:T(8,128)(2,1)S(1)} %fusion.26), channel_id=1, source_target_pairs={{0,16},{4,20},{8,24},{12,28},{16,0},{20,4},{24,8},{28,12},{1,17},{... | collective-permute-start | bytes 589832 | tf_op jit(solution)/shard_map/ppermute | solution.py:115
  36.8 16.2 %collective-permute-done.2 = bf16[1,2,2,1,1,192,128]{5,6,4,3,2,1,0:T(8,128)(2,1)S(1)} collective-permute-done((bf16[1,2,2,1,1,192,128]{5,6,4,3,2,1,0:T(8,128)(2,1)S(1)}, bf16[1,2,2,1,1,192,128]{5,6,4,3,2,1,0:T(8,128)(2,1)S(1)}, u32[]{:S(2)}, u32[]{:S(2)}) %collective-permute-start.2) | collective-permute-done | bytes 196640 | tf_op jit(solution)/shard_map/ppermute | solution.py:115
  53.0 1.0 fusion.23
  54.0 0.8 collective-permute-start.3
  54.8 0.5 slice.193
  55.3 0.6 slice.194
  57.3 7.4 %collective-permute-done.3 = bf16[2,2,2,1,1,192,128]{5,6,4,3,2,1,0:T(8,128)(2,1)S(1)} collective-permute-done((bf16[2,2,2,1,1,192,128]{5,6,4,3,2,1,0:T(8,128)(2,1)}, bf16[2,2,2,1,1,192,128]{5,6,4,3,2,1,0:T(8,128)(2,1)S(1)}, u32[]{:S(2)}, u32[]{:S(2)}) %collective-permute-start.3) | collective-permute-done | bytes 393248 | tf_op jit(solution)/shard_map/ppermute | solution.py:115
  64.7 0.3 maximum_select_fusion
  65.0 1.3 copy.120
  66.3 1.3 collective-permute-start.4
  67.8 1.9 fusion.65
  69.8 13.4 %collective-permute-done.4 = bf16[2,2,2,1,2,192,128]{6,5,4,3,2,1,0:T(8,128)(2,1)} collective-permute-done((bf16[2,2,2,1,2,192,128]{6,5,4,3,2,1,0:T(8,128)(2,1)}, bf16[2,2,2,1,2,192,128]{6,5,4,3,2,1,0:T(8,128)(2,1)}, u32[]{:S(2)}, u32[]{:S(2)}) %collective-permute-start.4) | collective-permute-done | bytes 786464 | tf_op jit(solution)/shard_map/ppermute | solution.py:115
  83.2 1.4 copy.121
  84.7 2.7 %pad_maximum_fusion.1 = (bf16[2,2,2,2,2,192,128]{5,6,4,3,2,1,0:T(8,128)(2,1)}, bf16[2,2,2,2,2,192,128]{5,6,4,3,2,1,0:T(8,128)(2,1)}) fusion(bf16[2,2,2,1,2,192,128]{5,6,4,3,2,1,0:T(8,128)(2,1)S(1)} %maximum_select_fusion, bf16[2,2,2,1,2,192,128]{5,6,4,3,2,1,0:T(8,128)(2,1)S(1)} %copy.121), kind=kLoop, calls=%fused_computation.28 | loop fusion | flops 1572864 | bytes 4718592 | tf_op jit(solution)/shard_map/concatenate | solution.py:119
  87.3 36.3 %conditional.1 = (f32[1,4,192]{2,1,0:T(4,128)S(1)}, f32[1,4,192,64]{2,3,1,0:T(8,128)S(1)}) conditional(s32[]{:T(128)} %bitcast.10, (s32[6144]{0:T(1024)S(1)}, s32[6144]{0:T(1024)S(1)}, s32[192]{0:T(256)S(1)}, s32[192]{0:T(256)S(1)}, s32[]{:T(128)}, /*index=5*/bf16[2,2,2,2,2,192,128]{5,6,4,3,2,1,0:T(8,128)(2,1)}, ...), branch_computations={%region_3.6_spmd, %region_6.7_spmd} | conditional | flops 1273625856 | bytes 82153136 | solution.py:151
  87.3 4.2 %copy.124 = bf16[2,2,2,2,2,192,128]{6,5,4,3,2,1,0:T(8,128)(2,1)} copy(bf16[2,2,2,2,2,192,128]{5,6,4,3,2,1,0:T(8,128)(2,1)} %get-tuple-element.149) | data formatting | bytes 3145728 | tf_op jit(solution)/shard_map
  91.5 2.3 copy.125
  93.8 1.6 broadcast_select_fusion
  95.4 1.0 compare_and_fusion
  96.4 8.2 %fusion = (f32[4,192]{1,0:T(4,128)S(1)}, f32[6144,192,4]{0,1,2:T(8,128)}) fusion(pred[192,6144]{1,0:T(8,128)(4,1)S(1)} %compare_and_fusion, bf16[192,1,4,64]{0,3,2,1:T(8,128)(2,1)S(1)} %get-tuple-element.99, bf16[6144,128]{1,0:T(8,128)(2,1)S(1)} %bitcast.175), kind=kOutput, calls=%fused_computation.2 | convolution fusion | flops 618134784 | bytes 21728256 | tf_op jit(solution)/shard_map/cond/branch_0_fun/tkgd,skd->kgts/dot_general | solution.py:131
  104.6 9.4 %fusion.8 = f32[1,4,192,64]{2,3,1,0:T(8,128)S(1)} fusion(bf16[6144,128]{1,0:T(8,128)(2,1)S(1)} %bitcast.176, f32[6144,192,4]{0,1,2:T(8,128)} %get-tuple-element.167, f32[4,192]{1,0:T(4,128)S(1)} %broadcast_maximum_fusion, pred[192,6144]{1,0:T(8,128)(4,1)S(1)} %compare_and_fusion), kind=kOutput, calls=%fused_computation.13 | convolution fusion | flops 627572736 | bytes 21826560 | tf_op jit(solution)/shard_map/cond/branch_0_fun/kgts,skd->kgtd/dot_general | solution.py:142
  114.0 9.6 %fusion.2 = f32[4,192]{1,0:T(4,128)S(1)} fusion(f32[6144,192,4]{0,1,2:T(8,128)} %get-tuple-element.167, f32[4,192]{1,0:T(4,128)S(1)} %broadcast_maximum_fusion, pred[192,6144]{1,0:T(8,128)(4,1)S(1)} %compare_and_fusion), kind=kLoop, calls=%fused_computation.4 | loop fusion | flops 23592192 | bytes 20060160 | tf_op jit(solution)/shard_map/cond/branch_0_fun/reduce_sum | solution.py:141
  124.0 0.4 fusion.18
  124.6 2.4 collective-permute-done.5
  127.0 1.3 fusion.21
  128.3 1.6 collective-permute-start.6
  129.9 9.7 %collective-permute-done.6 = f32[2,24,2048]{2,1,0:T(8,128)S(1)} collective-permute-done((f32[2,24,2048]{2,1,0:T(8,128)S(1)}, f32[2,24,2048]{2,1,0:T(8,128)S(1)}, u32[]{:S(2)}, u32[]{:S(2)}) %collective-permute-start.6) | collective-permute-done | bytes 393248 | tf_op jit(solution)/shard_map/ppermute | solution.py:174
  139.7 3.0 %collective-permute-start.7 = (f32[24,2048]{1,0:T(8,128)S(1)}, f32[24,2048]{1,0:T(8,128)S(1)}, u32[]{:S(2)}, u32[]{:S(2)}) collective-permute-start(f32[24,2048]{1,0:T(8,128)S(1)} %select_bitcast_fusion.2), channel_id=1, source_target_pairs={{0,128},{32,160},{64,192},{96,224},{128,0},{160,32},{192,64},{224,... | collective-permute-start | bytes 589832 | tf_op jit(solution)/shard_map/ppermute | solution.py:174
  142.7 1.3 convert_element_type.59
  144.0 3.4 %collective-permute-done.7 = f32[24,2048]{1,0:T(8,128)S(1)} collective-permute-done((f32[24,2048]{1,0:T(8,128)S(1)}, f32[24,2048]{1,0:T(8,128)S(1)}, u32[]{:S(2)}, u32[]{:S(2)}) %collective-permute-start.7) | collective-permute-done | bytes 196640 | tf_op jit(solution)/shard_map/ppermute | solution.py:174
  147.6 3.0 %collective-permute-start.8 = (bf16[1,24,2048]{2,1,0:T(8,128)(2,1)S(1)}, bf16[1,24,2048]{2,1,0:T(8,128)(2,1)S(1)}, u32[]{:S(2)}, u32[]{:S(2)}) collective-permute-start(bf16[1,24,2048]{2,1,0:T(8,128)(2,1)S(1)} %get-tuple-element.176), channel_id=1, source_target_pairs={{0,128},{32,160},{64,192},{96,224},{128,0},{160,32},{192,64},{224,... | collective-permute-start | bytes 294920 | tf_op jit(solution)/shard_map/ppermute | solution.py:182
  150.6 3.2 %collective-permute-done.8 = bf16[1,24,2048]{2,1,0:T(8,128)(2,1)S(1)} collective-permute-done((bf16[1,24,2048]{2,1,0:T(8,128)(2,1)S(1)}, bf16[1,24,2048]{2,1,0:T(8,128)(2,1)S(1)}, u32[]{:S(2)}, u32[]{:S(2)}) %collective-permute-start.8) | collective-permute-done | bytes 98336 | tf_op jit(solution)/shard_map/ppermute | solution.py:182
  153.8 1.6 collective-permute-start.9
  155.4 4.2 %collective-permute-done.9 = bf16[2,24,2048]{2,1,0:T(8,128)(2,1)S(1)} collective-permute-done((bf16[2,24,2048]{2,1,0:T(8,128)(2,1)S(1)}, bf16[2,24,2048]{2,1,0:T(8,128)(2,1)S(1)}, u32[]{:S(2)}, u32[]{:S(2)}) %collective-permute-start.9) | collective-permute-done | bytes 196640 | tf_op jit(solution)/shard_map/ppermute | solution.py:182
  159.7 0.3 collective-permute-start.10
  160.0 1.7 collective-permute-done.10
  161.8 0.9 copy.137
  163.0 0.8 dynamic_slice.19
  163.8 1.3 compare_reduce_fusion
  165.1 40.8 %all-gather.5.cloned.1.call-done = bf16[768,2048]{1,0:T(8,128)(2,1)} async-done(((bf16[192,2048]{1,0:T(8,128)(2,1)}), bf16[768,2048]{1,0:T(8,128)(2,1)}) %all-gather.5.cloned.1.call-update) | async-done | bytes 3145744 | tf_op jit(solution)/shard_map/all_gather | solution.py:186
  206.0 11.3 %select_reduce_fusion.1 = (f32[768]{0:T(1024)S(1)}, f32[768,1664]{1,0:T(8,128)}) fusion(pred[1664]{0:T(1024)(128)(4,1)S(1)} %compare_reduce_fusion, bf16[768,2048]{1,0:T(8,128)(2,1)} %all-gather.5.cloned.1.call-done, bf16[2064,1664]{0,1:T(8,128)(2,1)} %all-gather.3.cloned.1.call-done), kind=kOutput, calls=%fused_computation.26 | convolution fusion | flops 5238324224 | bytes 15078016 | tf_op jit(solution)/shard_map/dot_general | solution.py:202
  217.3 4.8 %fusion.17 = (f32[768]{0:T(1024)S(1)}, f32[768]{0:T(1024)S(1)}, f32[768]{0:T(1024)S(1)}) fusion(f32[768,1664]{1,0:T(8,128)} %get-tuple-element.214, f32[768]{0:T(1024)S(1)} %get-tuple-element.213, pred[1664]{0:T(1024)(128)(4,1)S(1)} %compare_reduce_fusion, s32[1664]{0:T(1024)S(1)} %select_n.528, s32[768]{0:T(1024)S(1)} %dynamic_slice.19), kind=kLoop, calls=%fused_computation.24 | loop fusion | flops 14055168 | bytes 5135488 | tf_op jit(solution)/shard_map/reduce_sum | solution.py:209
  222.4 2.6 %collective-permute-start.11 = (f32[4,2,192]{2,0,1:T(4,128)S(1)}, f32[4,2,192]{2,0,1:T(4,128)S(1)}, u32[]{:S(2)}, u32[]{:S(2)}) collective-permute-start(f32[4,2,192]{2,0,1:T(4,128)S(1)} %constant_dynamic-slice_fusion.1), channel_id=1, source_target_pairs={{0,2},{1,3},{2,0},{3,1},{4,6},{5,7},{6,4},{7,5},{8,10},{9,11},{10,... | collective-permute-start | bytes 18440 | tf_op jit(solution)/shard_map/ppermute | solution.py:215
  225.0 2.6 %collective-permute-done.11 = f32[4,2,192]{2,0,1:T(4,128)S(1)} collective-permute-done((f32[4,2,192]{2,0,1:T(4,128)S(1)}, f32[4,2,192]{2,0,1:T(4,128)S(1)}, u32[]{:S(2)}, u32[]{:S(2)}) %collective-permute-start.11) | collective-permute-done | bytes 6176 | tf_op jit(solution)/shard_map/ppermute | solution.py:215
  227.7 1.7 collective-permute-start.12
  229.4 2.0 collective-permute-done.12
  231.6 1.1 collective-permute-done.13
  232.8 1.7 collective-permute-start.14
  234.5 2.0 collective-permute-done.14
  236.6 3.2 %collective-permute-start.15 = (f32[4,192]{1,0:T(4,128)S(1)}, f32[4,192]{1,0:T(4,128)S(1)}, u32[]{:S(2)}, u32[]{:S(2)}) collective-permute-start(f32[4,192]{1,0:T(4,128)S(1)} %pad_maximum_fusion.7), channel_id=1, source_target_pairs={{0,128},{32,160},{64,192},{96,224},{128,0},{160,32},{192,64},{224,... | collective-permute-start | bytes 9224 | tf_op jit(solution)/shard_map/ppermute | solution.py:228
  239.7 2.0 collective-permute-done.15
  241.8 0.6 divide_subtract_fusion
  (84 shorter events, 3.5 us)
Async XLA Ops:
  7.2 116.9 %copy-start = (bf16[256,2048]{1,0:T(8,128)(2,1)S(1)}, bf16[256,2048]{1,0:T(8,128)(2,1)}, u32[]{:S(2)}) copy-start(bf16[256,2048]{1,0:T(8,128)(2,1)} %param.18) | copy-start | bytes 3145732
  7.2 5.2 %copy-start.2 = (bf16[192,2048]{1,0:T(8,128)(2,1)S(1)}, bf16[192,2048]{1,0:T(8,128)(2,1)}, u32[]{:S(2)}) copy-start(bf16[192,2048]{1,0:T(8,128)(2,1)} %param.13) | copy-start | bytes 2359300
  7.2 5.5 %copy-start.5 = (f32[2048]{0:T(1024)S(1)}, f32[2048]{0:T(1024)}, u32[]{:S(2)}) copy-start(f32[2048]{0:T(1024)} %param.14) | copy-start | bytes 24580
  7.2 5.5 %copy-start.4 = (bf16[2048,64]{0,1:T(8,128)(2,1)S(1)}, bf16[2048,64]{0,1:T(8,128)(2,1)}, u32[]{:S(2)}) copy-start(bf16[2048,64]{0,1:T(8,128)(2,1)} %param.16) | copy-start | bytes 786436
  7.2 156.6 %all-gather.3.cloned.1.call-start = ((), (), s32[]{:S(2)}) async-start(), calls=%async_computation | async-start | bytes 8146944 | tf_op jit(solution)/shard_map/all_gather | solution.py:192
  10.7 195.3 %all-gather.5.cloned.1.call-start = ((), (), s32[]{:S(2)}) async-start(), calls=%async_computation.1 | async-start | bytes 3932160 | tf_op jit(solution)/shard_map/all_gather | solution.py:186
  14.8 4.4 %collective-permute-start = (bf16[1,1,1,1,1,192,128]{5,6,4,3,2,1,0:T(8,128)(2,1)S(1)}, bf16[1,1,1,1,1,192,128]{5,6,4,3,2,1,0:T(8,128)(2,1)S(1)}, u32[]{:S(2)}, u32[]{:S(2)}) collective-permute-start(bf16[1,1,1,1,1,192,128]{5,6,4,3,2,1,0:T(8,128)(2,1)S(1)} %get-tuple-element.183), channel_id=1, source_target_pairs={{0,4},{4,0},{8,12},{12,8},{16,20},{20,16},{24,28},{28,24},{1,5},{5... | collective-permute-start | bytes 147464 | tf_op jit(solution)/shard_map/ppermute | solution.py:115
  19.2 9.1 %collective-permute-start.1 = (bf16[1,1,2,1,1,192,128]{5,6,4,3,2,1,0:T(8,128)(2,1)S(1)}, bf16[1,1,2,1,1,192,128]{5,6,4,3,2,1,0:T(8,128)(2,1)S(1)}, u32[]{:S(2)}, u32[]{:S(2)}) collective-permute-start(bf16[1,1,2,1,1,192,128]{5,6,4,3,2,1,0:T(8,128)(2,1)S(1)} %maximum_select_fusion.8), channel_id=1, source_target_pairs={{0,8},{4,12},{8,0},{12,4},{16,24},{20,28},{24,16},{28,20},{1,9},{5... | collective-permute-start | bytes 294920 | tf_op jit(solution)/shard_map/ppermute | solution.py:115
  28.4 24.6 %collective-permute-start.2 = (bf16[1,2,2,1,1,192,128]{5,6,4,3,2,1,0:T(8,128)(2,1)S(1)}, bf16[1,2,2,1,1,192,128]{5,6,4,3,2,1,0:T(8,128)(2,1)S(1)}, u32[]{:S(2)}, u32[]{:S(2)}) collective-permute-start(bf16[1,2,2,1,1,192,128]{5,6,4,3,2,1,0:T(8,128)(2,1)S(1)} %fusion.26), channel_id=1, source_target_pairs={{0,16},{4,20},{8,24},{12,28},{16,0},{20,4},{24,8},{28,12},{1,17},{... | collective-permute-start | bytes 589832 | tf_op jit(solution)/shard_map/ppermute | solution.py:115
  54.0 10.8 %collective-permute-start.3 = (bf16[2,2,2,1,1,192,128]{5,6,4,3,2,1,0:T(8,128)(2,1)}, bf16[2,2,2,1,1,192,128]{5,6,4,3,2,1,0:T(8,128)(2,1)S(1)}, u32[]{:S(2)}, u32[]{:S(2)}) collective-permute-start(bf16[2,2,2,1,1,192,128]{5,6,4,3,2,1,0:T(8,128)(2,1)} %fusion.23), channel_id=1, source_target_pairs={{0,1},{1,0},{2,3},{3,2},{4,5},{5,4},{6,7},{7,6},{8,9},{9,8},{10,11... | collective-permute-start | bytes 1179656 | tf_op jit(solution)/shard_map/ppermute | solution.py:115
  66.3 16.9 %collective-permute-start.4 = (bf16[2,2,2,1,2,192,128]{6,5,4,3,2,1,0:T(8,128)(2,1)}, bf16[2,2,2,1,2,192,128]{6,5,4,3,2,1,0:T(8,128)(2,1)}, u32[]{:S(2)}, u32[]{:S(2)}) collective-permute-start(bf16[2,2,2,1,2,192,128]{6,5,4,3,2,1,0:T(8,128)(2,1)} %copy.120), channel_id=1, source_target_pairs={{0,2},{1,3},{2,0},{3,1},{4,6},{5,7},{6,4},{7,5},{8,10},{9,11},{10,... | collective-permute-start | bytes 2359304 | tf_op jit(solution)/shard_map/ppermute | solution.py:115
  87.3 4.2 %copy-start.1 = (bf16[2,2,2,2,2,192,128]{5,6,4,3,2,1,0:T(8,128)(2,1)S(1)}, bf16[2,2,2,2,2,192,128]{5,6,4,3,2,1,0:T(8,128)(2,1)}, u32[]{:S(2)}) copy-start(bf16[2,2,2,2,2,192,128]{5,6,4,3,2,1,0:T(8,128)(2,1)} %get-tuple-element.150) | copy-start | bytes 4718596 | tf_op jit(solution)/shard_map/cond
  124.5 2.5 %collective-permute-start.5 = (f32[2,2,24,2048]{3,2,1,0:T(8,128)S(1)}, f32[2,2,24,2048]{3,2,1,0:T(8,128)}, u32[]{:S(2)}, u32[]{:S(2)}) collective-permute-start(f32[2,2,24,2048]{3,2,1,0:T(8,128)S(1)} %select_bitcast_fusion), channel_id=1, source_target_pairs={{0,32},{32,0},{64,96},{96,64},{128,160},{160,128},{192,224},{224,1... | collective-permute-start | bytes 2359304 | tf_op jit(solution)/shard_map/ppermute | solution.py:174
  124.6 22.9 %copy-start.3 = (f32[2048]{0:T(1024)S(1)}, f32[2048]{0:T(1024)}, u32[]{:S(2)}) copy-start(f32[2048]{0:T(1024)} %param.19) | copy-start | bytes 24580
  128.3 11.2 %collective-permute-start.6 = (f32[2,24,2048]{2,1,0:T(8,128)S(1)}, f32[2,24,2048]{2,1,0:T(8,128)S(1)}, u32[]{:S(2)}, u32[]{:S(2)}) collective-permute-start(f32[2,24,2048]{2,1,0:T(8,128)S(1)} %select_bitcast_fusion.1), channel_id=1, source_target_pairs={{0,64},{32,96},{64,0},{96,32},{128,192},{160,224},{192,128},{224,1... | collective-permute-start | bytes 1179656 | tf_op jit(solution)/shard_map/ppermute | solution.py:174
  139.7 7.7 %collective-permute-start.7 = (f32[24,2048]{1,0:T(8,128)S(1)}, f32[24,2048]{1,0:T(8,128)S(1)}, u32[]{:S(2)}, u32[]{:S(2)}) collective-permute-start(f32[24,2048]{1,0:T(8,128)S(1)} %select_bitcast_fusion.2), channel_id=1, source_target_pairs={{0,128},{32,160},{64,192},{96,224},{128,0},{160,32},{192,64},{224,... | collective-permute-start | bytes 589832 | tf_op jit(solution)/shard_map/ppermute | solution.py:174
  147.6 6.2 %collective-permute-start.8 = (bf16[1,24,2048]{2,1,0:T(8,128)(2,1)S(1)}, bf16[1,24,2048]{2,1,0:T(8,128)(2,1)S(1)}, u32[]{:S(2)}, u32[]{:S(2)}) collective-permute-start(bf16[1,24,2048]{2,1,0:T(8,128)(2,1)S(1)} %get-tuple-element.176), channel_id=1, source_target_pairs={{0,128},{32,160},{64,192},{96,224},{128,0},{160,32},{192,64},{224,... | collective-permute-start | bytes 294920 | tf_op jit(solution)/shard_map/ppermute | solution.py:182
  153.8 5.8 %collective-permute-start.9 = (bf16[2,24,2048]{2,1,0:T(8,128)(2,1)S(1)}, bf16[2,24,2048]{2,1,0:T(8,128)(2,1)S(1)}, u32[]{:S(2)}, u32[]{:S(2)}) collective-permute-start(bf16[2,24,2048]{2,1,0:T(8,128)(2,1)S(1)} %maximum_select_fusion.6), channel_id=1, source_target_pairs={{0,64},{32,96},{64,0},{96,32},{128,192},{160,224},{192,128},{224,1... | collective-permute-start | bytes 589832 | tf_op jit(solution)/shard_map/ppermute | solution.py:182
  159.7 2.0 collective-permute-start.10
  222.4 5.2 %collective-permute-start.11 = (f32[4,2,192]{2,0,1:T(4,128)S(1)}, f32[4,2,192]{2,0,1:T(4,128)S(1)}, u32[]{:S(2)}, u32[]{:S(2)}) collective-permute-start(f32[4,2,192]{2,0,1:T(4,128)S(1)} %constant_dynamic-slice_fusion.1), channel_id=1, source_target_pairs={{0,2},{1,3},{2,0},{3,1},{4,6},{5,7},{6,4},{7,5},{8,10},{9,11},{10,... | collective-permute-start | bytes 18440 | tf_op jit(solution)/shard_map/ppermute | solution.py:215
  227.7 3.7 %collective-permute-start.12 = (f32[4,1,192]{2,0,1:T(4,128)S(1)}, f32[4,1,192]{2,0,1:T(4,128)S(1)}, u32[]{:S(2)}, u32[]{:S(2)}) collective-permute-start(f32[4,1,192]{2,0,1:T(4,128)S(1)} %constant_dynamic-slice_fusion), channel_id=1, source_target_pairs={{0,1},{1,0},{2,3},{3,2},{4,5},{5,4},{6,7},{7,6},{8,9},{9,8},{10,11... | collective-permute-start | bytes 9224 | tf_op jit(solution)/shard_map/ppermute | solution.py:223
  231.5 1.3 collective-permute-start.13
  232.8 3.7 %collective-permute-start.14 = (f32[4,192]{1,0:T(4,128)S(1)}, f32[4,192]{1,0:T(4,128)S(1)}, u32[]{:S(2)}, u32[]{:S(2)}) collective-permute-start(f32[4,192]{1,0:T(4,128)S(1)} %pad_maximum_fusion.6), channel_id=1, source_target_pairs={{0,64},{32,96},{64,0},{96,32},{128,192},{160,224},{192,128},{224,1... | collective-permute-start | bytes 9224 | tf_op jit(solution)/shard_map/ppermute | solution.py:228
  236.6 5.2 %collective-permute-start.15 = (f32[4,192]{1,0:T(4,128)S(1)}, f32[4,192]{1,0:T(4,128)S(1)}, u32[]{:S(2)}, u32[]{:S(2)}) collective-permute-start(f32[4,192]{1,0:T(4,128)S(1)} %pad_maximum_fusion.7), channel_id=1, source_target_pairs={{0,128},{32,160},{64,192},{96,224},{128,0},{160,32},{192,64},{224,... | collective-permute-start | bytes 9224 | tf_op jit(solution)/shard_map/ppermute | solution.py:228
Sparse Core Ops, SparseCore 0:
  10.8 97.2 all-gather.2
  162.9 42.9 all-gather.4

commit v6 on v5

--- a/solution.py
+++ b/solution.py
@@ -94,8 +94,6 @@
     packed = jnp.concatenate(
         [rotated_k.reshape(tok_rows, key_width), value_proj.astype(jnp.bfloat16)], axis=1
     )
-    earliest = doc_start[0]
-    latest = token_pos[tok_rows - 1]
     initial = (
         jnp.full((kv_local, group_size, tok_rows), NEG_FILL, jnp.float32),
         jnp.zeros((kv_local, group_size, tok_rows), jnp.float32),
@@ -103,25 +101,29 @@
     )
     z_count = lax.psum(1, "z")
     y_count = lax.psum(1, "y")
-    z_bits = z_count.bit_length() - 1
     y_bits = y_count.bit_length() - 1
     z_pos = lax.axis_index("z")
     y_pos = lax.axis_index("y")
-    gathered = packed.reshape((1,) * (z_bits + y_bits) + packed.shape)
-    order = [("z", bit, z_pos, z_count, z_bits - 1 - bit) for bit in range(z_bits)]
-    order += [("y", bit, y_pos, y_count, z_bits + y_bits - 1 - bit) for bit in range(y_bits)]
-    for name, bit, pos, count, axis in order:
-        mine_low = (pos >> bit) % 2 == 0
-        got = lax.ppermute(gathered, name, [(p, p ^ (1 << bit)) for p in range(count)])
-        gathered = jnp.where(
-            mine_low,
-            jnp.concatenate([gathered, got], axis=axis),
-            jnp.concatenate([got, gathered], axis=axis),
-        )
-    shard_rows = gathered.reshape((-1,) + packed.shape[1:])
-    offset = jnp.int32(0)
+    plane = packed[None]
+    for bit in range(y_bits):
+        mine_low = (y_pos >> bit) % 2 == 0
+        got = lax.ppermute(plane, "y", [(p, p ^ (1 << bit)) for p in range(y_count)])
+        plane = jnp.where(
+            mine_low, jnp.concatenate([plane, got], axis=0), jnp.concatenate([got, plane], axis=0)
+        )
+    plane_rows = y_count * tok_rows
+    plane = plane.reshape(plane_rows, packed.shape[1])
+    max_doc = (z_count * plane_rows) // 2
+    back = min(-(-(max_doc - 1) // plane_rows), z_count - 1)
+    held = plane[None]
+    while held.shape[0] < back + 1:
+        need = min(held.shape[0], back + 1 - held.shape[0])
+        got = lax.ppermute(held[:need], "z", [(p, (p + need) % z_count) for p in range(z_count)])
+        held = jnp.concatenate([got, held], axis=0)
+    shard_rows = held.reshape(-1, packed.shape[1])
+    plane_ids = (z_pos - back + jnp.arange(back + 1, dtype=jnp.int32)) % z_count
+    key_pos = (plane_ids[:, None] * plane_rows + jnp.arange(plane_rows, dtype=jnp.int32)[None, :]).reshape(-1)
     row_count = shard_rows.shape[0]
-    key_pos = jnp.arange(row_count, dtype=jnp.int32)
 
     def update(current):
         top_score, totals, context_sum = current
@@ -147,8 +149,7 @@
         )
         return (new_top, totals, context_sum)
 
-    skip_piece = (offset + row_count <= earliest) | (offset > latest)
-    top_score, totals, context_sum = lax.cond(skip_piece, lambda current: current, update, initial)
+    top_score, totals, context_sum = update(initial)
     context = (
         (context_sum / totals[..., None])
         .transpose(2, 0, 1, 3)
@@ -189,6 +190,7 @@
     head_pad = jnp.zeros((16 - 1, vocab_local), w_head.dtype)
     head_ext = jnp.concatenate([w_head, vocab_mask.astype(w_head.dtype)[None, :], head_pad], axis=0)
     head_ext = jnp.pad(head_ext, ((0, 0), (0, padded_local - vocab_local)))
+    head_ext, shard_rows = lax.optimization_barrier((head_ext, shard_rows))
     head_ext = lax.all_gather(head_ext, "z", axis=1, tiled=True)
     head_cols = head_ext[: w_head.shape[0]]
     mask_cols = head_ext[w_head.shape[0]]

time: 252 us -> 233 us (0.925)
  waiting for transfers between devices: 120 us -> 144 us
  starting transfers between devices: 34.7 us -> 23.7 us
  matrix products: 33 us -> 22.2 us
  other arithmetic: 29.4 us -> 18.9 us
  local copies, waits for them, and re-layouts: 16.1 us -> 6.79 us
    all_gather x1, waiting for transfers between devices: 0.01 us -> 31.4 us  [local(): head_ext = lax.all_gather(head_ext, 'z', axis=1, tiled=True)]
    ppermute x5, starting transfers between devices: 15.8 us -> 4.37 us  [the longest x2 2.29 us: local(): got = lax.ppermute(plane, 'y', [(p, p ^ 1 << bit) for p in range(y_count)])]
    another operation x3 -> x1, local copies, waits for them, and re-layouts: 7.2 us -> 0.82 us
    dot_general x1, matrix products: 9.44 us -> 3.27 us  [update(): jnp.einsum('kgts,skd->kgtd', weights.astype(jnp.bfloat16), value_rows, pr...]
    dot_general x1, matrix products: 8.16 us -> 2.19 us  [update(): jnp.einsum('tkgd,skd->kgts', rotated_q, key_rows, preferred_element_type=...]
    reduce_sum x1, other arithmetic: 9.6 us -> 3.74 us  [update(): totals = jnp.sum(weights, axis=-1)]
    ppermute x5, waiting for transfers between devices: 45 us -> 39.5 us  [the longest x3 30.9 us: local(): lax.ppermute(held[:need], 'z', [(p, (p + need) % z_count) for p in range(...]
    select_n x5 -> x2, other arithmetic: 3.08 us -> 0.14 us  [local(): jnp.where(mine_low, jnp.concatenate([plane, got], axis=0), jnp.concatenat...]
  transfers between devices with their start and end apart: 18 -> 18, of which waited for: 17 -> 18; matrix products, arithmetic and copies ran while one was open for 23% -> 9% of each run, Pallas kernels for 0% -> 0%
where the time goes in v6:
time: 233 us; the launch traced here: 230 us
  waiting for transfers between devices  144 us (62%)
  starting transfers between devices  23.7 us (10%)
  matrix products  22.2 us (10%)
  other arithmetic  18.9 us (8%)
  between operations  14.6 us (6%)
  local copies, waits for them, and re-layouts  6.79 us (3%)
    all_gather x1, waiting for transfers between devices, local(): head_rows = lax.all_gather(final_in, 'y', axis=0, tiled=True)  39.3 us
    all_gather x1, waiting for transfers between devices, local(): head_ext = lax.all_gather(head_ext, 'z', axis=1, tiled=True)  31.4 us
    ppermute x3, waiting for transfers between devices, local(): lax.ppermute(held[:need], 'z', [(p, (p + need) % z_count) for p in range(...  30.9 us
    ppermute x3, waiting for transfers between devices, local(): got = lax.ppermute(send, 'kv', [(p, p ^ 1 << bit) for p in range(kv_count)])  15.4 us
    dot_general x1, matrix products, local(): jnp.dot(head_rows, head_cols, preferred_element_type=jnp.float32)  11.2 us
    ppermute x3, waiting for transfers between devices, local(): got = lax.ppermute(rows, 'kv', [(p, p ^ 1 << bit) for p in range(kv_count)])  8.96 us
    ppermute x2, waiting for transfers between devices, local(): got = lax.ppermute(plane, 'y', [(p, p ^ 1 << bit) for p in range(y_count)])  8.62 us
    ppermute x3, waiting for transfers between devices, local(): got = lax.ppermute(merged, 'kv', [(p, p ^ step) for p in range(kv_count)])  5.19 us
  transfers between devices with their start and end apart: 18, of which 18 were waited for; matrix products, arithmetic and copies ran while one was open for 9% of the time, Pallas kernels for 0%

profile of v6, /device:TPU:24, one launch (start us, length us, event | category | flops | bytes accessed | tf_op | source)
XLA Modules:
  0.0 230.4 jit_solution(4153063575954485732)
XLA Ops:
  7.3 0.8 copy.61
  8.1 0.1 reduce.2
  8.3 0.7 sub.117
  9.0 1.4 multiply_reduce_fusion.1
  10.4 1.6 convolution_bitcast_fusion
  12.1 1.6 convolution_convert_fusion
  13.7 0.2 fusion.40
  14.0 0.8 collective-permute-start
  14.8 3.5 %collective-permute-done = bf16[1,192,128]{1,2,0:T(8,128)(2,1)S(1)} collective-permute-done((bf16[1,192,128]{1,2,0:T(8,128)(2,1)S(1)}, bf16[1,192,128]{1,2,0:T(8,128)(2,1)S(1)}, u32[]{:S(2)}, u32[]{:S(2)}) %collective-permute-start) | collective-permute-done | bytes 49184 | tf_op jit(solution)/shard_map/ppermute | solution.py:110
  18.4 1.5 collective-permute-start.1
  19.8 5.1 %collective-permute-done.1 = bf16[2,192,128]{1,2,0:T(8,128)(2,1)S(1)} collective-permute-done((bf16[2,192,128]{1,2,0:T(8,128)(2,1)S(1)}, bf16[2,192,128]{1,2,0:T(8,128)(2,1)S(1)}, u32[]{:S(2)}, u32[]{:S(2)}) %collective-permute-start.1) | collective-permute-done | bytes 98336 | tf_op jit(solution)/shard_map/ppermute | solution.py:110
  24.9 0.1 maximum_select_fusion.2
  25.0 0.2 copy.62
  25.2 2.0 collective-permute-start.2
  27.2 8.2 %collective-permute-done.2 = bf16[1,768,128]{2,1,0:T(8,128)(2,1)S(1)} collective-permute-done((bf16[1,768,128]{2,1,0:T(8,128)(2,1)S(1)}, bf16[1,768,128]{2,1,0:T(8,128)(2,1)S(1)}, u32[]{:S(2)}, u32[]{:S(2)}) %collective-permute-start.2) | collective-permute-done | bytes 196640 | tf_op jit(solution)/shard_map/ppermute | solution.py:121
  35.5 18.1 %collective-permute-done.3 = bf16[2,768,128]{2,1,0:T(8,128)(2,1)S(1)} collective-permute-done((bf16[2,768,128]{2,1,0:T(8,128)(2,1)S(1)}, bf16[2,768,128]{2,1,0:T(8,128)(2,1)S(1)}, u32[]{:S(2)}, u32[]{:S(2)}) %collective-permute-start.3) | collective-permute-done | bytes 393248 | tf_op jit(solution)/shard_map/ppermute | solution.py:121
  53.6 0.7 slice.242
  54.4 1.4 concatenate.62
  55.8 1.0 pad.4
  56.8 4.6 %collective-permute-done.4 = bf16[1,768,128]{2,1,0:T(8,128)(2,1)} collective-permute-done((bf16[1,768,128]{2,1,0:T(8,128)(2,1)}, bf16[1,768,128]{2,1,0:T(8,128)(2,1)}, u32[]{:S(2)}, u32[]{:S(2)}) %collective-permute-start.4) | collective-permute-done | bytes 196640 | tf_op jit(solution)/shard_map/ppermute | solution.py:121
  61.5 1.2 pad_maximum_fusion
  62.6 0.2 all-gather.5.cloned.1.call-start
  63.0 0.2 multiply_cosine_fusion
  63.2 1.8 fusion.62
  65.1 0.6 compare_and_fusion
  65.7 2.2 fusion
  67.9 3.7 %fusion.1 = f32[4,192]{1,0:T(4,128)S(1)} fusion(f32[3840,192,4]{0,1,2:T(8,128)S(1)} %get-tuple-element.53, f32[4,192]{1,0:T(4,128)S(1)} %broadcast_maximum_fusion, pred[192,3840]{1,0:T(8,128)(4,1)S(1)} %compare_and_fusion), kind=kLoop, calls=%fused_computation.3 | loop fusion | flops 14744832 | bytes 12539904 | tf_op jit(solution)/shard_map/reduce_sum | solution.py:143
  71.7 3.3 %fusion.16 = bf16[192,1,4,64]{0,3,2,1:T(8,128)(2,1)S(1)} fusion(f32[3840,192,4]{0,1,2:T(8,128)S(1)} %get-tuple-element.53, f32[4,192]{1,0:T(4,128)S(1)} %broadcast_maximum_fusion, pred[192,3840]{1,0:T(8,128)(4,1)S(1)} %compare_and_fusion, bf16[3840,128]{1,0:T(8,128)(2,1)S(1)} %bitcast.143, f32[4,192]{1,0:T(4,128)S(1)} %fusion.1), kind=kOutput, calls=%fused_computation.23 | convolution fusion | flops 392331264 | bytes 13621248 | tf_op jit(solution)/shard_map/kgts,skd->kgtd/dot_general | solution.py:144
  74.9 0.2 copy.66
  75.1 0.2 convert_element_type.57
  75.3 0.4 fusion.19
  75.8 0.1 collective-permute-start.5
  75.9 2.4 %collective-permute-done.5 = f32[2,2,24,2048]{3,2,1,0:T(8,128)} collective-permute-done((f32[2,2,24,2048]{3,2,1,0:T(8,128)S(1)}, f32[2,2,24,2048]{3,2,1,0:T(8,128)}, u32[]{:S(2)}, u32[]{:S(2)}) %collective-permute-start.5) | collective-permute-done | bytes 786464 | tf_op jit(solution)/shard_map/ppermute | solution.py:175
  78.3 1.3 fusion.23
  79.6 1.6 collective-permute-start.6
  81.2 9.7 %collective-permute-done.6 = f32[2,24,2048]{2,1,0:T(8,128)S(1)} collective-permute-done((f32[2,24,2048]{2,1,0:T(8,128)S(1)}, f32[2,24,2048]{2,1,0:T(8,128)S(1)}, u32[]{:S(2)}, u32[]{:S(2)}) %collective-permute-start.6) | collective-permute-done | bytes 393248 | tf_op jit(solution)/shard_map/ppermute | solution.py:175
  91.0 3.1 %collective-permute-start.7 = (f32[24,2048]{1,0:T(8,128)S(1)}, f32[24,2048]{1,0:T(8,128)S(1)}, u32[]{:S(2)}, u32[]{:S(2)}) collective-permute-start(f32[24,2048]{1,0:T(8,128)S(1)} %select_bitcast_fusion.2), channel_id=1, source_target_pairs={{0,128},{32,160},{64,192},{96,224},{128,0},{160,32},{192,64},{224,... | collective-permute-start | bytes 589832 | tf_op jit(solution)/shard_map/ppermute | solution.py:175
  94.1 1.3 convert_element_type.49
  95.4 3.3 %collective-permute-done.7 = f32[24,2048]{1,0:T(8,128)S(1)} collective-permute-done((f32[24,2048]{1,0:T(8,128)S(1)}, f32[24,2048]{1,0:T(8,128)S(1)}, u32[]{:S(2)}, u32[]{:S(2)}) %collective-permute-start.7) | collective-permute-done | bytes 196640 | tf_op jit(solution)/shard_map/ppermute | solution.py:175
  98.8 0.2 multiply_reduce_fusion.2
  99.0 3.1 %collective-permute-start.8 = (bf16[1,24,2048]{2,1,0:T(8,128)(2,1)S(1)}, bf16[1,24,2048]{2,1,0:T(8,128)(2,1)S(1)}, u32[]{:S(2)}, u32[]{:S(2)}) collective-permute-start(bf16[1,24,2048]{2,1,0:T(8,128)(2,1)S(1)} %get-tuple-element.20), channel_id=1, source_target_pairs={{0,128},{32,160},{64,192},{96,224},{128,0},{160,32},{192,64},{224,... | collective-permute-start | bytes 294920 | tf_op jit(solution)/shard_map/ppermute | solution.py:183
  102.2 3.1 %collective-permute-done.8 = bf16[1,24,2048]{2,1,0:T(8,128)(2,1)S(1)} collective-permute-done((bf16[1,24,2048]{2,1,0:T(8,128)(2,1)S(1)}, bf16[1,24,2048]{2,1,0:T(8,128)(2,1)S(1)}, u32[]{:S(2)}, u32[]{:S(2)}) %collective-permute-start.8) | collective-permute-done | bytes 98336 | tf_op jit(solution)/shard_map/ppermute | solution.py:183
  105.3 1.6 collective-permute-start.9
  106.8 4.2 %collective-permute-done.9 = bf16[2,24,2048]{2,1,0:T(8,128)(2,1)S(1)} collective-permute-done((bf16[2,24,2048]{2,1,0:T(8,128)(2,1)S(1)}, bf16[2,24,2048]{2,1,0:T(8,128)(2,1)S(1)}, u32[]{:S(2)}, u32[]{:S(2)}) %collective-permute-start.9) | collective-permute-done | bytes 196640 | tf_op jit(solution)/shard_map/ppermute | solution.py:183
  111.1 0.3 collective-permute-start.10
  111.4 1.7 collective-permute-done.10
  113.1 0.1 maximum_select_fusion
  113.3 1.0 copy.77
  114.5 0.8 dynamic_slice.19
  115.3 31.4 %all-gather.3.cloned.1.call-done = bf16[2064,1664]{0,1:T(8,128)(2,1)} async-done(((bf16[2064,208]{0,1:T(8,128)(2,1)}), bf16[2064,1664]{0,1:T(8,128)(2,1)}) %all-gather.3.cloned.1.call-update) | async-done | bytes 6869008 | tf_op jit(solution)/shard_map/all_gather | solution.py:194
  146.7 1.3 compare_reduce_fusion
  148.0 39.3 %all-gather.5.cloned.1.call-done = bf16[768,2048]{1,0:T(8,128)(2,1)} async-done(((bf16[192,2048]{1,0:T(8,128)(2,1)}), bf16[768,2048]{1,0:T(8,128)(2,1)}) %all-gather.5.cloned.1.call-update) | async-done | bytes 3145744 | tf_op jit(solution)/shard_map/all_gather | solution.py:187
  187.3 11.2 %select_reduce_fusion.1 = (f32[768]{0:T(1024)S(1)}, f32[768,1664]{1,0:T(8,128)}) fusion(pred[1664]{0:T(1024)(128)(4,1)S(1)} %compare_reduce_fusion, bf16[768,2048]{1,0:T(8,128)(2,1)} %all-gather.5.cloned.1.call-done, bf16[2064,1664]{0,1:T(8,128)(2,1)} %all-gather.3.cloned.1.call-done), kind=kOutput, calls=%fused_computation.15 | convolution fusion | flops 5238324224 | bytes 15078016 | tf_op jit(solution)/shard_map/dot_general | solution.py:204
  198.5 4.8 %fusion.9 = (f32[768]{0:T(1024)S(1)}, f32[768]{0:T(1024)S(1)}, f32[768]{0:T(1024)S(1)}) fusion(f32[768,1664]{1,0:T(8,128)} %get-tuple-element.55, f32[768]{0:T(1024)S(1)} %get-tuple-element.54, pred[1664]{0:T(1024)(128)(4,1)S(1)} %compare_reduce_fusion, s32[1664]{0:T(1024)S(1)} %select_n.377, s32[768]{0:T(1024)S(1)} %dynamic_slice.19), kind=kLoop, calls=%fused_computation.13 | loop fusion | flops 14055168 | bytes 5135488 | tf_op jit(solution)/shard_map/reduce_sum | solution.py:211
  203.6 2.6 %collective-permute-start.11 = (f32[4,2,192]{2,0,1:T(4,128)S(1)}, f32[4,2,192]{2,0,1:T(4,128)S(1)}, u32[]{:S(2)}, u32[]{:S(2)}) collective-permute-start(f32[4,2,192]{2,0,1:T(4,128)S(1)} %constant_dynamic-slice_fusion.1), channel_id=1, source_target_pairs={{0,2},{1,3},{2,0},{3,1},{4,6},{5,7},{6,4},{7,5},{8,10},{9,11},{10,... | collective-permute-start | bytes 18440 | tf_op jit(solution)/shard_map/ppermute | solution.py:217
  206.2 2.6 %collective-permute-done.11 = f32[4,2,192]{2,0,1:T(4,128)S(1)} collective-permute-done((f32[4,2,192]{2,0,1:T(4,128)S(1)}, f32[4,2,192]{2,0,1:T(4,128)S(1)}, u32[]{:S(2)}, u32[]{:S(2)}) %collective-permute-start.11) | collective-permute-done | bytes 6176 | tf_op jit(solution)/shard_map/ppermute | solution.py:217
  208.9 1.7 collective-permute-start.12
  210.6 2.0 collective-permute-done.12
  212.8 1.1 collective-permute-done.13
  214.0 1.7 collective-permute-start.14
  215.7 2.0 collective-permute-done.14
  217.8 3.2 %collective-permute-start.15 = (f32[4,192]{1,0:T(4,128)S(1)}, f32[4,192]{1,0:T(4,128)S(1)}, u32[]{:S(2)}, u32[]{:S(2)}) collective-permute-start(f32[4,192]{1,0:T(4,128)S(1)} %pad_maximum_fusion.5), channel_id=1, source_target_pairs={{0,128},{32,160},{64,192},{96,224},{128,0},{160,32},{192,64},{224,... | collective-permute-start | bytes 9224 | tf_op jit(solution)/shard_map/ppermute | solution.py:230
  220.9 2.0 collective-permute-done.15
  223.0 0.6 divide_subtract_fusion
  (74 shorter events, 2.0 us)
Async XLA Ops:
  7.2 68.1 %copy-start = (bf16[256,2048]{1,0:T(8,128)(2,1)S(1)}, bf16[256,2048]{1,0:T(8,128)(2,1)}, u32[]{:S(2)}) copy-start(bf16[256,2048]{1,0:T(8,128)(2,1)} %param.16) | copy-start | bytes 3145732
  7.2 47.1 %copy-start.5 = (s32[193]{0:T(256)S(1)}, s32[193]{0:T(256)}, u32[]{:S(2)}) copy-start(s32[193]{0:T(256)} %param.21) | copy-start | bytes 2320
  7.2 139.5 %all-gather.3.cloned.1.call-start = ((), (), s32[]{:S(2)}) async-start(), calls=%async_computation | async-start | bytes 8146944 | tf_op jit(solution)/shard_map/all_gather | solution.py:194
  13.7 49.5 %copy-start.1 = (bf16[192,2048]{1,0:T(8,128)(2,1)S(1)}, bf16[192,2048]{1,0:T(8,128)(2,1)}, u32[]{:S(2)}) copy-start(bf16[192,2048]{1,0:T(8,128)(2,1)} %param.11) | copy-start | bytes 2359300
  13.7 49.5 %copy-start.4 = (f32[2048]{0:T(1024)S(1)}, f32[2048]{0:T(1024)}, u32[]{:S(2)}) copy-start(f32[2048]{0:T(1024)} %param.12) | copy-start | bytes 24580
  14.0 4.4 %collective-permute-start = (bf16[1,192,128]{1,2,0:T(8,128)(2,1)S(1)}, bf16[1,192,128]{1,2,0:T(8,128)(2,1)S(1)}, u32[]{:S(2)}, u32[]{:S(2)}) collective-permute-start(bf16[1,192,128]{1,2,0:T(8,128)(2,1)S(1)} %maximum_bitcast_fusion), channel_id=1, source_target_pairs={{0,1},{1,0},{2,3},{3,2},{4,5},{5,4},{6,7},{7,6},{8,9},{9,8},{10,11... | collective-permute-start | bytes 147464 | tf_op jit(solution)/shard_map/ppermute | solution.py:110
  18.4 6.6 %collective-permute-start.1 = (bf16[2,192,128]{1,2,0:T(8,128)(2,1)S(1)}, bf16[2,192,128]{1,2,0:T(8,128)(2,1)S(1)}, u32[]{:S(2)}, u32[]{:S(2)}) collective-permute-start(bf16[2,192,128]{1,2,0:T(8,128)(2,1)S(1)} %maximum_select_fusion.5), channel_id=1, source_target_pairs={{0,2},{1,3},{2,0},{3,1},{4,6},{5,7},{6,4},{7,5},{8,10},{9,11},{10,... | collective-permute-start | bytes 294920 | tf_op jit(solution)/shard_map/ppermute | solution.py:110
  25.2 10.2 %collective-permute-start.2 = (bf16[1,768,128]{2,1,0:T(8,128)(2,1)S(1)}, bf16[1,768,128]{2,1,0:T(8,128)(2,1)S(1)}, u32[]{:S(2)}, u32[]{:S(2)}) collective-permute-start(bf16[1,768,128]{2,1,0:T(8,128)(2,1)S(1)} %bitcast.137), channel_id=1, source_target_pairs={{0,4},{4,8},{8,12},{12,16},{16,20},{20,24},{24,28},{28,0},{1,5},{5... | collective-permute-start | bytes 589832 | tf_op jit(solution)/shard_map/ppermute | solution.py:121
  35.4 19.0 %copy-start.2 = (bf16[1,768,128]{2,1,0:T(8,128)(2,1)}, bf16[1,768,128]{2,1,0:T(8,128)(2,1)S(1)}, u32[]{:S(2)}) copy-start(bf16[1,768,128]{2,1,0:T(8,128)(2,1)S(1)} %collective-permute-done.2) | copy-start | bytes 589828
  35.4 18.1 %collective-permute-start.3 = (bf16[2,768,128]{2,1,0:T(8,128)(2,1)S(1)}, bf16[2,768,128]{2,1,0:T(8,128)(2,1)S(1)}, u32[]{:S(2)}, u32[]{:S(2)}) collective-permute-start(bf16[2,768,128]{2,1,0:T(8,128)(2,1)S(1)} %pad_maximum_fusion.1), channel_id=1, source_target_pairs={{0,8},{4,12},{8,16},{12,20},{16,24},{20,28},{24,0},{28,4},{1,9},{5... | collective-permute-start | bytes 1179656 | tf_op jit(solution)/shard_map/ppermute | solution.py:121
  54.3 7.2 %collective-permute-start.4 = (bf16[1,768,128]{2,1,0:T(8,128)(2,1)}, bf16[1,768,128]{2,1,0:T(8,128)(2,1)}, u32[]{:S(2)}, u32[]{:S(2)}) collective-permute-start(bf16[1,768,128]{2,1,0:T(8,128)(2,1)} %slice.242), channel_id=1, source_target_pairs={{0,4},{4,8},{8,12},{12,16},{16,20},{20,24},{24,28},{28,0},{1,5},{5... | collective-permute-start | bytes 589832 | tf_op jit(solution)/shard_map/ppermute | solution.py:121
  62.6 124.6 %all-gather.5.cloned.1.call-start = ((), (), s32[]{:S(2)}) async-start(), calls=%async_computation.1 | async-start | bytes 3932160 | tf_op jit(solution)/shard_map/all_gather | solution.py:187
  75.8 23.1 %copy-start.3 = (f32[2048]{0:T(1024)S(1)}, f32[2048]{0:T(1024)}, u32[]{:S(2)}) copy-start(f32[2048]{0:T(1024)} %param.17) | copy-start | bytes 24580
  75.8 2.5 %collective-permute-start.5 = (f32[2,2,24,2048]{3,2,1,0:T(8,128)S(1)}, f32[2,2,24,2048]{3,2,1,0:T(8,128)}, u32[]{:S(2)}, u32[]{:S(2)}) collective-permute-start(f32[2,2,24,2048]{3,2,1,0:T(8,128)S(1)} %select_bitcast_fusion), channel_id=1, source_target_pairs={{0,32},{32,0},{64,96},{96,64},{128,160},{160,128},{192,224},{224,1... | collective-permute-start | bytes 2359304 | tf_op jit(solution)/shard_map/ppermute | solution.py:175
  79.6 11.2 %collective-permute-start.6 = (f32[2,24,2048]{2,1,0:T(8,128)S(1)}, f32[2,24,2048]{2,1,0:T(8,128)S(1)}, u32[]{:S(2)}, u32[]{:S(2)}) collective-permute-start(f32[2,24,2048]{2,1,0:T(8,128)S(1)} %select_bitcast_fusion.1), channel_id=1, source_target_pairs={{0,64},{32,96},{64,0},{96,32},{128,192},{160,224},{192,128},{224,1... | collective-permute-start | bytes 1179656 | tf_op jit(solution)/shard_map/ppermute | solution.py:175
  91.0 7.8 %collective-permute-start.7 = (f32[24,2048]{1,0:T(8,128)S(1)}, f32[24,2048]{1,0:T(8,128)S(1)}, u32[]{:S(2)}, u32[]{:S(2)}) collective-permute-start(f32[24,2048]{1,0:T(8,128)S(1)} %select_bitcast_fusion.2), channel_id=1, source_target_pairs={{0,128},{32,160},{64,192},{96,224},{128,0},{160,32},{192,64},{224,... | collective-permute-start | bytes 589832 | tf_op jit(solution)/shard_map/ppermute | solution.py:175
  99.0 6.2 %collective-permute-start.8 = (bf16[1,24,2048]{2,1,0:T(8,128)(2,1)S(1)}, bf16[1,24,2048]{2,1,0:T(8,128)(2,1)S(1)}, u32[]{:S(2)}, u32[]{:S(2)}) collective-permute-start(bf16[1,24,2048]{2,1,0:T(8,128)(2,1)S(1)} %get-tuple-element.20), channel_id=1, source_target_pairs={{0,128},{32,160},{64,192},{96,224},{128,0},{160,32},{192,64},{224,... | collective-permute-start | bytes 294920 | tf_op jit(solution)/shard_map/ppermute | solution.py:183
  105.3 5.8 %collective-permute-start.9 = (bf16[2,24,2048]{2,1,0:T(8,128)(2,1)S(1)}, bf16[2,24,2048]{2,1,0:T(8,128)(2,1)S(1)}, u32[]{:S(2)}, u32[]{:S(2)}) collective-permute-start(bf16[2,24,2048]{2,1,0:T(8,128)(2,1)S(1)} %maximum_select_fusion.4), channel_id=1, source_target_pairs={{0,64},{32,96},{64,0},{96,32},{128,192},{160,224},{192,128},{224,1... | collective-permute-start | bytes 589832 | tf_op jit(solution)/shard_map/ppermute | solution.py:183
  111.1 2.0 collective-permute-start.10
  203.6 5.2 %collective-permute-start.11 = (f32[4,2,192]{2,0,1:T(4,128)S(1)}, f32[4,2,192]{2,0,1:T(4,128)S(1)}, u32[]{:S(2)}, u32[]{:S(2)}) collective-permute-start(f32[4,2,192]{2,0,1:T(4,128)S(1)} %constant_dynamic-slice_fusion.1), channel_id=1, source_target_pairs={{0,2},{1,3},{2,0},{3,1},{4,6},{5,7},{6,4},{7,5},{8,10},{9,11},{10,... | collective-permute-start | bytes 18440 | tf_op jit(solution)/shard_map/ppermute | solution.py:217
  208.9 3.7 %collective-permute-start.12 = (f32[4,1,192]{2,0,1:T(4,128)S(1)}, f32[4,1,192]{2,0,1:T(4,128)S(1)}, u32[]{:S(2)}, u32[]{:S(2)}) collective-permute-start(f32[4,1,192]{2,0,1:T(4,128)S(1)} %constant_dynamic-slice_fusion), channel_id=1, source_target_pairs={{0,1},{1,0},{2,3},{3,2},{4,5},{5,4},{6,7},{7,6},{8,9},{9,8},{10,11... | collective-permute-start | bytes 9224 | tf_op jit(solution)/shard_map/ppermute | solution.py:225
  212.7 1.3 collective-permute-start.13
  214.0 3.7 %collective-permute-start.14 = (f32[4,192]{1,0:T(4,128)S(1)}, f32[4,192]{1,0:T(4,128)S(1)}, u32[]{:S(2)}, u32[]{:S(2)}) collective-permute-start(f32[4,192]{1,0:T(4,128)S(1)} %pad_maximum_fusion.4), channel_id=1, source_target_pairs={{0,64},{32,96},{64,0},{96,32},{128,192},{160,224},{192,128},{224,1... | collective-permute-start | bytes 9224 | tf_op jit(solution)/shard_map/ppermute | solution.py:230
  217.8 5.2 %collective-permute-start.15 = (f32[4,192]{1,0:T(4,128)S(1)}, f32[4,192]{1,0:T(4,128)S(1)}, u32[]{:S(2)}, u32[]{:S(2)}) collective-permute-start(f32[4,192]{1,0:T(4,128)S(1)} %pad_maximum_fusion.5), channel_id=1, source_target_pairs={{0,128},{32,160},{64,192},{96,224},{128,0},{160,32},{192,64},{224,... | collective-permute-start | bytes 9224 | tf_op jit(solution)/shard_map/ppermute | solution.py:230
Sparse Core Ops, SparseCore 0:
  62.8 83.8 all-gather.2
  148.5 38.7 all-gather.4

commit v7 on v6

--- a/solution.py
+++ b/solution.py
@@ -190,7 +190,6 @@
     head_pad = jnp.zeros((16 - 1, vocab_local), w_head.dtype)
     head_ext = jnp.concatenate([w_head, vocab_mask.astype(w_head.dtype)[None, :], head_pad], axis=0)
     head_ext = jnp.pad(head_ext, ((0, 0), (0, padded_local - vocab_local)))
-    head_ext, shard_rows = lax.optimization_barrier((head_ext, shard_rows))
     head_ext = lax.all_gather(head_ext, "z", axis=1, tiled=True)
     head_cols = head_ext[: w_head.shape[0]]
     mask_cols = head_ext[w_head.shape[0]]

time: 233 us -> 216 us (0.927)
  waiting for transfers between devices: 144 us -> 132 us
  matrix products: 22.2 us -> 19.8 us
    all_gather x1, waiting for transfers between devices: 31.4 us -> 0.01 us  [local(): head_ext = lax.all_gather(head_ext, 'z', axis=1, tiled=True)]
    ppermute x3, waiting for transfers between devices: 30.9 us -> 50.9 us  [local(): lax.ppermute(held[:need], 'z', [(p, (p + need) % z_count) for p in range(...]
  transfers between devices with their start and end apart: 18 -> 18, of which waited for: 18 -> 17; matrix products, arithmetic and copies ran while one was open for 9% -> 11% of each run, Pallas kernels for 0% -> 0%
where the time goes in v7:
time: 216 us; the launch traced here: 213 us
  waiting for transfers between devices  132 us (61%)
  starting transfers between devices  23.8 us (11%)
  matrix products  19.8 us (9%)
  other arithmetic  17.6 us (8%)
  between operations  14.6 us (7%)
  local copies, waits for them, and re-layouts  6.06 us (3%)
    ppermute x3, waiting for transfers between devices, local(): lax.ppermute(held[:need], 'z', [(p, (p + need) % z_count) for p in range(...  50.9 us
    all_gather x1, waiting for transfers between devices, local(): head_rows = lax.all_gather(final_in, 'y', axis=0, tiled=True)  38 us
    ppermute x3, waiting for transfers between devices, local(): got = lax.ppermute(send, 'kv', [(p, p ^ 1 << bit) for p in range(kv_count)])  15.4 us
    dot_general x1, matrix products, local(): jnp.dot(head_rows, head_cols, preferred_element_type=jnp.float32)  11.2 us
    ppermute x3, waiting for transfers between devices, local(): got = lax.ppermute(rows, 'kv', [(p, p ^ 1 << bit) for p in range(kv_count)])  8.94 us
    ppermute x2, waiting for transfers between devices, local(): got = lax.ppermute(plane, 'y', [(p, p ^ 1 << bit) for p in range(y_count)])  8.53 us
    ppermute x3, waiting for transfers between devices, local(): got = lax.ppermute(merged, 'kv', [(p, p ^ step) for p in range(kv_count)])  5.19 us
    ppermute x3, starting transfers between devices, local(): got = lax.ppermute(rows, 'kv', [(p, p ^ 1 << bit) for p in range(kv_count)])  5.02 us
  transfers between devices with their start and end apart: 18, of which 17 were waited for; matrix products, arithmetic and copies ran while one was open for 11% of the time, Pallas kernels for 0%

profile of v7, /device:TPU:24, one launch (start us, length us, event | category | flops | bytes accessed | tf_op | source)
XLA Modules:
  0.0 213.4 jit_solution(1583945019474275758)
XLA Ops:
  7.3 0.8 convert_element_type.48
  8.2 1.4 concatenate.62
  9.6 1.0 pad.4
  10.8 0.8 copy.61
  11.6 0.1 reduce.3
  11.7 0.7 sub.118
  12.4 0.2 multiply_reduce_fusion.1
  12.7 0.4 convolution_bitcast_fusion
  13.2 0.4 convolution_convert_fusion
  13.6 0.2 fusion.40
  13.8 0.8 collective-permute-start
  14.7 3.5 %collective-permute-done = bf16[1,192,128]{1,2,0:T(8,128)(2,1)S(1)} collective-permute-done((bf16[1,192,128]{1,2,0:T(8,128)(2,1)S(1)}, bf16[1,192,128]{1,2,0:T(8,128)(2,1)S(1)}, u32[]{:S(2)}, u32[]{:S(2)}) %collective-permute-start) | collective-permute-done | bytes 49184 | tf_op jit(solution)/shard_map/ppermute | solution.py:110
  18.2 1.5 collective-permute-start.1
  19.8 5.0 %collective-permute-done.1 = bf16[2,192,128]{1,2,0:T(8,128)(2,1)S(1)} collective-permute-done((bf16[2,192,128]{1,2,0:T(8,128)(2,1)S(1)}, bf16[2,192,128]{1,2,0:T(8,128)(2,1)S(1)}, u32[]{:S(2)}, u32[]{:S(2)}) %collective-permute-start.1) | collective-permute-done | bytes 98336 | tf_op jit(solution)/shard_map/ppermute | solution.py:110
  24.8 0.1 maximum_select_fusion.2
  24.9 0.2 copy.62
  25.1 2.0 collective-permute-start.2
  27.1 0.6 compare_and_fusion
  27.7 12.2 %collective-permute-done.2 = bf16[1,768,128]{2,1,0:T(8,128)(2,1)S(1)} collective-permute-done((bf16[1,768,128]{2,1,0:T(8,128)(2,1)S(1)}, bf16[1,768,128]{2,1,0:T(8,128)(2,1)S(1)}, u32[]{:S(2)}, u32[]{:S(2)}) %collective-permute-start.2) | collective-permute-done | bytes 196640 | tf_op jit(solution)/shard_map/ppermute | solution.py:121
  40.1 0.2 multiply_cosine_fusion
  40.3 1.8 fusion.62
  42.2 27.2 %collective-permute-done.3 = bf16[2,768,128]{2,1,0:T(8,128)(2,1)S(1)} collective-permute-done((bf16[2,768,128]{2,1,0:T(8,128)(2,1)S(1)}, bf16[2,768,128]{2,1,0:T(8,128)(2,1)S(1)}, u32[]{:S(2)}, u32[]{:S(2)}) %collective-permute-start.3) | collective-permute-done | bytes 393248 | tf_op jit(solution)/shard_map/ppermute | solution.py:121
  69.4 0.3 collective-permute-start.4
  69.7 11.5 %collective-permute-done.4 = bf16[1,768,128]{2,1,0:T(8,128)(2,1)S(1)} collective-permute-done((bf16[1,768,128]{2,1,0:T(8,128)(2,1)S(1)}, bf16[1,768,128]{2,1,0:T(8,128)(2,1)S(1)}, u32[]{:S(2)}, u32[]{:S(2)}) %collective-permute-start.4) | collective-permute-done | bytes 196640 | tf_op jit(solution)/shard_map/ppermute | solution.py:121
  81.2 0.1 pad_maximum_fusion
  81.3 2.2 %fusion = (f32[4,192]{1,0:T(4,128)S(1)}, f32[3840,192,4]{0,1,2:T(8,128)S(1)}) fusion(pred[192,3840]{1,0:T(8,128)(4,1)S(1)} %compare_and_fusion, bf16[192,4,32]{0,2,1:T(8,128)(2,1)S(1)} %get-tuple-element.16, bf16[192,4,32]{0,2,1:T(8,128)(2,1)S(1)} %get-tuple-element.15, bf16[3840,128]{1,0:T(8,128)(2,1)S(1)} %bitcast.142), kind=kOutput, calls=%fused_computation.2 | convolution fusion | flops 386530560 | bytes 13618176 | tf_op jit(solution)/shard_map/tkgd,skd->kgts/dot_general | solution.py:133
  83.5 3.8 %fusion.1 = f32[4,192]{1,0:T(4,128)S(1)} fusion(f32[3840,192,4]{0,1,2:T(8,128)S(1)} %get-tuple-element.51, f32[4,192]{1,0:T(4,128)S(1)} %broadcast_maximum_fusion, pred[192,3840]{1,0:T(8,128)(4,1)S(1)} %compare_and_fusion), kind=kLoop, calls=%fused_computation.3 | loop fusion | flops 14744832 | bytes 12539904 | tf_op jit(solution)/shard_map/reduce_sum | solution.py:143
  87.3 3.3 %fusion.16 = bf16[192,1,4,64]{0,3,2,1:T(8,128)(2,1)S(1)} fusion(f32[3840,192,4]{0,1,2:T(8,128)S(1)} %get-tuple-element.51, f32[4,192]{1,0:T(4,128)S(1)} %broadcast_maximum_fusion, pred[192,3840]{1,0:T(8,128)(4,1)S(1)} %compare_and_fusion, bf16[3840,128]{1,0:T(8,128)(2,1)S(1)} %bitcast.143, f32[4,192]{1,0:T(4,128)S(1)} %fusion.1), kind=kOutput, calls=%fused_computation.23 | convolution fusion | flops 392331264 | bytes 13621248 | tf_op jit(solution)/shard_map/kgts,skd->kgtd/dot_general | solution.py:144
  90.6 0.2 copy.66
  90.7 0.2 convert_element_type.57
  90.9 0.4 fusion.19
  91.4 0.1 collective-permute-start.5
  91.5 2.4 %collective-permute-done.5 = f32[2,2,24,2048]{3,2,1,0:T(8,128)} collective-permute-done((f32[2,2,24,2048]{3,2,1,0:T(8,128)S(1)}, f32[2,2,24,2048]{3,2,1,0:T(8,128)}, u32[]{:S(2)}, u32[]{:S(2)}) %collective-permute-start.5) | collective-permute-done | bytes 786464 | tf_op jit(solution)/shard_map/ppermute | solution.py:175
  93.9 1.3 fusion.23
  95.3 1.6 collective-permute-start.6
  96.9 9.6 %collective-permute-done.6 = f32[2,24,2048]{2,1,0:T(8,128)S(1)} collective-permute-done((f32[2,24,2048]{2,1,0:T(8,128)S(1)}, f32[2,24,2048]{2,1,0:T(8,128)S(1)}, u32[]{:S(2)}, u32[]{:S(2)}) %collective-permute-start.6) | collective-permute-done | bytes 393248 | tf_op jit(solution)/shard_map/ppermute | solution.py:175
  106.6 3.1 %collective-permute-start.7 = (f32[24,2048]{1,0:T(8,128)S(1)}, f32[24,2048]{1,0:T(8,128)S(1)}, u32[]{:S(2)}, u32[]{:S(2)}) collective-permute-start(f32[24,2048]{1,0:T(8,128)S(1)} %select_bitcast_fusion.2), channel_id=1, source_target_pairs={{0,128},{32,160},{64,192},{96,224},{128,0},{160,32},{192,64},{224,... | collective-permute-start | bytes 589832 | tf_op jit(solution)/shard_map/ppermute | solution.py:175
  109.7 1.3 convert_element_type.49
  111.0 3.4 %collective-permute-done.7 = f32[24,2048]{1,0:T(8,128)S(1)} collective-permute-done((f32[24,2048]{1,0:T(8,128)S(1)}, f32[24,2048]{1,0:T(8,128)S(1)}, u32[]{:S(2)}, u32[]{:S(2)}) %collective-permute-start.7) | collective-permute-done | bytes 196640 | tf_op jit(solution)/shard_map/ppermute | solution.py:175
  114.4 0.2 multiply_reduce_fusion.2
  114.6 3.1 %collective-permute-start.8 = (bf16[1,24,2048]{2,1,0:T(8,128)(2,1)S(1)}, bf16[1,24,2048]{2,1,0:T(8,128)(2,1)S(1)}, u32[]{:S(2)}, u32[]{:S(2)}) collective-permute-start(bf16[1,24,2048]{2,1,0:T(8,128)(2,1)S(1)} %get-tuple-element.18), channel_id=1, source_target_pairs={{0,128},{32,160},{64,192},{96,224},{128,0},{160,32},{192,64},{224,... | collective-permute-start | bytes 294920 | tf_op jit(solution)/shard_map/ppermute | solution.py:183
  117.8 3.1 %collective-permute-done.8 = bf16[1,24,2048]{2,1,0:T(8,128)(2,1)S(1)} collective-permute-done((bf16[1,24,2048]{2,1,0:T(8,128)(2,1)S(1)}, bf16[1,24,2048]{2,1,0:T(8,128)(2,1)S(1)}, u32[]{:S(2)}, u32[]{:S(2)}) %collective-permute-start.8) | collective-permute-done | bytes 98336 | tf_op jit(solution)/shard_map/ppermute | solution.py:183
  120.9 1.6 collective-permute-start.9
  122.5 4.1 %collective-permute-done.9 = bf16[2,24,2048]{2,1,0:T(8,128)(2,1)S(1)} collective-permute-done((bf16[2,24,2048]{2,1,0:T(8,128)(2,1)S(1)}, bf16[2,24,2048]{2,1,0:T(8,128)(2,1)S(1)}, u32[]{:S(2)}, u32[]{:S(2)}) %collective-permute-start.9) | collective-permute-done | bytes 196640 | tf_op jit(solution)/shard_map/ppermute | solution.py:183
  126.7 0.3 collective-permute-start.10
  127.0 1.7 collective-permute-done.10
  128.8 0.1 maximum_select_fusion
  128.9 1.0 copy.77
  130.1 0.8 dynamic_slice.19
  130.9 1.3 compare_reduce_fusion
  132.2 38.0 %all-gather.5.cloned.1.call-done = bf16[768,2048]{1,0:T(8,128)(2,1)} async-done(((bf16[192,2048]{1,0:T(8,128)(2,1)}), bf16[768,2048]{1,0:T(8,128)(2,1)}) %all-gather.5.cloned.1.call-update) | async-done | bytes 3145744 | tf_op jit(solution)/shard_map/all_gather | solution.py:187
  170.2 11.2 %select_reduce_fusion.1 = (f32[768]{0:T(1024)S(1)}, f32[768,1664]{1,0:T(8,128)}) fusion(pred[1664]{0:T(1024)(128)(4,1)S(1)} %compare_reduce_fusion, bf16[768,2048]{1,0:T(8,128)(2,1)} %all-gather.5.cloned.1.call-done, bf16[2064,1664]{0,1:T(8,128)(2,1)} %all-gather.3.cloned.1.call-done), kind=kOutput, calls=%fused_computation.15 | convolution fusion | flops 5238324224 | bytes 15078016 | tf_op jit(solution)/shard_map/dot_general | solution.py:203
  181.5 4.8 %fusion.9 = (f32[768]{0:T(1024)S(1)}, f32[768]{0:T(1024)S(1)}, f32[768]{0:T(1024)S(1)}) fusion(f32[768,1664]{1,0:T(8,128)} %get-tuple-element.53, f32[768]{0:T(1024)S(1)} %get-tuple-element.52, pred[1664]{0:T(1024)(128)(4,1)S(1)} %compare_reduce_fusion, s32[1664]{0:T(1024)S(1)} %select_n.377, s32[768]{0:T(1024)S(1)} %dynamic_slice.19), kind=kLoop, calls=%fused_computation.13 | loop fusion | flops 14055168 | bytes 5135488 | tf_op jit(solution)/shard_map/reduce_sum | solution.py:210
  186.5 2.6 %collective-permute-start.11 = (f32[4,2,192]{2,0,1:T(4,128)S(1)}, f32[4,2,192]{2,0,1:T(4,128)S(1)}, u32[]{:S(2)}, u32[]{:S(2)}) collective-permute-start(f32[4,2,192]{2,0,1:T(4,128)S(1)} %constant_dynamic-slice_fusion.1), channel_id=1, source_target_pairs={{0,2},{1,3},{2,0},{3,1},{4,6},{5,7},{6,4},{7,5},{8,10},{9,11},{10,... | collective-permute-start | bytes 18440 | tf_op jit(solution)/shard_map/ppermute | solution.py:216
  189.1 2.6 %collective-permute-done.11 = f32[4,2,192]{2,0,1:T(4,128)S(1)} collective-permute-done((f32[4,2,192]{2,0,1:T(4,128)S(1)}, f32[4,2,192]{2,0,1:T(4,128)S(1)}, u32[]{:S(2)}, u32[]{:S(2)}) %collective-permute-start.11) | collective-permute-done | bytes 6176 | tf_op jit(solution)/shard_map/ppermute | solution.py:216
  191.9 1.7 collective-permute-start.12
  193.6 2.0 collective-permute-done.12
  195.6 0.1 collective-permute-start.13
  195.7 1.1 collective-permute-done.13
  197.0 1.7 collective-permute-start.14
  198.6 2.0 collective-permute-done.14
  200.7 3.2 %collective-permute-start.15 = (f32[4,192]{1,0:T(4,128)S(1)}, f32[4,192]{1,0:T(4,128)S(1)}, u32[]{:S(2)}, u32[]{:S(2)}) collective-permute-start(f32[4,192]{1,0:T(4,128)S(1)} %pad_maximum_fusion.5), channel_id=1, source_target_pairs={{0,128},{32,160},{64,192},{96,224},{128,0},{160,32},{192,64},{224,... | collective-permute-start | bytes 9224 | tf_op jit(solution)/shard_map/ppermute | solution.py:229
  203.9 2.0 collective-permute-done.15
  206.0 0.6 divide_subtract_fusion
  (74 shorter events, 1.9 us)
Async XLA Ops:
  7.2 83.8 %copy-start = (bf16[256,2048]{1,0:T(8,128)(2,1)S(1)}, bf16[256,2048]{1,0:T(8,128)(2,1)}, u32[]{:S(2)}) copy-start(bf16[256,2048]{1,0:T(8,128)(2,1)} %param.16) | copy-start | bytes 3145732
  7.2 5.3 %copy-start.1 = (bf16[192,2048]{1,0:T(8,128)(2,1)S(1)}, bf16[192,2048]{1,0:T(8,128)(2,1)}, u32[]{:S(2)}) copy-start(bf16[192,2048]{1,0:T(8,128)(2,1)} %param.11) | copy-start | bytes 2359300
  7.2 5.5 %copy-start.5 = (f32[2048]{0:T(1024)S(1)}, f32[2048]{0:T(1024)}, u32[]{:S(2)}) copy-start(f32[2048]{0:T(1024)} %param.12) | copy-start | bytes 24580
  7.2 5.5 %copy-start.3 = (bf16[2048,64]{0,1:T(8,128)(2,1)S(1)}, bf16[2048,64]{0,1:T(8,128)(2,1)}, u32[]{:S(2)}) copy-start(bf16[2048,64]{0,1:T(8,128)(2,1)} %param.14) | copy-start | bytes 786436
  7.2 5.9 %copy-start.4 = (bf16[2048,64]{0,1:T(8,128)(2,1)S(1)}, bf16[2048,64]{0,1:T(8,128)(2,1)}, u32[]{:S(2)}) copy-start(bf16[2048,64]{0,1:T(8,128)(2,1)} %param.15) | copy-start | bytes 786436
  7.2 123.7 %all-gather.3.cloned.1.call-start = ((), (), s32[]{:S(2)}) async-start(), calls=%async_computation | async-start | bytes 8146944 | tf_op jit(solution)/shard_map/all_gather | solution.py:193
  10.7 159.5 %all-gather.5.cloned.1.call-start = ((), (), s32[]{:S(2)}) async-start(), calls=%async_computation.1 | async-start | bytes 3932160 | tf_op jit(solution)/shard_map/all_gather | solution.py:187
  13.8 4.4 %collective-permute-start = (bf16[1,192,128]{1,2,0:T(8,128)(2,1)S(1)}, bf16[1,192,128]{1,2,0:T(8,128)(2,1)S(1)}, u32[]{:S(2)}, u32[]{:S(2)}) collective-permute-start(bf16[1,192,128]{1,2,0:T(8,128)(2,1)S(1)} %maximum_bitcast_fusion), channel_id=1, source_target_pairs={{0,1},{1,0},{2,3},{3,2},{4,5},{5,4},{6,7},{7,6},{8,9},{9,8},{10,11... | collective-permute-start | bytes 147464 | tf_op jit(solution)/shard_map/ppermute | solution.py:110
  18.2 6.6 %collective-permute-start.1 = (bf16[2,192,128]{1,2,0:T(8,128)(2,1)S(1)}, bf16[2,192,128]{1,2,0:T(8,128)(2,1)S(1)}, u32[]{:S(2)}, u32[]{:S(2)}) collective-permute-start(bf16[2,192,128]{1,2,0:T(8,128)(2,1)S(1)} %maximum_select_fusion.5), channel_id=1, source_target_pairs={{0,2},{1,3},{2,0},{3,1},{4,6},{5,7},{6,4},{7,5},{8,10},{9,11},{10,... | collective-permute-start | bytes 294920 | tf_op jit(solution)/shard_map/ppermute | solution.py:110
  25.1 14.9 %collective-permute-start.2 = (bf16[1,768,128]{2,1,0:T(8,128)(2,1)S(1)}, bf16[1,768,128]{2,1,0:T(8,128)(2,1)S(1)}, u32[]{:S(2)}, u32[]{:S(2)}) collective-permute-start(bf16[1,768,128]{2,1,0:T(8,128)(2,1)S(1)} %bitcast.137), channel_id=1, source_target_pairs={{0,4},{4,8},{8,12},{12,16},{16,20},{20,24},{24,28},{28,0},{1,5},{5... | collective-permute-start | bytes 589832 | tf_op jit(solution)/shard_map/ppermute | solution.py:121
  40.0 29.3 %collective-permute-start.3 = (bf16[2,768,128]{2,1,0:T(8,128)(2,1)S(1)}, bf16[2,768,128]{2,1,0:T(8,128)(2,1)S(1)}, u32[]{:S(2)}, u32[]{:S(2)}) collective-permute-start(bf16[2,768,128]{2,1,0:T(8,128)(2,1)S(1)} %pad_maximum_fusion.1), channel_id=1, source_target_pairs={{0,8},{4,12},{8,16},{12,20},{16,24},{20,28},{24,0},{28,4},{1,9},{5... | collective-permute-start | bytes 1179656 | tf_op jit(solution)/shard_map/ppermute | solution.py:121
  69.4 11.8 %collective-permute-start.4 = (bf16[1,768,128]{2,1,0:T(8,128)(2,1)S(1)}, bf16[1,768,128]{2,1,0:T(8,128)(2,1)S(1)}, u32[]{:S(2)}, u32[]{:S(2)}) collective-permute-start(bf16[1,768,128]{2,1,0:T(8,128)(2,1)S(1)} %slice.243), channel_id=1, source_target_pairs={{0,4},{4,8},{8,12},{12,16},{16,20},{20,24},{24,28},{28,0},{1,5},{5... | collective-permute-start | bytes 589832 | tf_op jit(solution)/shard_map/ppermute | solution.py:121
  91.4 23.1 %copy-start.2 = (f32[2048]{0:T(1024)S(1)}, f32[2048]{0:T(1024)}, u32[]{:S(2)}) copy-start(f32[2048]{0:T(1024)} %param.17) | copy-start | bytes 24580
  91.4 2.5 %collective-permute-start.5 = (f32[2,2,24,2048]{3,2,1,0:T(8,128)S(1)}, f32[2,2,24,2048]{3,2,1,0:T(8,128)}, u32[]{:S(2)}, u32[]{:S(2)}) collective-permute-start(f32[2,2,24,2048]{3,2,1,0:T(8,128)S(1)} %select_bitcast_fusion), channel_id=1, source_target_pairs={{0,32},{32,0},{64,96},{96,64},{128,160},{160,128},{192,224},{224,1... | collective-permute-start | bytes 2359304 | tf_op jit(solution)/shard_map/ppermute | solution.py:175
  95.3 11.2 %collective-permute-start.6 = (f32[2,24,2048]{2,1,0:T(8,128)S(1)}, f32[2,24,2048]{2,1,0:T(8,128)S(1)}, u32[]{:S(2)}, u32[]{:S(2)}) collective-permute-start(f32[2,24,2048]{2,1,0:T(8,128)S(1)} %select_bitcast_fusion.1), channel_id=1, source_target_pairs={{0,64},{32,96},{64,0},{96,32},{128,192},{160,224},{192,128},{224,1... | collective-permute-start | bytes 1179656 | tf_op jit(solution)/shard_map/ppermute | solution.py:175
  106.6 7.8 %collective-permute-start.7 = (f32[24,2048]{1,0:T(8,128)S(1)}, f32[24,2048]{1,0:T(8,128)S(1)}, u32[]{:S(2)}, u32[]{:S(2)}) collective-permute-start(f32[24,2048]{1,0:T(8,128)S(1)} %select_bitcast_fusion.2), channel_id=1, source_target_pairs={{0,128},{32,160},{64,192},{96,224},{128,0},{160,32},{192,64},{224,... | collective-permute-start | bytes 589832 | tf_op jit(solution)/shard_map/ppermute | solution.py:175
  114.6 6.2 %collective-permute-start.8 = (bf16[1,24,2048]{2,1,0:T(8,128)(2,1)S(1)}, bf16[1,24,2048]{2,1,0:T(8,128)(2,1)S(1)}, u32[]{:S(2)}, u32[]{:S(2)}) collective-permute-start(bf16[1,24,2048]{2,1,0:T(8,128)(2,1)S(1)} %get-tuple-element.18), channel_id=1, source_target_pairs={{0,128},{32,160},{64,192},{96,224},{128,0},{160,32},{192,64},{224,... | collective-permute-start | bytes 294920 | tf_op jit(solution)/shard_map/ppermute | solution.py:183
  120.9 5.8 %collective-permute-start.9 = (bf16[2,24,2048]{2,1,0:T(8,128)(2,1)S(1)}, bf16[2,24,2048]{2,1,0:T(8,128)(2,1)S(1)}, u32[]{:S(2)}, u32[]{:S(2)}) collective-permute-start(bf16[2,24,2048]{2,1,0:T(8,128)(2,1)S(1)} %maximum_select_fusion.4), channel_id=1, source_target_pairs={{0,64},{32,96},{64,0},{96,32},{128,192},{160,224},{192,128},{224,1... | collective-permute-start | bytes 589832 | tf_op jit(solution)/shard_map/ppermute | solution.py:183
  126.7 2.0 collective-permute-start.10
  186.5 5.2 %collective-permute-start.11 = (f32[4,2,192]{2,0,1:T(4,128)S(1)}, f32[4,2,192]{2,0,1:T(4,128)S(1)}, u32[]{:S(2)}, u32[]{:S(2)}) collective-permute-start(f32[4,2,192]{2,0,1:T(4,128)S(1)} %constant_dynamic-slice_fusion.1), channel_id=1, source_target_pairs={{0,2},{1,3},{2,0},{3,1},{4,6},{5,7},{6,4},{7,5},{8,10},{9,11},{10,... | collective-permute-start | bytes 18440 | tf_op jit(solution)/shard_map/ppermute | solution.py:216
  191.9 3.7 %collective-permute-start.12 = (f32[4,1,192]{2,0,1:T(4,128)S(1)}, f32[4,1,192]{2,0,1:T(4,128)S(1)}, u32[]{:S(2)}, u32[]{:S(2)}) collective-permute-start(f32[4,1,192]{2,0,1:T(4,128)S(1)} %constant_dynamic-slice_fusion), channel_id=1, source_target_pairs={{0,1},{1,0},{2,3},{3,2},{4,5},{5,4},{6,7},{7,6},{8,9},{9,8},{10,11... | collective-permute-start | bytes 9224 | tf_op jit(solution)/shard_map/ppermute | solution.py:224
  195.6 1.3 collective-permute-start.13
  197.0 3.7 %collective-permute-start.14 = (f32[4,192]{1,0:T(4,128)S(1)}, f32[4,192]{1,0:T(4,128)S(1)}, u32[]{:S(2)}, u32[]{:S(2)}) collective-permute-start(f32[4,192]{1,0:T(4,128)S(1)} %pad_maximum_fusion.4), channel_id=1, source_target_pairs={{0,64},{32,96},{64,0},{96,32},{128,192},{160,224},{192,128},{224,1... | collective-permute-start | bytes 9224 | tf_op jit(solution)/shard_map/ppermute | solution.py:229
  200.7 5.2 %collective-permute-start.15 = (f32[4,192]{1,0:T(4,128)S(1)}, f32[4,192]{1,0:T(4,128)S(1)}, u32[]{:S(2)}, u32[]{:S(2)}) collective-permute-start(f32[4,192]{1,0:T(4,128)S(1)} %pad_maximum_fusion.5), channel_id=1, source_target_pairs={{0,128},{32,160},{64,192},{96,224},{128,0},{160,32},{192,64},{224,... | collective-permute-start | bytes 9224 | tf_op jit(solution)/shard_map/ppermute | solution.py:229
Sparse Core Ops, SparseCore 0:
  10.8 111.2 all-gather.2
  130.0 40.1 all-gather.4

commit v8 on v7

--- a/solution.py
+++ b/solution.py
@@ -52,6 +52,16 @@
     total = first[1] * scale_a + second[1] * scale_b
     spread = scale_a * (first[2] + gap_a * first[1]) + scale_b * (second[2] + gap_b * second[1])
     target = first[3] + second[3]
+    return jnp.stack([top, total, spread, target])
+
+
+def merge_many(parts):
+    top = jnp.max(parts[:, 0], axis=0)
+    gap = parts[:, 0] - top[None]
+    scale = jnp.exp(gap)
+    total = jnp.sum(parts[:, 1] * scale, axis=0)
+    spread = jnp.sum(scale * (parts[:, 2] + gap * parts[:, 1]), axis=0)
+    target = jnp.sum(parts[:, 3], axis=0)
     return jnp.stack([top, total, spread, target])
 
 
@@ -164,25 +174,15 @@
     kv_bits = kv_count.bit_length() - 1
     partial = jnp.dot(context, w_o, preferred_element_type=jnp.float32)
     chunk = tok_rows // kv_count
-    blocks = partial.reshape((2,) * kv_bits + (chunk, partial.shape[1]))
-    for bit in range(kv_bits):
-        mine_low = (kv_index >> bit) % 2 == 0
-        axis = kv_bits - 1 - bit
-        low = lax.index_in_dim(blocks, 0, axis, keepdims=False)
-        high = lax.index_in_dim(blocks, 1, axis, keepdims=False)
-        keep = jnp.where(mine_low, low, high)
-        send = jnp.where(mine_low, high, low)
-        got = lax.ppermute(send, "kv", [(p, p ^ (1 << bit)) for p in range(kv_count)])
-        blocks = jnp.where(mine_low, keep + got, got + keep)
-    attn_part = blocks
+    pieces = lax.all_to_all(
+        partial.reshape(kv_count, chunk, partial.shape[1]), "kv", 0, 0, tiled=False
+    )
+    attn_part = jnp.sum(pieces, axis=0)
     stream_part = lax.dynamic_slice_in_dim(stream, kv_index * chunk, chunk, 0)
     final_part = rms_norm(stream_part + RESID_SCALE * attn_part, final_gain).astype(jnp.bfloat16)
-    rows = final_part[None]
-    for bit in reversed(range(kv_bits)):
-        mine_low = (kv_index >> bit) % 2 == 0
-        got = lax.ppermute(rows, "kv", [(p, p ^ (1 << bit)) for p in range(kv_count)])
-        rows = jnp.where(mine_low, jnp.stack([rows, got], axis=1), jnp.stack([got, rows], axis=1))
-        rows = rows.reshape((rows.shape[0] * 2,) + rows.shape[2:])
+    rows = lax.all_to_all(
+        jnp.broadcast_to(final_part[None], (kv_count,) + final_part.shape), "kv", 0, 0, tiled=False
+    )
     final_in = rows.reshape(tok_rows, final_part.shape[1])
     head_rows = lax.all_gather(final_in, "y", axis=0, tiled=True)
     group_rows = head_rows.shape[0]
@@ -209,26 +209,12 @@
     row_stats = jnp.stack(
         [top_row, jnp.sum(expw, axis=1), jnp.sum(expw * shifted, axis=1), target]
     ).reshape(4, y_count, tok_rows)
-    half = y_count // 2
-    my_half = y_index // half
-    keep = lax.dynamic_slice_in_dim(row_stats, my_half * half, half, 1)
-    send = lax.dynamic_slice_in_dim(row_stats, (1 - my_half) * half, half, 1)
-    got = lax.ppermute(send, "y", [(p, p ^ half) for p in range(y_count)])
-    merged = merge_stats(keep, got, my_half == 0)
-    width = half
-    while width > 1:
-        width //= 2
-        my_part = (y_index // width) % 2
-        keep = lax.dynamic_slice_in_dim(merged, my_part * width, width, 1)
-        send = lax.dynamic_slice_in_dim(merged, (1 - my_part) * width, width, 1)
-        got = lax.ppermute(send, "y", [(p, p ^ width) for p in range(y_count)])
-        merged = merge_stats(keep, got, my_part == 0)
-    merged = merged[:, 0]
-    step = 1
-    while step < kv_count:
-        got = lax.ppermute(merged, "kv", [(p, p ^ step) for p in range(kv_count)])
-        merged = merge_stats(merged, got, (kv_index // step) % 2 == 0)
-        step *= 2
+    from_y = lax.all_to_all(row_stats.transpose(1, 0, 2), "y", 0, 0, tiled=False)
+    merged = merge_many(from_y)
+    from_kv = lax.all_to_all(
+        jnp.broadcast_to(merged[None], (kv_count,) + merged.shape), "kv", 0, 0, tiled=False
+    )
+    merged = merge_many(from_kv)
     top_all, total_all, spread_all, target_all = merged[0], merged[1], merged[2], merged[3]
     log_probs = target_all - top_all - jnp.log(total_all)
     entropies = jnp.log(total_all) - spread_all / total_all

time: 216 us -> 222 us (1.028)
  blocking collectives: 0 us -> 34.4 us
  waiting for transfers between devices: 132 us -> 117 us
  starting transfers between devices: 23.8 us -> 9 us
    all_to_all x0 -> x3, blocking collectives: none -> 34.4 us  [the longest x1 16.3 us: local(): lax.all_to_all(jnp.broadcast_to(final_part[None], (kv_count,) + final_par...]
    ppermute x11 -> x0, waiting for transfers between devices: 34.1 us -> none  [the longest x3 15.4 us: local(): got = lax.ppermute(send, 'kv', [(p, p ^ 1 << bit) for p in range(kv_count)])]
    all_to_all x0 -> x1, waiting for transfers between devices: none -> 20.1 us  [local(): lax.all_to_all(partial.reshape(kv_count, chunk, partial.shape[1]), 'kv',...]
    ppermute x11 -> x0, starting transfers between devices: 19.1 us -> none  [the longest x3 5.02 us: local(): got = lax.ppermute(rows, 'kv', [(p, p ^ 1 << bit) for p in range(kv_count)])]
    all_to_all x0 -> x1, starting transfers between devices: none -> 4.3 us  [local(): lax.all_to_all(partial.reshape(kv_count, chunk, partial.shape[1]), 'kv',...]
    all_gather x1, waiting for transfers between devices: 38 us -> 35.8 us  [local(): head_rows = lax.all_gather(final_in, 'y', axis=0, tiled=True)]
  transfers between devices with their start and end apart: 18 -> 8, of which waited for: 17 -> 7; matrix products, arithmetic and copies ran while one was open for 11% -> 11% of each run, Pallas kernels for 0% -> 0%
where the time goes in v8:
time: 222 us; the launch traced here: 219 us
  waiting for transfers between devices  117 us (53%)
  blocking collectives  34.4 us (15%)
  matrix products  21.7 us (10%)
  other arithmetic  17.7 us (8%)
  between operations  14.3 us (6%)
  starting transfers between devices  9 us (4%)
  local copies, waits for them, and re-layouts  5.16 us (2%)
    ppermute x3, waiting for transfers between devices, local(): lax.ppermute(held[:need], 'z', [(p, (p + need) % z_count) for p in range(...  52.4 us
    all_gather x1, waiting for transfers between devices, local(): head_rows = lax.all_gather(final_in, 'y', axis=0, tiled=True)  35.8 us
    all_to_all x1, waiting for transfers between devices, local(): lax.all_to_all(partial.reshape(kv_count, chunk, partial.shape[1]), 'kv',...  20.1 us
    all_to_all x1, blocking collectives, local(): lax.all_to_all(jnp.broadcast_to(final_part[None], (kv_count,) + final_par...  16.3 us
    dot_general x1, matrix products, local(): jnp.dot(head_rows, head_cols, preferred_element_type=jnp.float32)  11.2 us
    all_to_all x1, blocking collectives, local(): lax.all_to_all(jnp.broadcast_to(merged[None], (kv_count,) + merged.shape)...  9.5 us
    all_to_all x1, blocking collectives, local(): lax.all_to_all(row_stats.transpose(1, 0, 2), 'y', 0, 0, tiled=False)  8.69 us
    ppermute x2, waiting for transfers between devices, local(): got = lax.ppermute(plane, 'y', [(p, p ^ 1 << bit) for p in range(y_count)])  8.53 us
  transfers between devices with their start and end apart: 8, of which 7 were waited for; matrix products, arithmetic and copies ran while one was open for 11% of the time, Pallas kernels for 0%

profile of v8, /device:TPU:24, one launch (start us, length us, event | category | flops | bytes accessed | tf_op | source)
XLA Modules:
  0.0 219.1 jit_solution(9936815190538578945)
XLA Ops:
  7.2 0.0 copy-start
  7.2 0.0 all-gather.3.cloned.1.call-start
  7.2 0.8 convert_element_type.48
  8.0 0.1 broadcast_in_dim.131
  8.2 1.4 concatenate.42
  9.6 1.0 pad.4
  10.6 0.0 all-gather.3.cloned.1.call-update
  10.6 0.8 copy.49
  11.5 0.1 reduce.7
  11.6 0.7 sub.61
  12.3 0.1 select_reduce_fusion.2
  12.4 0.2 multiply_reduce_fusion.1
  12.6 1.4 convolution_bitcast_fusion
  14.1 0.2 fusion.34
  14.3 1.4 convolution_convert_fusion
  15.7 0.8 collective-permute-start
  16.5 3.5 %collective-permute-done = bf16[1,192,128]{1,2,0:T(8,128)(2,1)S(1)} collective-permute-done((bf16[1,192,128]{1,2,0:T(8,128)(2,1)S(1)}, bf16[1,192,128]{1,2,0:T(8,128)(2,1)S(1)}, u32[]{:S(2)}, u32[]{:S(2)}) %collective-permute-start) | collective-permute-done | bytes 49184 | tf_op jit(solution)/shard_map/ppermute | solution.py:120
  20.1 1.5 collective-permute-start.1
  21.5 0.1 iota_add_fusion
  21.6 5.0 %collective-permute-done.1 = bf16[2,192,128]{1,2,0:T(8,128)(2,1)S(1)} collective-permute-done((bf16[2,192,128]{1,2,0:T(8,128)(2,1)S(1)}, bf16[2,192,128]{1,2,0:T(8,128)(2,1)S(1)}, u32[]{:S(2)}, u32[]{:S(2)}) %collective-permute-start.1) | collective-permute-done | bytes 98336 | tf_op jit(solution)/shard_map/ppermute | solution.py:120
  26.6 0.1 maximum_select_fusion
  26.7 0.2 copy.50
  26.9 2.0 collective-permute-start.2
  28.9 0.6 compare_and_fusion
  29.5 12.3 %collective-permute-done.2 = bf16[1,768,128]{2,1,0:T(8,128)(2,1)S(1)} collective-permute-done((bf16[1,768,128]{2,1,0:T(8,128)(2,1)S(1)}, bf16[1,768,128]{2,1,0:T(8,128)(2,1)S(1)}, u32[]{:S(2)}, u32[]{:S(2)}) %collective-permute-start.2) | collective-permute-done | bytes 196640 | tf_op jit(solution)/shard_map/ppermute | solution.py:131
  41.9 0.1 collective-permute-start.3
  42.0 0.2 multiply_cosine_fusion
  42.2 0.0 copy-done.3
  42.2 0.6 fusion.47
  42.8 28.5 %collective-permute-done.3 = bf16[2,768,128]{2,1,0:T(8,128)(2,1)S(1)} collective-permute-done((bf16[2,768,128]{2,1,0:T(8,128)(2,1)S(1)}, bf16[2,768,128]{2,1,0:T(8,128)(2,1)S(1)}, u32[]{:S(2)}, u32[]{:S(2)}) %collective-permute-start.3) | collective-permute-done | bytes 393248 | tf_op jit(solution)/shard_map/ppermute | solution.py:131
  71.3 0.3 collective-permute-start.4
  71.6 11.6 %collective-permute-done.4 = bf16[1,768,128]{2,1,0:T(8,128)(2,1)S(1)} collective-permute-done((bf16[1,768,128]{2,1,0:T(8,128)(2,1)S(1)}, bf16[1,768,128]{2,1,0:T(8,128)(2,1)S(1)}, u32[]{:S(2)}, u32[]{:S(2)}) %collective-permute-start.4) | collective-permute-done | bytes 196640 | tf_op jit(solution)/shard_map/ppermute | solution.py:131
  83.3 0.1 pad_maximum_fusion
  83.4 2.2 fusion
  85.6 3.7 %fusion.1 = f32[4,192]{1,0:T(4,128)S(1)} fusion(f32[3840,192,4]{0,1,2:T(8,128)S(1)} %get-tuple-element.32, f32[4,192]{1,0:T(4,128)S(1)} %broadcast_maximum_fusion, pred[192,3840]{1,0:T(8,128)(4,1)S(1)} %compare_and_fusion), kind=kLoop, calls=%fused_computation.3 | loop fusion | flops 14744832 | bytes 12539904 | tf_op jit(solution)/shard_map/reduce_sum | solution.py:153
  89.3 3.3 %fusion.16 = bf16[192,1,4,64]{0,3,2,1:T(8,128)(2,1)S(1)} fusion(f32[3840,192,4]{0,1,2:T(8,128)S(1)} %get-tuple-element.32, f32[4,192]{1,0:T(4,128)S(1)} %broadcast_maximum_fusion, pred[192,3840]{1,0:T(8,128)(4,1)S(1)} %compare_and_fusion, bf16[3840,128]{1,0:T(8,128)(2,1)S(1)} %bitcast.118, f32[4,192]{1,0:T(4,128)S(1)} %fusion.1), kind=kOutput, calls=%fused_computation.23 | convolution fusion | flops 392331264 | bytes 13621248 | tf_op jit(solution)/shard_map/kgts,skd->kgtd/dot_general | solution.py:154
  92.6 0.2 copy.54
  92.8 0.2 convert_element_type.57
  93.0 0.0 copy-start.2
  93.0 1.6 fusion.19
  94.6 4.3 %all-to-all-start = ((f32[8,24,2048]{2,1,0:T(8,128)}), f32[8,24,2048]{2,1,0:T(8,128)S(1)}, u32[]{:S(2)}, u32[]{:S(2)}) async-start(f32[8,24,2048]{2,1,0:T(8,128)} %fusion.19), calls=%async_computation | async-start | bytes 3145728 | tf_op jit(solution)/shard_map/all_to_all | solution.py:177
  98.9 0.0 all-gather.5.cloned.1.call-start
  98.9 1.4 convert_element_type.49
  100.3 20.1 %all-to-all-done = f32[8,24,2048]{2,1,0:T(8,128)S(1)} async-done(((f32[8,24,2048]{2,1,0:T(8,128)}), f32[8,24,2048]{2,1,0:T(8,128)S(1)}, u32[]{:S(2)}, u32[]{:S(2)}) %all-to-all-start) | async-done | bytes 1572896 | tf_op jit(solution)/shard_map/all_to_all | solution.py:177
  120.4 0.1 reduce_sum.119
  120.5 1.1 multiply_reduce_fusion.2
  121.6 1.0 multiply_convert_fusion.1
  122.7 0.1 broadcast_in_dim.125
  122.7 16.3 %all_to_all.20 = bf16[8,24,2048]{2,1,0:T(8,128)(2,1)} all-to-all(bf16[8,24,2048]{2,1,0:T(8,128)(2,1)S(1)} %broadcast_in_dim.125), channel_id=1, replica_groups=mesh['kv'=8,'z'=8,'y'=4] {'kv'}, dimensions={0} | all-to-all | bytes 1572864 | tf_op jit(solution)/shard_map/all_to_all | solution.py:183
  139.0 0.0 all-gather.5.cloned.1.call-update
  139.0 0.1 add_select_fusion
  139.1 0.1 select_n.106
  139.2 0.8 dynamic_slice.7
  140.0 1.3 compare_reduce_fusion
  141.3 35.8 %all-gather.5.cloned.1.call-done = bf16[768,2048]{1,0:T(8,128)(2,1)} async-done(((bf16[192,2048]{1,0:T(8,128)(2,1)}), bf16[768,2048]{1,0:T(8,128)(2,1)}) %all-gather.5.cloned.1.call-update) | async-done | bytes 3145744 | tf_op jit(solution)/shard_map/all_gather | solution.py:187
  177.1 11.2 %select_reduce_fusion.1 = (f32[768]{0:T(1024)S(1)}, f32[768,1664]{1,0:T(8,128)}) fusion(pred[1664]{0:T(1024)(128)(4,1)S(1)} %compare_reduce_fusion, bf16[768,2048]{1,0:T(8,128)(2,1)} %all-gather.5.cloned.1.call-done, bf16[2064,1664]{0,1:T(8,128)(2,1)} %all-gather.3.cloned.1.call-done), kind=kOutput, calls=%fused_computation.15 | convolution fusion | flops 5238324224 | bytes 15078016 | tf_op jit(solution)/shard_map/dot_general | solution.py:203
  188.3 0.1 stack.30
  188.3 4.8 %fusion.9 = (f32[768]{0:T(1024)S(1)}, f32[768]{0:T(1024)S(1)}, f32[768]{0:T(1024)S(1)}) fusion(f32[768,1664]{1,0:T(8,128)} %get-tuple-element.34, f32[768]{0:T(1024)S(1)} %get-tuple-element.33, pred[1664]{0:T(1024)(128)(4,1)S(1)} %compare_reduce_fusion, s32[1664]{0:T(1024)S(1)} %select_n.106, s32[768]{0:T(1024)S(1)} %dynamic_slice.7), kind=kLoop, calls=%fused_computation.13 | loop fusion | flops 14055168 | bytes 5135488 | tf_op jit(solution)/shard_map/reduce_sum | solution.py:210
  193.1 0.1 stack.31
  193.2 0.1 stack.32
  193.3 0.1 stack.33
  193.4 8.7 %all_to_all.21 = f32[4,4,192]{2,1,0:T(4,128)S(1)} all-to-all(f32[4,4,192]{2,1,0:T(4,128)S(1)} %maximum_bitcast_fusion.1), channel_id=1, replica_groups=mesh['kv'=8,'z'=8,'y'=4] {'y'}, dimensions={0} | all-to-all | bytes 24576 | tf_op jit(solution)/shard_map/all_to_all | solution.py:212
  202.1 9.5 %all_to_all.22 = f32[8,4,192]{2,1,0:T(4,128)S(1)} all-to-all(f32[8,4,192]{2,1,0:T(4,128)S(1)} %broadcast_in_dim.130), channel_id=1, replica_groups=mesh['kv'=8,'z'=8,'y'=4] {'kv'}, dimensions={0} | all-to-all | bytes 49152 | tf_op jit(solution)/shard_map/all_to_all | solution.py:214
  211.7 0.6 divide_subtract_fusion
  (32 shorter events, 0.5 us)
Async XLA Ops:
  7.2 85.8 %copy-start = (bf16[256,2048]{1,0:T(8,128)(2,1)S(1)}, bf16[256,2048]{1,0:T(8,128)(2,1)}, u32[]{:S(2)}) copy-start(bf16[256,2048]{1,0:T(8,128)(2,1)} %param.16) | copy-start | bytes 3145732
  7.2 5.2 %copy-start.1 = (bf16[192,2048]{1,0:T(8,128)(2,1)S(1)}, bf16[192,2048]{1,0:T(8,128)(2,1)}, u32[]{:S(2)}) copy-start(bf16[192,2048]{1,0:T(8,128)(2,1)} %param.11) | copy-start | bytes 2359300
  7.2 5.5 %copy-start.4 = (f32[2048]{0:T(1024)S(1)}, f32[2048]{0:T(1024)}, u32[]{:S(2)}) copy-start(f32[2048]{0:T(1024)} %param.12) | copy-start | bytes 24580
  7.2 132.8 %all-gather.3.cloned.1.call-start = ((), (), s32[]{:S(2)}) async-start(), calls=%async_computation.4 | async-start | bytes 8146944 | tf_op jit(solution)/shard_map/all_gather | solution.py:193
  10.6 31.6 %copy-start.3 = (bf16[2048,256]{1,0:T(8,128)(2,1)S(1)}, bf16[2048,256]{1,0:T(8,128)(2,1)}, u32[]{:S(2)}) copy-start(bf16[2048,256]{1,0:T(8,128)(2,1)} %param.13) | copy-start | bytes 3145732
  15.7 4.4 %collective-permute-start = (bf16[1,192,128]{1,2,0:T(8,128)(2,1)S(1)}, bf16[1,192,128]{1,2,0:T(8,128)(2,1)S(1)}, u32[]{:S(2)}, u32[]{:S(2)}) collective-permute-start(bf16[1,192,128]{1,2,0:T(8,128)(2,1)S(1)} %maximum_bitcast_fusion), channel_id=1, source_target_pairs={{0,1},{1,0},{2,3},{3,2},{4,5},{5,4},{6,7},{7,6},{8,9},{9,8},{10,11... | collective-permute-start | bytes 147464 | tf_op jit(solution)/shard_map/ppermute | solution.py:120
  20.1 6.6 %collective-permute-start.1 = (bf16[2,192,128]{1,2,0:T(8,128)(2,1)S(1)}, bf16[2,192,128]{1,2,0:T(8,128)(2,1)S(1)}, u32[]{:S(2)}, u32[]{:S(2)}) collective-permute-start(bf16[2,192,128]{1,2,0:T(8,128)(2,1)S(1)} %maximum_select_fusion.1), channel_id=1, source_target_pairs={{0,2},{1,3},{2,0},{3,1},{4,6},{5,7},{6,4},{7,5},{8,10},{9,11},{10,... | collective-permute-start | bytes 294920 | tf_op jit(solution)/shard_map/ppermute | solution.py:120
  26.9 15.0 %collective-permute-start.2 = (bf16[1,768,128]{2,1,0:T(8,128)(2,1)S(1)}, bf16[1,768,128]{2,1,0:T(8,128)(2,1)S(1)}, u32[]{:S(2)}, u32[]{:S(2)}) collective-permute-start(bf16[1,768,128]{2,1,0:T(8,128)(2,1)S(1)} %bitcast.114), channel_id=1, source_target_pairs={{0,4},{4,8},{8,12},{12,16},{16,20},{20,24},{24,28},{28,0},{1,5},{5... | collective-permute-start | bytes 589832 | tf_op jit(solution)/shard_map/ppermute | solution.py:131
  41.9 29.4 %collective-permute-start.3 = (bf16[2,768,128]{2,1,0:T(8,128)(2,1)S(1)}, bf16[2,768,128]{2,1,0:T(8,128)(2,1)S(1)}, u32[]{:S(2)}, u32[]{:S(2)}) collective-permute-start(bf16[2,768,128]{2,1,0:T(8,128)(2,1)S(1)} %pad_maximum_fusion.1), channel_id=1, source_target_pairs={{0,8},{4,12},{8,16},{12,20},{16,24},{20,28},{24,0},{28,4},{1,9},{5... | collective-permute-start | bytes 1179656 | tf_op jit(solution)/shard_map/ppermute | solution.py:131
  71.3 11.9 %collective-permute-start.4 = (bf16[1,768,128]{2,1,0:T(8,128)(2,1)S(1)}, bf16[1,768,128]{2,1,0:T(8,128)(2,1)S(1)}, u32[]{:S(2)}, u32[]{:S(2)}) collective-permute-start(bf16[1,768,128]{2,1,0:T(8,128)(2,1)S(1)} %slice.75), channel_id=1, source_target_pairs={{0,4},{4,8},{8,12},{12,16},{16,20},{20,24},{24,28},{28,0},{1,5},{5... | collective-permute-start | bytes 589832 | tf_op jit(solution)/shard_map/ppermute | solution.py:131
  93.0 28.6 %copy-start.2 = (f32[2048]{0:T(1024)S(1)}, f32[2048]{0:T(1024)}, u32[]{:S(2)}) copy-start(f32[2048]{0:T(1024)} %param.17) | copy-start | bytes 24580
  94.6 25.8 %all-to-all-start = ((f32[8,24,2048]{2,1,0:T(8,128)}), f32[8,24,2048]{2,1,0:T(8,128)S(1)}, u32[]{:S(2)}, u32[]{:S(2)}) async-start(f32[8,24,2048]{2,1,0:T(8,128)} %fusion.19), calls=%async_computation | async-start | bytes 3145728 | tf_op jit(solution)/shard_map/all_to_all | solution.py:177
  98.9 78.2 %all-gather.5.cloned.1.call-start = ((), (), s32[]{:S(2)}) async-start(), calls=%async_computation.5 | async-start | bytes 3932160 | tf_op jit(solution)/shard_map/all_gather | solution.py:187
Sparse Core Ops, SparseCore 0:
  10.7 111.3 all-gather.2
  139.1 37.8 all-gather.4

commit v9 on v7

--- a/solution.py
+++ b/solution.py
@@ -104,22 +104,21 @@
     y_bits = y_count.bit_length() - 1
     z_pos = lax.axis_index("z")
     y_pos = lax.axis_index("y")
-    plane = packed[None]
-    for bit in range(y_bits):
-        mine_low = (y_pos >> bit) % 2 == 0
-        got = lax.ppermute(plane, "y", [(p, p ^ (1 << bit)) for p in range(y_count)])
-        plane = jnp.where(
-            mine_low, jnp.concatenate([plane, got], axis=0), jnp.concatenate([got, plane], axis=0)
-        )
     plane_rows = y_count * tok_rows
-    plane = plane.reshape(plane_rows, packed.shape[1])
     max_doc = (z_count * plane_rows) // 2
     back = min(-(-(max_doc - 1) // plane_rows), z_count - 1)
-    held = plane[None]
+    held = packed[None]
     while held.shape[0] < back + 1:
         need = min(held.shape[0], back + 1 - held.shape[0])
         got = lax.ppermute(held[:need], "z", [(p, (p + need) % z_count) for p in range(z_count)])
         held = jnp.concatenate([got, held], axis=0)
+    held = held[:, None]
+    for bit in range(y_bits):
+        mine_low = (y_pos >> bit) % 2 == 0
+        got = lax.ppermute(held, "y", [(p, p ^ (1 << bit)) for p in range(y_count)])
+        held = jnp.where(
+            mine_low, jnp.concatenate([held, got], axis=1), jnp.concatenate([got, held], axis=1)
+        )
     shard_rows = held.reshape(-1, packed.shape[1])
     plane_ids = (z_pos - back + jnp.arange(back + 1, dtype=jnp.int32)) % z_count
     key_pos = (plane_ids[:, None] * plane_rows + jnp.arange(plane_rows, dtype=jnp.int32)[None, :]).reshape(-1)

time: 216 us -> 202 us (0.935)
  waiting for transfers between devices: 132 us -> 112 us
  local copies, waits for them, and re-layouts: 6.06 us -> 9.43 us
  other arithmetic: 17.6 us -> 20.2 us
    ppermute x3, waiting for transfers between devices: 50.9 us -> 25.7 us  [local(): lax.ppermute(held[:need], 'z', [(p, (p + need) % z_count) for p in range(...]
    ppermute x2, waiting for transfers between devices: 8.53 us -> 16.8 us  [local(): got = lax.ppermute(held, 'y', [(p, p ^ 1 << bit) for p in range(y_count)])]
    all_gather x1, waiting for transfers between devices: 38 us -> 35.2 us  [local(): head_rows = lax.all_gather(final_in, 'y', axis=0, tiled=True)]
    select_n x1 -> x2, local copies, waits for them, and re-layouts: 0.17 us -> 2.42 us  [local(): jnp.where(mine_low, jnp.concatenate([held, got], axis=1), jnp.concatenate...]
  transfers between devices with their start and end apart: 18 -> 18, of which waited for: 17 -> 17; matrix products, arithmetic and copies ran while one was open for 11% -> 15% of each run, Pallas kernels for 0% -> 0%
where the time goes in v9:
time: 202 us; the launch traced here: 200 us
  waiting for transfers between devices  112 us (55%)
  starting transfers between devices  22.2 us (11%)
  matrix products  21.7 us (11%)
  other arithmetic  20.2 us (10%)
  between operations  14.6 us (7%)
  local copies, waits for them, and re-layouts  9.43 us (5%)
    all_gather x1, waiting for transfers between devices, local(): head_rows = lax.all_gather(final_in, 'y', axis=0, tiled=True)  35.2 us
    ppermute x3, waiting for transfers between devices, local(): lax.ppermute(held[:need], 'z', [(p, (p + need) % z_count) for p in range(...  25.7 us
    ppermute x2, waiting for transfers between devices, local(): got = lax.ppermute(held, 'y', [(p, p ^ 1 << bit) for p in range(y_count)])  16.8 us
    ppermute x3, waiting for transfers between devices, local(): got = lax.ppermute(send, 'kv', [(p, p ^ 1 << bit) for p in range(kv_count)])  15.4 us
    dot_general x1, matrix products, local(): jnp.dot(head_rows, head_cols, preferred_element_type=jnp.float32)  11.2 us
    ppermute x3, waiting for transfers between devices, local(): got = lax.ppermute(rows, 'kv', [(p, p ^ 1 << bit) for p in range(kv_count)])  8.91 us
    ppermute x3, waiting for transfers between devices, local(): got = lax.ppermute(merged, 'kv', [(p, p ^ step) for p in range(kv_count)])  5.18 us
    ppermute x3, starting transfers between devices, local(): got = lax.ppermute(rows, 'kv', [(p, p ^ 1 << bit) for p in range(kv_count)])  5.05 us
  transfers between devices with their start and end apart: 18, of which 17 were waited for; matrix products, arithmetic and copies ran while one was open for 15% of the time, Pallas kernels for 0%

profile of v9, /device:TPU:24, one launch (start us, length us, event | category | flops | bytes accessed | tf_op | source)
XLA Modules:
  0.0 199.7 jit_solution(14702346559204472011)
XLA Ops:
  7.3 0.8 convert_element_type.48
  8.2 1.4 concatenate.62
  9.6 1.1 pad.4
  10.8 0.8 copy.82
  11.6 0.1 reduce.3
  11.7 0.7 sub.118
  12.5 0.2 multiply_reduce_fusion.1
  12.8 0.4 convolution_bitcast_fusion
  13.2 0.4 convolution_convert_fusion
  13.7 0.2 fusion.40
  13.9 2.0 %collective-permute-start = (bf16[1,192,128]{1,2,0:T(8,128)(2,1)S(1)}, bf16[1,192,128]{1,2,0:T(8,128)(2,1)S(1)}, u32[]{:S(2)}, u32[]{:S(2)}) collective-permute-start(bf16[1,192,128]{1,2,0:T(8,128)(2,1)S(1)} %maximum_bitcast_fusion.1), channel_id=1, source_target_pairs={{0,4},{4,8},{8,12},{12,16},{16,20},{20,24},{24,28},{28,0},{1,5},{5... | collective-permute-start | bytes 147464 | tf_op jit(solution)/shard_map/ppermute | solution.py:113
  15.9 6.2 %collective-permute-done = bf16[1,192,128]{1,2,0:T(8,128)(2,1)S(1)} collective-permute-done((bf16[1,192,128]{1,2,0:T(8,128)(2,1)S(1)}, bf16[1,192,128]{1,2,0:T(8,128)(2,1)S(1)}, u32[]{:S(2)}, u32[]{:S(2)}) %collective-permute-start) | collective-permute-done | bytes 49184 | tf_op jit(solution)/shard_map/ppermute | solution.py:113
  22.2 12.6 %collective-permute-done.1 = bf16[2,192,128]{1,2,0:T(8,128)(2,1)S(1)} collective-permute-done((bf16[2,192,128]{1,2,0:T(8,128)(2,1)S(1)}, bf16[2,192,128]{1,2,0:T(8,128)(2,1)S(1)}, u32[]{:S(2)}, u32[]{:S(2)}) %collective-permute-start.1) | collective-permute-done | bytes 98336 | tf_op jit(solution)/shard_map/ppermute | solution.py:113
  34.9 6.9 %collective-permute-done.2 = bf16[1,192,128]{1,2,0:T(8,128)(2,1)S(1)} collective-permute-done((bf16[1,192,128]{1,2,0:T(8,128)(2,1)S(1)}, bf16[1,192,128]{1,2,0:T(8,128)(2,1)S(1)}, u32[]{:S(2)}, u32[]{:S(2)}) %collective-permute-start.2) | collective-permute-done | bytes 49184 | tf_op jit(solution)/shard_map/ppermute | solution.py:113
  41.9 0.8 collective-permute-start.3
  42.7 1.5 compare_and_fusion
  44.2 0.2 multiply_cosine_fusion
  44.4 8.1 %collective-permute-done.3 = bf16[5,1,192,128]{2,3,0,1:T(8,128)(2,1)S(1)} collective-permute-done((bf16[5,1,192,128]{2,3,0,1:T(8,128)(2,1)S(1)}, bf16[5,1,192,128]{2,3,0,1:T(8,128)(2,1)S(1)}, u32[]{:S(2)}, u32[]{:S(2)}) %collective-permute-start.3) | collective-permute-done | bytes 245792 | tf_op jit(solution)/shard_map/ppermute | solution.py:118
  52.6 0.2 maximum_select_fusion.2
  52.8 1.0 copy.83
  53.8 1.9 fusion.62
  55.7 8.6 %collective-permute-done.4 = bf16[5,2,192,128]{3,2,1,0:T(8,128)(2,1)S(1)} collective-permute-done((bf16[5,2,192,128]{3,2,1,0:T(8,128)(2,1)}, bf16[5,2,192,128]{3,2,1,0:T(8,128)(2,1)S(1)}, u32[]{:S(2)}, u32[]{:S(2)}) %collective-permute-start.4) | collective-permute-done | bytes 491552 | tf_op jit(solution)/shard_map/ppermute | solution.py:118
  64.3 1.1 copy.84
  65.4 1.8 maximum_select_fusion
  67.2 1.4 copy.86
  68.6 4.1 %fusion = (f32[4,192]{1,0:T(4,128)S(1)}, f32[3840,192,4]{0,1,2:T(8,128)S(1)}) fusion(pred[192,3840]{1,0:T(8,128)(4,1)} %compare_and_fusion, bf16[192,4,32]{0,2,1:T(8,128)(2,1)S(1)} %get-tuple-element.16, bf16[192,4,32]{0,2,1:T(8,128)(2,1)S(1)} %get-tuple-element.15, bf16[3840,128]{1,0:T(8,128)(2,1)} %bitcast.140), kind=kOutput, calls=%fused_computation.2 | convolution fusion | flops 386530560 | bytes 13618176 | tf_op jit(solution)/shard_map/tkgd,skd->kgts/dot_general | solution.py:132
  72.7 3.7 %fusion.1 = f32[4,192]{1,0:T(4,128)S(1)} fusion(f32[3840,192,4]{0,1,2:T(8,128)S(1)} %get-tuple-element.51, f32[4,192]{1,0:T(4,128)S(1)} %broadcast_maximum_fusion, pred[192,3840]{1,0:T(8,128)(4,1)S(1)} %copy-done.2), kind=kLoop, calls=%fused_computation.3 | loop fusion | flops 14744832 | bytes 12539904 | tf_op jit(solution)/shard_map/reduce_sum | solution.py:142
  76.5 3.3 %fusion.16 = bf16[192,1,4,64]{0,3,2,1:T(8,128)(2,1)S(1)} fusion(f32[3840,192,4]{0,1,2:T(8,128)S(1)} %get-tuple-element.51, f32[4,192]{1,0:T(4,128)S(1)} %broadcast_maximum_fusion, pred[192,3840]{1,0:T(8,128)(4,1)S(1)} %copy-done.2, bf16[3840,128]{1,0:T(8,128)(2,1)S(1)} %bitcast.141, f32[4,192]{1,0:T(4,128)S(1)} %fusion.1), kind=kOutput, calls=%fused_computation.24 | convolution fusion | flops 392331264 | bytes 13621248 | tf_op jit(solution)/shard_map/kgts,skd->kgtd/dot_general | solution.py:143
  79.7 0.2 copy.90
  79.9 0.2 convert_element_type.57
  80.1 0.4 fusion.19
  80.6 0.1 collective-permute-start.5
  80.7 2.4 %collective-permute-done.5 = f32[2,2,24,2048]{3,2,1,0:T(8,128)} collective-permute-done((f32[2,2,24,2048]{3,2,1,0:T(8,128)S(1)}, f32[2,2,24,2048]{3,2,1,0:T(8,128)}, u32[]{:S(2)}, u32[]{:S(2)}) %collective-permute-start.5) | collective-permute-done | bytes 786464 | tf_op jit(solution)/shard_map/ppermute | solution.py:174
  83.1 1.3 fusion.23
  84.4 1.6 collective-permute-start.6
  86.0 9.6 %collective-permute-done.6 = f32[2,24,2048]{2,1,0:T(8,128)S(1)} collective-permute-done((f32[2,24,2048]{2,1,0:T(8,128)S(1)}, f32[2,24,2048]{2,1,0:T(8,128)S(1)}, u32[]{:S(2)}, u32[]{:S(2)}) %collective-permute-start.6) | collective-permute-done | bytes 393248 | tf_op jit(solution)/shard_map/ppermute | solution.py:174
  95.8 3.1 %collective-permute-start.7 = (f32[24,2048]{1,0:T(8,128)S(1)}, f32[24,2048]{1,0:T(8,128)S(1)}, u32[]{:S(2)}, u32[]{:S(2)}) collective-permute-start(f32[24,2048]{1,0:T(8,128)S(1)} %select_bitcast_fusion.2), channel_id=1, source_target_pairs={{0,128},{32,160},{64,192},{96,224},{128,0},{160,32},{192,64},{224,... | collective-permute-start | bytes 589832 | tf_op jit(solution)/shard_map/ppermute | solution.py:174
  98.9 1.3 convert_element_type.49
  100.2 3.3 %collective-permute-done.7 = f32[24,2048]{1,0:T(8,128)S(1)} collective-permute-done((f32[24,2048]{1,0:T(8,128)S(1)}, f32[24,2048]{1,0:T(8,128)S(1)}, u32[]{:S(2)}, u32[]{:S(2)}) %collective-permute-start.7) | collective-permute-done | bytes 196640 | tf_op jit(solution)/shard_map/ppermute | solution.py:174
  103.6 0.2 multiply_reduce_fusion.2
  103.8 3.1 %collective-permute-start.8 = (bf16[1,24,2048]{2,1,0:T(8,128)(2,1)S(1)}, bf16[1,24,2048]{2,1,0:T(8,128)(2,1)S(1)}, u32[]{:S(2)}, u32[]{:S(2)}) collective-permute-start(bf16[1,24,2048]{2,1,0:T(8,128)(2,1)S(1)} %get-tuple-element.18), channel_id=1, source_target_pairs={{0,128},{32,160},{64,192},{96,224},{128,0},{160,32},{192,64},{224,... | collective-permute-start | bytes 294920 | tf_op jit(solution)/shard_map/ppermute | solution.py:182
  107.0 3.1 %collective-permute-done.8 = bf16[1,24,2048]{2,1,0:T(8,128)(2,1)S(1)} collective-permute-done((bf16[1,24,2048]{2,1,0:T(8,128)(2,1)S(1)}, bf16[1,24,2048]{2,1,0:T(8,128)(2,1)S(1)}, u32[]{:S(2)}, u32[]{:S(2)}) %collective-permute-start.8) | collective-permute-done | bytes 98336 | tf_op jit(solution)/shard_map/ppermute | solution.py:182
  110.1 1.6 collective-permute-start.9
  111.7 4.1 %collective-permute-done.9 = bf16[2,24,2048]{2,1,0:T(8,128)(2,1)S(1)} collective-permute-done((bf16[2,24,2048]{2,1,0:T(8,128)(2,1)S(1)}, bf16[2,24,2048]{2,1,0:T(8,128)(2,1)S(1)}, u32[]{:S(2)}, u32[]{:S(2)}) %collective-permute-start.9) | collective-permute-done | bytes 196640 | tf_op jit(solution)/shard_map/ppermute | solution.py:182
  115.9 0.3 collective-permute-start.10
  116.2 1.7 collective-permute-done.10
  117.9 0.1 maximum_select_fusion.1
  118.1 0.9 copy.101
  119.2 0.8 dynamic_slice.19
  120.0 1.3 compare_reduce_fusion
  121.3 35.2 %all-gather.5.cloned.1.call-done = bf16[768,2048]{1,0:T(8,128)(2,1)} async-done(((bf16[192,2048]{1,0:T(8,128)(2,1)}), bf16[768,2048]{1,0:T(8,128)(2,1)}) %all-gather.5.cloned.1.call-update) | async-done | bytes 3145744 | tf_op jit(solution)/shard_map/all_gather | solution.py:186
  156.5 11.2 %select_reduce_fusion.1 = (f32[768]{0:T(1024)S(1)}, f32[768,1664]{1,0:T(8,128)}) fusion(pred[1664]{0:T(1024)(128)(4,1)S(1)} %compare_reduce_fusion, bf16[768,2048]{1,0:T(8,128)(2,1)} %all-gather.5.cloned.1.call-done, bf16[2064,1664]{0,1:T(8,128)(2,1)} %all-gather.3.cloned.1.call-done), kind=kOutput, calls=%fused_computation.15 | convolution fusion | flops 5238324224 | bytes 15078016 | tf_op jit(solution)/shard_map/dot_general | solution.py:202
  167.8 4.8 %fusion.9 = (f32[768]{0:T(1024)S(1)}, f32[768]{0:T(1024)S(1)}, f32[768]{0:T(1024)S(1)}) fusion(f32[768,1664]{1,0:T(8,128)} %get-tuple-element.53, f32[768]{0:T(1024)S(1)} %get-tuple-element.52, pred[1664]{0:T(1024)(128)(4,1)S(1)} %compare_reduce_fusion, s32[1664]{0:T(1024)S(1)} %select_n.371, s32[768]{0:T(1024)S(1)} %dynamic_slice.19), kind=kLoop, calls=%fused_computation.13 | loop fusion | flops 14055168 | bytes 5135488 | tf_op jit(solution)/shard_map/reduce_sum | solution.py:209
  172.8 2.6 %collective-permute-start.11 = (f32[4,2,192]{2,0,1:T(4,128)S(1)}, f32[4,2,192]{2,0,1:T(4,128)S(1)}, u32[]{:S(2)}, u32[]{:S(2)}) collective-permute-start(f32[4,2,192]{2,0,1:T(4,128)S(1)} %constant_dynamic-slice_fusion.1), channel_id=1, source_target_pairs={{0,2},{1,3},{2,0},{3,1},{4,6},{5,7},{6,4},{7,5},{8,10},{9,11},{10,... | collective-permute-start | bytes 18440 | tf_op jit(solution)/shard_map/ppermute | solution.py:215
  175.5 2.6 %collective-permute-done.11 = f32[4,2,192]{2,0,1:T(4,128)S(1)} collective-permute-done((f32[4,2,192]{2,0,1:T(4,128)S(1)}, f32[4,2,192]{2,0,1:T(4,128)S(1)}, u32[]{:S(2)}, u32[]{:S(2)}) %collective-permute-start.11) | collective-permute-done | bytes 6176 | tf_op jit(solution)/shard_map/ppermute | solution.py:215
  178.2 1.7 collective-permute-start.12
  179.9 2.0 collective-permute-done.12
  182.0 0.1 collective-permute-start.13
  182.1 1.1 collective-permute-done.13
  183.3 1.7 collective-permute-start.14
  185.0 2.0 %collective-permute-done.14 = f32[4,192]{1,0:T(4,128)S(1)} collective-permute-done((f32[4,192]{1,0:T(4,128)S(1)}, f32[4,192]{1,0:T(4,128)S(1)}, u32[]{:S(2)}, u32[]{:S(2)}) %collective-permute-start.14) | collective-permute-done | bytes 3104 | tf_op jit(solution)/shard_map/ppermute | solution.py:228
  187.1 3.2 %collective-permute-start.15 = (f32[4,192]{1,0:T(4,128)S(1)}, f32[4,192]{1,0:T(4,128)S(1)}, u32[]{:S(2)}, u32[]{:S(2)}) collective-permute-start(f32[4,192]{1,0:T(4,128)S(1)} %pad_maximum_fusion.4), channel_id=1, source_target_pairs={{0,128},{32,160},{64,192},{96,224},{128,0},{160,32},{192,64},{224,... | collective-permute-start | bytes 9224 | tf_op jit(solution)/shard_map/ppermute | solution.py:228
  190.2 2.0 %collective-permute-done.15 = f32[4,192]{1,0:T(4,128)S(1)} collective-permute-done((f32[4,192]{1,0:T(4,128)S(1)}, f32[4,192]{1,0:T(4,128)S(1)}, u32[]{:S(2)}, u32[]{:S(2)}) %collective-permute-start.15) | collective-permute-done | bytes 3104 | tf_op jit(solution)/shard_map/ppermute | solution.py:228
  192.3 0.6 divide_subtract_fusion
  (80 shorter events, 2.0 us)
Async XLA Ops:
  7.2 72.9 %copy-start = (bf16[256,2048]{1,0:T(8,128)(2,1)S(1)}, bf16[256,2048]{1,0:T(8,128)(2,1)}, u32[]{:S(2)}) copy-start(bf16[256,2048]{1,0:T(8,128)(2,1)} %param.16) | copy-start | bytes 3145732
  7.2 5.3 %copy-start.1 = (bf16[192,2048]{1,0:T(8,128)(2,1)S(1)}, bf16[192,2048]{1,0:T(8,128)(2,1)}, u32[]{:S(2)}) copy-start(bf16[192,2048]{1,0:T(8,128)(2,1)} %param.11) | copy-start | bytes 2359300
  7.2 5.6 %copy-start.7 = (f32[2048]{0:T(1024)S(1)}, f32[2048]{0:T(1024)}, u32[]{:S(2)}) copy-start(f32[2048]{0:T(1024)} %param.12) | copy-start | bytes 24580
  7.2 5.6 %copy-start.5 = (bf16[2048,64]{0,1:T(8,128)(2,1)S(1)}, bf16[2048,64]{0,1:T(8,128)(2,1)}, u32[]{:S(2)}) copy-start(bf16[2048,64]{0,1:T(8,128)(2,1)} %param.14) | copy-start | bytes 786436
  7.2 6.0 %copy-start.6 = (bf16[2048,64]{0,1:T(8,128)(2,1)S(1)}, bf16[2048,64]{0,1:T(8,128)(2,1)}, u32[]{:S(2)}) copy-start(bf16[2048,64]{0,1:T(8,128)(2,1)} %param.15) | copy-start | bytes 786436
  7.2 112.8 %all-gather.3.cloned.1.call-start = ((), (), s32[]{:S(2)}) async-start(), calls=%async_computation | async-start | bytes 8146944 | tf_op jit(solution)/shard_map/all_gather | solution.py:192
  10.7 145.8 %all-gather.5.cloned.1.call-start = ((), (), s32[]{:S(2)}) async-start(), calls=%async_computation.1 | async-start | bytes 3932160 | tf_op jit(solution)/shard_map/all_gather | solution.py:186
  13.9 8.2 %collective-permute-start = (bf16[1,192,128]{1,2,0:T(8,128)(2,1)S(1)}, bf16[1,192,128]{1,2,0:T(8,128)(2,1)S(1)}, u32[]{:S(2)}, u32[]{:S(2)}) collective-permute-start(bf16[1,192,128]{1,2,0:T(8,128)(2,1)S(1)} %maximum_bitcast_fusion.1), channel_id=1, source_target_pairs={{0,4},{4,8},{8,12},{12,16},{16,20},{20,24},{24,28},{28,0},{1,5},{5... | collective-permute-start | bytes 147464 | tf_op jit(solution)/shard_map/ppermute | solution.py:113
  22.1 12.7 %collective-permute-start.1 = (bf16[2,192,128]{1,2,0:T(8,128)(2,1)S(1)}, bf16[2,192,128]{1,2,0:T(8,128)(2,1)S(1)}, u32[]{:S(2)}, u32[]{:S(2)}) collective-permute-start(bf16[2,192,128]{1,2,0:T(8,128)(2,1)S(1)} %pad_maximum_fusion), channel_id=1, source_target_pairs={{0,8},{4,12},{8,16},{12,20},{16,24},{20,28},{24,0},{28,4},{1,9},{5... | collective-permute-start | bytes 294920 | tf_op jit(solution)/shard_map/ppermute | solution.py:113
  34.8 7.0 %collective-permute-start.2 = (bf16[1,192,128]{1,2,0:T(8,128)(2,1)S(1)}, bf16[1,192,128]{1,2,0:T(8,128)(2,1)S(1)}, u32[]{:S(2)}, u32[]{:S(2)}) collective-permute-start(bf16[1,192,128]{1,2,0:T(8,128)(2,1)S(1)} %slice.243), channel_id=1, source_target_pairs={{0,4},{4,8},{8,12},{12,16},{16,20},{20,24},{24,28},{28,0},{1,5},{5... | collective-permute-start | bytes 147464 | tf_op jit(solution)/shard_map/ppermute | solution.py:113
  41.9 10.7 %collective-permute-start.3 = (bf16[5,1,192,128]{2,3,0,1:T(8,128)(2,1)S(1)}, bf16[5,1,192,128]{2,3,0,1:T(8,128)(2,1)S(1)}, u32[]{:S(2)}, u32[]{:S(2)}) collective-permute-start(bf16[5,1,192,128]{2,3,0,1:T(8,128)(2,1)S(1)} %maximum_bitcast_fusion), channel_id=1, source_target_pairs={{0,1},{1,0},{2,3},{3,2},{4,5},{5,4},{6,7},{7,6},{8,9},{9,8},{10,11... | collective-permute-start | bytes 737288 | tf_op jit(solution)/shard_map/ppermute | solution.py:118
  53.8 10.5 %collective-permute-start.4 = (bf16[5,2,192,128]{3,2,1,0:T(8,128)(2,1)}, bf16[5,2,192,128]{3,2,1,0:T(8,128)(2,1)S(1)}, u32[]{:S(2)}, u32[]{:S(2)}) collective-permute-start(bf16[5,2,192,128]{3,2,1,0:T(8,128)(2,1)} %copy.83), channel_id=1, source_target_pairs={{0,2},{1,3},{2,0},{3,1},{4,6},{5,7},{6,4},{7,5},{8,10},{9,11},{10,... | collective-permute-start | bytes 1474568 | tf_op jit(solution)/shard_map/ppermute | solution.py:118
  68.6 4.1 %copy-start.2 = (pred[192,3840]{1,0:T(8,128)(4,1)S(1)}, pred[192,3840]{1,0:T(8,128)(4,1)}, u32[]{:S(2)}) copy-start(pred[192,3840]{1,0:T(8,128)(4,1)} %compare_and_fusion) | copy-start | bytes 2211844
  72.7 3.8 %copy-start.3 = (bf16[5,4,192,128]{3,2,1,0:T(8,128)(2,1)S(1)}, bf16[5,4,192,128]{3,2,1,0:T(8,128)(2,1)}, u32[]{:S(2)}) copy-start(bf16[5,4,192,128]{3,2,1,0:T(8,128)(2,1)} %copy.86) | copy-start | bytes 2949124
  80.6 23.1 %copy-start.4 = (f32[2048]{0:T(1024)S(1)}, f32[2048]{0:T(1024)}, u32[]{:S(2)}) copy-start(f32[2048]{0:T(1024)} %param.17) | copy-start | bytes 24580
  80.6 2.5 %collective-permute-start.5 = (f32[2,2,24,2048]{3,2,1,0:T(8,128)S(1)}, f32[2,2,24,2048]{3,2,1,0:T(8,128)}, u32[]{:S(2)}, u32[]{:S(2)}) collective-permute-start(f32[2,2,24,2048]{3,2,1,0:T(8,128)S(1)} %select_bitcast_fusion), channel_id=1, source_target_pairs={{0,32},{32,0},{64,96},{96,64},{128,160},{160,128},{192,224},{224,1... | collective-permute-start | bytes 2359304 | tf_op jit(solution)/shard_map/ppermute | solution.py:174
  84.4 11.2 %collective-permute-start.6 = (f32[2,24,2048]{2,1,0:T(8,128)S(1)}, f32[2,24,2048]{2,1,0:T(8,128)S(1)}, u32[]{:S(2)}, u32[]{:S(2)}) collective-permute-start(f32[2,24,2048]{2,1,0:T(8,128)S(1)} %select_bitcast_fusion.1), channel_id=1, source_target_pairs={{0,64},{32,96},{64,0},{96,32},{128,192},{160,224},{192,128},{224,1... | collective-permute-start | bytes 1179656 | tf_op jit(solution)/shard_map/ppermute | solution.py:174
  95.8 7.8 %collective-permute-start.7 = (f32[24,2048]{1,0:T(8,128)S(1)}, f32[24,2048]{1,0:T(8,128)S(1)}, u32[]{:S(2)}, u32[]{:S(2)}) collective-permute-start(f32[24,2048]{1,0:T(8,128)S(1)} %select_bitcast_fusion.2), channel_id=1, source_target_pairs={{0,128},{32,160},{64,192},{96,224},{128,0},{160,32},{192,64},{224,... | collective-permute-start | bytes 589832 | tf_op jit(solution)/shard_map/ppermute | solution.py:174
  103.8 6.2 %collective-permute-start.8 = (bf16[1,24,2048]{2,1,0:T(8,128)(2,1)S(1)}, bf16[1,24,2048]{2,1,0:T(8,128)(2,1)S(1)}, u32[]{:S(2)}, u32[]{:S(2)}) collective-permute-start(bf16[1,24,2048]{2,1,0:T(8,128)(2,1)S(1)} %get-tuple-element.18), channel_id=1, source_target_pairs={{0,128},{32,160},{64,192},{96,224},{128,0},{160,32},{192,64},{224,... | collective-permute-start | bytes 294920 | tf_op jit(solution)/shard_map/ppermute | solution.py:182
  110.1 5.8 %collective-permute-start.9 = (bf16[2,24,2048]{2,1,0:T(8,128)(2,1)S(1)}, bf16[2,24,2048]{2,1,0:T(8,128)(2,1)S(1)}, u32[]{:S(2)}, u32[]{:S(2)}) collective-permute-start(bf16[2,24,2048]{2,1,0:T(8,128)(2,1)S(1)} %maximum_select_fusion.5), channel_id=1, source_target_pairs={{0,64},{32,96},{64,0},{96,32},{128,192},{160,224},{192,128},{224,1... | collective-permute-start | bytes 589832 | tf_op jit(solution)/shard_map/ppermute | solution.py:182
  115.9 2.0 %collective-permute-start.10 = (bf16[4,24,2048]{2,1,0:T(8,128)(2,1)S(1)}, bf16[4,24,2048]{2,1,0:T(8,128)(2,1)S(1)}, u32[]{:S(2)}, u32[]{:S(2)}) collective-permute-start(bf16[4,24,2048]{2,1,0:T(8,128)(2,1)S(1)} %bitcast.138), channel_id=1, source_target_pairs={{0,32},{32,0},{64,96},{96,64},{128,160},{160,128},{192,224},{224,1... | collective-permute-start | bytes 1179656 | tf_op jit(solution)/shard_map/ppermute | solution.py:182
  172.8 5.2 %collective-permute-start.11 = (f32[4,2,192]{2,0,1:T(4,128)S(1)}, f32[4,2,192]{2,0,1:T(4,128)S(1)}, u32[]{:S(2)}, u32[]{:S(2)}) collective-permute-start(f32[4,2,192]{2,0,1:T(4,128)S(1)} %constant_dynamic-slice_fusion.1), channel_id=1, source_target_pairs={{0,2},{1,3},{2,0},{3,1},{4,6},{5,7},{6,4},{7,5},{8,10},{9,11},{10,... | collective-permute-start | bytes 18440 | tf_op jit(solution)/shard_map/ppermute | solution.py:215
  178.2 3.7 %collective-permute-start.12 = (f32[4,1,192]{2,0,1:T(4,128)S(1)}, f32[4,1,192]{2,0,1:T(4,128)S(1)}, u32[]{:S(2)}, u32[]{:S(2)}) collective-permute-start(f32[4,1,192]{2,0,1:T(4,128)S(1)} %constant_dynamic-slice_fusion), channel_id=1, source_target_pairs={{0,1},{1,0},{2,3},{3,2},{4,5},{5,4},{6,7},{7,6},{8,9},{9,8},{10,11... | collective-permute-start | bytes 9224 | tf_op jit(solution)/shard_map/ppermute | solution.py:223
  182.0 1.3 collective-permute-start.13
  183.3 3.7 %collective-permute-start.14 = (f32[4,192]{1,0:T(4,128)S(1)}, f32[4,192]{1,0:T(4,128)S(1)}, u32[]{:S(2)}, u32[]{:S(2)}) collective-permute-start(f32[4,192]{1,0:T(4,128)S(1)} %pad_maximum_fusion.3), channel_id=1, source_target_pairs={{0,64},{32,96},{64,0},{96,32},{128,192},{160,224},{192,128},{224,1... | collective-permute-start | bytes 9224 | tf_op jit(solution)/shard_map/ppermute | solution.py:228
  187.1 5.2 %collective-permute-start.15 = (f32[4,192]{1,0:T(4,128)S(1)}, f32[4,192]{1,0:T(4,128)S(1)}, u32[]{:S(2)}, u32[]{:S(2)}) collective-permute-start(f32[4,192]{1,0:T(4,128)S(1)} %pad_maximum_fusion.4), channel_id=1, source_target_pairs={{0,128},{32,160},{64,192},{96,224},{128,0},{160,32},{192,64},{224,... | collective-permute-start | bytes 9224 | tf_op jit(solution)/shard_map/ppermute | solution.py:228
Sparse Core Ops, SparseCore 0:
  10.9 88.9 all-gather.2
  119.2 37.3 all-gather.4

commit v10 on v9

--- a/solution.py
+++ b/solution.py
@@ -176,14 +176,19 @@
     attn_part = blocks
     stream_part = lax.dynamic_slice_in_dim(stream, kv_index * chunk, chunk, 0)
     final_part = rms_norm(stream_part + RESID_SCALE * attn_part, final_gain).astype(jnp.bfloat16)
-    rows = final_part[None]
-    for bit in reversed(range(kv_bits)):
-        mine_low = (kv_index >> bit) % 2 == 0
-        got = lax.ppermute(rows, "kv", [(p, p ^ (1 << bit)) for p in range(kv_count)])
-        rows = jnp.where(mine_low, jnp.stack([rows, got], axis=1), jnp.stack([got, rows], axis=1))
-        rows = rows.reshape((rows.shape[0] * 2,) + rows.shape[2:])
-    final_in = rows.reshape(tok_rows, final_part.shape[1])
-    head_rows = lax.all_gather(final_in, "y", axis=0, tiled=True)
+    y_bits = y_count.bit_length() - 1
+    head_rows = final_part.reshape((1,) * (y_bits + kv_bits) + final_part.shape)
+    order = [("y", bit, y_index, y_count, y_bits - 1 - bit) for bit in range(y_bits)]
+    order += [("kv", bit, kv_index, kv_count, y_bits + kv_bits - 1 - bit) for bit in reversed(range(kv_bits))]
+    for name, bit, pos, count, axis in order:
+        mine_low = (pos >> bit) % 2 == 0
+        got = lax.ppermute(head_rows, name, [(p, p ^ (1 << bit)) for p in range(count)])
+        head_rows = jnp.where(
+            mine_low,
+            jnp.concatenate([head_rows, got], axis=axis),
+            jnp.concatenate([got, head_rows], axis=axis),
+        )
+    head_rows = head_rows.reshape(-1, final_part.shape[1])
     group_rows = head_rows.shape[0]
     padded_local = -(-vocab_local // 16) * 16
     head_pad = jnp.zeros((16 - 1, vocab_local), w_head.dtype)

time: 202 us -> 192 us (0.950)
  waiting for transfers between devices: 112 us -> 104 us
  starting transfers between devices: 22.2 us -> 16.4 us
  other arithmetic: 20.2 us -> 24.7 us
  matrix products: 21.7 us -> 24.1 us
    all_gather x1 -> x0, waiting for transfers between devices: 35.2 us -> none  [local(): head_rows = lax.all_gather(final_in, 'y', axis=0, tiled=True)]
    ppermute x3 -> x5, waiting for transfers between devices: 8.91 us -> 36.7 us  [local(): lax.ppermute(head_rows, name, [(p, p ^ 1 << bit) for p in range(count)])]
    ppermute x3, waiting for transfers between devices: 25.7 us -> 19.6 us  [local(): lax.ppermute(held[:need], 'z', [(p, (p + need) % z_count) for p in range(...]
    select_n x4 -> x5, other arithmetic: 0.22 us -> 4.23 us  [local(): jnp.where(mine_low, jnp.concatenate([head_rows, got], axis=axis), jnp.con...]
    ppermute x1, starting transfers between devices: 2.6 us -> 0.09 us  [local(): got = lax.ppermute(send, 'y', [(p, p ^ half) for p in range(y_count)])]
    ppermute x1, waiting for transfers between devices: 2.64 us -> 5.12 us  [local(): got = lax.ppermute(send, 'y', [(p, p ^ half) for p in range(y_count)])]
    ppermute x3 -> x5, starting transfers between devices: 5.05 us -> 4.99 us  [local(): lax.ppermute(head_rows, name, [(p, p ^ 1 << bit) for p in range(count)])]
  transfers between devices with their start and end apart: 18 -> 19, of which waited for: 17 -> 18; matrix products, arithmetic and copies ran while one was open for 15% -> 16% of each run, Pallas kernels for 0% -> 0%
where the time goes in v10:
time: 192 us; the launch traced here: 191 us
  waiting for transfers between devices  104 us (54%)
  other arithmetic  24.7 us (13%)
  matrix products  24.1 us (13%)
  starting transfers between devices  16.4 us (9%)
  between operations  14.7 us (8%)
  local copies, waits for them, and re-layouts  7.92 us (4%)
    ppermute x5, waiting for transfers between devices, local(): lax.ppermute(head_rows, name, [(p, p ^ 1 << bit) for p in range(count)])  36.7 us
    ppermute x3, waiting for transfers between devices, local(): lax.ppermute(held[:need], 'z', [(p, (p + need) % z_count) for p in range(...  19.6 us
    ppermute x2, waiting for transfers between devices, local(): got = lax.ppermute(held, 'y', [(p, p ^ 1 << bit) for p in range(y_count)])  16.5 us
    ppermute x3, waiting for transfers between devices, local(): got = lax.ppermute(send, 'kv', [(p, p ^ 1 << bit) for p in range(kv_count)])  15.4 us
    dot_general x1, matrix products, local(): jnp.dot(head_rows, head_cols, preferred_element_type=jnp.float32)  11.2 us
    ppermute x3, waiting for transfers between devices, local(): got = lax.ppermute(merged, 'kv', [(p, p ^ step) for p in range(kv_count)])  6.7 us
    ppermute x1, waiting for transfers between devices, local(): got = lax.ppermute(send, 'y', [(p, p ^ half) for p in range(y_count)])  5.12 us
    ppermute x5, starting transfers between devices, local(): lax.ppermute(head_rows, name, [(p, p ^ 1 << bit) for p in range(count)])  4.99 us
  transfers between devices with their start and end apart: 19, of which 18 were waited for; matrix products, arithmetic and copies ran while one was open for 16% of the time, Pallas kernels for 0%

profile of v10, /device:TPU:24, one launch (start us, length us, event | category | flops | bytes accessed | tf_op | source)
XLA Modules:
  0.0 191.4 jit_solution(16434051566893293069)
XLA Ops:
  7.3 0.9 copy.77
  8.2 0.1 reduce.3
  8.3 0.7 sub.118
  9.1 1.4 multiply_reduce_fusion.1
  10.5 1.6 convolution_bitcast_fusion
  12.1 1.6 convolution_convert_fusion
  13.8 0.2 fusion.42
  14.0 2.0 %collective-permute-start = (bf16[1,192,128]{1,2,0:T(8,128)(2,1)S(1)}, bf16[1,192,128]{1,2,0:T(8,128)(2,1)S(1)}, u32[]{:S(2)}, u32[]{:S(2)}) collective-permute-start(bf16[1,192,128]{1,2,0:T(8,128)(2,1)S(1)} %maximum_bitcast_fusion.2), channel_id=1, source_target_pairs={{0,4},{4,8},{8,12},{12,16},{16,20},{20,24},{24,28},{28,0},{1,5},{5... | collective-permute-start | bytes 147464 | tf_op jit(solution)/shard_map/ppermute | solution.py:113
  16.2 0.7 concatenate.304
  16.9 1.0 pad.4
  18.0 4.3 %collective-permute-done = bf16[1,192,128]{1,2,0:T(8,128)(2,1)S(1)} collective-permute-done((bf16[1,192,128]{1,2,0:T(8,128)(2,1)S(1)}, bf16[1,192,128]{1,2,0:T(8,128)(2,1)S(1)}, u32[]{:S(2)}, u32[]{:S(2)}) %collective-permute-start) | collective-permute-done | bytes 49184 | tf_op jit(solution)/shard_map/ppermute | solution.py:113
  22.3 8.7 %collective-permute-done.1 = bf16[2,192,128]{1,2,0:T(8,128)(2,1)S(1)} collective-permute-done((bf16[2,192,128]{1,2,0:T(8,128)(2,1)S(1)}, bf16[2,192,128]{1,2,0:T(8,128)(2,1)S(1)}, u32[]{:S(2)}, u32[]{:S(2)}) %collective-permute-start.1) | collective-permute-done | bytes 98336 | tf_op jit(solution)/shard_map/ppermute | solution.py:113
  31.1 6.7 %collective-permute-done.2 = bf16[1,192,128]{1,2,0:T(8,128)(2,1)S(1)} collective-permute-done((bf16[1,192,128]{1,2,0:T(8,128)(2,1)S(1)}, bf16[1,192,128]{1,2,0:T(8,128)(2,1)S(1)}, u32[]{:S(2)}, u32[]{:S(2)}) %collective-permute-start.2) | collective-permute-done | bytes 49184 | tf_op jit(solution)/shard_map/ppermute | solution.py:113
  37.9 0.8 collective-permute-start.3
  38.7 1.5 compare_and_fusion
  40.2 0.2 multiply_cosine_fusion
  40.4 7.9 %collective-permute-done.3 = bf16[5,1,192,128]{2,3,0,1:T(8,128)(2,1)S(1)} collective-permute-done((bf16[5,1,192,128]{2,3,0,1:T(8,128)(2,1)S(1)}, bf16[5,1,192,128]{2,3,0,1:T(8,128)(2,1)S(1)}, u32[]{:S(2)}, u32[]{:S(2)}) %collective-permute-start.3) | collective-permute-done | bytes 245792 | tf_op jit(solution)/shard_map/ppermute | solution.py:118
  48.4 0.2 maximum_select_fusion.5
  48.6 1.0 copy.78
  49.6 1.9 fusion.70
  51.5 8.6 %collective-permute-done.4 = bf16[5,2,192,128]{3,2,1,0:T(8,128)(2,1)S(1)} collective-permute-done((bf16[5,2,192,128]{3,2,1,0:T(8,128)(2,1)}, bf16[5,2,192,128]{3,2,1,0:T(8,128)(2,1)S(1)}, u32[]{:S(2)}, u32[]{:S(2)}) %collective-permute-start.4) | collective-permute-done | bytes 491552 | tf_op jit(solution)/shard_map/ppermute | solution.py:118
  60.1 1.1 copy.79
  61.3 1.8 maximum_select_fusion.2
  63.0 1.4 copy.81
  64.5 4.1 %fusion = (f32[4,192]{1,0:T(4,128)S(1)}, f32[3840,192,4]{0,1,2:T(8,128)S(1)}) fusion(pred[192,3840]{1,0:T(8,128)(4,1)} %compare_and_fusion, bf16[192,4,32]{0,2,1:T(8,128)(2,1)S(1)} %get-tuple-element.19, bf16[192,4,32]{0,2,1:T(8,128)(2,1)S(1)} %get-tuple-element.18, bf16[3840,128]{1,0:T(8,128)(2,1)} %bitcast.162), kind=kOutput, calls=%fused_computation.2 | convolution fusion | flops 386530560 | bytes 13618176 | tf_op jit(solution)/shard_map/tkgd,skd->kgts/dot_general | solution.py:132
  68.6 3.7 %fusion.1 = f32[4,192]{1,0:T(4,128)S(1)} fusion(f32[3840,192,4]{0,1,2:T(8,128)S(1)} %get-tuple-element.57, f32[4,192]{1,0:T(4,128)S(1)} %broadcast_maximum_fusion, pred[192,3840]{1,0:T(8,128)(4,1)S(1)} %copy-done.2), kind=kLoop, calls=%fused_computation.3 | loop fusion | flops 14744832 | bytes 12539904 | tf_op jit(solution)/shard_map/reduce_sum | solution.py:142
  72.3 3.3 %fusion.16 = bf16[192,1,4,64]{0,3,2,1:T(8,128)(2,1)S(1)} fusion(f32[3840,192,4]{0,1,2:T(8,128)S(1)} %get-tuple-element.57, f32[4,192]{1,0:T(4,128)S(1)} %broadcast_maximum_fusion, pred[192,3840]{1,0:T(8,128)(4,1)S(1)} %copy-done.2, bf16[3840,128]{1,0:T(8,128)(2,1)S(1)} %bitcast.163, f32[4,192]{1,0:T(4,128)S(1)} %fusion.1), kind=kOutput, calls=%fused_computation.26 | convolution fusion | flops 392331264 | bytes 13621248 | tf_op jit(solution)/shard_map/kgts,skd->kgtd/dot_general | solution.py:143
  75.6 0.2 copy.85
  75.8 0.2 convert_element_type.57
  76.0 0.4 fusion.19
  76.5 0.1 collective-permute-start.5
  76.6 2.4 %collective-permute-done.5 = f32[2,2,24,2048]{3,2,1,0:T(8,128)} collective-permute-done((f32[2,2,24,2048]{3,2,1,0:T(8,128)S(1)}, f32[2,2,24,2048]{3,2,1,0:T(8,128)}, u32[]{:S(2)}, u32[]{:S(2)}) %collective-permute-start.5) | collective-permute-done | bytes 786464 | tf_op jit(solution)/shard_map/ppermute | solution.py:174
  79.0 1.3 fusion.24
  80.3 1.6 collective-permute-start.6
  81.9 9.7 %collective-permute-done.6 = f32[2,24,2048]{2,1,0:T(8,128)S(1)} collective-permute-done((f32[2,24,2048]{2,1,0:T(8,128)S(1)}, f32[2,24,2048]{2,1,0:T(8,128)S(1)}, u32[]{:S(2)}, u32[]{:S(2)}) %collective-permute-start.6) | collective-permute-done | bytes 393248 | tf_op jit(solution)/shard_map/ppermute | solution.py:174
  91.7 3.2 %collective-permute-start.7 = (f32[24,2048]{1,0:T(8,128)S(1)}, f32[24,2048]{1,0:T(8,128)S(1)}, u32[]{:S(2)}, u32[]{:S(2)}) collective-permute-start(f32[24,2048]{1,0:T(8,128)S(1)} %select_bitcast_fusion.2), channel_id=1, source_target_pairs={{0,128},{32,160},{64,192},{96,224},{128,0},{160,32},{192,64},{224,... | collective-permute-start | bytes 589832 | tf_op jit(solution)/shard_map/ppermute | solution.py:174
  94.8 1.3 convert_element_type.49
  96.1 3.3 %collective-permute-done.7 = f32[24,2048]{1,0:T(8,128)S(1)} collective-permute-done((f32[24,2048]{1,0:T(8,128)S(1)}, f32[24,2048]{1,0:T(8,128)S(1)}, u32[]{:S(2)}, u32[]{:S(2)}) %collective-permute-start.7) | collective-permute-done | bytes 196640 | tf_op jit(solution)/shard_map/ppermute | solution.py:174
  99.5 0.2 multiply_reduce_fusion.2
  99.8 5.6 %collective-permute-done.8 = bf16[1,1,1,1,1,24,2048]{6,5,4,3,2,1,0:T(8,128)(2,1)S(1)} collective-permute-done((bf16[1,1,1,1,1,24,2048]{6,5,4,3,2,1,0:T(8,128)(2,1)S(1)}, bf16[1,1,1,1,1,24,2048]{6,5,4,3,2,1,0:T(8,128)(2,1)S(1)}, u32[]{:S(2)}, u32[]{:S(2)}) %collective-permute-start.8) | collective-permute-done | bytes 98336 | tf_op jit(solution)/shard_map/ppermute | solution.py:185
  105.4 0.1 collective-permute-start.9
  105.6 7.1 %collective-permute-done.9 = bf16[1,2,1,1,1,24,2048]{6,5,4,3,2,1,0:T(8,128)(2,1)S(1)} collective-permute-done((bf16[1,2,1,1,1,24,2048]{6,5,4,3,2,1,0:T(8,128)(2,1)S(1)}, bf16[1,2,1,1,1,24,2048]{6,5,4,3,2,1,0:T(8,128)(2,1)S(1)}, u32[]{:S(2)}, u32[]{:S(2)}) %collective-permute-start.9) | collective-permute-done | bytes 196640 | tf_op jit(solution)/shard_map/ppermute | solution.py:185
  112.7 3.3 %collective-permute-start.10 = (bf16[2,2,1,1,1,24,2048]{6,5,4,3,2,1,0:T(8,128)(2,1)S(1)}, bf16[2,2,1,1,1,24,2048]{6,5,4,3,2,1,0:T(8,128)(2,1)S(1)}, u32[]{:S(2)}, u32[]{:S(2)}) collective-permute-start(bf16[2,2,1,1,1,24,2048]{6,5,4,3,2,1,0:T(8,128)(2,1)S(1)} %fusion.25), channel_id=1, source_target_pairs={{0,128},{32,160},{64,192},{96,224},{128,0},{160,32},{192,64},{224,... | collective-permute-start | bytes 1179656 | tf_op jit(solution)/shard_map/ppermute | solution.py:185
  116.1 7.6 %collective-permute-done.10 = bf16[2,2,1,1,1,24,2048]{6,5,4,3,2,1,0:T(8,128)(2,1)S(1)} collective-permute-done((bf16[2,2,1,1,1,24,2048]{6,5,4,3,2,1,0:T(8,128)(2,1)S(1)}, bf16[2,2,1,1,1,24,2048]{6,5,4,3,2,1,0:T(8,128)(2,1)S(1)}, u32[]{:S(2)}, u32[]{:S(2)}) %collective-permute-start.10) | collective-permute-done | bytes 393248 | tf_op jit(solution)/shard_map/ppermute | solution.py:185
  123.7 0.3 maximum_select_fusion.4
  124.0 1.4 collective-permute-start.11
  125.5 13.9 %collective-permute-done.11 = bf16[2,2,2,1,1,24,2048]{6,5,4,3,2,1,0:T(8,128)(2,1)S(1)} collective-permute-done((bf16[2,2,2,1,1,24,2048]{6,5,4,3,2,1,0:T(8,128)(2,1)S(1)}, bf16[2,2,2,1,1,24,2048]{6,5,4,3,2,1,0:T(8,128)(2,1)S(1)}, u32[]{:S(2)}, u32[]{:S(2)}) %collective-permute-start.11) | collective-permute-done | bytes 786464 | tf_op jit(solution)/shard_map/ppermute | solution.py:185
  139.3 0.1 maximum_select_fusion.1
  139.5 0.1 collective-permute-start.12
  139.8 0.8 dynamic_slice.19
  140.6 2.5 %collective-permute-done.12 = bf16[2,2,2,2,1,24,2048]{6,5,4,3,2,1,0:T(8,128)(2,1)} collective-permute-done((bf16[2,2,2,2,1,24,2048]{6,5,4,3,2,1,0:T(8,128)(2,1)S(1)}, bf16[2,2,2,2,1,24,2048]{6,5,4,3,2,1,0:T(8,128)(2,1)}, u32[]{:S(2)}, u32[]{:S(2)}) %collective-permute-start.12) | collective-permute-done | bytes 1572896 | tf_op jit(solution)/shard_map/ppermute | solution.py:185
  143.1 3.7 %maximum_select_fusion = bf16[2,2,2,2,2,24,2048]{6,5,4,3,2,1,0:T(8,128)(2,1)} fusion(bf16[2,2,2,2,1,24,2048]{6,5,4,3,2,1,0:T(8,128)(2,1)} %collective-permute-done.12, bf16[2,2,2,2,1,24,2048]{6,5,4,3,2,1,0:T(8,128)(2,1)S(1)} %maximum_select_fusion.1, pred[]{:T(512)S(6)} %eq.79), kind=kLoop, calls=%fused_computation.16 | loop fusion | flops 4718592 | bytes 6291457 | tf_op jit(solution)/shard_map/jit(_where)/select_n | solution.py:186
  146.8 1.3 compare_reduce_fusion
  148.2 11.2 %select_reduce_fusion.1 = (f32[768]{0:T(1024)S(1)}, f32[768,1664]{1,0:T(8,128)}) fusion(pred[1664]{0:T(1024)(128)(4,1)S(1)} %compare_reduce_fusion, bf16[768,2048]{1,0:T(8,128)(2,1)} %bitcast.159, bf16[2064,1664]{0,1:T(8,128)(2,1)} %all-gather.2.cloned.1.call-done), kind=kOutput, calls=%fused_computation.15 | convolution fusion | flops 5238324224 | bytes 15078016 | tf_op jit(solution)/shard_map/dot_general | solution.py:207
  159.5 4.8 %fusion.9 = (f32[768]{0:T(1024)S(1)}, f32[768]{0:T(1024)S(1)}, f32[768]{0:T(1024)S(1)}) fusion(f32[768,1664]{1,0:T(8,128)} %get-tuple-element.59, f32[768]{0:T(1024)S(1)} %get-tuple-element.58, pred[1664]{0:T(1024)(128)(4,1)S(1)} %compare_reduce_fusion, s32[1664]{0:T(1024)S(1)} %select_n.482, s32[768]{0:T(1024)S(1)} %dynamic_slice.19), kind=kLoop, calls=%fused_computation.13 | loop fusion | flops 14055168 | bytes 5135488 | tf_op jit(solution)/shard_map/reduce_sum | solution.py:214
  164.6 5.1 %collective-permute-done.13 = f32[4,2,192]{2,0,1:T(4,128)S(1)} collective-permute-done((f32[4,2,192]{2,0,1:T(4,128)S(1)}, f32[4,2,192]{2,0,1:T(4,128)S(1)}, u32[]{:S(2)}, u32[]{:S(2)}) %collective-permute-start.13) | collective-permute-done | bytes 6176 | tf_op jit(solution)/shard_map/ppermute | solution.py:220
  169.8 0.1 collective-permute-start.14
  169.9 3.6 %collective-permute-done.14 = f32[4,1,192]{2,0,1:T(4,128)S(1)} collective-permute-done((f32[4,1,192]{2,0,1:T(4,128)S(1)}, f32[4,1,192]{2,0,1:T(4,128)S(1)}, u32[]{:S(2)}, u32[]{:S(2)}) %collective-permute-start.14) | collective-permute-done | bytes 3104 | tf_op jit(solution)/shard_map/ppermute | solution.py:228
  173.7 1.1 collective-permute-done.15
  174.9 1.4 collective-permute-start.16
  176.3 2.3 %collective-permute-done.16 = f32[4,192]{1,0:T(4,128)S(1)} collective-permute-done((f32[4,192]{1,0:T(4,128)S(1)}, f32[4,192]{1,0:T(4,128)S(1)}, u32[]{:S(2)}, u32[]{:S(2)}) %collective-permute-start.16) | collective-permute-done | bytes 3104 | tf_op jit(solution)/shard_map/ppermute | solution.py:233
  178.7 1.9 %collective-permute-start.17 = (f32[4,192]{1,0:T(4,128)S(1)}, f32[4,192]{1,0:T(4,128)S(1)}, u32[]{:S(2)}, u32[]{:S(2)}) collective-permute-start(f32[4,192]{1,0:T(4,128)S(1)} %pad_maximum_fusion.5), channel_id=1, source_target_pairs={{0,128},{32,160},{64,192},{96,224},{128,0},{160,32},{192,64},{224,... | collective-permute-start | bytes 9224 | tf_op jit(solution)/shard_map/ppermute | solution.py:233
  180.6 3.3 %collective-permute-done.17 = f32[4,192]{1,0:T(4,128)S(1)} collective-permute-done((f32[4,192]{1,0:T(4,128)S(1)}, f32[4,192]{1,0:T(4,128)S(1)}, u32[]{:S(2)}, u32[]{:S(2)}) %collective-permute-start.17) | collective-permute-done | bytes 3104 | tf_op jit(solution)/shard_map/ppermute | solution.py:233
  183.9 0.6 divide_subtract_fusion
  (83 shorter events, 2.4 us)
Async XLA Ops:
  7.2 68.8 %copy-start = (bf16[256,2048]{1,0:T(8,128)(2,1)S(1)}, bf16[256,2048]{1,0:T(8,128)(2,1)}, u32[]{:S(2)}) copy-start(bf16[256,2048]{1,0:T(8,128)(2,1)} %param.16) | copy-start | bytes 3145732
  7.2 8.8 %copy-start.7 = (s32[193]{0:T(256)S(1)}, s32[193]{0:T(256)}, u32[]{:S(2)}) copy-start(s32[193]{0:T(256)} %param.21) | copy-start | bytes 2320
  7.2 9.0 %copy-start.4 = (bf16[2048,193]{0,1:T(8,128)(2,1)S(1)}, bf16[2048,193]{0,1:T(8,128)(2,1)}, u32[]{:S(2)}) copy-start(bf16[2048,193]{0,1:T(8,128)(2,1)} %param.18) | copy-start | bytes 2371588
  7.2 139.6 %all-gather.2.cloned.1.call-start = ((), (), s32[]{:S(2)}) async-start(), calls=%async_computation | async-start | bytes 8146944 | tf_op jit(solution)/shard_map/all_gather | solution.py:197
  14.0 8.2 %collective-permute-start = (bf16[1,192,128]{1,2,0:T(8,128)(2,1)S(1)}, bf16[1,192,128]{1,2,0:T(8,128)(2,1)S(1)}, u32[]{:S(2)}, u32[]{:S(2)}) collective-permute-start(bf16[1,192,128]{1,2,0:T(8,128)(2,1)S(1)} %maximum_bitcast_fusion.2), channel_id=1, source_target_pairs={{0,4},{4,8},{8,12},{12,16},{16,20},{20,24},{24,28},{28,0},{1,5},{5... | collective-permute-start | bytes 147464 | tf_op jit(solution)/shard_map/ppermute | solution.py:113
  16.9 32.7 %copy-start.1 = (bf16[192,2048]{1,0:T(8,128)(2,1)S(1)}, bf16[192,2048]{1,0:T(8,128)(2,1)}, u32[]{:S(2)}) copy-start(bf16[192,2048]{1,0:T(8,128)(2,1)} %param.11) | copy-start | bytes 2359300
  16.9 32.7 %copy-start.6 = (f32[2048]{0:T(1024)S(1)}, f32[2048]{0:T(1024)}, u32[]{:S(2)}) copy-start(f32[2048]{0:T(1024)} %param.12) | copy-start | bytes 24580
  22.2 8.8 %collective-permute-start.1 = (bf16[2,192,128]{1,2,0:T(8,128)(2,1)S(1)}, bf16[2,192,128]{1,2,0:T(8,128)(2,1)S(1)}, u32[]{:S(2)}, u32[]{:S(2)}) collective-permute-start(bf16[2,192,128]{1,2,0:T(8,128)(2,1)S(1)} %pad_maximum_fusion.1), channel_id=1, source_target_pairs={{0,8},{4,12},{8,16},{12,20},{16,24},{20,28},{24,0},{28,4},{1,9},{5... | collective-permute-start | bytes 294920 | tf_op jit(solution)/shard_map/ppermute | solution.py:113
  31.1 6.8 %collective-permute-start.2 = (bf16[1,192,128]{1,2,0:T(8,128)(2,1)S(1)}, bf16[1,192,128]{1,2,0:T(8,128)(2,1)S(1)}, u32[]{:S(2)}, u32[]{:S(2)}) collective-permute-start(bf16[1,192,128]{1,2,0:T(8,128)(2,1)S(1)} %slice.243), channel_id=1, source_target_pairs={{0,4},{4,8},{8,12},{12,16},{16,20},{20,24},{24,28},{28,0},{1,5},{5... | collective-permute-start | bytes 147464 | tf_op jit(solution)/shard_map/ppermute | solution.py:113
  37.9 10.5 %collective-permute-start.3 = (bf16[5,1,192,128]{2,3,0,1:T(8,128)(2,1)S(1)}, bf16[5,1,192,128]{2,3,0,1:T(8,128)(2,1)S(1)}, u32[]{:S(2)}, u32[]{:S(2)}) collective-permute-start(bf16[5,1,192,128]{2,3,0,1:T(8,128)(2,1)S(1)} %maximum_bitcast_fusion.1), channel_id=1, source_target_pairs={{0,1},{1,0},{2,3},{3,2},{4,5},{5,4},{6,7},{7,6},{8,9},{9,8},{10,11... | collective-permute-start | bytes 737288 | tf_op jit(solution)/shard_map/ppermute | solution.py:118
  49.6 10.5 %collective-permute-start.4 = (bf16[5,2,192,128]{3,2,1,0:T(8,128)(2,1)}, bf16[5,2,192,128]{3,2,1,0:T(8,128)(2,1)S(1)}, u32[]{:S(2)}, u32[]{:S(2)}) collective-permute-start(bf16[5,2,192,128]{3,2,1,0:T(8,128)(2,1)} %copy.78), channel_id=1, source_target_pairs={{0,2},{1,3},{2,0},{3,1},{4,6},{5,7},{6,4},{7,5},{8,10},{9,11},{10,... | collective-permute-start | bytes 1474568 | tf_op jit(solution)/shard_map/ppermute | solution.py:118
  64.5 4.1 %copy-start.2 = (pred[192,3840]{1,0:T(8,128)(4,1)S(1)}, pred[192,3840]{1,0:T(8,128)(4,1)}, u32[]{:S(2)}) copy-start(pred[192,3840]{1,0:T(8,128)(4,1)} %compare_and_fusion) | copy-start | bytes 2211844
  68.6 3.8 %copy-start.3 = (bf16[5,4,192,128]{3,2,1,0:T(8,128)(2,1)S(1)}, bf16[5,4,192,128]{3,2,1,0:T(8,128)(2,1)}, u32[]{:S(2)}) copy-start(bf16[5,4,192,128]{3,2,1,0:T(8,128)(2,1)} %copy.81) | copy-start | bytes 2949124
  76.5 2.5 %collective-permute-start.5 = (f32[2,2,24,2048]{3,2,1,0:T(8,128)S(1)}, f32[2,2,24,2048]{3,2,1,0:T(8,128)}, u32[]{:S(2)}, u32[]{:S(2)}) collective-permute-start(f32[2,2,24,2048]{3,2,1,0:T(8,128)S(1)} %select_bitcast_fusion), channel_id=1, source_target_pairs={{0,32},{32,0},{64,96},{96,64},{128,160},{160,128},{192,224},{224,1... | collective-permute-start | bytes 2359304 | tf_op jit(solution)/shard_map/ppermute | solution.py:174
  80.2 19.4 %copy-start.5 = (f32[2048]{0:T(1024)S(1)}, f32[2048]{0:T(1024)}, u32[]{:S(2)}) copy-start(f32[2048]{0:T(1024)} %param.17) | copy-start | bytes 24580
  80.3 11.3 %collective-permute-start.6 = (f32[2,24,2048]{2,1,0:T(8,128)S(1)}, f32[2,24,2048]{2,1,0:T(8,128)S(1)}, u32[]{:S(2)}, u32[]{:S(2)}) collective-permute-start(f32[2,24,2048]{2,1,0:T(8,128)S(1)} %select_bitcast_fusion.1), channel_id=1, source_target_pairs={{0,64},{32,96},{64,0},{96,32},{128,192},{160,224},{192,128},{224,1... | collective-permute-start | bytes 1179656 | tf_op jit(solution)/shard_map/ppermute | solution.py:174
  91.7 7.8 %collective-permute-start.7 = (f32[24,2048]{1,0:T(8,128)S(1)}, f32[24,2048]{1,0:T(8,128)S(1)}, u32[]{:S(2)}, u32[]{:S(2)}) collective-permute-start(f32[24,2048]{1,0:T(8,128)S(1)} %select_bitcast_fusion.2), channel_id=1, source_target_pairs={{0,128},{32,160},{64,192},{96,224},{128,0},{160,32},{192,64},{224,... | collective-permute-start | bytes 589832 | tf_op jit(solution)/shard_map/ppermute | solution.py:174
  99.7 5.7 %collective-permute-start.8 = (bf16[1,1,1,1,1,24,2048]{6,5,4,3,2,1,0:T(8,128)(2,1)S(1)}, bf16[1,1,1,1,1,24,2048]{6,5,4,3,2,1,0:T(8,128)(2,1)S(1)}, u32[]{:S(2)}, u32[]{:S(2)}) collective-permute-start(bf16[1,1,1,1,1,24,2048]{6,5,4,3,2,1,0:T(8,128)(2,1)S(1)} %get-tuple-element.20), channel_id=1, source_target_pairs={{0,1},{1,0},{2,3},{3,2},{4,5},{5,4},{6,7},{7,6},{8,9},{9,8},{10,11... | collective-permute-start | bytes 294920 | tf_op jit(solution)/shard_map/ppermute | solution.py:185
  105.4 7.3 %collective-permute-start.9 = (bf16[1,2,1,1,1,24,2048]{6,5,4,3,2,1,0:T(8,128)(2,1)S(1)}, bf16[1,2,1,1,1,24,2048]{6,5,4,3,2,1,0:T(8,128)(2,1)S(1)}, u32[]{:S(2)}, u32[]{:S(2)}) collective-permute-start(bf16[1,2,1,1,1,24,2048]{6,5,4,3,2,1,0:T(8,128)(2,1)S(1)} %maximum_select_fusion.8), channel_id=1, source_target_pairs={{0,2},{1,3},{2,0},{3,1},{4,6},{5,7},{6,4},{7,5},{8,10},{9,11},{10,... | collective-permute-start | bytes 589832 | tf_op jit(solution)/shard_map/ppermute | solution.py:185
  112.7 11.0 %collective-permute-start.10 = (bf16[2,2,1,1,1,24,2048]{6,5,4,3,2,1,0:T(8,128)(2,1)S(1)}, bf16[2,2,1,1,1,24,2048]{6,5,4,3,2,1,0:T(8,128)(2,1)S(1)}, u32[]{:S(2)}, u32[]{:S(2)}) collective-permute-start(bf16[2,2,1,1,1,24,2048]{6,5,4,3,2,1,0:T(8,128)(2,1)S(1)} %fusion.25), channel_id=1, source_target_pairs={{0,128},{32,160},{64,192},{96,224},{128,0},{160,32},{192,64},{224,... | collective-permute-start | bytes 1179656 | tf_op jit(solution)/shard_map/ppermute | solution.py:185
  124.0 15.4 %collective-permute-start.11 = (bf16[2,2,2,1,1,24,2048]{6,5,4,3,2,1,0:T(8,128)(2,1)S(1)}, bf16[2,2,2,1,1,24,2048]{6,5,4,3,2,1,0:T(8,128)(2,1)S(1)}, u32[]{:S(2)}, u32[]{:S(2)}) collective-permute-start(bf16[2,2,2,1,1,24,2048]{6,5,4,3,2,1,0:T(8,128)(2,1)S(1)} %maximum_select_fusion.4), channel_id=1, source_target_pairs={{0,64},{32,96},{64,0},{96,32},{128,192},{160,224},{192,128},{224,1... | collective-permute-start | bytes 2359304 | tf_op jit(solution)/shard_map/ppermute | solution.py:185
  139.5 3.6 %collective-permute-start.12 = (bf16[2,2,2,2,1,24,2048]{6,5,4,3,2,1,0:T(8,128)(2,1)S(1)}, bf16[2,2,2,2,1,24,2048]{6,5,4,3,2,1,0:T(8,128)(2,1)}, u32[]{:S(2)}, u32[]{:S(2)}) collective-permute-start(bf16[2,2,2,2,1,24,2048]{6,5,4,3,2,1,0:T(8,128)(2,1)S(1)} %maximum_select_fusion.1), channel_id=1, source_target_pairs={{0,32},{32,0},{64,96},{96,64},{128,160},{160,128},{192,224},{224,1... | collective-permute-start | bytes 4718600 | tf_op jit(solution)/shard_map/ppermute | solution.py:185
  164.5 5.2 %collective-permute-start.13 = (f32[4,2,192]{2,0,1:T(4,128)S(1)}, f32[4,2,192]{2,0,1:T(4,128)S(1)}, u32[]{:S(2)}, u32[]{:S(2)}) collective-permute-start(f32[4,2,192]{2,0,1:T(4,128)S(1)} %constant_dynamic-slice_fusion.1), channel_id=1, source_target_pairs={{0,2},{1,3},{2,0},{3,1},{4,6},{5,7},{6,4},{7,5},{8,10},{9,11},{10,... | collective-permute-start | bytes 18440 | tf_op jit(solution)/shard_map/ppermute | solution.py:220
  169.8 3.7 %collective-permute-start.14 = (f32[4,1,192]{2,0,1:T(4,128)S(1)}, f32[4,1,192]{2,0,1:T(4,128)S(1)}, u32[]{:S(2)}, u32[]{:S(2)}) collective-permute-start(f32[4,1,192]{2,0,1:T(4,128)S(1)} %constant_dynamic-slice_fusion), channel_id=1, source_target_pairs={{0,1},{1,0},{2,3},{3,2},{4,5},{5,4},{6,7},{7,6},{8,9},{9,8},{10,11... | collective-permute-start | bytes 9224 | tf_op jit(solution)/shard_map/ppermute | solution.py:228
  173.6 1.3 collective-permute-start.15
  174.9 3.7 %collective-permute-start.16 = (f32[4,192]{1,0:T(4,128)S(1)}, f32[4,192]{1,0:T(4,128)S(1)}, u32[]{:S(2)}, u32[]{:S(2)}) collective-permute-start(f32[4,192]{1,0:T(4,128)S(1)} %pad_maximum_fusion.4), channel_id=1, source_target_pairs={{0,64},{32,96},{64,0},{96,32},{128,192},{160,224},{192,128},{224,1... | collective-permute-start | bytes 9224 | tf_op jit(solution)/shard_map/ppermute | solution.py:233
  178.7 5.2 %collective-permute-start.17 = (f32[4,192]{1,0:T(4,128)S(1)}, f32[4,192]{1,0:T(4,128)S(1)}, u32[]{:S(2)}, u32[]{:S(2)}) collective-permute-start(f32[4,192]{1,0:T(4,128)S(1)} %pad_maximum_fusion.5), channel_id=1, source_target_pairs={{0,128},{32,160},{64,192},{96,224},{128,0},{160,32},{192,64},{224,... | collective-permute-start | bytes 9224 | tf_op jit(solution)/shard_map/ppermute | solution.py:233
Sparse Core Ops, SparseCore 0:
  18.1 85.8 all-gather.1

commit v11 on v10

--- a/solution.py
+++ b/solution.py
@@ -194,11 +194,27 @@
     head_pad = jnp.zeros((16 - 1, vocab_local), w_head.dtype)
     head_ext = jnp.concatenate([w_head, vocab_mask.astype(w_head.dtype)[None, :], head_pad], axis=0)
     head_ext = jnp.pad(head_ext, ((0, 0), (0, padded_local - vocab_local)))
-    head_ext = lax.all_gather(head_ext, "z", axis=1, tiled=True)
+    ahead = head_ext
+    behind = head_ext
+    ring = [head_ext]
+    offsets = [0]
+    for step in range(1, z_count // 2):
+        ahead = lax.ppermute(ahead, "z", [(p, (p + 1) % z_count) for p in range(z_count)])
+        behind = lax.ppermute(behind, "z", [(p, (p - 1) % z_count) for p in range(z_count)])
+        ring += [ahead, behind]
+        offsets += [-step, step]
+    if z_count % 2 == 0 and z_count > 1:
+        split = 1024
+        top = lax.ppermute(ahead[:split], "z", [(p, (p + 1) % z_count) for p in range(z_count)])
+        bottom = lax.ppermute(behind[split:], "z", [(p, (p - 1) % z_count) for p in range(z_count)])
+        ring.append(jnp.concatenate([top, bottom], axis=0))
+        offsets.append(z_count // 2)
+    head_ext = jnp.concatenate(ring, axis=1)
+    ring_z = (z_index + jnp.array(offsets, dtype=jnp.int32)) % z_count
     head_cols = head_ext[: w_head.shape[0]]
     mask_cols = head_ext[w_head.shape[0]]
     live_mask = mask_cols == 1.0
-    shard_ids = kv_index * (z_count * y_count) + jnp.arange(z_count, dtype=jnp.int32) * y_count + y_index
+    shard_ids = kv_index * (z_count * y_count) + ring_z * y_count + y_index
     local_cols = jnp.arange(padded_local, dtype=jnp.int32)
     columns = jnp.where(
         local_cols[None, :] < vocab_local, shard_ids[:, None] * vocab_local + local_cols[None, :], -1

time: 192 us -> 197 us (1.026)
  starting transfers between devices: 16.4 us -> 31.2 us
  between operations: 14.7 us -> 1.23 us
  local copies, waits for them, and re-layouts: 7.92 us -> 18.4 us
  waiting for transfers between devices: 104 us -> 96.2 us
    ppermute x0 -> x8, waiting for transfers between devices: none -> 18.2 us  [the longest x1 7.3 us: local(): lax.ppermute(ahead[:split], 'z', [(p, (p + 1) % z_count) for p in range(z...]
    ppermute x5, waiting for transfers between devices: 36.7 us -> 20.9 us  [local(): lax.ppermute(head_rows, name, [(p, p ^ 1 << bit) for p in range(count)])]
    ppermute x0 -> x8, starting transfers between devices: none -> 13.6 us  [the longest x3 9.7 us: local(): lax.ppermute(behind, 'z', [(p, (p - 1) % z_count) for p in range(z_count)])]
    unnamed x16 -> x26, local copies, waits for them, and re-layouts: 0.04 us -> 8.43 us
    ppermute x3, waiting for transfers between devices: 15.4 us -> 8.04 us  [local(): got = lax.ppermute(send, 'kv', [(p, p ^ 1 << bit) for p in range(kv_count)])]
    select_n x5, other arithmetic: 4.23 us -> 0.87 us  [local(): jnp.where(mine_low, jnp.concatenate([head_rows, got], axis=axis), jnp.con...]
  transfers between devices with their start and end apart: 19 -> 26, of which waited for: 18 -> 19; matrix products, arithmetic and copies ran while one was open for 16% -> 12% of each run, Pallas kernels for 0% -> 0%
where the time goes in v11:
time: 197 us; the launch traced here: 195 us
  waiting for transfers between devices  96.2 us (49%)
  starting transfers between devices  31.2 us (16%)
  other arithmetic  24.7 us (13%)
  matrix products  23.6 us (12%)
  local copies, waits for them, and re-layouts  18.4 us (9%)
    ppermute x5, waiting for transfers between devices, local(): lax.ppermute(head_rows, name, [(p, p ^ 1 << bit) for p in range(count)])  20.9 us
    ppermute x3, waiting for transfers between devices, local(): lax.ppermute(held[:need], 'z', [(p, (p + need) % z_count) for p in range(...  20.3 us
    ppermute x2, waiting for transfers between devices, local(): got = lax.ppermute(held, 'y', [(p, p ^ 1 << bit) for p in range(y_count)])  15.5 us
    dot_general x1, matrix products, local(): jnp.dot(head_rows, head_cols, preferred_element_type=jnp.float32)  10.7 us
    ppermute x3, starting transfers between devices, local(): lax.ppermute(behind, 'z', [(p, (p - 1) % z_count) for p in range(z_count)])  9.7 us
    unnamed x26, local copies, waits for them, and re-layouts  8.43 us
    ppermute x3, waiting for transfers between devices, local(): got = lax.ppermute(send, 'kv', [(p, p ^ 1 << bit) for p in range(kv_count)])  8.04 us
    ppermute x1, waiting for transfers between devices, local(): lax.ppermute(ahead[:split], 'z', [(p, (p + 1) % z_count) for p in range(z...  7.3 us
  transfers between devices with their start and end apart: 26, of which 19 were waited for; matrix products, arithmetic and copies ran while one was open for 12% of the time, Pallas kernels for 0%

profile of v11, /device:TPU:24, one launch (start us, length us, event | category | flops | bytes accessed | tf_op | source)
XLA Modules:
  0.0 195.4 jit_solution(3622953254223195103)
XLA Ops:
  0.7 0.9 copy.78
  1.7 0.7 sub.118
  2.5 1.4 multiply_reduce_fusion.1
  3.9 1.6 convolution_bitcast_fusion
  5.5 1.6 convolution_convert_fusion
  7.4 2.0 %collective-permute-start.8 = (bf16[1,192,128]{1,2,0:T(8,128)(2,1)S(1)}, bf16[1,192,128]{1,2,0:T(8,128)(2,1)S(1)}, u32[]{:S(2)}, u32[]{:S(2)}) collective-permute-start(bf16[1,192,128]{1,2,0:T(8,128)(2,1)S(1)} %maximum_bitcast_fusion.2), channel_id=1, source_target_pairs={{0,4},{4,8},{8,12},{12,16},{16,20},{20,24},{24,28},{28,0},{1,5},{5... | collective-permute-start | bytes 147464 | tf_op jit(solution)/shard_map/ppermute | solution.py:113
  9.4 6.2 %collective-permute-done.8 = bf16[1,192,128]{1,2,0:T(8,128)(2,1)S(1)} collective-permute-done((bf16[1,192,128]{1,2,0:T(8,128)(2,1)S(1)}, bf16[1,192,128]{1,2,0:T(8,128)(2,1)S(1)}, u32[]{:S(2)}, u32[]{:S(2)}) %collective-permute-start.8) | collective-permute-done | bytes 49184 | tf_op jit(solution)/shard_map/ppermute | solution.py:113
  15.7 8.7 %collective-permute-done.9 = bf16[2,192,128]{1,2,0:T(8,128)(2,1)S(1)} collective-permute-done((bf16[2,192,128]{1,2,0:T(8,128)(2,1)S(1)}, bf16[2,192,128]{1,2,0:T(8,128)(2,1)S(1)}, u32[]{:S(2)}, u32[]{:S(2)}) %collective-permute-start.9) | collective-permute-done | bytes 98336 | tf_op jit(solution)/shard_map/ppermute | solution.py:113
  24.5 5.4 %collective-permute-done.10 = bf16[1,192,128]{1,2,0:T(8,128)(2,1)S(1)} collective-permute-done((bf16[1,192,128]{1,2,0:T(8,128)(2,1)S(1)}, bf16[1,192,128]{1,2,0:T(8,128)(2,1)S(1)}, u32[]{:S(2)}, u32[]{:S(2)}) %collective-permute-start.10) | collective-permute-done | bytes 49184 | tf_op jit(solution)/shard_map/ppermute | solution.py:113
  30.0 0.8 collective-permute-start.11
  30.8 1.5 compare_and_fusion
  32.6 7.7 %collective-permute-done.11 = bf16[5,1,192,128]{2,3,0,1:T(8,128)(2,1)S(1)} collective-permute-done((bf16[5,1,192,128]{2,3,0,1:T(8,128)(2,1)S(1)}, bf16[5,1,192,128]{2,3,0,1:T(8,128)(2,1)S(1)}, u32[]{:S(2)}, u32[]{:S(2)}) %collective-permute-start.11) | collective-permute-done | bytes 245792 | tf_op jit(solution)/shard_map/ppermute | solution.py:118
  41.1 1.8 fusion.75
  42.9 0.7 subtract_convert_fusion
  43.6 7.8 %collective-permute-done.12 = bf16[5,2,192,128]{3,2,1,0:T(8,128)(2,1)S(1)} collective-permute-done((bf16[5,2,192,128]{3,2,1,0:T(8,128)(2,1)S(1)}, bf16[5,2,192,128]{3,2,1,0:T(8,128)(2,1)S(1)}, u32[]{:S(2)}, u32[]{:S(2)}) %collective-permute-start.12) | collective-permute-done | bytes 491552 | tf_op jit(solution)/shard_map/ppermute | solution.py:118
  51.4 1.1 copy.80
  52.5 1.8 maximum_select_fusion.2
  54.3 1.4 copy.82
  55.7 4.1 %fusion = (f32[4,192]{1,0:T(4,128)S(1)}, f32[3840,192,4]{0,1,2:T(8,128)S(1)}) fusion(pred[192,3840]{1,0:T(8,128)(4,1)} %compare_and_fusion, bf16[192,4,32]{0,2,1:T(8,128)(2,1)S(1)} %copy-done.5, bf16[192,4,32]{0,2,1:T(8,128)(2,1)S(1)} %copy-done.4, bf16[3840,128]{1,0:T(8,128)(2,1)} %bitcast.162), kind=kOutput, calls=%fused_computation.2 | convolution fusion | flops 386530560 | bytes 13618176 | tf_op jit(solution)/shard_map/tkgd,skd->kgts/dot_general | solution.py:132
  59.8 3.7 %fusion.1 = f32[4,192]{1,0:T(4,128)S(1)} fusion(f32[3840,192,4]{0,1,2:T(8,128)S(1)} %get-tuple-element.59, f32[4,192]{1,0:T(4,128)S(1)} %broadcast_maximum_fusion, pred[192,3840]{1,0:T(8,128)(4,1)S(1)} %copy-done.2), kind=kLoop, calls=%fused_computation.3 | loop fusion | flops 14744832 | bytes 12539904 | tf_op jit(solution)/shard_map/reduce_sum | solution.py:142
  63.5 3.3 %fusion.16 = bf16[192,1,4,64]{0,3,2,1:T(8,128)(2,1)S(1)} fusion(f32[3840,192,4]{0,1,2:T(8,128)S(1)} %get-tuple-element.59, f32[4,192]{1,0:T(4,128)S(1)} %broadcast_maximum_fusion, pred[192,3840]{1,0:T(8,128)(4,1)S(1)} %copy-done.2, bf16[3840,128]{1,0:T(8,128)(2,1)S(1)} %bitcast.163, f32[4,192]{1,0:T(4,128)S(1)} %fusion.1), kind=kOutput, calls=%fused_computation.26 | convolution fusion | flops 392331264 | bytes 13621248 | tf_op jit(solution)/shard_map/kgts,skd->kgtd/dot_general | solution.py:143
  67.2 0.4 fusion.19
  67.9 2.1 %concatenate.310 = bf16[2064,193]{0,1:T(8,128)(2,1)} concatenate(bf16[2048,193]{0,1:T(8,128)(2,1)} %param.19, bf16[1,193]{0,1:T(8,128)(2,1)S(1)} %broadcast_in_dim.119, bf16[15,193]{0,1:T(8,128)(2,1)S(1)} %broadcast_in_dim.105), dimensions={0} | concatenate | bytes 1593408 | tf_op jit(solution)/shard_map/concatenate | solution.py:195
  70.2 1.3 fusion.24
  71.4 0.8 select_bitcast_fusion.1
  72.3 1.4 collective-permute-start.14
  73.7 2.5 %fusion.77 = (bf16[2064,208]{0,1:T(8,128)(2,1)}, bf16[2064,1664]{0,1:T(8,128)(2,1)}) fusion(bf16[2064,193]{0,1:T(8,128)(2,1)} %concatenate.310), kind=kLoop, calls=%fused_computation.187 | loop fusion | bytes 2607136 | tf_op jit(solution)/shard_map/jit(_pad)/pad | solution.py:196
  76.3 3.2 %collective-permute-start.1 = (bf16[2064,208]{0,1:T(8,128)(2,1)}, bf16[2064,208]{0,1:T(8,128)(2,1)}, u32[]{:S(2)}, u32[]{:S(2)}) collective-permute-start(bf16[2064,208]{0,1:T(8,128)(2,1)} %get-tuple-element.15), channel_id=1, source_target_pairs={{0,28},{4,0},{8,4},{12,8},{16,12},{20,16},{24,20},{28,24},{1,29},{... | collective-permute-start | bytes 2575880 | tf_op jit(solution)/shard_map/ppermute | solution.py:203
  79.5 1.3 convert_element_type.49
  80.8 3.1 %collective-permute-done.14 = f32[2,24,2048]{2,1,0:T(8,128)} collective-permute-done((f32[2,24,2048]{2,1,0:T(8,128)}, f32[2,24,2048]{2,1,0:T(8,128)}, u32[]{:S(2)}, u32[]{:S(2)}) %collective-permute-start.14) | collective-permute-done | bytes 393248 | tf_op jit(solution)/shard_map/ppermute | solution.py:174
  83.9 1.1 fusion.27
  85.0 3.3 %collective-permute-start.15 = (f32[24,2048]{1,0:T(8,128)S(1)}, f32[24,2048]{1,0:T(8,128)S(1)}, u32[]{:S(2)}, u32[]{:S(2)}) collective-permute-start(f32[24,2048]{1,0:T(8,128)S(1)} %select_bitcast_fusion.2), channel_id=1, source_target_pairs={{0,128},{32,160},{64,192},{96,224},{128,0},{160,32},{192,64},{224,... | collective-permute-start | bytes 589832 | tf_op jit(solution)/shard_map/ppermute | solution.py:174
  88.3 4.8 %collective-permute-done.15 = f32[24,2048]{1,0:T(8,128)S(1)} collective-permute-done((f32[24,2048]{1,0:T(8,128)S(1)}, f32[24,2048]{1,0:T(8,128)S(1)}, u32[]{:S(2)}, u32[]{:S(2)}) %collective-permute-start.15) | collective-permute-done | bytes 196640 | tf_op jit(solution)/shard_map/ppermute | solution.py:174
  93.6 0.8 dynamic_slice.19
  94.4 5.4 %collective-permute-done = bf16[2064,208]{0,1:T(8,128)(2,1)} collective-permute-done((bf16[2064,208]{0,1:T(8,128)(2,1)}, bf16[2064,208]{0,1:T(8,128)(2,1)}, u32[]{:S(2)}, u32[]{:S(2)}) %collective-permute-start) | collective-permute-done | bytes 858656 | tf_op jit(solution)/shard_map/ppermute | solution.py:202
  99.8 3.2 %collective-permute-start.3 = (bf16[2064,208]{0,1:T(8,128)(2,1)}, bf16[2064,208]{0,1:T(8,128)(2,1)S(1)}, u32[]{:S(2)}, u32[]{:S(2)}) collective-permute-start(bf16[2064,208]{0,1:T(8,128)(2,1)} %collective-permute-done.1), channel_id=1, source_target_pairs={{0,28},{4,0},{8,4},{12,8},{16,12},{20,16},{24,20},{28,24},{1,29},{... | collective-permute-start | bytes 2575880 | tf_op jit(solution)/shard_map/ppermute | solution.py:203
  103.2 7.1 %collective-permute-done.17 = bf16[1,2,1,1,1,24,2048]{6,5,4,3,2,1,0:T(8,128)(2,1)S(1)} collective-permute-done((bf16[1,2,1,1,1,24,2048]{6,5,4,3,2,1,0:T(8,128)(2,1)S(1)}, bf16[1,2,1,1,1,24,2048]{6,5,4,3,2,1,0:T(8,128)(2,1)S(1)}, u32[]{:S(2)}, u32[]{:S(2)}) %collective-permute-start.17) | collective-permute-done | bytes 196640 | tf_op jit(solution)/shard_map/ppermute | solution.py:185
  110.4 2.9 %collective-permute-start.18 = (bf16[2,2,1,1,1,24,2048]{6,5,4,3,2,1,0:T(8,128)(2,1)S(1)}, bf16[2,2,1,1,1,24,2048]{6,5,4,3,2,1,0:T(8,128)(2,1)S(1)}, u32[]{:S(2)}, u32[]{:S(2)}) collective-permute-start(bf16[2,2,1,1,1,24,2048]{6,5,4,3,2,1,0:T(8,128)(2,1)S(1)} %fusion.25), channel_id=1, source_target_pairs={{0,128},{32,160},{64,192},{96,224},{128,0},{160,32},{192,64},{224,... | collective-permute-start | bytes 1179656 | tf_op jit(solution)/shard_map/ppermute | solution.py:185
  113.3 2.2 %constant_dynamic-update-slice_fusion.5 = bf16[2064,1664]{0,1:T(8,128)(2,1)} fusion(bf16[2064,1664]{0,1:T(8,128)(2,1)} %get-tuple-element.16, bf16[2064,208]{0,1:T(8,128)(2,1)} %collective-permute-done), kind=kLoop, calls=%fused_computation.85 | loop fusion | bytes 1810432
  115.6 4.9 %collective-permute-done.18 = bf16[2,2,1,1,1,24,2048]{6,5,4,3,2,1,0:T(8,128)(2,1)S(1)} collective-permute-done((bf16[2,2,1,1,1,24,2048]{6,5,4,3,2,1,0:T(8,128)(2,1)S(1)}, bf16[2,2,1,1,1,24,2048]{6,5,4,3,2,1,0:T(8,128)(2,1)S(1)}, u32[]{:S(2)}, u32[]{:S(2)}) %collective-permute-start.18) | collective-permute-done | bytes 393248 | tf_op jit(solution)/shard_map/ppermute | solution.py:185
  120.7 0.7 collective-permute-start.19
  121.4 2.2 %constant_dynamic-update-slice_fusion.4 = bf16[2064,1664]{0,1:T(8,128)(2,1)} fusion(bf16[2064,1664]{0,1:T(8,128)(2,1)} %constant_dynamic-update-slice_fusion.5, bf16[2064,208]{0,1:T(8,128)(2,1)} %collective-permute-done.1), kind=kLoop, calls=%fused_computation.84 | loop fusion | bytes 1810432
  123.6 3.2 %collective-permute-start.5 = (bf16[2064,208]{0,1:T(8,128)(2,1)S(1)}, bf16[2064,208]{0,1:T(8,128)(2,1)S(1)}, u32[]{:S(2)}, u32[]{:S(2)}) collective-permute-start(bf16[2064,208]{0,1:T(8,128)(2,1)S(1)} %collective-permute-done.3), channel_id=1, source_target_pairs={{0,28},{4,0},{8,4},{12,8},{16,12},{20,16},{24,20},{28,24},{1,29},{... | collective-permute-start | bytes 2575880 | tf_op jit(solution)/shard_map/ppermute | solution.py:203
  126.8 1.0 constant_dynamic-update-slice_fusion.3
  127.9 9.0 %collective-permute-done.19 = bf16[2,2,2,1,1,24,2048]{6,5,4,3,2,1,0:T(8,128)(2,1)S(1)} collective-permute-done((bf16[2,2,2,1,1,24,2048]{6,5,4,3,2,1,0:T(8,128)(2,1)S(1)}, bf16[2,2,2,1,1,24,2048]{6,5,4,3,2,1,0:T(8,128)(2,1)S(1)}, u32[]{:S(2)}, u32[]{:S(2)}) %collective-permute-start.19) | collective-permute-done | bytes 786464 | tf_op jit(solution)/shard_map/ppermute | solution.py:185
  137.1 1.0 constant_dynamic-update-slice_fusion.2
  138.1 5.4 %collective-permute-done.5 = bf16[2064,208]{0,1:T(8,128)(2,1)S(1)} collective-permute-done((bf16[2064,208]{0,1:T(8,128)(2,1)S(1)}, bf16[2064,208]{0,1:T(8,128)(2,1)S(1)}, u32[]{:S(2)}, u32[]{:S(2)}) %collective-permute-start.5) | collective-permute-done | bytes 858656 | tf_op jit(solution)/shard_map/ppermute | solution.py:203
  143.6 3.5 %collective-permute-start.7 = (bf16[1040,208]{0,1:T(8,128)(2,1)S(1)}, bf16[1040,208]{0,1:T(8,128)(2,1)S(1)}, u32[]{:S(2)}, u32[]{:S(2)}) collective-permute-start(bf16[1040,208]{0,1:T(8,128)(2,1)S(1)} %slice.249), channel_id=1, source_target_pairs={{0,28},{4,0},{8,4},{12,8},{16,12},{20,16},{24,20},{28,24},{1,29},{... | collective-permute-start | bytes 1297928 | tf_op jit(solution)/shard_map/ppermute | solution.py:209
  147.5 1.0 constant_dynamic-update-slice_fusion.1
  148.5 1.0 constant_dynamic-update-slice_fusion
  149.5 7.3 %collective-permute-done.6 = bf16[1024,208]{0,1:T(8,128)(2,1)S(1)} collective-permute-done((bf16[1024,208]{0,1:T(8,128)(2,1)S(1)}, bf16[1024,208]{0,1:T(8,128)(2,1)S(1)}, u32[]{:S(2)}, u32[]{:S(2)}) %collective-permute-start.6) | collective-permute-done | bytes 426016 | tf_op jit(solution)/shard_map/ppermute | solution.py:208
  156.8 1.0 maximum_dynamic-update-slice_fusion
  157.8 1.3 compare_reduce_fusion
  159.5 10.7 %select_reduce_fusion.1 = (f32[768]{0:T(1024)S(1)}, f32[768,1664]{1,0:T(8,128)}) fusion(pred[1664]{0:T(1024)(128)(4,1)S(1)} %compare_reduce_fusion, bf16[768,2048]{1,0:T(8,128)(2,1)S(1)} %bitcast.159, bf16[2064,1664]{0,1:T(8,128)(2,1)} %maximum_dynamic-update-slice_fusion), kind=kOutput, calls=%fused_computation.15 | convolution fusion | flops 5238324224 | bytes 15078016 | tf_op jit(solution)/shard_map/dot_general | solution.py:223
  170.3 4.8 %fusion.9 = (f32[768]{0:T(1024)S(1)}, f32[768]{0:T(1024)S(1)}, f32[768]{0:T(1024)S(1)}) fusion(f32[768,1664]{1,0:T(8,128)} %get-tuple-element.61, f32[768]{0:T(1024)S(1)} %get-tuple-element.60, pred[1664]{0:T(1024)(128)(4,1)S(1)} %compare_reduce_fusion, s32[1664]{0:T(1024)S(1)} %select_n.489, s32[768]{0:T(1024)S(1)} %dynamic_slice.19), kind=kLoop, calls=%fused_computation.13 | loop fusion | flops 14055168 | bytes 5135488 | tf_op jit(solution)/shard_map/reduce_sum | solution.py:230
  175.4 0.7 collective-permute-start.21
  176.0 4.6 %collective-permute-done.21 = f32[4,2,192]{2,0,1:T(4,128)S(1)} collective-permute-done((f32[4,2,192]{2,0,1:T(4,128)S(1)}, f32[4,2,192]{2,0,1:T(4,128)S(1)}, u32[]{:S(2)}, u32[]{:S(2)}) %collective-permute-start.21) | collective-permute-done | bytes 6176 | tf_op jit(solution)/shard_map/ppermute | solution.py:236
  180.8 3.6 %collective-permute-done.22 = f32[4,1,192]{2,0,1:T(4,128)S(1)} collective-permute-done((f32[4,1,192]{2,0,1:T(4,128)S(1)}, f32[4,1,192]{2,0,1:T(4,128)S(1)}, u32[]{:S(2)}, u32[]{:S(2)}) %collective-permute-start.22) | collective-permute-done | bytes 3104 | tf_op jit(solution)/shard_map/ppermute | solution.py:244
  184.6 1.1 collective-permute-done.23
  185.8 1.5 collective-permute-start.24
  187.3 2.2 %collective-permute-done.24 = f32[4,192]{1,0:T(4,128)S(1)} collective-permute-done((f32[4,192]{1,0:T(4,128)S(1)}, f32[4,192]{1,0:T(4,128)S(1)}, u32[]{:S(2)}, u32[]{:S(2)}) %collective-permute-start.24) | collective-permute-done | bytes 3104 | tf_op jit(solution)/shard_map/ppermute | solution.py:249
  189.6 3.4 %collective-permute-start.25 = (f32[4,192]{1,0:T(4,128)S(1)}, f32[4,192]{1,0:T(4,128)S(1)}, u32[]{:S(2)}, u32[]{:S(2)}) collective-permute-start(f32[4,192]{1,0:T(4,128)S(1)} %pad_maximum_fusion.5), channel_id=1, source_target_pairs={{0,128},{32,160},{64,192},{96,224},{128,0},{160,32},{192,64},{224,... | collective-permute-start | bytes 9224 | tf_op jit(solution)/shard_map/ppermute | solution.py:249
  193.0 1.8 collective-permute-done.25
  194.8 0.6 divide_subtract_fusion
  (109 shorter events, 5.7 us)
Async XLA Ops:
  0.6 66.5 %copy-start = (bf16[256,2048]{1,0:T(8,128)(2,1)S(1)}, bf16[256,2048]{1,0:T(8,128)(2,1)}, u32[]{:S(2)}) copy-start(bf16[256,2048]{1,0:T(8,128)(2,1)} %param.17) | copy-start | bytes 3145732
  0.6 40.4 %copy-start.1 = (bf16[192,2048]{1,0:T(8,128)(2,1)S(1)}, bf16[192,2048]{1,0:T(8,128)(2,1)}, u32[]{:S(2)}) copy-start(bf16[192,2048]{1,0:T(8,128)(2,1)} %param.12) | copy-start | bytes 2359300
  0.7 40.4 %copy-start.8 = (f32[2048]{0:T(1024)S(1)}, f32[2048]{0:T(1024)}, u32[]{:S(2)}) copy-start(f32[2048]{0:T(1024)} %param.13) | copy-start | bytes 24580
  7.4 8.2 %collective-permute-start.8 = (bf16[1,192,128]{1,2,0:T(8,128)(2,1)S(1)}, bf16[1,192,128]{1,2,0:T(8,128)(2,1)S(1)}, u32[]{:S(2)}, u32[]{:S(2)}) collective-permute-start(bf16[1,192,128]{1,2,0:T(8,128)(2,1)S(1)} %maximum_bitcast_fusion.2), channel_id=1, source_target_pairs={{0,4},{4,8},{8,12},{12,16},{16,20},{20,24},{24,28},{28,0},{1,5},{5... | collective-permute-start | bytes 147464 | tf_op jit(solution)/shard_map/ppermute | solution.py:113
  15.6 8.8 %collective-permute-start.9 = (bf16[2,192,128]{1,2,0:T(8,128)(2,1)S(1)}, bf16[2,192,128]{1,2,0:T(8,128)(2,1)S(1)}, u32[]{:S(2)}, u32[]{:S(2)}) collective-permute-start(bf16[2,192,128]{1,2,0:T(8,128)(2,1)S(1)} %pad_maximum_fusion.1), channel_id=1, source_target_pairs={{0,8},{4,12},{8,16},{12,20},{16,24},{20,28},{24,0},{28,4},{1,9},{5... | collective-permute-start | bytes 294920 | tf_op jit(solution)/shard_map/ppermute | solution.py:113
  24.5 5.5 %collective-permute-start.10 = (bf16[1,192,128]{1,2,0:T(8,128)(2,1)S(1)}, bf16[1,192,128]{1,2,0:T(8,128)(2,1)S(1)}, u32[]{:S(2)}, u32[]{:S(2)}) collective-permute-start(bf16[1,192,128]{1,2,0:T(8,128)(2,1)S(1)} %slice.253), channel_id=1, source_target_pairs={{0,4},{4,8},{8,12},{12,16},{16,20},{20,24},{24,28},{28,0},{1,5},{5... | collective-permute-start | bytes 147464 | tf_op jit(solution)/shard_map/ppermute | solution.py:113
  30.0 10.2 %collective-permute-start.11 = (bf16[5,1,192,128]{2,3,0,1:T(8,128)(2,1)S(1)}, bf16[5,1,192,128]{2,3,0,1:T(8,128)(2,1)S(1)}, u32[]{:S(2)}, u32[]{:S(2)}) collective-permute-start(bf16[5,1,192,128]{2,3,0,1:T(8,128)(2,1)S(1)} %maximum_bitcast_fusion.1), channel_id=1, source_target_pairs={{0,1},{1,0},{2,3},{3,2},{4,5},{5,4},{6,7},{7,6},{8,9},{9,8},{10,11... | collective-permute-start | bytes 737288 | tf_op jit(solution)/shard_map/ppermute | solution.py:118
  40.8 10.6 %collective-permute-start.12 = (bf16[5,2,192,128]{3,2,1,0:T(8,128)(2,1)S(1)}, bf16[5,2,192,128]{3,2,1,0:T(8,128)(2,1)S(1)}, u32[]{:S(2)}, u32[]{:S(2)}) collective-permute-start(bf16[5,2,192,128]{3,2,1,0:T(8,128)(2,1)S(1)} %copy.79), channel_id=1, source_target_pairs={{0,2},{1,3},{2,0},{3,1},{4,6},{5,7},{6,4},{7,5},{8,10},{9,11},{10,... | collective-permute-start | bytes 1474568 | tf_op jit(solution)/shard_map/ppermute | solution.py:118
  43.6 12.1 %copy-start.4 = (bf16[192,4,32]{0,2,1:T(8,128)(2,1)S(1)}, bf16[192,4,32]{0,2,1:T(8,128)(2,1)}, u32[]{:S(2)}) copy-start(bf16[192,4,32]{0,2,1:T(8,128)(2,1)} %get-tuple-element.20) | copy-start | bytes 147460
  51.4 4.3 %copy-start.5 = (bf16[192,4,32]{0,2,1:T(8,128)(2,1)S(1)}, bf16[192,4,32]{0,2,1:T(8,128)(2,1)}, u32[]{:S(2)}) copy-start(bf16[192,4,32]{0,2,1:T(8,128)(2,1)} %get-tuple-element.21) | copy-start | bytes 147460
  55.7 4.1 %copy-start.2 = (pred[192,3840]{1,0:T(8,128)(4,1)S(1)}, pred[192,3840]{1,0:T(8,128)(4,1)}, u32[]{:S(2)}) copy-start(pred[192,3840]{1,0:T(8,128)(4,1)} %compare_and_fusion) | copy-start | bytes 2211844
  59.8 3.8 %copy-start.3 = (bf16[5,4,192,128]{3,2,1,0:T(8,128)(2,1)S(1)}, bf16[5,4,192,128]{3,2,1,0:T(8,128)(2,1)}, u32[]{:S(2)}) copy-start(bf16[5,4,192,128]{3,2,1,0:T(8,128)(2,1)} %copy.82) | copy-start | bytes 2949124
  66.8 1.0 copy-start.9
  67.7 2.5 %collective-permute-start.13 = (f32[2,2,24,2048]{3,2,1,0:T(8,128)S(1)}, f32[2,2,24,2048]{3,2,1,0:T(8,128)}, u32[]{:S(2)}, u32[]{:S(2)}) collective-permute-start(f32[2,2,24,2048]{3,2,1,0:T(8,128)S(1)} %select_bitcast_fusion), channel_id=1, source_target_pairs={{0,32},{32,0},{64,96},{96,64},{128,160},{160,128},{192,224},{224,1... | collective-permute-start | bytes 2359304 | tf_op jit(solution)/shard_map/ppermute | solution.py:174
  70.0 18.3 %copy-start.7 = (s32[8]{0:T(128)S(1)}, s32[8]{0:T(128)}, u32[]{:S(2)}) copy-start(s32[8]{0:T(128)} %constant.190.clone) | copy-start | bytes 100
  71.4 21.8 %copy-start.6 = (f32[2048]{0:T(1024)S(1)}, f32[2048]{0:T(1024)}, u32[]{:S(2)}) copy-start(f32[2048]{0:T(1024)} %param.18) | copy-start | bytes 24580
  72.3 11.6 %collective-permute-start.14 = (f32[2,24,2048]{2,1,0:T(8,128)}, f32[2,24,2048]{2,1,0:T(8,128)}, u32[]{:S(2)}, u32[]{:S(2)}) collective-permute-start(f32[2,24,2048]{2,1,0:T(8,128)} %select_bitcast_fusion.1), channel_id=1, source_target_pairs={{0,64},{32,96},{64,0},{96,32},{128,192},{160,224},{192,128},{224,1... | collective-permute-start | bytes 1179656 | tf_op jit(solution)/shard_map/ppermute | solution.py:174
  76.3 23.5 %collective-permute-start = (bf16[2064,208]{0,1:T(8,128)(2,1)}, bf16[2064,208]{0,1:T(8,128)(2,1)}, u32[]{:S(2)}, u32[]{:S(2)}) collective-permute-start(bf16[2064,208]{0,1:T(8,128)(2,1)} %get-tuple-element.15), channel_id=1, source_target_pairs={{0,4},{4,8},{8,12},{12,16},{16,20},{20,24},{24,28},{28,0},{1,5},{5... | collective-permute-start | bytes 2575880 | tf_op jit(solution)/shard_map/ppermute | solution.py:202
  76.3 23.5 %collective-permute-start.1 = (bf16[2064,208]{0,1:T(8,128)(2,1)}, bf16[2064,208]{0,1:T(8,128)(2,1)}, u32[]{:S(2)}, u32[]{:S(2)}) collective-permute-start(bf16[2064,208]{0,1:T(8,128)(2,1)} %get-tuple-element.15), channel_id=1, source_target_pairs={{0,28},{4,0},{8,4},{12,8},{16,12},{20,16},{24,20},{28,24},{1,29},{... | collective-permute-start | bytes 2575880 | tf_op jit(solution)/shard_map/ppermute | solution.py:203
  85.0 8.1 %collective-permute-start.15 = (f32[24,2048]{1,0:T(8,128)S(1)}, f32[24,2048]{1,0:T(8,128)S(1)}, u32[]{:S(2)}, u32[]{:S(2)}) collective-permute-start(f32[24,2048]{1,0:T(8,128)S(1)} %select_bitcast_fusion.2), channel_id=1, source_target_pairs={{0,128},{32,160},{64,192},{96,224},{128,0},{160,32},{192,64},{224,... | collective-permute-start | bytes 589832 | tf_op jit(solution)/shard_map/ppermute | solution.py:174
  93.3 9.7 %collective-permute-start.16 = (bf16[1,1,1,1,1,24,2048]{6,5,4,3,2,1,0:T(8,128)(2,1)S(1)}, bf16[1,1,1,1,1,24,2048]{6,5,4,3,2,1,0:T(8,128)(2,1)S(1)}, u32[]{:S(2)}, u32[]{:S(2)}) collective-permute-start(bf16[1,1,1,1,1,24,2048]{6,5,4,3,2,1,0:T(8,128)(2,1)S(1)} %get-tuple-element.22), channel_id=1, source_target_pairs={{0,1},{1,0},{2,3},{3,2},{4,5},{5,4},{6,7},{7,6},{8,9},{9,8},{10,11... | collective-permute-start | bytes 294920 | tf_op jit(solution)/shard_map/ppermute | solution.py:185
  99.8 23.8 %collective-permute-start.2 = (bf16[2064,208]{0,1:T(8,128)(2,1)}, bf16[2064,208]{0,1:T(8,128)(2,1)S(1)}, u32[]{:S(2)}, u32[]{:S(2)}) collective-permute-start(bf16[2064,208]{0,1:T(8,128)(2,1)} %collective-permute-done), channel_id=1, source_target_pairs={{0,4},{4,8},{8,12},{12,16},{16,20},{20,24},{24,28},{28,0},{1,5},{5... | collective-permute-start | bytes 2575880 | tf_op jit(solution)/shard_map/ppermute | solution.py:202
  99.8 23.8 %collective-permute-start.3 = (bf16[2064,208]{0,1:T(8,128)(2,1)}, bf16[2064,208]{0,1:T(8,128)(2,1)S(1)}, u32[]{:S(2)}, u32[]{:S(2)}) collective-permute-start(bf16[2064,208]{0,1:T(8,128)(2,1)} %collective-permute-done.1), channel_id=1, source_target_pairs={{0,28},{4,0},{8,4},{12,8},{16,12},{20,16},{24,20},{28,24},{1,29},{... | collective-permute-start | bytes 2575880 | tf_op jit(solution)/shard_map/ppermute | solution.py:203
  103.1 7.3 %collective-permute-start.17 = (bf16[1,2,1,1,1,24,2048]{6,5,4,3,2,1,0:T(8,128)(2,1)S(1)}, bf16[1,2,1,1,1,24,2048]{6,5,4,3,2,1,0:T(8,128)(2,1)S(1)}, u32[]{:S(2)}, u32[]{:S(2)}) collective-permute-start(bf16[1,2,1,1,1,24,2048]{6,5,4,3,2,1,0:T(8,128)(2,1)S(1)} %maximum_select_fusion.8), channel_id=1, source_target_pairs={{0,2},{1,3},{2,0},{3,1},{4,6},{5,7},{6,4},{7,5},{8,10},{9,11},{10,... | collective-permute-start | bytes 589832 | tf_op jit(solution)/shard_map/ppermute | solution.py:185
  110.4 10.1 %collective-permute-start.18 = (bf16[2,2,1,1,1,24,2048]{6,5,4,3,2,1,0:T(8,128)(2,1)S(1)}, bf16[2,2,1,1,1,24,2048]{6,5,4,3,2,1,0:T(8,128)(2,1)S(1)}, u32[]{:S(2)}, u32[]{:S(2)}) collective-permute-start(bf16[2,2,1,1,1,24,2048]{6,5,4,3,2,1,0:T(8,128)(2,1)S(1)} %fusion.25), channel_id=1, source_target_pairs={{0,128},{32,160},{64,192},{96,224},{128,0},{160,32},{192,64},{224,... | collective-permute-start | bytes 1179656 | tf_op jit(solution)/shard_map/ppermute | solution.py:185
  120.7 16.1 %collective-permute-start.19 = (bf16[2,2,2,1,1,24,2048]{6,5,4,3,2,1,0:T(8,128)(2,1)S(1)}, bf16[2,2,2,1,1,24,2048]{6,5,4,3,2,1,0:T(8,128)(2,1)S(1)}, u32[]{:S(2)}, u32[]{:S(2)}) collective-permute-start(bf16[2,2,2,1,1,24,2048]{6,5,4,3,2,1,0:T(8,128)(2,1)S(1)} %maximum_select_fusion.4), channel_id=1, source_target_pairs={{0,64},{32,96},{64,0},{96,32},{128,192},{160,224},{192,128},{224,1... | collective-permute-start | bytes 2359304 | tf_op jit(solution)/shard_map/ppermute | solution.py:185
  123.6 23.5 %collective-permute-start.4 = (bf16[2064,208]{0,1:T(8,128)(2,1)S(1)}, bf16[2064,208]{0,1:T(8,128)(2,1)S(1)}, u32[]{:S(2)}, u32[]{:S(2)}) collective-permute-start(bf16[2064,208]{0,1:T(8,128)(2,1)S(1)} %collective-permute-done.2), channel_id=1, source_target_pairs={{0,4},{4,8},{8,12},{12,16},{16,20},{20,24},{24,28},{28,0},{1,5},{5... | collective-permute-start | bytes 2575880 | tf_op jit(solution)/shard_map/ppermute | solution.py:202
  123.6 19.9 %collective-permute-start.5 = (bf16[2064,208]{0,1:T(8,128)(2,1)S(1)}, bf16[2064,208]{0,1:T(8,128)(2,1)S(1)}, u32[]{:S(2)}, u32[]{:S(2)}) collective-permute-start(bf16[2064,208]{0,1:T(8,128)(2,1)S(1)} %collective-permute-done.3), channel_id=1, source_target_pairs={{0,28},{4,0},{8,4},{12,8},{16,12},{20,16},{24,20},{28,24},{1,29},{... | collective-permute-start | bytes 2575880 | tf_op jit(solution)/shard_map/ppermute | solution.py:203
  137.0 22.1 %collective-permute-start.20 = (bf16[2,2,2,2,1,24,2048]{6,5,4,3,2,1,0:T(8,128)(2,1)S(1)}, bf16[2,2,2,2,1,24,2048]{6,5,4,3,2,1,0:T(8,128)(2,1)S(1)}, u32[]{:S(2)}, u32[]{:S(2)}) collective-permute-start(bf16[2,2,2,2,1,24,2048]{6,5,4,3,2,1,0:T(8,128)(2,1)S(1)} %maximum_select_fusion.1), channel_id=1, source_target_pairs={{0,32},{32,0},{64,96},{96,64},{128,160},{160,128},{192,224},{224,1... | collective-permute-start | bytes 4718600 | tf_op jit(solution)/shard_map/ppermute | solution.py:185
  143.6 13.2 %collective-permute-start.7 = (bf16[1040,208]{0,1:T(8,128)(2,1)S(1)}, bf16[1040,208]{0,1:T(8,128)(2,1)S(1)}, u32[]{:S(2)}, u32[]{:S(2)}) collective-permute-start(bf16[1040,208]{0,1:T(8,128)(2,1)S(1)} %slice.249), channel_id=1, source_target_pairs={{0,28},{4,0},{8,4},{12,8},{16,12},{20,16},{24,20},{28,24},{1,29},{... | collective-permute-start | bytes 1297928 | tf_op jit(solution)/shard_map/ppermute | solution.py:209
  147.1 9.7 %collective-permute-start.6 = (bf16[1024,208]{0,1:T(8,128)(2,1)S(1)}, bf16[1024,208]{0,1:T(8,128)(2,1)S(1)}, u32[]{:S(2)}, u32[]{:S(2)}) collective-permute-start(bf16[1024,208]{0,1:T(8,128)(2,1)S(1)} %slice.248), channel_id=1, source_target_pairs={{0,4},{4,8},{8,12},{12,16},{16,20},{20,24},{24,28},{28,0},{1,5},{5... | collective-permute-start | bytes 1277960 | tf_op jit(solution)/shard_map/ppermute | solution.py:208
  175.4 5.2 %collective-permute-start.21 = (f32[4,2,192]{2,0,1:T(4,128)S(1)}, f32[4,2,192]{2,0,1:T(4,128)S(1)}, u32[]{:S(2)}, u32[]{:S(2)}) collective-permute-start(f32[4,2,192]{2,0,1:T(4,128)S(1)} %constant_dynamic-slice_fusion.1), channel_id=1, source_target_pairs={{0,2},{1,3},{2,0},{3,1},{4,6},{5,7},{6,4},{7,5},{8,10},{9,11},{10,... | collective-permute-start | bytes 18440 | tf_op jit(solution)/shard_map/ppermute | solution.py:236
  180.7 3.7 %collective-permute-start.22 = (f32[4,1,192]{2,0,1:T(4,128)S(1)}, f32[4,1,192]{2,0,1:T(4,128)S(1)}, u32[]{:S(2)}, u32[]{:S(2)}) collective-permute-start(f32[4,1,192]{2,0,1:T(4,128)S(1)} %constant_dynamic-slice_fusion), channel_id=1, source_target_pairs={{0,1},{1,0},{2,3},{3,2},{4,5},{5,4},{6,7},{7,6},{8,9},{9,8},{10,11... | collective-permute-start | bytes 9224 | tf_op jit(solution)/shard_map/ppermute | solution.py:244
  184.5 1.3 collective-permute-start.23
  185.8 3.7 %collective-permute-start.24 = (f32[4,192]{1,0:T(4,128)S(1)}, f32[4,192]{1,0:T(4,128)S(1)}, u32[]{:S(2)}, u32[]{:S(2)}) collective-permute-start(f32[4,192]{1,0:T(4,128)S(1)} %pad_maximum_fusion.4), channel_id=1, source_target_pairs={{0,64},{32,96},{64,0},{96,32},{128,192},{160,224},{192,128},{224,1... | collective-permute-start | bytes 9224 | tf_op jit(solution)/shard_map/ppermute | solution.py:249
  189.6 5.2 %collective-permute-start.25 = (f32[4,192]{1,0:T(4,128)S(1)}, f32[4,192]{1,0:T(4,128)S(1)}, u32[]{:S(2)}, u32[]{:S(2)}) collective-permute-start(f32[4,192]{1,0:T(4,128)S(1)} %pad_maximum_fusion.5), channel_id=1, source_target_pairs={{0,128},{32,160},{64,192},{96,224},{128,0},{160,32},{192,64},{224,... | collective-permute-start | bytes 9224 | tf_op jit(solution)/shard_map/ppermute | solution.py:249

commit v12 on v10

--- a/solution.py
+++ b/solution.py
@@ -75,6 +75,20 @@
     group_size = q_local // kv_local
     key_width = kv_local * HEAD_DIM
     stream = hidden_states.astype(jnp.float32)
+    vocab_local = w_head.shape[1]
+    z_count = lax.psum(1, "z")
+    z_index = lax.axis_index("z")
+    padded_local = -(-vocab_local // 16) * 16
+    head_pad = jnp.zeros((16 - 1, vocab_local), w_head.dtype)
+    head_ext = jnp.concatenate([w_head, vocab_mask.astype(w_head.dtype)[None, :], head_pad], axis=0)
+    head_ext = jnp.pad(head_ext, ((0, 0), (0, padded_local - vocab_local)))
+    forward = [(p, (p + 1) % z_count) for p in range(z_count)]
+    backward = [(p, (p - 1) % z_count) for p in range(z_count)]
+    ring_steps = z_count // 2
+    ahead = lax.ppermute(head_ext, "z", forward)
+    behind = lax.ppermute(head_ext, "z", backward)
+    ring = [head_ext, ahead, behind]
+    offsets = [0, -1, 1]
     normed_in = rms_norm(stream, attn_gain).astype(jnp.bfloat16)
     queries = jnp.dot(normed_in, w_q, preferred_element_type=jnp.float32)
     key_proj = jnp.dot(normed_in, w_k, preferred_element_type=jnp.float32)
@@ -120,6 +134,11 @@
             mine_low, jnp.concatenate([held, got], axis=1), jnp.concatenate([got, held], axis=1)
         )
     shard_rows = held.reshape(-1, packed.shape[1])
+    shard_rows, ahead, behind = lax.optimization_barrier((shard_rows, ahead, behind))
+    ahead = lax.ppermute(ahead, "z", forward)
+    behind = lax.ppermute(behind, "z", backward)
+    ring += [ahead, behind]
+    offsets += [-2, 2]
     plane_ids = (z_pos - back + jnp.arange(back + 1, dtype=jnp.int32)) % z_count
     key_pos = (plane_ids[:, None] * plane_rows + jnp.arange(plane_rows, dtype=jnp.int32)[None, :]).reshape(-1)
     row_count = shard_rows.shape[0]
@@ -149,13 +168,17 @@
         return (new_top, totals, context_sum)
 
     top_score, totals, context_sum = update(initial)
+    context_sum, ahead, behind = lax.optimization_barrier((context_sum, ahead, behind))
+    ahead = lax.ppermute(ahead, "z", forward)
+    behind = lax.ppermute(behind, "z", backward)
+    ring += [ahead, behind]
+    offsets += [-3, 3]
     context = (
         (context_sum / totals[..., None])
         .transpose(2, 0, 1, 3)
         .reshape(tok_rows, q_local * HEAD_DIM)
         .astype(jnp.bfloat16)
     )
-    vocab_local = w_head.shape[1]
     z_index = lax.axis_index("z")
     y_index = lax.axis_index("y")
     kv_index = lax.axis_index("kv")
@@ -174,6 +197,16 @@
         got = lax.ppermute(send, "kv", [(p, p ^ (1 << bit)) for p in range(kv_count)])
         blocks = jnp.where(mine_low, keep + got, got + keep)
     attn_part = blocks
+    attn_part, ahead, behind = lax.optimization_barrier((attn_part, ahead, behind))
+    split = 1024
+    top = lax.ppermute(ahead[:split], "z", forward)
+    bottom = lax.ppermute(behind[split:], "z", backward)
+    ring.append(jnp.concatenate([top, bottom], axis=0))
+    offsets.append(ring_steps)
+    head_ext = jnp.concatenate(ring, axis=1)
+    ring_z = (z_index + jnp.array(offsets, dtype=jnp.int32)) % z_count
+    head_cols = head_ext[: w_head.shape[0]]
+    mask_cols = head_ext[w_head.shape[0]]
     stream_part = lax.dynamic_slice_in_dim(stream, kv_index * chunk, chunk, 0)
     final_part = rms_norm(stream_part + RESID_SCALE * attn_part, final_gain).astype(jnp.bfloat16)
     y_bits = y_count.bit_length() - 1
@@ -190,15 +223,8 @@
         )
     head_rows = head_rows.reshape(-1, final_part.shape[1])
     group_rows = head_rows.shape[0]
-    padded_local = -(-vocab_local // 16) * 16
-    head_pad = jnp.zeros((16 - 1, vocab_local), w_head.dtype)
-    head_ext = jnp.concatenate([w_head, vocab_mask.astype(w_head.dtype)[None, :], head_pad], axis=0)
-    head_ext = jnp.pad(head_ext, ((0, 0), (0, padded_local - vocab_local)))
-    head_ext = lax.all_gather(head_ext, "z", axis=1, tiled=True)
-    head_cols = head_ext[: w_head.shape[0]]
-    mask_cols = head_ext[w_head.shape[0]]
     live_mask = mask_cols == 1.0
-    shard_ids = kv_index * (z_count * y_count) + jnp.arange(z_count, dtype=jnp.int32) * y_count + y_index
+    shard_ids = kv_index * (z_count * y_count) + ring_z * y_count + y_index
     local_cols = jnp.arange(padded_local, dtype=jnp.int32)
     columns = jnp.where(
         local_cols[None, :] < vocab_local, shard_ids[:, None] * vocab_local + local_cols[None, :], -1

time: 192 us -> 230 us (1.20); the launches traced: 191 us -> 226 us
  starting transfers between devices: 16.4 us -> 39.5 us
  local copies, waits for them, and re-layouts: 7.92 us -> 23.1 us
  between operations: 14.7 us -> 1.2 us
  waiting for transfers between devices: 104 us -> 112 us
  other arithmetic: 24.7 us -> 27.1 us
    ppermute x0 -> x8, waiting for transfers between devices: none -> 25.8 us  [the longest x2 10.9 us: local(): ahead = lax.ppermute(ahead, 'z', forward)]
    ppermute x5, waiting for transfers between devices: 36.7 us -> 22.8 us  [local(): lax.ppermute(head_rows, name, [(p, p ^ 1 << bit) for p in range(count)])]
    unnamed x16 -> x29, local copies, waits for them, and re-layouts: 0.04 us -> 12.9 us
    ppermute x0 -> x8, starting transfers between devices: none -> 12.6 us  [the longest x2 5.13 us: local(): behind = lax.ppermute(behind, 'z', backward)]
    ppermute x3, waiting for transfers between devices: 19.6 us -> 25.9 us  [local(): lax.ppermute(held[:need], 'z', [(p, (p + need) % z_count) for p in range(...]
    ppermute x3, starting transfers between devices: 2.09 us -> 6.16 us  [local(): lax.ppermute(held[:need], 'z', [(p, (p + need) % z_count) for p in range(...]
    select_n x5, other arithmetic: 4.23 us -> 0.87 us  [local(): jnp.where(mine_low, jnp.concatenate([head_rows, got], axis=axis), jnp.con...]
    ppermute x2, waiting for transfers between devices: 16.5 us -> 13.4 us  [local(): got = lax.ppermute(held, 'y', [(p, p ^ 1 << bit) for p in range(y_count)])]
  transfers between devices with their start and end apart: 19 -> 26, of which waited for: 18 -> 20; matrix products, arithmetic and copies ran while one was open for 16% -> 17% of each run, Pallas kernels for 0% -> 0%
where the time goes in v12:
time: 230 us; the launch traced here: 226 us
  waiting for transfers between devices  112 us (49%)
  starting transfers between devices  39.5 us (17%)
  other arithmetic  27.1 us (12%)
  local copies, waits for them, and re-layouts  23.1 us (10%)
  matrix products  23 us (10%)
    ppermute x3, waiting for transfers between devices, local(): lax.ppermute(held[:need], 'z', [(p, (p + need) % z_count) for p in range(...  25.9 us
    ppermute x5, waiting for transfers between devices, local(): lax.ppermute(head_rows, name, [(p, p ^ 1 << bit) for p in range(count)])  22.8 us
    ppermute x2, waiting for transfers between devices, local(): got = lax.ppermute(held, 'y', [(p, p ^ 1 << bit) for p in range(y_count)])  13.4 us
    unnamed x29, local copies, waits for them, and re-layouts  12.9 us
    ppermute x3, waiting for transfers between devices, local(): got = lax.ppermute(send, 'kv', [(p, p ^ 1 << bit) for p in range(kv_count)])  12.6 us
    ppermute x2, waiting for transfers between devices, local(): ahead = lax.ppermute(ahead, 'z', forward)  10.9 us
    dot_general x1, matrix products, local(): jnp.dot(head_rows, head_cols, preferred_element_type=jnp.float32)  10.7 us
    ppermute x1, waiting for transfers between devices, local(): top = lax.ppermute(ahead[:split], 'z', forward)  9.71 us
  transfers between devices with their start and end apart: 26, of which 20 were waited for; matrix products, arithmetic and copies ran while one was open for 17% of the time, Pallas kernels for 0%

profile of v12, /device:TPU:24, one launch (start us, length us, event | category | flops | bytes accessed | tf_op | source)
XLA Modules:
  0.0 225.7 jit_solution(13877068300851942969)
XLA Ops:
  2.5 1.4 multiply_reduce_fusion.1
  3.9 1.6 convolution_bitcast_fusion
  5.6 1.7 convolution_convert_fusion
  8.1 1.9 collective-permute-start.2
  12.1 1.2 concatenate.310
  13.3 1.4 constant_dynamic-update-slice_fusion.6
  14.6 1.9 collective-permute-start
  16.6 2.0 collective-permute-start.1
  19.5 2.5 %collective-permute-start.3 = (bf16[2,192,128]{1,2,0:T(8,128)(2,1)S(1)}, bf16[2,192,128]{1,2,0:T(8,128)(2,1)S(1)}, u32[]{:S(2)}, u32[]{:S(2)}) collective-permute-start(bf16[2,192,128]{1,2,0:T(8,128)(2,1)S(1)} %pad_maximum_fusion.1), channel_id=1, source_target_pairs={{0,8},{4,12},{8,16},{12,20},{16,24},{20,28},{24,0},{28,4},{1,9},{5... | collective-permute-start | bytes 294920 | tf_op jit(solution)/shard_map/ppermute | solution.py:127
  22.0 22.2 %collective-permute-done.3 = bf16[2,192,128]{1,2,0:T(8,128)(2,1)S(1)} collective-permute-done((bf16[2,192,128]{1,2,0:T(8,128)(2,1)S(1)}, bf16[2,192,128]{1,2,0:T(8,128)(2,1)S(1)}, u32[]{:S(2)}, u32[]{:S(2)}) %collective-permute-start.3) | collective-permute-done | bytes 98336 | tf_op jit(solution)/shard_map/ppermute | solution.py:127
  44.3 1.7 collective-permute-start.4
  46.0 3.7 %collective-permute-done.4 = bf16[1,192,128]{1,2,0:T(8,128)(2,1)S(1)} collective-permute-done((bf16[1,192,128]{1,2,0:T(8,128)(2,1)S(1)}, bf16[1,192,128]{1,2,0:T(8,128)(2,1)S(1)}, u32[]{:S(2)}, u32[]{:S(2)}) %collective-permute-start.4) | collective-permute-done | bytes 49184 | tf_op jit(solution)/shard_map/ppermute | solution.py:127
  51.5 1.5 compare_and_fusion
  53.2 5.3 %collective-permute-done.5 = bf16[5,1,192,128]{2,3,0,1:T(8,128)(2,1)S(1)} collective-permute-done((bf16[5,1,192,128]{2,3,0,1:T(8,128)(2,1)S(1)}, bf16[5,1,192,128]{2,3,0,1:T(8,128)(2,1)S(1)}, u32[]{:S(2)}, u32[]{:S(2)}) %collective-permute-start.5) | collective-permute-done | bytes 245792 | tf_op jit(solution)/shard_map/ppermute | solution.py:132
  58.8 1.0 copy.79
  60.3 1.9 fusion.66
  62.2 8.1 %collective-permute-done.6 = bf16[5,2,192,128]{3,2,1,0:T(8,128)(2,1)S(1)} collective-permute-done((bf16[5,2,192,128]{3,2,1,0:T(8,128)(2,1)}, bf16[5,2,192,128]{3,2,1,0:T(8,128)(2,1)S(1)}, u32[]{:S(2)}, u32[]{:S(2)}) %collective-permute-start.6) | collective-permute-done | bytes 491552 | tf_op jit(solution)/shard_map/ppermute | solution.py:132
  70.3 1.1 copy.80
  71.4 1.8 maximum_select_fusion.2
  73.2 1.4 copy.82
  74.6 1.6 copy.83
  76.2 3.4 %fusion = (f32[4,192]{1,0:T(4,128)S(1)}, f32[3840,192,4]{0,1,2:T(8,128)S(1)}) fusion(pred[192,3840]{1,0:T(8,128)(4,1)} %compare_and_fusion, bf16[192,4,32]{0,2,1:T(8,128)(2,1)S(1)} %get-tuple-element.37, bf16[192,4,32]{0,2,1:T(8,128)(2,1)S(1)} %get-tuple-element.36, bf16[3840,128]{0,1:T(8,128)(2,1)S(1)} %copy.83), kind=kOutput, calls=%fused_computation.2 | convolution fusion | flops 386530560 | bytes 13159424 | tf_op jit(solution)/shard_map/tkgd,skd->kgts/dot_general | solution.py:151
  79.6 1.3 collective-permute-start.7
  80.9 2.1 collective-permute-start.8
  83.1 3.3 %fusion.10 = f32[1,4,192,64]{2,3,1,0:T(8,128)S(1)} fusion(f32[3840,192,4]{0,1,2:T(8,128)S(1)} %get-tuple-element.73, f32[4,192]{1,0:T(4,128)S(1)} %broadcast_maximum_fusion, pred[192,3840]{1,0:T(8,128)(4,1)S(1)} %copy-done.2, bf16[3840,128]{0,1:T(8,128)(2,1)S(1)} %copy.83), kind=kOutput, calls=%fused_computation.22 | convolution fusion | flops 392232960 | bytes 13225984 | tf_op jit(solution)/shard_map/kgts,skd->kgtd/dot_general | solution.py:162
  86.3 3.8 %fusion.1 = f32[4,192]{1,0:T(4,128)S(1)} fusion(f32[3840,192,4]{0,1,2:T(8,128)S(1)} %get-tuple-element.73, f32[4,192]{1,0:T(4,128)S(1)} %broadcast_maximum_fusion, pred[192,3840]{1,0:T(8,128)(4,1)S(1)} %copy-done.2), kind=kLoop, calls=%fused_computation.3 | loop fusion | flops 14744832 | bytes 12539904 | tf_op jit(solution)/shard_map/reduce_sum | solution.py:161
  90.1 7.6 %collective-permute-done.7 = bf16[2064,208]{0,1:T(8,128)(2,1)} collective-permute-done((bf16[2064,208]{0,1:T(8,128)(2,1)}, bf16[2064,208]{0,1:T(8,128)(2,1)}, u32[]{:S(2)}, u32[]{:S(2)}) %collective-permute-start.7) | collective-permute-done | bytes 858656 | tf_op jit(solution)/shard_map/ppermute | solution.py:138
  98.7 2.4 %collective-permute-done.11 = f32[2,2,24,2048]{3,2,1,0:T(8,128)} collective-permute-done((f32[2,2,24,2048]{3,2,1,0:T(8,128)S(1)}, f32[2,2,24,2048]{3,2,1,0:T(8,128)}, u32[]{:S(2)}, u32[]{:S(2)}) %collective-permute-start.11) | collective-permute-done | bytes 786464 | tf_op jit(solution)/shard_map/ppermute | solution.py:197
  101.1 1.3 fusion.17
  103.1 1.5 collective-permute-start.12
  104.7 1.3 convert_element_type.46
  106.0 3.0 %collective-permute-start.10 = (bf16[2064,208]{0,1:T(8,128)(2,1)}, bf16[2064,208]{0,1:T(8,128)(2,1)S(1)}, u32[]{:S(2)}, u32[]{:S(2)}) collective-permute-start(bf16[2064,208]{0,1:T(8,128)(2,1)} %collective-permute-done.8), channel_id=1, source_target_pairs={{0,28},{4,0},{8,4},{12,8},{16,12},{20,16},{24,20},{28,24},{1,29},{... | collective-permute-start | bytes 2575880 | tf_op jit(solution)/shard_map/ppermute | solution.py:173
  109.0 5.6 %collective-permute-done.12 = f32[2,24,2048]{2,1,0:T(8,128)} collective-permute-done((f32[2,24,2048]{2,1,0:T(8,128)}, f32[2,24,2048]{2,1,0:T(8,128)}, u32[]{:S(2)}, u32[]{:S(2)}) %collective-permute-start.12) | collective-permute-done | bytes 393248 | tf_op jit(solution)/shard_map/ppermute | solution.py:197
  114.6 1.1 fusion.21
  115.7 3.1 %collective-permute-start.13 = (f32[24,2048]{1,0:T(8,128)S(1)}, f32[24,2048]{1,0:T(8,128)S(1)}, u32[]{:S(2)}, u32[]{:S(2)}) collective-permute-start(f32[24,2048]{1,0:T(8,128)S(1)} %select_bitcast_fusion.2), channel_id=1, source_target_pairs={{0,128},{32,160},{64,192},{96,224},{128,0},{160,32},{192,64},{224,... | collective-permute-start | bytes 589832 | tf_op jit(solution)/shard_map/ppermute | solution.py:197
  118.8 4.5 %collective-permute-done.13 = f32[24,2048]{1,0:T(8,128)S(1)} collective-permute-done((f32[24,2048]{1,0:T(8,128)S(1)}, f32[24,2048]{1,0:T(8,128)S(1)}, u32[]{:S(2)}, u32[]{:S(2)}) %collective-permute-start.13) | collective-permute-done | bytes 196640 | tf_op jit(solution)/shard_map/ppermute | solution.py:197
  123.4 5.3 %collective-permute-done.10 = bf16[2064,208]{0,1:T(8,128)(2,1)S(1)} collective-permute-done((bf16[2064,208]{0,1:T(8,128)(2,1)}, bf16[2064,208]{0,1:T(8,128)(2,1)S(1)}, u32[]{:S(2)}, u32[]{:S(2)}) %collective-permute-start.10) | collective-permute-done | bytes 858656 | tf_op jit(solution)/shard_map/ppermute | solution.py:173
  128.7 3.3 %collective-permute-done.9 = bf16[2064,208]{0,1:T(8,128)(2,1)S(1)} collective-permute-done((bf16[2064,208]{0,1:T(8,128)(2,1)}, bf16[2064,208]{0,1:T(8,128)(2,1)S(1)}, u32[]{:S(2)}, u32[]{:S(2)}) %collective-permute-start.9) | collective-permute-done | bytes 858656 | tf_op jit(solution)/shard_map/ppermute | solution.py:172
  132.9 1.6 collective-permute-start.16
  135.4 2.1 collective-permute-done.16
  137.5 2.1 collective-permute-start.17
  139.7 5.1 %collective-permute-done.17 = bf16[1,2,1,1,1,24,2048]{6,5,4,3,2,1,0:T(8,128)(2,1)S(1)} collective-permute-done((bf16[1,2,1,1,1,24,2048]{6,5,4,3,2,1,0:T(8,128)(2,1)S(1)}, bf16[1,2,1,1,1,24,2048]{6,5,4,3,2,1,0:T(8,128)(2,1)S(1)}, u32[]{:S(2)}, u32[]{:S(2)}) %collective-permute-start.17) | collective-permute-done | bytes 196640 | tf_op jit(solution)/shard_map/ppermute | solution.py:218
  144.9 3.0 %collective-permute-start.18 = (bf16[2,2,1,1,1,24,2048]{6,5,4,3,2,1,0:T(8,128)(2,1)S(1)}, bf16[2,2,1,1,1,24,2048]{6,5,4,3,2,1,0:T(8,128)(2,1)S(1)}, u32[]{:S(2)}, u32[]{:S(2)}) collective-permute-start(bf16[2,2,1,1,1,24,2048]{6,5,4,3,2,1,0:T(8,128)(2,1)S(1)} %fusion.19), channel_id=1, source_target_pairs={{0,128},{32,160},{64,192},{96,224},{128,0},{160,32},{192,64},{224,... | collective-permute-start | bytes 1179656 | tf_op jit(solution)/shard_map/ppermute | solution.py:218
  147.9 2.2 constant_dynamic-update-slice_fusion.5
  150.2 5.4 %collective-permute-done.18 = bf16[2,2,1,1,1,24,2048]{6,5,4,3,2,1,0:T(8,128)(2,1)S(1)} collective-permute-done((bf16[2,2,1,1,1,24,2048]{6,5,4,3,2,1,0:T(8,128)(2,1)S(1)}, bf16[2,2,1,1,1,24,2048]{6,5,4,3,2,1,0:T(8,128)(2,1)S(1)}, u32[]{:S(2)}, u32[]{:S(2)}) %collective-permute-start.18) | collective-permute-done | bytes 393248 | tf_op jit(solution)/shard_map/ppermute | solution.py:218
  156.0 2.3 %constant_dynamic-update-slice_fusion.4 = bf16[2064,1664]{0,1:T(8,128)(2,1)} fusion(bf16[2064,1664]{0,1:T(8,128)(2,1)} %constant_dynamic-update-slice_fusion.5, bf16[2064,208]{0,1:T(8,128)(2,1)} %collective-permute-done.1), kind=kLoop, calls=%fused_computation.83 | loop fusion | bytes 1810432
  158.2 2.2 constant_dynamic-update-slice_fusion.3
  160.5 10.2 %collective-permute-done.19 = bf16[2,2,2,1,1,24,2048]{6,5,4,3,2,1,0:T(8,128)(2,1)S(1)} collective-permute-done((bf16[2,2,2,1,1,24,2048]{6,5,4,3,2,1,0:T(8,128)(2,1)S(1)}, bf16[2,2,2,1,1,24,2048]{6,5,4,3,2,1,0:T(8,128)(2,1)S(1)}, u32[]{:S(2)}, u32[]{:S(2)}) %collective-permute-start.19) | collective-permute-done | bytes 786464 | tf_op jit(solution)/shard_map/ppermute | solution.py:218
  171.0 2.2 constant_dynamic-update-slice_fusion.2
  173.9 1.5 collective-permute-start.14
  175.4 1.0 constant_dynamic-update-slice_fusion.1
  177.4 9.7 %collective-permute-done.14 = bf16[1024,208]{0,1:T(8,128)(2,1)S(1)} collective-permute-done((bf16[1024,208]{0,1:T(8,128)(2,1)S(1)}, bf16[1024,208]{0,1:T(8,128)(2,1)S(1)}, u32[]{:S(2)}, u32[]{:S(2)}) %collective-permute-start.14) | collective-permute-done | bytes 426016 | tf_op jit(solution)/shard_map/ppermute | solution.py:202
  188.2 1.3 compare_reduce_fusion
  189.9 10.7 %select_reduce_fusion.1 = (f32[768]{0:T(1024)S(1)}, f32[768,1664]{1,0:T(8,128)}) fusion(pred[1664]{0:T(1024)(128)(4,1)S(1)} %compare_reduce_fusion, bf16[768,2048]{1,0:T(8,128)(2,1)S(1)} %bitcast.143, bf16[2064,1664]{0,1:T(8,128)(2,1)} %maximum_dynamic-update-slice_fusion), kind=kOutput, calls=%fused_computation.15 | convolution fusion | flops 5238324224 | bytes 15078016 | tf_op jit(solution)/shard_map/dot_general | solution.py:233
  200.7 4.8 %fusion.9 = (f32[768]{0:T(1024)S(1)}, f32[768]{0:T(1024)S(1)}, f32[768]{0:T(1024)S(1)}) fusion(f32[768,1664]{1,0:T(8,128)} %get-tuple-element.75, f32[768]{0:T(1024)S(1)} %get-tuple-element.74, pred[1664]{0:T(1024)(128)(4,1)S(1)} %compare_reduce_fusion, s32[1664]{0:T(1024)S(1)} %select_n.489, s32[768]{0:T(1024)S(1)} %dynamic_slice.19), kind=kLoop, calls=%fused_computation.13 | loop fusion | flops 14055168 | bytes 5135488 | tf_op jit(solution)/shard_map/reduce_sum | solution.py:240
  205.7 2.2 collective-permute-start.21
  207.9 3.1 %collective-permute-done.21 = f32[4,2,192]{2,0,1:T(4,128)S(1)} collective-permute-done((f32[4,2,192]{2,0,1:T(4,128)S(1)}, f32[4,2,192]{2,0,1:T(4,128)S(1)}, u32[]{:S(2)}, u32[]{:S(2)}) %collective-permute-start.21) | collective-permute-done | bytes 6176 | tf_op jit(solution)/shard_map/ppermute | solution.py:246
  211.1 1.6 collective-permute-start.22
  212.7 2.1 collective-permute-done.22
  214.9 1.1 collective-permute-done.23
  216.2 1.9 collective-permute-start.24
  218.0 1.8 collective-permute-done.24
  219.9 1.9 collective-permute-start.25
  221.8 3.3 %collective-permute-done.25 = f32[4,192]{1,0:T(4,128)S(1)} collective-permute-done((f32[4,192]{1,0:T(4,128)S(1)}, f32[4,192]{1,0:T(4,128)S(1)}, u32[]{:S(2)}, u32[]{:S(2)}) %collective-permute-start.25) | collective-permute-done | bytes 3104 | tf_op jit(solution)/shard_map/ppermute | solution.py:259
  (114 shorter events, 17.4 us)
Async XLA Ops:
  0.6 97.4 %copy-start = (bf16[256,2048]{1,0:T(8,128)(2,1)S(1)}, bf16[256,2048]{1,0:T(8,128)(2,1)}, u32[]{:S(2)}) copy-start(bf16[256,2048]{1,0:T(8,128)(2,1)} %param.17) | copy-start | bytes 3145732
  0.6 11.4 %copy-start.7 = (bf16[2048,193]{0,1:T(8,128)(2,1)S(1)}, bf16[2048,193]{0,1:T(8,128)(2,1)}, u32[]{:S(2)}) copy-start(bf16[2048,193]{0,1:T(8,128)(2,1)} %param.19) | copy-start | bytes 2371588
  5.5 54.8 %copy-start.1 = (bf16[192,2048]{1,0:T(8,128)(2,1)S(1)}, bf16[192,2048]{1,0:T(8,128)(2,1)}, u32[]{:S(2)}) copy-start(bf16[192,2048]{1,0:T(8,128)(2,1)} %param.12) | copy-start | bytes 2359300
  5.5 54.8 %copy-start.10 = (f32[2048]{0:T(1024)S(1)}, f32[2048]{0:T(1024)}, u32[]{:S(2)}) copy-start(f32[2048]{0:T(1024)} %param.13) | copy-start | bytes 24580
  8.1 10.5 %collective-permute-start.2 = (bf16[1,192,128]{1,2,0:T(8,128)(2,1)}, bf16[1,192,128]{1,2,0:T(8,128)(2,1)}, u32[]{:S(2)}, u32[]{:S(2)}) collective-permute-start(bf16[1,192,128]{1,2,0:T(8,128)(2,1)} %maximum_bitcast_fusion.2), channel_id=1, source_target_pairs={{0,4},{4,8},{8,12},{12,16},{16,20},{20,24},{24,28},{28,0},{1,5},{5... | collective-permute-start | bytes 147464 | tf_op jit(solution)/shard_map/ppermute | solution.py:127
  14.6 60.0 %collective-permute-start = (bf16[2064,208]{0,1:T(8,128)(2,1)}, bf16[2064,208]{0,1:T(8,128)(2,1)}, u32[]{:S(2)}, u32[]{:S(2)}) collective-permute-start(bf16[2064,208]{0,1:T(8,128)(2,1)} %get-tuple-element.32), channel_id=1, source_target_pairs={{0,4},{4,8},{8,12},{12,16},{16,20},{20,24},{24,28},{28,0},{1,5},{5... | collective-permute-start | bytes 2575880 | tf_op jit(solution)/shard_map/ppermute | solution.py:88
  16.6 58.0 %collective-permute-start.1 = (bf16[2064,208]{0,1:T(8,128)(2,1)}, bf16[2064,208]{0,1:T(8,128)(2,1)}, u32[]{:S(2)}, u32[]{:S(2)}) collective-permute-start(bf16[2064,208]{0,1:T(8,128)(2,1)} %get-tuple-element.32), channel_id=1, source_target_pairs={{0,28},{4,0},{8,4},{12,8},{16,12},{20,16},{24,20},{28,24},{1,29},{... | collective-permute-start | bytes 2575880 | tf_op jit(solution)/shard_map/ppermute | solution.py:89
  19.5 24.8 %collective-permute-start.3 = (bf16[2,192,128]{1,2,0:T(8,128)(2,1)S(1)}, bf16[2,192,128]{1,2,0:T(8,128)(2,1)S(1)}, u32[]{:S(2)}, u32[]{:S(2)}) collective-permute-start(bf16[2,192,128]{1,2,0:T(8,128)(2,1)S(1)} %pad_maximum_fusion.1), channel_id=1, source_target_pairs={{0,8},{4,12},{8,16},{12,20},{16,24},{20,28},{24,0},{28,4},{1,9},{5... | collective-permute-start | bytes 294920 | tf_op jit(solution)/shard_map/ppermute | solution.py:127
  44.3 5.5 %collective-permute-start.4 = (bf16[1,192,128]{1,2,0:T(8,128)(2,1)S(1)}, bf16[1,192,128]{1,2,0:T(8,128)(2,1)S(1)}, u32[]{:S(2)}, u32[]{:S(2)}) collective-permute-start(bf16[1,192,128]{1,2,0:T(8,128)(2,1)S(1)} %slice.250), channel_id=1, source_target_pairs={{0,4},{4,8},{8,12},{12,16},{16,20},{20,24},{24,28},{28,0},{1,5},{5... | collective-permute-start | bytes 147464 | tf_op jit(solution)/shard_map/ppermute | solution.py:127
  50.7 7.9 %collective-permute-start.5 = (bf16[5,1,192,128]{2,3,0,1:T(8,128)(2,1)S(1)}, bf16[5,1,192,128]{2,3,0,1:T(8,128)(2,1)S(1)}, u32[]{:S(2)}, u32[]{:S(2)}) collective-permute-start(bf16[5,1,192,128]{2,3,0,1:T(8,128)(2,1)S(1)} %maximum_bitcast_fusion.1), channel_id=1, source_target_pairs={{0,1},{1,0},{2,3},{3,2},{4,5},{5,4},{6,7},{7,6},{8,9},{9,8},{10,11... | collective-permute-start | bytes 737288 | tf_op jit(solution)/shard_map/ppermute | solution.py:132
  59.8 10.5 %collective-permute-start.6 = (bf16[5,2,192,128]{3,2,1,0:T(8,128)(2,1)}, bf16[5,2,192,128]{3,2,1,0:T(8,128)(2,1)S(1)}, u32[]{:S(2)}, u32[]{:S(2)}) collective-permute-start(bf16[5,2,192,128]{3,2,1,0:T(8,128)(2,1)} %copy.79), channel_id=1, source_target_pairs={{0,2},{1,3},{2,0},{3,1},{4,6},{5,7},{6,4},{7,5},{8,10},{9,11},{10,... | collective-permute-start | bytes 1474568 | tf_op jit(solution)/shard_map/ppermute | solution.py:132
  76.2 6.9 %copy-start.2 = (pred[192,3840]{1,0:T(8,128)(4,1)S(1)}, pred[192,3840]{1,0:T(8,128)(4,1)}, u32[]{:S(2)}) copy-start(pred[192,3840]{1,0:T(8,128)(4,1)} %compare_and_fusion) | copy-start | bytes 2211844
  79.6 18.1 %collective-permute-start.7 = (bf16[2064,208]{0,1:T(8,128)(2,1)}, bf16[2064,208]{0,1:T(8,128)(2,1)}, u32[]{:S(2)}, u32[]{:S(2)}) collective-permute-start(bf16[2064,208]{0,1:T(8,128)(2,1)} %collective-permute-done), channel_id=1, source_target_pairs={{0,4},{4,8},{8,12},{12,16},{16,20},{20,24},{24,28},{28,0},{1,5},{5... | collective-permute-start | bytes 2575880 | tf_op jit(solution)/shard_map/ppermute | solution.py:138
  80.9 16.8 %collective-permute-start.8 = (bf16[2064,208]{0,1:T(8,128)(2,1)}, bf16[2064,208]{0,1:T(8,128)(2,1)}, u32[]{:S(2)}, u32[]{:S(2)}) collective-permute-start(bf16[2064,208]{0,1:T(8,128)(2,1)} %collective-permute-done.1), channel_id=1, source_target_pairs={{0,28},{4,0},{8,4},{12,8},{16,12},{20,16},{24,20},{28,24},{1,29},{... | collective-permute-start | bytes 2575880 | tf_op jit(solution)/shard_map/ppermute | solution.py:139
  98.5 20.3 %copy-start.9 = (s32[8]{0:T(128)S(1)}, s32[8]{0:T(128)}, u32[]{:S(2)}) copy-start(s32[8]{0:T(128)} %constant.190.clone) | copy-start | bytes 100
  98.6 33.6 %copy-start.8 = (f32[2048]{0:T(1024)S(1)}, f32[2048]{0:T(1024)}, u32[]{:S(2)}) copy-start(f32[2048]{0:T(1024)} %param.18) | copy-start | bytes 24580
  98.6 2.5 %collective-permute-start.11 = (f32[2,2,24,2048]{3,2,1,0:T(8,128)S(1)}, f32[2,2,24,2048]{3,2,1,0:T(8,128)}, u32[]{:S(2)}, u32[]{:S(2)}) collective-permute-start(f32[2,2,24,2048]{3,2,1,0:T(8,128)S(1)} %select_bitcast_fusion), channel_id=1, source_target_pairs={{0,32},{32,0},{64,96},{96,64},{128,160},{160,128},{192,224},{224,1... | collective-permute-start | bytes 2359304 | tf_op jit(solution)/shard_map/ppermute | solution.py:197
  103.1 11.5 %collective-permute-start.12 = (f32[2,24,2048]{2,1,0:T(8,128)}, f32[2,24,2048]{2,1,0:T(8,128)}, u32[]{:S(2)}, u32[]{:S(2)}) collective-permute-start(f32[2,24,2048]{2,1,0:T(8,128)} %select_bitcast_fusion.1), channel_id=1, source_target_pairs={{0,64},{32,96},{64,0},{96,32},{128,192},{160,224},{192,128},{224,1... | collective-permute-start | bytes 1179656 | tf_op jit(solution)/shard_map/ppermute | solution.py:197
  106.0 22.7 %collective-permute-start.10 = (bf16[2064,208]{0,1:T(8,128)(2,1)}, bf16[2064,208]{0,1:T(8,128)(2,1)S(1)}, u32[]{:S(2)}, u32[]{:S(2)}) collective-permute-start(bf16[2064,208]{0,1:T(8,128)(2,1)} %collective-permute-done.8), channel_id=1, source_target_pairs={{0,28},{4,0},{8,4},{12,8},{16,12},{20,16},{24,20},{28,24},{1,29},{... | collective-permute-start | bytes 2575880 | tf_op jit(solution)/shard_map/ppermute | solution.py:173
  109.0 23.0 %collective-permute-start.9 = (bf16[2064,208]{0,1:T(8,128)(2,1)}, bf16[2064,208]{0,1:T(8,128)(2,1)S(1)}, u32[]{:S(2)}, u32[]{:S(2)}) collective-permute-start(bf16[2064,208]{0,1:T(8,128)(2,1)} %collective-permute-done.7), channel_id=1, source_target_pairs={{0,4},{4,8},{8,12},{12,16},{16,20},{20,24},{24,28},{28,0},{1,5},{5... | collective-permute-start | bytes 2575880 | tf_op jit(solution)/shard_map/ppermute | solution.py:172
  115.7 7.7 %collective-permute-start.13 = (f32[24,2048]{1,0:T(8,128)S(1)}, f32[24,2048]{1,0:T(8,128)S(1)}, u32[]{:S(2)}, u32[]{:S(2)}) collective-permute-start(f32[24,2048]{1,0:T(8,128)S(1)} %select_bitcast_fusion.2), channel_id=1, source_target_pairs={{0,128},{32,160},{64,192},{96,224},{128,0},{160,32},{192,64},{224,... | collective-permute-start | bytes 589832 | tf_op jit(solution)/shard_map/ppermute | solution.py:197
  128.7 3.6 %copy-start.3 = (bf16[2064,208]{0,1:T(8,128)(2,1)}, bf16[2064,208]{0,1:T(8,128)(2,1)S(1)}, u32[]{:S(2)}) copy-start(bf16[2064,208]{0,1:T(8,128)(2,1)S(1)} %collective-permute-done.10) | copy-start | bytes 2575876
  132.0 0.9 copy-start.5
  132.9 4.6 %collective-permute-start.16 = (bf16[1,1,1,1,1,24,2048]{6,5,4,3,2,1,0:T(8,128)(2,1)S(1)}, bf16[1,1,1,1,1,24,2048]{6,5,4,3,2,1,0:T(8,128)(2,1)S(1)}, u32[]{:S(2)}, u32[]{:S(2)}) collective-permute-start(bf16[1,1,1,1,1,24,2048]{6,5,4,3,2,1,0:T(8,128)(2,1)S(1)} %bitcast.146), channel_id=1, source_target_pairs={{0,1},{1,0},{2,3},{3,2},{4,5},{5,4},{6,7},{7,6},{8,9},{9,8},{10,11... | collective-permute-start | bytes 294920 | tf_op jit(solution)/shard_map/ppermute | solution.py:218
  137.5 7.3 %collective-permute-start.17 = (bf16[1,2,1,1,1,24,2048]{6,5,4,3,2,1,0:T(8,128)(2,1)S(1)}, bf16[1,2,1,1,1,24,2048]{6,5,4,3,2,1,0:T(8,128)(2,1)S(1)}, u32[]{:S(2)}, u32[]{:S(2)}) collective-permute-start(bf16[1,2,1,1,1,24,2048]{6,5,4,3,2,1,0:T(8,128)(2,1)S(1)} %maximum_select_fusion.8), channel_id=1, source_target_pairs={{0,2},{1,3},{2,0},{3,1},{4,6},{5,7},{6,4},{7,5},{8,10},{9,11},{10,... | collective-permute-start | bytes 589832 | tf_op jit(solution)/shard_map/ppermute | solution.py:218
  144.9 10.7 %collective-permute-start.18 = (bf16[2,2,1,1,1,24,2048]{6,5,4,3,2,1,0:T(8,128)(2,1)S(1)}, bf16[2,2,1,1,1,24,2048]{6,5,4,3,2,1,0:T(8,128)(2,1)S(1)}, u32[]{:S(2)}, u32[]{:S(2)}) collective-permute-start(bf16[2,2,1,1,1,24,2048]{6,5,4,3,2,1,0:T(8,128)(2,1)S(1)} %fusion.19), channel_id=1, source_target_pairs={{0,128},{32,160},{64,192},{96,224},{128,0},{160,32},{192,64},{224,... | collective-permute-start | bytes 1179656 | tf_op jit(solution)/shard_map/ppermute | solution.py:218
  155.8 17.3 %copy-start.4 = (bf16[2064,208]{0,1:T(8,128)(2,1)S(1)}, bf16[2064,208]{0,1:T(8,128)(2,1)}, u32[]{:S(2)}) copy-start(bf16[2064,208]{0,1:T(8,128)(2,1)} %copy-done.3) | copy-start | bytes 2575876
  155.9 18.0 %copy-start.6 = (bf16[2064,208]{0,1:T(8,128)(2,1)S(1)}, bf16[2064,208]{0,1:T(8,128)(2,1)}, u32[]{:S(2)}) copy-start(bf16[2064,208]{0,1:T(8,128)(2,1)} %copy-done.5) | copy-start | bytes 2575876
  155.9 14.9 %collective-permute-start.19 = (bf16[2,2,2,1,1,24,2048]{6,5,4,3,2,1,0:T(8,128)(2,1)S(1)}, bf16[2,2,2,1,1,24,2048]{6,5,4,3,2,1,0:T(8,128)(2,1)S(1)}, u32[]{:S(2)}, u32[]{:S(2)}) collective-permute-start(bf16[2,2,2,1,1,24,2048]{6,5,4,3,2,1,0:T(8,128)(2,1)S(1)} %maximum_select_fusion.4), channel_id=1, source_target_pairs={{0,64},{32,96},{64,0},{96,32},{128,192},{160,224},{192,128},{224,1... | collective-permute-start | bytes 2359304 | tf_op jit(solution)/shard_map/ppermute | solution.py:218
  170.9 18.6 %collective-permute-start.20 = (bf16[2,2,2,2,1,24,2048]{6,5,4,3,2,1,0:T(8,128)(2,1)S(1)}, bf16[2,2,2,2,1,24,2048]{6,5,4,3,2,1,0:T(8,128)(2,1)S(1)}, u32[]{:S(2)}, u32[]{:S(2)}) collective-permute-start(bf16[2,2,2,2,1,24,2048]{6,5,4,3,2,1,0:T(8,128)(2,1)S(1)} %maximum_select_fusion.1), channel_id=1, source_target_pairs={{0,32},{32,0},{64,96},{96,64},{128,160},{160,128},{192,224},{224,1... | collective-permute-start | bytes 4718600 | tf_op jit(solution)/shard_map/ppermute | solution.py:218
  173.2 14.0 %collective-permute-start.15 = (bf16[1040,208]{0,1:T(8,128)(2,1)S(1)}, bf16[1040,208]{0,1:T(8,128)(2,1)S(1)}, u32[]{:S(2)}, u32[]{:S(2)}) collective-permute-start(bf16[1040,208]{0,1:T(8,128)(2,1)S(1)} %slice.205), channel_id=1, source_target_pairs={{0,28},{4,0},{8,4},{12,8},{16,12},{20,16},{24,20},{28,24},{1,29},{... | collective-permute-start | bytes 1297928 | tf_op jit(solution)/shard_map/ppermute | solution.py:203
  173.9 13.2 %collective-permute-start.14 = (bf16[1024,208]{0,1:T(8,128)(2,1)S(1)}, bf16[1024,208]{0,1:T(8,128)(2,1)S(1)}, u32[]{:S(2)}, u32[]{:S(2)}) collective-permute-start(bf16[1024,208]{0,1:T(8,128)(2,1)S(1)} %slice.204), channel_id=1, source_target_pairs={{0,4},{4,8},{8,12},{12,16},{16,20},{20,24},{24,28},{28,0},{1,5},{5... | collective-permute-start | bytes 1277960 | tf_op jit(solution)/shard_map/ppermute | solution.py:202
  205.7 5.2 %collective-permute-start.21 = (f32[4,2,192]{2,0,1:T(4,128)S(1)}, f32[4,2,192]{2,0,1:T(4,128)S(1)}, u32[]{:S(2)}, u32[]{:S(2)}) collective-permute-start(f32[4,2,192]{2,0,1:T(4,128)S(1)} %constant_dynamic-slice_fusion.1), channel_id=1, source_target_pairs={{0,2},{1,3},{2,0},{3,1},{4,6},{5,7},{6,4},{7,5},{8,10},{9,11},{10,... | collective-permute-start | bytes 18440 | tf_op jit(solution)/shard_map/ppermute | solution.py:246
  211.1 3.7 %collective-permute-start.22 = (f32[4,1,192]{2,0,1:T(4,128)S(1)}, f32[4,1,192]{2,0,1:T(4,128)S(1)}, u32[]{:S(2)}, u32[]{:S(2)}) collective-permute-start(f32[4,1,192]{2,0,1:T(4,128)S(1)} %constant_dynamic-slice_fusion), channel_id=1, source_target_pairs={{0,1},{1,0},{2,3},{3,2},{4,5},{5,4},{6,7},{7,6},{8,9},{9,8},{10,11... | collective-permute-start | bytes 9224 | tf_op jit(solution)/shard_map/ppermute | solution.py:254
  214.8 1.3 collective-permute-start.23
  216.2 3.7 %collective-permute-start.24 = (f32[4,192]{1,0:T(4,128)S(1)}, f32[4,192]{1,0:T(4,128)S(1)}, u32[]{:S(2)}, u32[]{:S(2)}) collective-permute-start(f32[4,192]{1,0:T(4,128)S(1)} %pad_maximum_fusion.4), channel_id=1, source_target_pairs={{0,64},{32,96},{64,0},{96,32},{128,192},{160,224},{192,128},{224,1... | collective-permute-start | bytes 9224 | tf_op jit(solution)/shard_map/ppermute | solution.py:259
  219.9 5.2 %collective-permute-start.25 = (f32[4,192]{1,0:T(4,128)S(1)}, f32[4,192]{1,0:T(4,128)S(1)}, u32[]{:S(2)}, u32[]{:S(2)}) collective-permute-start(f32[4,192]{1,0:T(4,128)S(1)} %pad_maximum_fusion.5), channel_id=1, source_target_pairs={{0,128},{32,160},{64,192},{96,224},{128,0},{160,32},{192,64},{224,... | collective-permute-start | bytes 9224 | tf_op jit(solution)/shard_map/ppermute | solution.py:259

commit v13 on v10

--- a/solution.py
+++ b/solution.py
@@ -112,6 +112,11 @@
         need = min(held.shape[0], back + 1 - held.shape[0])
         got = lax.ppermute(held[:need], "z", [(p, (p + need) % z_count) for p in range(z_count)])
         held = jnp.concatenate([got, held], axis=0)
+    padded_local = -(-w_head.shape[1] // 16) * 16
+    head_pad = jnp.zeros((16 - 1, w_head.shape[1]), w_head.dtype)
+    head_ext = jnp.concatenate([w_head, vocab_mask.astype(w_head.dtype)[None, :], head_pad], axis=0)
+    head_ext = jnp.pad(head_ext, ((0, 0), (0, padded_local - w_head.shape[1])))
+    held, head_ext = lax.optimization_barrier((held, head_ext))
     held = held[:, None]
     for bit in range(y_bits):
         mine_low = (y_pos >> bit) % 2 == 0
@@ -190,10 +195,6 @@
         )
     head_rows = head_rows.reshape(-1, final_part.shape[1])
     group_rows = head_rows.shape[0]
-    padded_local = -(-vocab_local // 16) * 16
-    head_pad = jnp.zeros((16 - 1, vocab_local), w_head.dtype)
-    head_ext = jnp.concatenate([w_head, vocab_mask.astype(w_head.dtype)[None, :], head_pad], axis=0)
-    head_ext = jnp.pad(head_ext, ((0, 0), (0, padded_local - vocab_local)))
     head_ext = lax.all_gather(head_ext, "z", axis=1, tiled=True)
     head_cols = head_ext[: w_head.shape[0]]
     mask_cols = head_ext[w_head.shape[0]]

time: 192 us -> 190 us (0.990)
  waiting for transfers between devices: 104 us -> 101 us
where the time goes in v13:
time: 190 us; the launch traced here: 189 us
  waiting for transfers between devices  101 us (53%)
  other arithmetic  24.8 us (13%)
  matrix products  24.1 us (13%)
  starting transfers between devices  16.5 us (9%)
  between operations  14.7 us (8%)
  local copies, waits for them, and re-layouts  7.92 us (4%)
    ppermute x5, waiting for transfers between devices, local(): lax.ppermute(head_rows, name, [(p, p ^ 1 << bit) for p in range(count)])  36.5 us
    ppermute x3, waiting for transfers between devices, local(): lax.ppermute(held[:need], 'z', [(p, (p + need) % z_count) for p in range(...  18.4 us
    ppermute x2, waiting for transfers between devices, local(): got = lax.ppermute(held, 'y', [(p, p ^ 1 << bit) for p in range(y_count)])  15.6 us
    ppermute x3, waiting for transfers between devices, local(): got = lax.ppermute(send, 'kv', [(p, p ^ 1 << bit) for p in range(kv_count)])  15.4 us
    dot_general x1, matrix products, local(): jnp.dot(head_rows, head_cols, preferred_element_type=jnp.float32)  11.2 us
    ppermute x3, waiting for transfers between devices, local(): got = lax.ppermute(merged, 'kv', [(p, p ^ step) for p in range(kv_count)])  6.64 us
    ppermute x1, waiting for transfers between devices, local(): got = lax.ppermute(send, 'y', [(p, p ^ half) for p in range(y_count)])  5.12 us
    ppermute x5, starting transfers between devices, local(): lax.ppermute(head_rows, name, [(p, p ^ 1 << bit) for p in range(count)])  5.09 us
  transfers between devices with their start and end apart: 19, of which 18 were waited for; matrix products, arithmetic and copies ran while one was open for 16% of the time, Pallas kernels for 0%

profile of v13, /device:TPU:24, one launch (start us, length us, event | category | flops | bytes accessed | tf_op | source)
XLA Modules:
  0.0 189.2 jit_solution(7111902788610342509)
XLA Ops:
  7.3 0.9 copy.76
  8.2 0.1 reduce.2
  8.3 0.7 sub.117
  9.1 1.4 multiply_reduce_fusion.1
  10.5 1.6 convolution_bitcast_fusion
  12.1 1.6 convolution_convert_fusion
  13.8 0.2 fusion.42
  14.0 2.0 %collective-permute-start = (bf16[1,192,128]{1,2,0:T(8,128)(2,1)S(1)}, bf16[1,192,128]{1,2,0:T(8,128)(2,1)S(1)}, u32[]{:S(2)}, u32[]{:S(2)}) collective-permute-start(bf16[1,192,128]{1,2,0:T(8,128)(2,1)S(1)} %maximum_bitcast_fusion.1), channel_id=1, source_target_pairs={{0,4},{4,8},{8,12},{12,16},{16,20},{20,24},{24,28},{28,0},{1,5},{5... | collective-permute-start | bytes 147464 | tf_op jit(solution)/shard_map/ppermute | solution.py:113
  16.0 6.2 %collective-permute-done = bf16[1,192,128]{1,2,0:T(8,128)(2,1)S(1)} collective-permute-done((bf16[1,192,128]{1,2,0:T(8,128)(2,1)S(1)}, bf16[1,192,128]{1,2,0:T(8,128)(2,1)S(1)}, u32[]{:S(2)}, u32[]{:S(2)}) %collective-permute-start) | collective-permute-done | bytes 49184 | tf_op jit(solution)/shard_map/ppermute | solution.py:113
  22.3 8.7 %collective-permute-done.1 = bf16[2,192,128]{1,2,0:T(8,128)(2,1)S(1)} collective-permute-done((bf16[2,192,128]{1,2,0:T(8,128)(2,1)S(1)}, bf16[2,192,128]{1,2,0:T(8,128)(2,1)S(1)}, u32[]{:S(2)}, u32[]{:S(2)}) %collective-permute-start.1) | collective-permute-done | bytes 98336 | tf_op jit(solution)/shard_map/ppermute | solution.py:113
  31.1 0.1 broadcast_in_dim.119
  31.3 0.7 concatenate.309
  32.0 1.0 pad.4
  33.1 3.5 %collective-permute-done.2 = bf16[1,192,128]{1,2,0:T(8,128)(2,1)S(1)} collective-permute-done((bf16[1,192,128]{1,2,0:T(8,128)(2,1)S(1)}, bf16[1,192,128]{1,2,0:T(8,128)(2,1)S(1)}, u32[]{:S(2)}, u32[]{:S(2)}) %collective-permute-start.2) | collective-permute-done | bytes 49184 | tf_op jit(solution)/shard_map/ppermute | solution.py:113
  36.6 0.8 collective-permute-start.3
  37.4 1.5 compare_and_fusion
  39.0 0.2 multiply_cosine_fusion
  39.2 7.0 %collective-permute-done.3 = bf16[5,1,192,128]{2,3,0,1:T(8,128)(2,1)S(1)} collective-permute-done((bf16[5,1,192,128]{2,3,0,1:T(8,128)(2,1)S(1)}, bf16[5,1,192,128]{2,3,0,1:T(8,128)(2,1)S(1)}, u32[]{:S(2)}, u32[]{:S(2)}) %collective-permute-start.3) | collective-permute-done | bytes 245792 | tf_op jit(solution)/shard_map/ppermute | solution.py:123
  46.2 0.2 maximum_select_fusion.5
  46.4 1.0 copy.78
  47.4 1.9 fusion.70
  49.4 8.6 %collective-permute-done.4 = bf16[5,2,192,128]{3,2,1,0:T(8,128)(2,1)S(1)} collective-permute-done((bf16[5,2,192,128]{3,2,1,0:T(8,128)(2,1)}, bf16[5,2,192,128]{3,2,1,0:T(8,128)(2,1)S(1)}, u32[]{:S(2)}, u32[]{:S(2)}) %collective-permute-start.4) | collective-permute-done | bytes 491552 | tf_op jit(solution)/shard_map/ppermute | solution.py:123
  58.0 1.1 copy.79
  59.1 1.9 maximum_select_fusion.2
  61.0 1.4 copy.81
  62.4 4.1 %fusion = (f32[4,192]{1,0:T(4,128)S(1)}, f32[3840,192,4]{0,1,2:T(8,128)S(1)}) fusion(pred[192,3840]{1,0:T(8,128)(4,1)} %compare_and_fusion, bf16[192,4,32]{0,2,1:T(8,128)(2,1)S(1)} %get-tuple-element.23, bf16[192,4,32]{0,2,1:T(8,128)(2,1)S(1)} %get-tuple-element.22, bf16[3840,128]{1,0:T(8,128)(2,1)} %bitcast.163), kind=kOutput, calls=%fused_computation.2 | convolution fusion | flops 386530560 | bytes 13618176 | tf_op jit(solution)/shard_map/tkgd,skd->kgts/dot_general | solution.py:137
  66.5 3.7 %fusion.1 = f32[4,192]{1,0:T(4,128)S(1)} fusion(f32[3840,192,4]{0,1,2:T(8,128)S(1)} %get-tuple-element.61, f32[4,192]{1,0:T(4,128)S(1)} %broadcast_maximum_fusion, pred[192,3840]{1,0:T(8,128)(4,1)S(1)} %copy-done.2), kind=kLoop, calls=%fused_computation.3 | loop fusion | flops 14744832 | bytes 12539904 | tf_op jit(solution)/shard_map/reduce_sum | solution.py:147
  70.3 3.3 %fusion.16 = bf16[192,1,4,64]{0,3,2,1:T(8,128)(2,1)S(1)} fusion(f32[3840,192,4]{0,1,2:T(8,128)S(1)} %get-tuple-element.61, f32[4,192]{1,0:T(4,128)S(1)} %broadcast_maximum_fusion, pred[192,3840]{1,0:T(8,128)(4,1)S(1)} %copy-done.2, bf16[3840,128]{1,0:T(8,128)(2,1)S(1)} %bitcast.164, f32[4,192]{1,0:T(4,128)S(1)} %fusion.1), kind=kOutput, calls=%fused_computation.26 | convolution fusion | flops 392331264 | bytes 13621248 | tf_op jit(solution)/shard_map/kgts,skd->kgtd/dot_general | solution.py:148
  73.5 0.2 copy.85
  73.7 0.2 convert_element_type.57
  73.9 0.4 fusion.19
  74.4 0.1 collective-permute-start.5
  74.5 2.4 %collective-permute-done.5 = f32[2,2,24,2048]{3,2,1,0:T(8,128)} collective-permute-done((f32[2,2,24,2048]{3,2,1,0:T(8,128)S(1)}, f32[2,2,24,2048]{3,2,1,0:T(8,128)}, u32[]{:S(2)}, u32[]{:S(2)}) %collective-permute-start.5) | collective-permute-done | bytes 786464 | tf_op jit(solution)/shard_map/ppermute | solution.py:179
  76.9 1.3 fusion.24
  78.3 1.6 collective-permute-start.6
  79.8 9.7 %collective-permute-done.6 = f32[2,24,2048]{2,1,0:T(8,128)S(1)} collective-permute-done((f32[2,24,2048]{2,1,0:T(8,128)S(1)}, f32[2,24,2048]{2,1,0:T(8,128)S(1)}, u32[]{:S(2)}, u32[]{:S(2)}) %collective-permute-start.6) | collective-permute-done | bytes 393248 | tf_op jit(solution)/shard_map/ppermute | solution.py:179
  89.6 3.1 %collective-permute-start.7 = (f32[24,2048]{1,0:T(8,128)S(1)}, f32[24,2048]{1,0:T(8,128)S(1)}, u32[]{:S(2)}, u32[]{:S(2)}) collective-permute-start(f32[24,2048]{1,0:T(8,128)S(1)} %select_bitcast_fusion.2), channel_id=1, source_target_pairs={{0,128},{32,160},{64,192},{96,224},{128,0},{160,32},{192,64},{224,... | collective-permute-start | bytes 589832 | tf_op jit(solution)/shard_map/ppermute | solution.py:179
  92.7 1.3 convert_element_type.48
  94.0 3.4 %collective-permute-done.7 = f32[24,2048]{1,0:T(8,128)S(1)} collective-permute-done((f32[24,2048]{1,0:T(8,128)S(1)}, f32[24,2048]{1,0:T(8,128)S(1)}, u32[]{:S(2)}, u32[]{:S(2)}) %collective-permute-start.7) | collective-permute-done | bytes 196640 | tf_op jit(solution)/shard_map/ppermute | solution.py:179
  97.3 0.2 multiply_reduce_fusion.2
  97.7 5.6 %collective-permute-done.8 = bf16[1,1,1,1,1,24,2048]{6,5,4,3,2,1,0:T(8,128)(2,1)S(1)} collective-permute-done((bf16[1,1,1,1,1,24,2048]{6,5,4,3,2,1,0:T(8,128)(2,1)S(1)}, bf16[1,1,1,1,1,24,2048]{6,5,4,3,2,1,0:T(8,128)(2,1)S(1)}, u32[]{:S(2)}, u32[]{:S(2)}) %collective-permute-start.8) | collective-permute-done | bytes 98336 | tf_op jit(solution)/shard_map/ppermute | solution.py:190
  103.5 7.1 %collective-permute-done.9 = bf16[1,2,1,1,1,24,2048]{6,5,4,3,2,1,0:T(8,128)(2,1)S(1)} collective-permute-done((bf16[1,2,1,1,1,24,2048]{6,5,4,3,2,1,0:T(8,128)(2,1)S(1)}, bf16[1,2,1,1,1,24,2048]{6,5,4,3,2,1,0:T(8,128)(2,1)S(1)}, u32[]{:S(2)}, u32[]{:S(2)}) %collective-permute-start.9) | collective-permute-done | bytes 196640 | tf_op jit(solution)/shard_map/ppermute | solution.py:190
  110.7 3.2 %collective-permute-start.10 = (bf16[2,2,1,1,1,24,2048]{6,5,4,3,2,1,0:T(8,128)(2,1)S(1)}, bf16[2,2,1,1,1,24,2048]{6,5,4,3,2,1,0:T(8,128)(2,1)S(1)}, u32[]{:S(2)}, u32[]{:S(2)}) collective-permute-start(bf16[2,2,1,1,1,24,2048]{6,5,4,3,2,1,0:T(8,128)(2,1)S(1)} %fusion.25), channel_id=1, source_target_pairs={{0,128},{32,160},{64,192},{96,224},{128,0},{160,32},{192,64},{224,... | collective-permute-start | bytes 1179656 | tf_op jit(solution)/shard_map/ppermute | solution.py:190
  114.0 7.1 %collective-permute-done.10 = bf16[2,2,1,1,1,24,2048]{6,5,4,3,2,1,0:T(8,128)(2,1)S(1)} collective-permute-done((bf16[2,2,1,1,1,24,2048]{6,5,4,3,2,1,0:T(8,128)(2,1)S(1)}, bf16[2,2,1,1,1,24,2048]{6,5,4,3,2,1,0:T(8,128)(2,1)S(1)}, u32[]{:S(2)}, u32[]{:S(2)}) %collective-permute-start.10) | collective-permute-done | bytes 393248 | tf_op jit(solution)/shard_map/ppermute | solution.py:190
  121.1 0.3 maximum_select_fusion.4
  121.4 1.6 collective-permute-start.11
  123.0 14.2 %collective-permute-done.11 = bf16[2,2,2,1,1,24,2048]{6,5,4,3,2,1,0:T(8,128)(2,1)S(1)} collective-permute-done((bf16[2,2,2,1,1,24,2048]{6,5,4,3,2,1,0:T(8,128)(2,1)S(1)}, bf16[2,2,2,1,1,24,2048]{6,5,4,3,2,1,0:T(8,128)(2,1)S(1)}, u32[]{:S(2)}, u32[]{:S(2)}) %collective-permute-start.11) | collective-permute-done | bytes 786464 | tf_op jit(solution)/shard_map/ppermute | solution.py:190
  137.2 0.1 maximum_select_fusion.1
  137.3 0.1 collective-permute-start.12
  137.7 0.8 dynamic_slice.19
  138.4 2.5 %collective-permute-done.12 = bf16[2,2,2,2,1,24,2048]{6,5,4,3,2,1,0:T(8,128)(2,1)} collective-permute-done((bf16[2,2,2,2,1,24,2048]{6,5,4,3,2,1,0:T(8,128)(2,1)S(1)}, bf16[2,2,2,2,1,24,2048]{6,5,4,3,2,1,0:T(8,128)(2,1)}, u32[]{:S(2)}, u32[]{:S(2)}) %collective-permute-start.12) | collective-permute-done | bytes 1572896 | tf_op jit(solution)/shard_map/ppermute | solution.py:190
  141.0 3.7 %maximum_select_fusion = bf16[2,2,2,2,2,24,2048]{6,5,4,3,2,1,0:T(8,128)(2,1)} fusion(bf16[2,2,2,2,1,24,2048]{6,5,4,3,2,1,0:T(8,128)(2,1)} %collective-permute-done.12, bf16[2,2,2,2,1,24,2048]{6,5,4,3,2,1,0:T(8,128)(2,1)S(1)} %maximum_select_fusion.1, pred[]{:T(512)S(6)} %eq.79), kind=kLoop, calls=%fused_computation.16 | loop fusion | flops 4718592 | bytes 6291457 | tf_op jit(solution)/shard_map/jit(_where)/select_n | solution.py:191
  144.7 1.3 compare_reduce_fusion
  146.0 11.2 %select_reduce_fusion.1 = (f32[768]{0:T(1024)S(1)}, f32[768,1664]{1,0:T(8,128)}) fusion(pred[1664]{0:T(1024)(128)(4,1)S(1)} %compare_reduce_fusion, bf16[768,2048]{1,0:T(8,128)(2,1)} %bitcast.158, bf16[2064,1664]{0,1:T(8,128)(2,1)} %all-gather.2.cloned.1.call-done), kind=kOutput, calls=%fused_computation.15 | convolution fusion | flops 5238324224 | bytes 15078016 | tf_op jit(solution)/shard_map/dot_general | solution.py:208
  157.3 4.8 %fusion.9 = (f32[768]{0:T(1024)S(1)}, f32[768]{0:T(1024)S(1)}, f32[768]{0:T(1024)S(1)}) fusion(f32[768,1664]{1,0:T(8,128)} %get-tuple-element.63, f32[768]{0:T(1024)S(1)} %get-tuple-element.62, pred[1664]{0:T(1024)(128)(4,1)S(1)} %compare_reduce_fusion, s32[1664]{0:T(1024)S(1)} %select_n.482, s32[768]{0:T(1024)S(1)} %dynamic_slice.19), kind=kLoop, calls=%fused_computation.13 | loop fusion | flops 14055168 | bytes 5135488 | tf_op jit(solution)/shard_map/reduce_sum | solution.py:215
  162.5 5.1 %collective-permute-done.13 = f32[4,2,192]{2,0,1:T(4,128)S(1)} collective-permute-done((f32[4,2,192]{2,0,1:T(4,128)S(1)}, f32[4,2,192]{2,0,1:T(4,128)S(1)}, u32[]{:S(2)}, u32[]{:S(2)}) %collective-permute-start.13) | collective-permute-done | bytes 6176 | tf_op jit(solution)/shard_map/ppermute | solution.py:221
  167.7 0.1 collective-permute-start.14
  167.8 3.6 %collective-permute-done.14 = f32[4,1,192]{2,0,1:T(4,128)S(1)} collective-permute-done((f32[4,1,192]{2,0,1:T(4,128)S(1)}, f32[4,1,192]{2,0,1:T(4,128)S(1)}, u32[]{:S(2)}, u32[]{:S(2)}) %collective-permute-start.14) | collective-permute-done | bytes 3104 | tf_op jit(solution)/shard_map/ppermute | solution.py:229
  171.6 1.1 collective-permute-done.15
  172.8 1.4 collective-permute-start.16
  174.2 2.3 %collective-permute-done.16 = f32[4,192]{1,0:T(4,128)S(1)} collective-permute-done((f32[4,192]{1,0:T(4,128)S(1)}, f32[4,192]{1,0:T(4,128)S(1)}, u32[]{:S(2)}, u32[]{:S(2)}) %collective-permute-start.16) | collective-permute-done | bytes 3104 | tf_op jit(solution)/shard_map/ppermute | solution.py:234
  176.6 2.0 %collective-permute-start.17 = (f32[4,192]{1,0:T(4,128)S(1)}, f32[4,192]{1,0:T(4,128)S(1)}, u32[]{:S(2)}, u32[]{:S(2)}) collective-permute-start(f32[4,192]{1,0:T(4,128)S(1)} %pad_maximum_fusion.6), channel_id=1, source_target_pairs={{0,128},{32,160},{64,192},{96,224},{128,0},{160,32},{192,64},{224,... | collective-permute-start | bytes 9224 | tf_op jit(solution)/shard_map/ppermute | solution.py:234
  178.6 3.2 %collective-permute-done.17 = f32[4,192]{1,0:T(4,128)S(1)} collective-permute-done((f32[4,192]{1,0:T(4,128)S(1)}, f32[4,192]{1,0:T(4,128)S(1)}, u32[]{:S(2)}, u32[]{:S(2)}) %collective-permute-start.17) | collective-permute-done | bytes 3104 | tf_op jit(solution)/shard_map/ppermute | solution.py:234
  181.8 0.6 divide_subtract_fusion
  (83 shorter events, 2.4 us)
Async XLA Ops:
  7.2 66.7 %copy-start = (bf16[256,2048]{1,0:T(8,128)(2,1)S(1)}, bf16[256,2048]{1,0:T(8,128)(2,1)}, u32[]{:S(2)}) copy-start(bf16[256,2048]{1,0:T(8,128)(2,1)} %param.16) | copy-start | bytes 3145732
  7.2 24.0 %copy-start.7 = (s32[193]{0:T(256)S(1)}, s32[193]{0:T(256)}, u32[]{:S(2)}) copy-start(s32[193]{0:T(256)} %param.21) | copy-start | bytes 2320
  7.2 24.1 %copy-start.4 = (bf16[2048,193]{0,1:T(8,128)(2,1)S(1)}, bf16[2048,193]{0,1:T(8,128)(2,1)}, u32[]{:S(2)}) copy-start(bf16[2048,193]{0,1:T(8,128)(2,1)} %param.18) | copy-start | bytes 2371588
  7.2 137.5 %all-gather.2.cloned.1.call-start = ((), (), s32[]{:S(2)}) async-start(), calls=%async_computation | async-start | bytes 8146944 | tf_op jit(solution)/shard_map/all_gather | solution.py:198
  14.0 8.2 %collective-permute-start = (bf16[1,192,128]{1,2,0:T(8,128)(2,1)S(1)}, bf16[1,192,128]{1,2,0:T(8,128)(2,1)S(1)}, u32[]{:S(2)}, u32[]{:S(2)}) collective-permute-start(bf16[1,192,128]{1,2,0:T(8,128)(2,1)S(1)} %maximum_bitcast_fusion.1), channel_id=1, source_target_pairs={{0,4},{4,8},{8,12},{12,16},{16,20},{20,24},{24,28},{28,0},{1,5},{5... | collective-permute-start | bytes 147464 | tf_op jit(solution)/shard_map/ppermute | solution.py:113
  22.2 8.8 %collective-permute-start.1 = (bf16[2,192,128]{1,2,0:T(8,128)(2,1)S(1)}, bf16[2,192,128]{1,2,0:T(8,128)(2,1)S(1)}, u32[]{:S(2)}, u32[]{:S(2)}) collective-permute-start(bf16[2,192,128]{1,2,0:T(8,128)(2,1)S(1)} %pad_maximum_fusion.2), channel_id=1, source_target_pairs={{0,8},{4,12},{8,16},{12,20},{16,24},{20,28},{24,0},{28,4},{1,9},{5... | collective-permute-start | bytes 294920 | tf_op jit(solution)/shard_map/ppermute | solution.py:113
  31.1 5.5 %collective-permute-start.2 = (bf16[1,192,128]{1,2,0:T(8,128)(2,1)S(1)}, bf16[1,192,128]{1,2,0:T(8,128)(2,1)S(1)}, u32[]{:S(2)}, u32[]{:S(2)}) collective-permute-start(bf16[1,192,128]{1,2,0:T(8,128)(2,1)S(1)} %slice.242), channel_id=1, source_target_pairs={{0,4},{4,8},{8,12},{12,16},{16,20},{20,24},{24,28},{28,0},{1,5},{5... | collective-permute-start | bytes 147464 | tf_op jit(solution)/shard_map/ppermute | solution.py:113
  32.0 15.4 %copy-start.1 = (bf16[192,2048]{1,0:T(8,128)(2,1)S(1)}, bf16[192,2048]{1,0:T(8,128)(2,1)}, u32[]{:S(2)}) copy-start(bf16[192,2048]{1,0:T(8,128)(2,1)} %param.11) | copy-start | bytes 2359300
  32.0 15.4 %copy-start.6 = (f32[2048]{0:T(1024)S(1)}, f32[2048]{0:T(1024)}, u32[]{:S(2)}) copy-start(f32[2048]{0:T(1024)} %param.12) | copy-start | bytes 24580
  36.6 9.6 %collective-permute-start.3 = (bf16[5,1,192,128]{2,3,0,1:T(8,128)(2,1)S(1)}, bf16[5,1,192,128]{2,3,0,1:T(8,128)(2,1)S(1)}, u32[]{:S(2)}, u32[]{:S(2)}) collective-permute-start(bf16[5,1,192,128]{2,3,0,1:T(8,128)(2,1)S(1)} %bitcast.161), channel_id=1, source_target_pairs={{0,1},{1,0},{2,3},{3,2},{4,5},{5,4},{6,7},{7,6},{8,9},{9,8},{10,11... | collective-permute-start | bytes 737288 | tf_op jit(solution)/shard_map/ppermute | solution.py:123
  47.4 10.5 %collective-permute-start.4 = (bf16[5,2,192,128]{3,2,1,0:T(8,128)(2,1)}, bf16[5,2,192,128]{3,2,1,0:T(8,128)(2,1)S(1)}, u32[]{:S(2)}, u32[]{:S(2)}) collective-permute-start(bf16[5,2,192,128]{3,2,1,0:T(8,128)(2,1)} %copy.78), channel_id=1, source_target_pairs={{0,2},{1,3},{2,0},{3,1},{4,6},{5,7},{6,4},{7,5},{8,10},{9,11},{10,... | collective-permute-start | bytes 1474568 | tf_op jit(solution)/shard_map/ppermute | solution.py:123
  62.4 4.1 %copy-start.2 = (pred[192,3840]{1,0:T(8,128)(4,1)S(1)}, pred[192,3840]{1,0:T(8,128)(4,1)}, u32[]{:S(2)}) copy-start(pred[192,3840]{1,0:T(8,128)(4,1)} %compare_and_fusion) | copy-start | bytes 2211844
  66.5 3.8 %copy-start.3 = (bf16[5,4,192,128]{3,2,1,0:T(8,128)(2,1)S(1)}, bf16[5,4,192,128]{3,2,1,0:T(8,128)(2,1)}, u32[]{:S(2)}) copy-start(bf16[5,4,192,128]{3,2,1,0:T(8,128)(2,1)} %copy.81) | copy-start | bytes 2949124
  74.4 2.5 %collective-permute-start.5 = (f32[2,2,24,2048]{3,2,1,0:T(8,128)S(1)}, f32[2,2,24,2048]{3,2,1,0:T(8,128)}, u32[]{:S(2)}, u32[]{:S(2)}) collective-permute-start(f32[2,2,24,2048]{3,2,1,0:T(8,128)S(1)} %select_bitcast_fusion), channel_id=1, source_target_pairs={{0,32},{32,0},{64,96},{96,64},{128,160},{160,128},{192,224},{224,1... | collective-permute-start | bytes 2359304 | tf_op jit(solution)/shard_map/ppermute | solution.py:179
  78.2 19.3 %copy-start.5 = (f32[2048]{0:T(1024)S(1)}, f32[2048]{0:T(1024)}, u32[]{:S(2)}) copy-start(f32[2048]{0:T(1024)} %param.17) | copy-start | bytes 24580
  78.3 11.2 %collective-permute-start.6 = (f32[2,24,2048]{2,1,0:T(8,128)S(1)}, f32[2,24,2048]{2,1,0:T(8,128)S(1)}, u32[]{:S(2)}, u32[]{:S(2)}) collective-permute-start(f32[2,24,2048]{2,1,0:T(8,128)S(1)} %select_bitcast_fusion.1), channel_id=1, source_target_pairs={{0,64},{32,96},{64,0},{96,32},{128,192},{160,224},{192,128},{224,1... | collective-permute-start | bytes 1179656 | tf_op jit(solution)/shard_map/ppermute | solution.py:179
  89.6 7.8 %collective-permute-start.7 = (f32[24,2048]{1,0:T(8,128)S(1)}, f32[24,2048]{1,0:T(8,128)S(1)}, u32[]{:S(2)}, u32[]{:S(2)}) collective-permute-start(f32[24,2048]{1,0:T(8,128)S(1)} %select_bitcast_fusion.2), channel_id=1, source_target_pairs={{0,128},{32,160},{64,192},{96,224},{128,0},{160,32},{192,64},{224,... | collective-permute-start | bytes 589832 | tf_op jit(solution)/shard_map/ppermute | solution.py:179
  97.6 5.7 %collective-permute-start.8 = (bf16[1,1,1,1,1,24,2048]{6,5,4,3,2,1,0:T(8,128)(2,1)S(1)}, bf16[1,1,1,1,1,24,2048]{6,5,4,3,2,1,0:T(8,128)(2,1)S(1)}, u32[]{:S(2)}, u32[]{:S(2)}) collective-permute-start(bf16[1,1,1,1,1,24,2048]{6,5,4,3,2,1,0:T(8,128)(2,1)S(1)} %get-tuple-element.24), channel_id=1, source_target_pairs={{0,1},{1,0},{2,3},{3,2},{4,5},{5,4},{6,7},{7,6},{8,9},{9,8},{10,11... | collective-permute-start | bytes 294920 | tf_op jit(solution)/shard_map/ppermute | solution.py:190
  103.3 7.3 %collective-permute-start.9 = (bf16[1,2,1,1,1,24,2048]{6,5,4,3,2,1,0:T(8,128)(2,1)S(1)}, bf16[1,2,1,1,1,24,2048]{6,5,4,3,2,1,0:T(8,128)(2,1)S(1)}, u32[]{:S(2)}, u32[]{:S(2)}) collective-permute-start(bf16[1,2,1,1,1,24,2048]{6,5,4,3,2,1,0:T(8,128)(2,1)S(1)} %maximum_select_fusion.8), channel_id=1, source_target_pairs={{0,2},{1,3},{2,0},{3,1},{4,6},{5,7},{6,4},{7,5},{8,10},{9,11},{10,... | collective-permute-start | bytes 589832 | tf_op jit(solution)/shard_map/ppermute | solution.py:190
  110.7 10.5 %collective-permute-start.10 = (bf16[2,2,1,1,1,24,2048]{6,5,4,3,2,1,0:T(8,128)(2,1)S(1)}, bf16[2,2,1,1,1,24,2048]{6,5,4,3,2,1,0:T(8,128)(2,1)S(1)}, u32[]{:S(2)}, u32[]{:S(2)}) collective-permute-start(bf16[2,2,1,1,1,24,2048]{6,5,4,3,2,1,0:T(8,128)(2,1)S(1)} %fusion.25), channel_id=1, source_target_pairs={{0,128},{32,160},{64,192},{96,224},{128,0},{160,32},{192,64},{224,... | collective-permute-start | bytes 1179656 | tf_op jit(solution)/shard_map/ppermute | solution.py:190
  121.4 15.8 %collective-permute-start.11 = (bf16[2,2,2,1,1,24,2048]{6,5,4,3,2,1,0:T(8,128)(2,1)S(1)}, bf16[2,2,2,1,1,24,2048]{6,5,4,3,2,1,0:T(8,128)(2,1)S(1)}, u32[]{:S(2)}, u32[]{:S(2)}) collective-permute-start(bf16[2,2,2,1,1,24,2048]{6,5,4,3,2,1,0:T(8,128)(2,1)S(1)} %maximum_select_fusion.4), channel_id=1, source_target_pairs={{0,64},{32,96},{64,0},{96,32},{128,192},{160,224},{192,128},{224,1... | collective-permute-start | bytes 2359304 | tf_op jit(solution)/shard_map/ppermute | solution.py:190
  137.3 3.6 %collective-permute-start.12 = (bf16[2,2,2,2,1,24,2048]{6,5,4,3,2,1,0:T(8,128)(2,1)S(1)}, bf16[2,2,2,2,1,24,2048]{6,5,4,3,2,1,0:T(8,128)(2,1)}, u32[]{:S(2)}, u32[]{:S(2)}) collective-permute-start(bf16[2,2,2,2,1,24,2048]{6,5,4,3,2,1,0:T(8,128)(2,1)S(1)} %maximum_select_fusion.1), channel_id=1, source_target_pairs={{0,32},{32,0},{64,96},{96,64},{128,160},{160,128},{192,224},{224,1... | collective-permute-start | bytes 4718600 | tf_op jit(solution)/shard_map/ppermute | solution.py:190
  162.4 5.2 %collective-permute-start.13 = (f32[4,2,192]{2,0,1:T(4,128)S(1)}, f32[4,2,192]{2,0,1:T(4,128)S(1)}, u32[]{:S(2)}, u32[]{:S(2)}) collective-permute-start(f32[4,2,192]{2,0,1:T(4,128)S(1)} %constant_dynamic-slice_fusion.1), channel_id=1, source_target_pairs={{0,2},{1,3},{2,0},{3,1},{4,6},{5,7},{6,4},{7,5},{8,10},{9,11},{10,... | collective-permute-start | bytes 18440 | tf_op jit(solution)/shard_map/ppermute | solution.py:221
  167.7 3.7 %collective-permute-start.14 = (f32[4,1,192]{2,0,1:T(4,128)S(1)}, f32[4,1,192]{2,0,1:T(4,128)S(1)}, u32[]{:S(2)}, u32[]{:S(2)}) collective-permute-start(f32[4,1,192]{2,0,1:T(4,128)S(1)} %constant_dynamic-slice_fusion), channel_id=1, source_target_pairs={{0,1},{1,0},{2,3},{3,2},{4,5},{5,4},{6,7},{7,6},{8,9},{9,8},{10,11... | collective-permute-start | bytes 9224 | tf_op jit(solution)/shard_map/ppermute | solution.py:229
  171.5 1.3 collective-permute-start.15
  172.8 3.7 %collective-permute-start.16 = (f32[4,192]{1,0:T(4,128)S(1)}, f32[4,192]{1,0:T(4,128)S(1)}, u32[]{:S(2)}, u32[]{:S(2)}) collective-permute-start(f32[4,192]{1,0:T(4,128)S(1)} %pad_maximum_fusion.5), channel_id=1, source_target_pairs={{0,64},{32,96},{64,0},{96,32},{128,192},{160,224},{192,128},{224,1... | collective-permute-start | bytes 9224 | tf_op jit(solution)/shard_map/ppermute | solution.py:234
  176.6 5.2 %collective-permute-start.17 = (f32[4,192]{1,0:T(4,128)S(1)}, f32[4,192]{1,0:T(4,128)S(1)}, u32[]{:S(2)}, u32[]{:S(2)}) collective-permute-start(f32[4,192]{1,0:T(4,128)S(1)} %pad_maximum_fusion.6), channel_id=1, source_target_pairs={{0,128},{32,160},{64,192},{96,224},{128,0},{160,32},{192,64},{224,... | collective-permute-start | bytes 9224 | tf_op jit(solution)/shard_map/ppermute | solution.py:234
Sparse Core Ops, SparseCore 0:
  49.5 82.2 all-gather.1

commit v14 on v13

--- a/solution.py
+++ b/solution.py
@@ -188,12 +188,22 @@
     for name, bit, pos, count, axis in order:
         mine_low = (pos >> bit) % 2 == 0
         got = lax.ppermute(head_rows, name, [(p, p ^ (1 << bit)) for p in range(count)])
-        head_rows = jnp.where(
-            mine_low,
-            jnp.concatenate([head_rows, got], axis=axis),
-            jnp.concatenate([got, head_rows], axis=axis),
-        )
+        if name == "kv" and bit == 0:
+            head_rows = jnp.concatenate([head_rows, got], axis=axis)
+        else:
+            head_rows = jnp.where(
+                mine_low,
+                jnp.concatenate([head_rows, got], axis=axis),
+                jnp.concatenate([got, head_rows], axis=axis),
+            )
     head_rows = head_rows.reshape(-1, final_part.shape[1])
+    pair_swapped = kv_index % 2 == 1
+
+    def unswap(values):
+        lead = values.shape[:-1]
+        split = values.reshape(lead + (values.shape[-1] // (2 * chunk), 2, chunk))
+        return jnp.where(pair_swapped, jnp.flip(split, axis=-2), split).reshape(values.shape)
+
     group_rows = head_rows.shape[0]
     head_ext = lax.all_gather(head_ext, "z", axis=1, tiled=True)
     head_cols = head_ext[: w_head.shape[0]]
@@ -204,7 +214,7 @@
     columns = jnp.where(
         local_cols[None, :] < vocab_local, shard_ids[:, None] * vocab_local + local_cols[None, :], -1
     ).reshape(-1)
-    row_ids = lax.dynamic_slice_in_dim(target_ids, z_index * group_rows, group_rows, 0)
+    row_ids = unswap(lax.dynamic_slice_in_dim(target_ids, z_index * group_rows, group_rows, 0))
     logits = jnp.dot(head_rows, head_cols, preferred_element_type=jnp.float32) * LOGIT_SCALE
     masked = jnp.where(live_mask[None, :], logits, NEG_FILL)
     top_row = jnp.max(masked, axis=1)
@@ -228,7 +238,7 @@
         send = lax.dynamic_slice_in_dim(merged, (1 - my_part) * width, width, 1)
         got = lax.ppermute(send, "y", [(p, p ^ width) for p in range(y_count)])
         merged = merge_stats(keep, got, my_part == 0)
-    merged = merged[:, 0]
+    merged = unswap(merged[:, 0])
     step = 1
     while step < kv_count:
         got = lax.ppermute(merged, "kv", [(p, p ^ step) for p in range(kv_count)])

time: 190 us -> 191 us (level)
    select_n x5 -> x4, other arithmetic: 4.23 us -> 0.49 us  [local(): jnp.where(mine_low, jnp.concatenate([head_rows, got], axis=axis), jnp.con...]
    concatenate x0 -> x1, other arithmetic: none -> 3.36 us  [local(): head_rows = jnp.concatenate([head_rows, got], axis=axis)]
where the time goes in v14:
time: 191 us; the launch traced here: 190 us
  waiting for transfers between devices  101 us (53%)
  other arithmetic  24.9 us (13%)
  matrix products  24.1 us (13%)
  starting transfers between devices  16.5 us (9%)
  between operations  14.7 us (8%)
  local copies, waits for them, and re-layouts  9.13 us (5%)
    ppermute x5, waiting for transfers between devices, local(): lax.ppermute(head_rows, name, [(p, p ^ 1 << bit) for p in range(count)])  36.2 us
    ppermute x3, waiting for transfers between devices, local(): lax.ppermute(held[:need], 'z', [(p, (p + need) % z_count) for p in range(...  18.3 us
    ppermute x2, waiting for transfers between devices, local(): got = lax.ppermute(held, 'y', [(p, p ^ 1 << bit) for p in range(y_count)])  15.7 us
    ppermute x3, waiting for transfers between devices, local(): got = lax.ppermute(send, 'kv', [(p, p ^ 1 << bit) for p in range(kv_count)])  15.4 us
    dot_general x1, matrix products, local(): jnp.dot(head_rows, head_cols, preferred_element_type=jnp.float32)  11.2 us
    ppermute x3, waiting for transfers between devices, local(): got = lax.ppermute(merged, 'kv', [(p, p ^ step) for p in range(kv_count)])  6.61 us
    ppermute x1, waiting for transfers between devices, local(): got = lax.ppermute(send, 'y', [(p, p ^ half) for p in range(y_count)])  5.12 us
    ppermute x5, starting transfers between devices, local(): lax.ppermute(head_rows, name, [(p, p ^ 1 << bit) for p in range(count)])  5.09 us
  transfers between devices with their start and end apart: 19, of which 18 were waited for; matrix products, arithmetic and copies ran while one was open for 16% of the time, Pallas kernels for 0%

profile of v14, /device:TPU:24, one launch (start us, length us, event | category | flops | bytes accessed | tf_op | source)
XLA Modules:
  0.0 190.3 jit_solution(3036662237187996855)
XLA Ops:
  7.3 0.9 copy.76
  8.2 0.1 reduce.2
  8.3 0.7 sub.117
  9.1 1.4 multiply_reduce_fusion.1
  10.5 1.6 convolution_bitcast_fusion
  12.1 1.6 convolution_convert_fusion
  13.8 0.2 fusion.42
  14.0 2.0 %collective-permute-start = (bf16[1,192,128]{1,2,0:T(8,128)(2,1)S(1)}, bf16[1,192,128]{1,2,0:T(8,128)(2,1)S(1)}, u32[]{:S(2)}, u32[]{:S(2)}) collective-permute-start(bf16[1,192,128]{1,2,0:T(8,128)(2,1)S(1)} %maximum_bitcast_fusion.1), channel_id=1, source_target_pairs={{0,4},{4,8},{8,12},{12,16},{16,20},{20,24},{24,28},{28,0},{1,5},{5... | collective-permute-start | bytes 147464 | tf_op jit(solution)/shard_map/ppermute | solution.py:113
  16.0 6.2 %collective-permute-done = bf16[1,192,128]{1,2,0:T(8,128)(2,1)S(1)} collective-permute-done((bf16[1,192,128]{1,2,0:T(8,128)(2,1)S(1)}, bf16[1,192,128]{1,2,0:T(8,128)(2,1)S(1)}, u32[]{:S(2)}, u32[]{:S(2)}) %collective-permute-start) | collective-permute-done | bytes 49184 | tf_op jit(solution)/shard_map/ppermute | solution.py:113
  22.3 8.7 %collective-permute-done.1 = bf16[2,192,128]{1,2,0:T(8,128)(2,1)S(1)} collective-permute-done((bf16[2,192,128]{1,2,0:T(8,128)(2,1)S(1)}, bf16[2,192,128]{1,2,0:T(8,128)(2,1)S(1)}, u32[]{:S(2)}, u32[]{:S(2)}) %collective-permute-start.1) | collective-permute-done | bytes 98336 | tf_op jit(solution)/shard_map/ppermute | solution.py:113
  31.3 0.7 concatenate.307
  32.0 1.1 pad.4
  33.1 3.4 %collective-permute-done.2 = bf16[1,192,128]{1,2,0:T(8,128)(2,1)S(1)} collective-permute-done((bf16[1,192,128]{1,2,0:T(8,128)(2,1)S(1)}, bf16[1,192,128]{1,2,0:T(8,128)(2,1)S(1)}, u32[]{:S(2)}, u32[]{:S(2)}) %collective-permute-start.2) | collective-permute-done | bytes 49184 | tf_op jit(solution)/shard_map/ppermute | solution.py:113
  36.6 0.8 collective-permute-start.3
  37.4 1.5 compare_and_fusion
  38.9 0.2 multiply_cosine_fusion
  39.1 7.1 %collective-permute-done.3 = bf16[5,1,192,128]{2,3,0,1:T(8,128)(2,1)S(1)} collective-permute-done((bf16[5,1,192,128]{2,3,0,1:T(8,128)(2,1)S(1)}, bf16[5,1,192,128]{2,3,0,1:T(8,128)(2,1)S(1)}, u32[]{:S(2)}, u32[]{:S(2)}) %collective-permute-start.3) | collective-permute-done | bytes 245792 | tf_op jit(solution)/shard_map/ppermute | solution.py:123
  46.2 0.2 maximum_select_fusion.4
  46.4 1.0 copy.78
  47.4 1.9 fusion.72
  49.4 8.6 %collective-permute-done.4 = bf16[5,2,192,128]{3,2,1,0:T(8,128)(2,1)S(1)} collective-permute-done((bf16[5,2,192,128]{3,2,1,0:T(8,128)(2,1)}, bf16[5,2,192,128]{3,2,1,0:T(8,128)(2,1)S(1)}, u32[]{:S(2)}, u32[]{:S(2)}) %collective-permute-start.4) | collective-permute-done | bytes 491552 | tf_op jit(solution)/shard_map/ppermute | solution.py:123
  58.0 1.1 copy.79
  59.0 1.9 maximum_select_fusion.1
  60.9 1.4 copy.81
  62.3 4.1 %fusion = (f32[4,192]{1,0:T(4,128)S(1)}, f32[3840,192,4]{0,1,2:T(8,128)S(1)}) fusion(pred[192,3840]{1,0:T(8,128)(4,1)} %compare_and_fusion, bf16[192,4,32]{0,2,1:T(8,128)(2,1)S(1)} %get-tuple-element.25, bf16[192,4,32]{0,2,1:T(8,128)(2,1)S(1)} %get-tuple-element.24, bf16[3840,128]{1,0:T(8,128)(2,1)} %bitcast.163), kind=kOutput, calls=%fused_computation.2 | convolution fusion | flops 386530560 | bytes 13618176 | tf_op jit(solution)/shard_map/tkgd,skd->kgts/dot_general | solution.py:137
  66.4 3.7 %fusion.1 = f32[4,192]{1,0:T(4,128)S(1)} fusion(f32[3840,192,4]{0,1,2:T(8,128)S(1)} %get-tuple-element.61, f32[4,192]{1,0:T(4,128)S(1)} %broadcast_maximum_fusion, pred[192,3840]{1,0:T(8,128)(4,1)S(1)} %copy-done.2), kind=kLoop, calls=%fused_computation.3 | loop fusion | flops 14744832 | bytes 12539904 | tf_op jit(solution)/shard_map/reduce_sum | solution.py:147
  70.2 3.3 %fusion.16 = bf16[192,1,4,64]{0,3,2,1:T(8,128)(2,1)S(1)} fusion(f32[3840,192,4]{0,1,2:T(8,128)S(1)} %get-tuple-element.61, f32[4,192]{1,0:T(4,128)S(1)} %broadcast_maximum_fusion, pred[192,3840]{1,0:T(8,128)(4,1)S(1)} %copy-done.2, bf16[3840,128]{1,0:T(8,128)(2,1)S(1)} %bitcast.164, f32[4,192]{1,0:T(4,128)S(1)} %fusion.1), kind=kOutput, calls=%fused_computation.26 | convolution fusion | flops 392331264 | bytes 13621248 | tf_op jit(solution)/shard_map/kgts,skd->kgtd/dot_general | solution.py:148
  73.4 0.2 copy.85
  73.6 0.2 convert_element_type.57
  73.8 0.4 fusion.19
  74.3 0.1 collective-permute-start.5
  74.4 2.4 %collective-permute-done.5 = f32[2,2,24,2048]{3,2,1,0:T(8,128)} collective-permute-done((f32[2,2,24,2048]{3,2,1,0:T(8,128)S(1)}, f32[2,2,24,2048]{3,2,1,0:T(8,128)}, u32[]{:S(2)}, u32[]{:S(2)}) %collective-permute-start.5) | collective-permute-done | bytes 786464 | tf_op jit(solution)/shard_map/ppermute | solution.py:179
  76.8 1.3 fusion.24
  78.2 1.6 collective-permute-start.6
  79.7 9.7 %collective-permute-done.6 = f32[2,24,2048]{2,1,0:T(8,128)S(1)} collective-permute-done((f32[2,24,2048]{2,1,0:T(8,128)S(1)}, f32[2,24,2048]{2,1,0:T(8,128)S(1)}, u32[]{:S(2)}, u32[]{:S(2)}) %collective-permute-start.6) | collective-permute-done | bytes 393248 | tf_op jit(solution)/shard_map/ppermute | solution.py:179
  89.5 3.1 %collective-permute-start.7 = (f32[24,2048]{1,0:T(8,128)S(1)}, f32[24,2048]{1,0:T(8,128)S(1)}, u32[]{:S(2)}, u32[]{:S(2)}) collective-permute-start(f32[24,2048]{1,0:T(8,128)S(1)} %select_bitcast_fusion.2), channel_id=1, source_target_pairs={{0,128},{32,160},{64,192},{96,224},{128,0},{160,32},{192,64},{224,... | collective-permute-start | bytes 589832 | tf_op jit(solution)/shard_map/ppermute | solution.py:179
  92.6 1.3 convert_element_type.48
  93.9 3.4 %collective-permute-done.7 = f32[24,2048]{1,0:T(8,128)S(1)} collective-permute-done((f32[24,2048]{1,0:T(8,128)S(1)}, f32[24,2048]{1,0:T(8,128)S(1)}, u32[]{:S(2)}, u32[]{:S(2)}) %collective-permute-start.7) | collective-permute-done | bytes 196640 | tf_op jit(solution)/shard_map/ppermute | solution.py:179
  97.2 0.2 multiply_reduce_fusion.2
  97.6 5.6 %collective-permute-done.8 = bf16[1,1,1,1,1,24,2048]{6,5,4,3,2,1,0:T(8,128)(2,1)S(1)} collective-permute-done((bf16[1,1,1,1,1,24,2048]{6,5,4,3,2,1,0:T(8,128)(2,1)S(1)}, bf16[1,1,1,1,1,24,2048]{6,5,4,3,2,1,0:T(8,128)(2,1)S(1)}, u32[]{:S(2)}, u32[]{:S(2)}) %collective-permute-start.8) | collective-permute-done | bytes 98336 | tf_op jit(solution)/shard_map/ppermute | solution.py:190
  103.4 7.1 %collective-permute-done.9 = bf16[1,2,1,1,1,24,2048]{6,5,4,3,2,1,0:T(8,128)(2,1)S(1)} collective-permute-done((bf16[1,2,1,1,1,24,2048]{6,5,4,3,2,1,0:T(8,128)(2,1)S(1)}, bf16[1,2,1,1,1,24,2048]{6,5,4,3,2,1,0:T(8,128)(2,1)S(1)}, u32[]{:S(2)}, u32[]{:S(2)}) %collective-permute-start.9) | collective-permute-done | bytes 196640 | tf_op jit(solution)/shard_map/ppermute | solution.py:190
  110.6 3.2 %collective-permute-start.10 = (bf16[2,2,1,1,1,24,2048]{6,5,4,3,2,1,0:T(8,128)(2,1)S(1)}, bf16[2,2,1,1,1,24,2048]{6,5,4,3,2,1,0:T(8,128)(2,1)S(1)}, u32[]{:S(2)}, u32[]{:S(2)}) collective-permute-start(bf16[2,2,1,1,1,24,2048]{6,5,4,3,2,1,0:T(8,128)(2,1)S(1)} %fusion.25), channel_id=1, source_target_pairs={{0,128},{32,160},{64,192},{96,224},{128,0},{160,32},{192,64},{224,... | collective-permute-start | bytes 1179656 | tf_op jit(solution)/shard_map/ppermute | solution.py:190
  113.9 7.1 %collective-permute-done.10 = bf16[2,2,1,1,1,24,2048]{6,5,4,3,2,1,0:T(8,128)(2,1)S(1)} collective-permute-done((bf16[2,2,1,1,1,24,2048]{6,5,4,3,2,1,0:T(8,128)(2,1)S(1)}, bf16[2,2,1,1,1,24,2048]{6,5,4,3,2,1,0:T(8,128)(2,1)S(1)}, u32[]{:S(2)}, u32[]{:S(2)}) %collective-permute-start.10) | collective-permute-done | bytes 393248 | tf_op jit(solution)/shard_map/ppermute | solution.py:190
  121.0 0.3 maximum_select_fusion.3
  121.3 1.6 collective-permute-start.11
  122.9 14.1 %collective-permute-done.11 = bf16[2,2,2,1,1,24,2048]{6,5,4,3,2,1,0:T(8,128)(2,1)S(1)} collective-permute-done((bf16[2,2,2,1,1,24,2048]{6,5,4,3,2,1,0:T(8,128)(2,1)S(1)}, bf16[2,2,2,1,1,24,2048]{6,5,4,3,2,1,0:T(8,128)(2,1)S(1)}, u32[]{:S(2)}, u32[]{:S(2)}) %collective-permute-start.11) | collective-permute-done | bytes 786464 | tf_op jit(solution)/shard_map/ppermute | solution.py:190
  137.1 0.1 maximum_select_fusion
  137.2 0.1 collective-permute-start.12
  137.4 0.8 dynamic_slice.19
  138.6 2.3 %collective-permute-done.12 = bf16[2,2,2,2,1,24,2048]{6,5,4,3,2,1,0:T(8,128)(2,1)} collective-permute-done((bf16[2,2,2,2,1,24,2048]{6,5,4,3,2,1,0:T(8,128)(2,1)S(1)}, bf16[2,2,2,2,1,24,2048]{6,5,4,3,2,1,0:T(8,128)(2,1)}, u32[]{:S(2)}, u32[]{:S(2)}) %collective-permute-start.12) | collective-permute-done | bytes 1572896 | tf_op jit(solution)/shard_map/ppermute | solution.py:190
  140.9 3.4 %pad_maximum_fusion = bf16[2,2,2,2,2,24,2048]{6,5,4,3,2,1,0:T(8,128)(2,1)} fusion(bf16[2,2,2,2,1,24,2048]{6,5,4,3,2,1,0:T(8,128)(2,1)} %collective-permute-done.12, bf16[2,2,2,2,1,24,2048]{6,5,4,3,2,1,0:T(8,128)(2,1)S(1)} %maximum_select_fusion), kind=kLoop, calls=%fused_computation.16 | loop fusion | flops 1572864 | bytes 6291456 | tf_op jit(solution)/shard_map/concatenate | solution.py:192
  144.2 1.3 compare_reduce_fusion
  145.5 11.2 %select_reduce_fusion.1 = (f32[768]{0:T(1024)S(1)}, f32[768,1664]{1,0:T(8,128)}) fusion(pred[1664]{0:T(1024)(128)(4,1)S(1)} %compare_reduce_fusion, bf16[768,2048]{1,0:T(8,128)(2,1)} %bitcast.158, bf16[2064,1664]{0,1:T(8,128)(2,1)} %all-gather.2.cloned.1.call-done), kind=kOutput, calls=%fused_computation.15 | convolution fusion | flops 5238324224 | bytes 15078016 | tf_op jit(solution)/shard_map/dot_general | solution.py:218
  156.8 4.7 %multiply_reduce_fusion = (f32[768]{0:T(1024)S(1)}, f32[768]{0:T(1024)S(1)}, f32[768]{0:T(1024)S(1)}) fusion(f32[768,1664]{1,0:T(8,128)} %get-tuple-element.63, f32[768]{0:T(1024)S(1)} %get-tuple-element.62, pred[1664]{0:T(1024)(128)(4,1)S(1)} %compare_reduce_fusion, s32[1664]{0:T(1024)S(1)} %select_n.486, s32[768]{0:T(1024)S(1)} %eq.89), kind=kLoop, calls=%fused_computation.11 | loop fusion | flops 14055168 | bytes 5135488 | tf_op jit(solution)/shard_map/reduce_sum | solution.py:225
  161.9 5.1 %collective-permute-done.13 = f32[4,2,192]{2,1,0:T(2,128)S(1)} collective-permute-done((f32[4,2,192]{2,1,0:T(2,128)S(1)}, f32[4,2,192]{2,1,0:T(2,128)S(1)}, u32[]{:S(2)}, u32[]{:S(2)}) %collective-permute-start.13) | collective-permute-done | bytes 6176 | tf_op jit(solution)/shard_map/ppermute | solution.py:231
  167.2 3.6 %collective-permute-done.14 = f32[4,1,192]{2,1,0:T(1,128)S(1)} collective-permute-done((f32[4,1,192]{2,1,0:T(1,128)S(1)}, f32[4,1,192]{2,1,0:T(1,128)S(1)}, u32[]{:S(2)}, u32[]{:S(2)}) %collective-permute-start.14) | collective-permute-done | bytes 3104 | tf_op jit(solution)/shard_map/ppermute | solution.py:239
  170.8 0.5 broadcast.367
  171.3 0.7 fusion.56
  172.6 1.1 collective-permute-done.15
  173.8 1.4 collective-permute-start.16
  175.3 2.3 %collective-permute-done.16 = f32[4,192]{1,0:T(4,128)S(1)} collective-permute-done((f32[4,192]{1,0:T(4,128)S(1)}, f32[4,192]{1,0:T(4,128)S(1)}, u32[]{:S(2)}, u32[]{:S(2)}) %collective-permute-start.16) | collective-permute-done | bytes 3104 | tf_op jit(solution)/shard_map/ppermute | solution.py:244
  177.6 2.0 %collective-permute-start.17 = (f32[4,192]{1,0:T(4,128)S(1)}, f32[4,192]{1,0:T(4,128)S(1)}, u32[]{:S(2)}, u32[]{:S(2)}) collective-permute-start(f32[4,192]{1,0:T(4,128)S(1)} %pad_maximum_fusion.6), channel_id=1, source_target_pairs={{0,128},{32,160},{64,192},{96,224},{128,0},{160,32},{192,64},{224,... | collective-permute-start | bytes 9224 | tf_op jit(solution)/shard_map/ppermute | solution.py:244
  179.6 3.2 %collective-permute-done.17 = f32[4,192]{1,0:T(4,128)S(1)} collective-permute-done((f32[4,192]{1,0:T(4,128)S(1)}, f32[4,192]{1,0:T(4,128)S(1)}, u32[]{:S(2)}, u32[]{:S(2)}) %collective-permute-start.17) | collective-permute-done | bytes 3104 | tf_op jit(solution)/shard_map/ppermute | solution.py:244
  182.8 0.6 divide_subtract_fusion
  (100 shorter events, 3.2 us)
Async XLA Ops:
  7.2 66.6 %copy-start = (bf16[256,2048]{1,0:T(8,128)(2,1)S(1)}, bf16[256,2048]{1,0:T(8,128)(2,1)}, u32[]{:S(2)}) copy-start(bf16[256,2048]{1,0:T(8,128)(2,1)} %param.16) | copy-start | bytes 3145732
  7.2 24.0 %copy-start.7 = (s32[193]{0:T(256)S(1)}, s32[193]{0:T(256)}, u32[]{:S(2)}) copy-start(s32[193]{0:T(256)} %param.21) | copy-start | bytes 2320
  7.2 24.1 %copy-start.4 = (bf16[2048,193]{0,1:T(8,128)(2,1)S(1)}, bf16[2048,193]{0,1:T(8,128)(2,1)}, u32[]{:S(2)}) copy-start(bf16[2048,193]{0,1:T(8,128)(2,1)} %param.18) | copy-start | bytes 2371588
  7.2 137.0 %all-gather.2.cloned.1.call-start = ((), (), s32[]{:S(2)}) async-start(), calls=%async_computation | async-start | bytes 8146944 | tf_op jit(solution)/shard_map/all_gather | solution.py:208
  14.0 8.2 %collective-permute-start = (bf16[1,192,128]{1,2,0:T(8,128)(2,1)S(1)}, bf16[1,192,128]{1,2,0:T(8,128)(2,1)S(1)}, u32[]{:S(2)}, u32[]{:S(2)}) collective-permute-start(bf16[1,192,128]{1,2,0:T(8,128)(2,1)S(1)} %maximum_bitcast_fusion.1), channel_id=1, source_target_pairs={{0,4},{4,8},{8,12},{12,16},{16,20},{20,24},{24,28},{28,0},{1,5},{5... | collective-permute-start | bytes 147464 | tf_op jit(solution)/shard_map/ppermute | solution.py:113
  22.2 8.8 %collective-permute-start.1 = (bf16[2,192,128]{1,2,0:T(8,128)(2,1)S(1)}, bf16[2,192,128]{1,2,0:T(8,128)(2,1)S(1)}, u32[]{:S(2)}, u32[]{:S(2)}) collective-permute-start(bf16[2,192,128]{1,2,0:T(8,128)(2,1)S(1)} %pad_maximum_fusion.3), channel_id=1, source_target_pairs={{0,8},{4,12},{8,16},{12,20},{16,24},{20,28},{24,0},{28,4},{1,9},{5... | collective-permute-start | bytes 294920 | tf_op jit(solution)/shard_map/ppermute | solution.py:113
  31.1 5.5 %collective-permute-start.2 = (bf16[1,192,128]{1,2,0:T(8,128)(2,1)S(1)}, bf16[1,192,128]{1,2,0:T(8,128)(2,1)S(1)}, u32[]{:S(2)}, u32[]{:S(2)}) collective-permute-start(bf16[1,192,128]{1,2,0:T(8,128)(2,1)S(1)} %slice.242), channel_id=1, source_target_pairs={{0,4},{4,8},{8,12},{12,16},{16,20},{20,24},{24,28},{28,0},{1,5},{5... | collective-permute-start | bytes 147464 | tf_op jit(solution)/shard_map/ppermute | solution.py:113
  32.0 15.4 %copy-start.1 = (bf16[192,2048]{1,0:T(8,128)(2,1)S(1)}, bf16[192,2048]{1,0:T(8,128)(2,1)}, u32[]{:S(2)}) copy-start(bf16[192,2048]{1,0:T(8,128)(2,1)} %param.11) | copy-start | bytes 2359300
  32.0 15.4 %copy-start.6 = (f32[2048]{0:T(1024)S(1)}, f32[2048]{0:T(1024)}, u32[]{:S(2)}) copy-start(f32[2048]{0:T(1024)} %param.12) | copy-start | bytes 24580
  36.6 9.6 %collective-permute-start.3 = (bf16[5,1,192,128]{2,3,0,1:T(8,128)(2,1)S(1)}, bf16[5,1,192,128]{2,3,0,1:T(8,128)(2,1)S(1)}, u32[]{:S(2)}, u32[]{:S(2)}) collective-permute-start(bf16[5,1,192,128]{2,3,0,1:T(8,128)(2,1)S(1)} %bitcast.161), channel_id=1, source_target_pairs={{0,1},{1,0},{2,3},{3,2},{4,5},{5,4},{6,7},{7,6},{8,9},{9,8},{10,11... | collective-permute-start | bytes 737288 | tf_op jit(solution)/shard_map/ppermute | solution.py:123
  47.4 10.5 %collective-permute-start.4 = (bf16[5,2,192,128]{3,2,1,0:T(8,128)(2,1)}, bf16[5,2,192,128]{3,2,1,0:T(8,128)(2,1)S(1)}, u32[]{:S(2)}, u32[]{:S(2)}) collective-permute-start(bf16[5,2,192,128]{3,2,1,0:T(8,128)(2,1)} %copy.78), channel_id=1, source_target_pairs={{0,2},{1,3},{2,0},{3,1},{4,6},{5,7},{6,4},{7,5},{8,10},{9,11},{10,... | collective-permute-start | bytes 1474568 | tf_op jit(solution)/shard_map/ppermute | solution.py:123
  62.3 4.1 %copy-start.2 = (pred[192,3840]{1,0:T(8,128)(4,1)S(1)}, pred[192,3840]{1,0:T(8,128)(4,1)}, u32[]{:S(2)}) copy-start(pred[192,3840]{1,0:T(8,128)(4,1)} %compare_and_fusion) | copy-start | bytes 2211844
  66.4 3.8 %copy-start.3 = (bf16[5,4,192,128]{3,2,1,0:T(8,128)(2,1)S(1)}, bf16[5,4,192,128]{3,2,1,0:T(8,128)(2,1)}, u32[]{:S(2)}) copy-start(bf16[5,4,192,128]{3,2,1,0:T(8,128)(2,1)} %copy.81) | copy-start | bytes 2949124
  74.3 2.5 %collective-permute-start.5 = (f32[2,2,24,2048]{3,2,1,0:T(8,128)S(1)}, f32[2,2,24,2048]{3,2,1,0:T(8,128)}, u32[]{:S(2)}, u32[]{:S(2)}) collective-permute-start(f32[2,2,24,2048]{3,2,1,0:T(8,128)S(1)} %select_bitcast_fusion), channel_id=1, source_target_pairs={{0,32},{32,0},{64,96},{96,64},{128,160},{160,128},{192,224},{224,1... | collective-permute-start | bytes 2359304 | tf_op jit(solution)/shard_map/ppermute | solution.py:179
  78.1 19.3 %copy-start.5 = (f32[2048]{0:T(1024)S(1)}, f32[2048]{0:T(1024)}, u32[]{:S(2)}) copy-start(f32[2048]{0:T(1024)} %param.17) | copy-start | bytes 24580
  78.2 11.2 %collective-permute-start.6 = (f32[2,24,2048]{2,1,0:T(8,128)S(1)}, f32[2,24,2048]{2,1,0:T(8,128)S(1)}, u32[]{:S(2)}, u32[]{:S(2)}) collective-permute-start(f32[2,24,2048]{2,1,0:T(8,128)S(1)} %select_bitcast_fusion.1), channel_id=1, source_target_pairs={{0,64},{32,96},{64,0},{96,32},{128,192},{160,224},{192,128},{224,1... | collective-permute-start | bytes 1179656 | tf_op jit(solution)/shard_map/ppermute | solution.py:179
  89.5 7.8 %collective-permute-start.7 = (f32[24,2048]{1,0:T(8,128)S(1)}, f32[24,2048]{1,0:T(8,128)S(1)}, u32[]{:S(2)}, u32[]{:S(2)}) collective-permute-start(f32[24,2048]{1,0:T(8,128)S(1)} %select_bitcast_fusion.2), channel_id=1, source_target_pairs={{0,128},{32,160},{64,192},{96,224},{128,0},{160,32},{192,64},{224,... | collective-permute-start | bytes 589832 | tf_op jit(solution)/shard_map/ppermute | solution.py:179
  97.5 5.7 %collective-permute-start.8 = (bf16[1,1,1,1,1,24,2048]{6,5,4,3,2,1,0:T(8,128)(2,1)S(1)}, bf16[1,1,1,1,1,24,2048]{6,5,4,3,2,1,0:T(8,128)(2,1)S(1)}, u32[]{:S(2)}, u32[]{:S(2)}) collective-permute-start(bf16[1,1,1,1,1,24,2048]{6,5,4,3,2,1,0:T(8,128)(2,1)S(1)} %get-tuple-element.26), channel_id=1, source_target_pairs={{0,1},{1,0},{2,3},{3,2},{4,5},{5,4},{6,7},{7,6},{8,9},{9,8},{10,11... | collective-permute-start | bytes 294920 | tf_op jit(solution)/shard_map/ppermute | solution.py:190
  103.2 7.3 %collective-permute-start.9 = (bf16[1,2,1,1,1,24,2048]{6,5,4,3,2,1,0:T(8,128)(2,1)S(1)}, bf16[1,2,1,1,1,24,2048]{6,5,4,3,2,1,0:T(8,128)(2,1)S(1)}, u32[]{:S(2)}, u32[]{:S(2)}) collective-permute-start(bf16[1,2,1,1,1,24,2048]{6,5,4,3,2,1,0:T(8,128)(2,1)S(1)} %maximum_select_fusion.7), channel_id=1, source_target_pairs={{0,2},{1,3},{2,0},{3,1},{4,6},{5,7},{6,4},{7,5},{8,10},{9,11},{10,... | collective-permute-start | bytes 589832 | tf_op jit(solution)/shard_map/ppermute | solution.py:190
  110.6 10.5 %collective-permute-start.10 = (bf16[2,2,1,1,1,24,2048]{6,5,4,3,2,1,0:T(8,128)(2,1)S(1)}, bf16[2,2,1,1,1,24,2048]{6,5,4,3,2,1,0:T(8,128)(2,1)S(1)}, u32[]{:S(2)}, u32[]{:S(2)}) collective-permute-start(bf16[2,2,1,1,1,24,2048]{6,5,4,3,2,1,0:T(8,128)(2,1)S(1)} %fusion.25), channel_id=1, source_target_pairs={{0,128},{32,160},{64,192},{96,224},{128,0},{160,32},{192,64},{224,... | collective-permute-start | bytes 1179656 | tf_op jit(solution)/shard_map/ppermute | solution.py:190
  121.3 15.8 %collective-permute-start.11 = (bf16[2,2,2,1,1,24,2048]{6,5,4,3,2,1,0:T(8,128)(2,1)S(1)}, bf16[2,2,2,1,1,24,2048]{6,5,4,3,2,1,0:T(8,128)(2,1)S(1)}, u32[]{:S(2)}, u32[]{:S(2)}) collective-permute-start(bf16[2,2,2,1,1,24,2048]{6,5,4,3,2,1,0:T(8,128)(2,1)S(1)} %maximum_select_fusion.3), channel_id=1, source_target_pairs={{0,64},{32,96},{64,0},{96,32},{128,192},{160,224},{192,128},{224,1... | collective-permute-start | bytes 2359304 | tf_op jit(solution)/shard_map/ppermute | solution.py:190
  137.2 3.6 %collective-permute-start.12 = (bf16[2,2,2,2,1,24,2048]{6,5,4,3,2,1,0:T(8,128)(2,1)S(1)}, bf16[2,2,2,2,1,24,2048]{6,5,4,3,2,1,0:T(8,128)(2,1)}, u32[]{:S(2)}, u32[]{:S(2)}) collective-permute-start(bf16[2,2,2,2,1,24,2048]{6,5,4,3,2,1,0:T(8,128)(2,1)S(1)} %maximum_select_fusion), channel_id=1, source_target_pairs={{0,32},{32,0},{64,96},{96,64},{128,160},{160,128},{192,224},{224,1... | collective-permute-start | bytes 4718600 | tf_op jit(solution)/shard_map/ppermute | solution.py:190
  161.8 5.2 %collective-permute-start.13 = (f32[4,2,192]{2,1,0:T(2,128)S(1)}, f32[4,2,192]{2,1,0:T(2,128)S(1)}, u32[]{:S(2)}, u32[]{:S(2)}) collective-permute-start(f32[4,2,192]{2,1,0:T(2,128)S(1)} %constant_dynamic-slice_fusion.1), channel_id=1, source_target_pairs={{0,2},{1,3},{2,0},{3,1},{4,6},{5,7},{6,4},{7,5},{8,10},{9,11},{10,... | collective-permute-start | bytes 18440 | tf_op jit(solution)/shard_map/ppermute | solution.py:231
  167.1 3.7 %collective-permute-start.14 = (f32[4,1,192]{2,1,0:T(1,128)S(1)}, f32[4,1,192]{2,1,0:T(1,128)S(1)}, u32[]{:S(2)}, u32[]{:S(2)}) collective-permute-start(f32[4,1,192]{2,1,0:T(1,128)S(1)} %constant_dynamic-slice_fusion), channel_id=1, source_target_pairs={{0,1},{1,0},{2,3},{3,2},{4,5},{5,4},{6,7},{7,6},{8,9},{9,8},{10,11... | collective-permute-start | bytes 9224 | tf_op jit(solution)/shard_map/ppermute | solution.py:239
  172.6 1.2 collective-permute-start.15
  173.8 3.7 %collective-permute-start.16 = (f32[4,192]{1,0:T(4,128)S(1)}, f32[4,192]{1,0:T(4,128)S(1)}, u32[]{:S(2)}, u32[]{:S(2)}) collective-permute-start(f32[4,192]{1,0:T(4,128)S(1)} %pad_maximum_fusion.5), channel_id=1, source_target_pairs={{0,64},{32,96},{64,0},{96,32},{128,192},{160,224},{192,128},{224,1... | collective-permute-start | bytes 9224 | tf_op jit(solution)/shard_map/ppermute | solution.py:244
  177.6 5.2 %collective-permute-start.17 = (f32[4,192]{1,0:T(4,128)S(1)}, f32[4,192]{1,0:T(4,128)S(1)}, u32[]{:S(2)}, u32[]{:S(2)}) collective-permute-start(f32[4,192]{1,0:T(4,128)S(1)} %pad_maximum_fusion.6), channel_id=1, source_target_pairs={{0,128},{32,160},{64,192},{96,224},{128,0},{160,32},{192,64},{224,... | collective-permute-start | bytes 9224 | tf_op jit(solution)/shard_map/ppermute | solution.py:244
Sparse Core Ops, SparseCore 0:
  49.5 82.2 all-gather.1
